TPU v7x, 32 devices: a whole 2x2x4 slice. The times are simulated.
32 devices in a mesh: real: 2 (over y), gx: 4 (over z), gy: 2 (over x), gz: 2 (over core).
Axes of the slice: x: 2, y: 2, z: 4, core: 2. Of those that a mesh axis runs over, the one named last changes fastest.
Arguments:
- log_noise: float32 [64, 128, 256], P(('real', 'gz'), 'gx', 'gy'), parts along dimension 0, may hold values from -3 to 3
- facies: int32 [64, 128, 256], P(('real', 'gz'), 'gx', 'gy'), parts along dimension 0, may hold values from 0 to 3
- facies_table: float32 [3, 4], replicated, may hold values from -1 to 1
- pressure_old: float32 [8, 4, 8], P(('real', 'gz'), 'gx', 'gy'), parts along dimension 0, may hold values from -6 to 6
- accumulation: float32 [8, 4, 8], P(('real', 'gz'), 'gx', 'gy'), parts along dimension 0, may hold values from 100 to 1000
- source: float32 [8, 4, 8], P(('real', 'gz'), 'gx', 'gy'), parts along dimension 0, may hold values from -600 to 600
Outputs:
- coarse_pressure: float32 [8, 4, 8], P(('real', 'gz'), 'gx', 'gy'), parts along dimension 0
- upscaled: float32 [3, 8, 4, 8], P(None, ('real', 'gz'), 'gx', 'gy'), parts along dimension 1
There are 2 independent parts, one for each index of `real`. A program takes and returns all parts, laid end to end along the dimension named above; an argument that names none is the same for every part. Nothing has to cross between parts.
All inputs are finite; a program needn't handle non-finite values.
Results may differ from a plain program's by a relative error of at most 0.0003.
Values sent between devices are 32-bit elements; how exact they have to be, the bound alone decides.
No kernel may reach another device: no remote copies, remote signals or barrier semaphores. Data moves between devices by JAX's collectives and lax.ppermute only.
A program may use at most 64 MiB of HBM per device.

v0:
```python
import jax
import jax.numpy as jnp
from jax import lax
from jax.sharding import PartitionSpec as P
from jax.experimental import pallas as pl
from jax.experimental.pallas import tpu as pltpu

NFAC = 4
CCX = 32
CCY = 32
CCZ = 8
RIM = 4
SWEEPS = 3


BOUND_MID = 1.0
BOUND_HALF = 0.9


def extended(cells, sides, width):
    for axis, dim in sides:
        count = lax.axis_size(axis)
        ends = count - 1
        head = lax.slice_in_dim(cells, 0, width, axis=dim)
        tail = lax.slice_in_dim(cells, cells.shape[dim] - width, cells.shape[dim], axis=dim)
        cells = jnp.concatenate(
            [
                lax.ppermute(tail, axis, [(i, (i + 1) % count) for i in range(ends)]),
                cells,
                lax.ppermute(head, axis, [((i + 1) % count, i) for i in range(ends)]),
            ],
            axis=dim,
        )
    return cells


def raise_flat(values, offset):
    zeros_block = jnp.zeros(values.shape[:-1] + (offset,), values.dtype)
    return jnp.concatenate([values[..., offset:], zeros_block], axis=-1)


def lower_flat(values, offset):
    zeros_block = jnp.zeros(values.shape[:-1] + (offset,), values.dtype)
    return jnp.concatenate([zeros_block, values[..., :-offset]], axis=-1)


def raise_depth(values):
    zeros_block = jnp.zeros(values.shape[:1] + (1,) + values.shape[2:], values.dtype)
    return jnp.concatenate([values[:, 1:], zeros_block], axis=1)


def lower_depth(values):
    zeros_block = jnp.zeros(values.shape[:1] + (1,) + values.shape[2:], values.dtype)
    return jnp.concatenate([zeros_block, values[:, :-1]], axis=1)


def log_fields(log_noise, facies, facies_table):
    base_log = log_noise
    extra_y = jnp.zeros_like(log_noise)
    extra_z = jnp.zeros_like(log_noise)
    for code_value in range(NFAC):
        matched = facies == code_value
        base_log = base_log + jnp.where(matched, facies_table[0, code_value], jnp.float32(0.0))
        extra_y = extra_y + jnp.where(matched, facies_table[1, code_value], jnp.float32(0.0))
        extra_z = extra_z + jnp.where(matched, facies_table[2, code_value], jnp.float32(0.0))
    return (base_log, base_log + extra_y, base_log + extra_z)


def upscale(perm_logs, inside):
    span_z = CCZ + 2 * RIM
    span_x = CCX + 2 * RIM
    span_y = CCY + 2 * RIM
    depth_pos = lax.broadcasted_iota(jnp.int32, (1, span_z, 1), 1)
    flat_pos = lax.broadcasted_iota(jnp.int32, (1, 1, span_x * span_y), 2)
    column_pos = flat_pos // span_y
    row_pos = flat_pos % span_y
    perm_x = jnp.exp(perm_logs[0])
    perm_y = jnp.exp(perm_logs[1])
    perm_z = jnp.exp(perm_logs[2])

    def links(perm, other_perm, other_inside):
        return inside * other_inside * 2.0 * perm * other_perm / (perm + other_perm)

    link_x = links(perm_x, raise_flat(perm_x, span_y), raise_flat(inside, span_y))
    link_y = links(perm_y, raise_flat(perm_y, 1), raise_flat(inside, 1)) * (
        row_pos < span_y - 1
    ).astype(jnp.float32)
    link_z = links(perm_z, raise_depth(perm_z), raise_depth(inside))
    diagonal = (
        link_x
        + lower_flat(link_x, span_y)
        + link_y
        + lower_flat(link_y, 1)
        + link_z
        + lower_depth(link_z)
    )

    def apply_operator(field):
        beside = link_x * raise_flat(field, span_y) + lower_flat(link_x * field, span_y)
        beside = beside + link_y * raise_flat(field, 1) + lower_flat(link_y * field, 1)
        beside = beside + link_z * raise_depth(field) + lower_depth(link_z * field)
        return diagonal * field - beside

    interior = (
        (depth_pos >= 1)
        & (depth_pos <= span_z - 2)
        & (column_pos >= 1)
        & (column_pos <= span_x - 2)
        & (row_pos >= 1)
        & (row_pos <= span_y - 2)
    )
    unknown = inside * interior.astype(jnp.float32)
    scaling = unknown / (diagonal + 1.0 - unknown)
    core_z = (depth_pos >= RIM) & (depth_pos < RIM + CCZ)
    core_x = (column_pos >= RIM) & (column_pos < RIM + CCX)
    core_y = (row_pos >= RIM) & (row_pos < RIM + CCY)
    face_x = (((column_pos == RIM - 1) | (column_pos == RIM + CCX - 1)) & core_z & core_y).astype(
        jnp.float32
    )
    face_y = (((row_pos == RIM - 1) | (row_pos == RIM + CCY - 1)) & core_z & core_x).astype(
        jnp.float32
    )
    face_z = (((depth_pos == RIM - 1) | (depth_pos == RIM + CCZ - 1)) & core_x & core_y).astype(
        jnp.float32
    )
    ramp_x = ((span_x - 1) / 2.0 - column_pos).astype(jnp.float32)
    ramp_y = ((span_y - 1) / 2.0 - row_pos).astype(jnp.float32)
    ramp_z = ((span_z - 1) / 2.0 - depth_pos).astype(jnp.float32)
    cheb_ratio = BOUND_MID / BOUND_HALF
    results = []
    cases = (
        (ramp_x, link_x, face_x, CCY * CCZ, 0),
        (ramp_y, link_y, face_y, CCX * CCZ, 1),
        (ramp_z, link_z, face_z, CCX * CCY, 2),
    )
    for ramp, link, face, area, direction in cases:
        ramp_full = jnp.broadcast_to(ramp, inside.shape)
        source_term = -unknown * apply_operator(ramp_full)
        update = scaling * source_term / BOUND_MID
        solution = update
        rho_old = 1.0 / cheb_ratio
        for sweep_index in range(SWEEPS - 1):
            residual = source_term - apply_operator(solution)
            rho_new = 1.0 / (2.0 * cheb_ratio - rho_old)
            update = rho_new * rho_old * update + 2.0 * rho_new / BOUND_HALF * (scaling * residual)
            solution = solution + update
            rho_old = rho_new
        pressure = ramp_full + solution
        if direction == 0:
            upper = raise_flat(pressure, span_y)
        elif direction == 1:
            upper = raise_flat(pressure, 1)
        else:
            upper = raise_depth(pressure)
        flux = link * (pressure - upper) * face
        results.append(jnp.sum(flux, axis=(1, 2)) * (0.5 / area))
    return jnp.stack(results)


LANES = 128


def window_kernel(w_ref, o_ref):
    span_z = CCZ + 2 * RIM
    span_x = CCX + 2 * RIM
    span_y = CCY + 2 * RIM
    shape = (span_z, span_x, LANES)
    log_x = w_ref[0, 0]
    log_y = w_ref[0, 1]
    log_z = w_ref[0, 2]
    inside = w_ref[0, 3]
    depth_pos = lax.broadcasted_iota(jnp.int32, shape, 0)
    column_pos = lax.broadcasted_iota(jnp.int32, shape, 1)
    row_pos = lax.broadcasted_iota(jnp.int32, shape, 2)
    perm_x = jnp.exp(log_x)
    perm_y = jnp.exp(log_y)
    perm_z = jnp.exp(log_z)

    def up_x(v):
        return pltpu.roll(v, span_x - 1, 1)

    def down_x(v):
        return pltpu.roll(v, 1, 1)

    def up_y(v):
        return pltpu.roll(v, LANES - 1, 2)

    def down_y(v):
        return pltpu.roll(v, 1, 2)

    def up_z(v):
        return jnp.concatenate([v[1:], v[:1]], axis=0)

    def down_z(v):
        return jnp.concatenate([v[-1:], v[:-1]], axis=0)

    def links(perm, other_perm, other_inside, valid):
        value = inside * other_inside * 2.0 * perm * other_perm / (perm + other_perm)
        return jnp.where(valid, value, 0.0)

    link_x = links(perm_x, up_x(perm_x), up_x(inside), column_pos < span_x - 1)
    link_y = links(perm_y, up_y(perm_y), up_y(inside), row_pos < span_y - 1)
    link_z = links(perm_z, up_z(perm_z), up_z(inside), depth_pos < span_z - 1)
    diagonal = link_x + down_x(link_x) + link_y + down_y(link_y) + link_z + down_z(link_z)

    def apply_operator(field):
        beside = link_x * up_x(field) + down_x(link_x * field)
        beside = beside + link_y * up_y(field) + down_y(link_y * field)
        beside = beside + link_z * up_z(field) + down_z(link_z * field)
        return diagonal * field - beside

    interior = (
        (depth_pos >= 1)
        & (depth_pos <= span_z - 2)
        & (column_pos >= 1)
        & (column_pos <= span_x - 2)
        & (row_pos >= 1)
        & (row_pos <= span_y - 2)
    )
    unknown = jnp.where(interior, inside, 0.0)
    scaling = unknown / (diagonal + 1.0 - unknown)
    core_z = (depth_pos >= RIM) & (depth_pos < RIM + CCZ)
    core_x = (column_pos >= RIM) & (column_pos < RIM + CCX)
    core_y = (row_pos >= RIM) & (row_pos < RIM + CCY)
    face_x = ((column_pos == RIM - 1) | (column_pos == RIM + CCX - 1)) & core_z & core_y
    face_y = ((row_pos == RIM - 1) | (row_pos == RIM + CCY - 1)) & core_z & core_x
    face_z = ((depth_pos == RIM - 1) | (depth_pos == RIM + CCZ - 1)) & core_x & core_y
    ramp_x = ((span_x - 1) / 2.0 - column_pos).astype(jnp.float32)
    ramp_y = ((span_y - 1) / 2.0 - row_pos).astype(jnp.float32)
    ramp_z = ((span_z - 1) / 2.0 - depth_pos).astype(jnp.float32)
    cheb_ratio = BOUND_MID / BOUND_HALF
    cases = (
        (ramp_x, link_x, face_x, CCY * CCZ, up_x),
        (ramp_y, link_y, face_y, CCX * CCZ, up_y),
        (ramp_z, link_z, face_z, CCX * CCY, up_z),
    )
    rows = []
    for ramp, link, face, area, upper_of in cases:
        source_term = -unknown * apply_operator(ramp)
        update = scaling * source_term / BOUND_MID
        solution = update
        rho_old = 1.0 / cheb_ratio
        for sweep_index in range(SWEEPS - 1):
            residual = source_term - apply_operator(solution)
            rho_new = 1.0 / (2.0 * cheb_ratio - rho_old)
            update = rho_new * rho_old * update + 2.0 * rho_new / BOUND_HALF * (scaling * residual)
            solution = solution + update
            rho_old = rho_new
        pressure = ramp + solution
        flux = jnp.where(face, link * (pressure - upper_of(pressure)), 0.0)
        total = jnp.sum(flux, axis=0)
        total = jnp.sum(total, axis=0, keepdims=True)
        total = jnp.sum(total, axis=1, keepdims=True)
        rows.append(jnp.broadcast_to(total * (0.5 / area), (1, LANES)))
    rows.append(jnp.zeros((8 - len(rows), LANES), jnp.float32))
    o_ref[0] = jnp.concatenate(rows, axis=0)


def upscale_windows(fields):
    span_z = CCZ + 2 * RIM
    span_x = CCX + 2 * RIM
    span_y = CCY + 2 * RIM
    count_z = (fields.shape[1] - 2 * RIM) // CCZ
    count_x = (fields.shape[2] - 2 * RIM) // CCX
    count_y = (fields.shape[3] - 2 * RIM) // CCY
    pieces = []
    for block_z in range(count_z):
        for block_x in range(count_x):
            for block_y in range(count_y):
                piece = fields[
                    :,
                    block_z * CCZ : block_z * CCZ + span_z,
                    block_x * CCX : block_x * CCX + span_x,
                    block_y * CCY : block_y * CCY + span_y,
                ]
                pieces.append(piece)
    windows = jnp.stack(pieces)
    windows = jnp.pad(windows, ((0, 0),) * 4 + ((0, LANES - span_y),))
    count = windows.shape[0]
    sums = pl.pallas_call(
        window_kernel,
        grid=(count,),
        in_specs=[pl.BlockSpec((1, 4, span_z, span_x, LANES), lambda i: (i, 0, 0, 0, 0))],
        out_specs=pl.BlockSpec((1, 8, LANES), lambda i: (i, 0, 0)),
        out_shape=jax.ShapeDtypeStruct((count, 8, LANES), jnp.float32),
    )(windows)
    return sums[:, :3, 0].T.reshape((3, count_z, count_x, count_y))


def coarse_sweep(perm_pad, press_pad, inside_pad, accumulation, fixed):
    centre = (slice(1, -1), slice(1, -1), slice(1, -1))
    factors = (CCY * CCZ / CCX, CCX * CCZ / CCY, CCX * CCY / CCZ)
    numer = fixed
    denom = accumulation
    for component, axis_dim in ((0, 1), (1, 2), (2, 0)):
        for offset in (-1, 1):
            window_slice = [slice(1, -1), slice(1, -1), slice(1, -1)]
            window_slice[axis_dim] = slice(1 + offset, press_pad.shape[axis_dim] - 1 + offset)
            beside = tuple(window_slice)
            link = (
                factors[component]
                * 0.5
                * (perm_pad[component][centre] + perm_pad[component][beside])
                * inside_pad[beside]
            )
            numer = numer + link * press_pad[beside]
            denom = denom + jnp.abs(link)
    return numer / denom


def span_mask(anchor, length, total, margin):
    coords = anchor - margin + jnp.arange(length + 2 * margin, dtype=jnp.int32)
    return ((coords >= 0) & (coords < total)).astype(jnp.float32)


def cut_windows(fields):
    span_z = CCZ + 2 * RIM
    span_x = CCX + 2 * RIM
    span_y = CCY + 2 * RIM
    count_z = (fields[0].shape[0] - 2 * RIM) // CCZ
    count_x = (fields[0].shape[1] - 2 * RIM) // CCX
    count_y = (fields[0].shape[2] - 2 * RIM) // CCY
    stacks = []
    for field in fields:
        pieces = []
        for block_z in range(count_z):
            for block_y in range(count_y):
                piece = field[
                    block_z * CCZ : block_z * CCZ + span_z,
                    0:span_x,
                    block_y * CCY : block_y * CCY + span_y,
                ]
                pieces.append(piece.reshape(span_z, span_x * span_y))
        stacks.append(jnp.stack(pieces))
    return (stacks, (count_z, count_x, count_y))


def faces(block, sides):
    got = []
    for axis, dim in sides:
        count = lax.axis_size(axis)
        ends = count - 1
        head = lax.slice_in_dim(block, 0, 1, axis=dim)
        tail = lax.slice_in_dim(block, block.shape[dim] - 1, block.shape[dim], axis=dim)
        lower = lax.ppermute(tail, axis, [(i, i + 1) for i in range(ends)])
        upper = lax.ppermute(head, axis, [(i + 1, i) for i in range(ends)])
        got.append((lower, upper))
    return got


def neighbour_views(block, got, dim_of):
    views = []
    for (lower, upper), dim in zip(got, dim_of):
        size = block.shape[dim]
        below = jnp.concatenate([lower, lax.slice_in_dim(block, 0, size - 1, axis=dim)], axis=dim)
        above = jnp.concatenate([lax.slice_in_dim(block, 1, size, axis=dim), upper], axis=dim)
        views.append((below, above))
    return views


def coarse_step(upscaled, views, inside_views, pressure, accumulation, fixed):
    factors = (CCY * CCZ / CCX, CCX * CCZ / CCY, CCX * CCY / CCZ)
    numer = fixed
    denom = accumulation
    for component in range(3):
        for side in range(2):
            beside = views[component][side]
            link = factors[component] * 0.5 * (upscaled[component] + beside[component]) * inside_views[component][side]
            numer = numer + link * pressure[component][side]
            denom = denom + jnp.abs(link)
    return numer / denom


def local(log_noise, facies, facies_table, pressure_old, accumulation, source):
    depth_len, rows_len, cols_len = log_noise.shape
    size_z = lax.axis_size("gz")
    size_x = lax.axis_size("gx")
    size_y = lax.axis_size("gy")
    index_z = lax.axis_index("gz")
    index_x = lax.axis_index("gx")
    index_y = lax.axis_index("gy")
    raw = jnp.stack([log_noise, facies.astype(jnp.float32)])
    raw = extended(raw, (("gx", 2), ("gy", 3), ("gz", 1)), RIM)
    log_x, log_y, log_z = log_fields(raw[0], raw[1], facies_table)
    anchor_z = index_z * depth_len
    anchor_y = index_y * cols_len
    anchor_x = index_x * rows_len
    mask_z = span_mask(anchor_z, log_x.shape[0] - 2 * RIM, depth_len * size_z, RIM)
    mask_x = span_mask(anchor_x, log_x.shape[1] - 2 * RIM, rows_len * size_x, RIM)
    mask_y = span_mask(anchor_y, log_x.shape[2] - 2 * RIM, cols_len * size_y, RIM)
    inside = mask_z[:, None, None] * mask_x[None, :, None] * mask_y[None, None, :]
    upscaled = upscale_windows(jnp.stack([log_x, log_y, log_z, inside]))
    fixed = accumulation * pressure_old + source
    ones = jnp.ones_like(pressure_old)
    bundle = jnp.stack([upscaled[0], upscaled[1], upscaled[2], pressure_old, ones])
    sides = (("gx", 2), ("gy", 3), ("gz", 1))
    dim_of = (2, 3, 1)
    views = neighbour_views(bundle, faces(bundle, sides), dim_of)
    inside_views = [(below[4], above[4]) for below, above in views]
    perm_views = [(below[:3], above[:3]) for below, above in views]
    press_views = [(below[3], above[3]) for below, above in views]
    pressure = coarse_step(upscaled, perm_views, inside_views, press_views, accumulation, fixed)
    got = faces(pressure, (("gx", 1), ("gy", 2), ("gz", 0)))
    press_views = neighbour_views(pressure, got, (1, 2, 0))
    pressure = coarse_step(upscaled, perm_views, inside_views, press_views, accumulation, fixed)
    return (pressure, upscaled)


def solution(mesh):
    placed = (
        P(("real", "gz"), "gx", "gy"),
        P(("real", "gz"), "gx", "gy"),
        P(),
        P(("real", "gz"), "gx", "gy"),
        P(("real", "gz"), "gx", "gy"),
        P(("real", "gz"), "gx", "gy"),
    )
    return jax.shard_map(
        local,
        mesh=mesh,
        in_specs=placed,
        out_specs=(P(("real", "gz"), "gx", "gy"), P(None, ("real", "gz"), "gx", "gy")),
        check_vma=False,
    )
```

profile of v0, /device:TPU:0, one launch (start us, length us, event | category | flops | bytes accessed | tf_op | source)
XLA Modules:
  0.0 103.5 jit_solution(3563389714492036063)
XLA Ops:
  0.6 1.0 convert_bitcast_fusion
  2.6 4.9 %collective-permute-start = (f32[2,16,4,128]{3,2,1,0:T(4,128)S(1)}, f32[2,16,4,128]{3,2,1,0:T(4,128)S(1)}, u32[]{:S(2)}, u32[]{:S(2)}) collective-permute-start(f32[2,16,4,128]{3,2,1,0:T(4,128)S(1)} %get-tuple-element.19), channel_id=1, source_target_pairs={{0,4},{4,8},{8,12},{1,5},{5,9},{9,13},{2,6},{6,10},{10,14},{3,7},{... | collective-permute-start | bytes 196616 | tf_op jit(solution)/shard_map/ppermute | solution.py:28
  7.5 1.3 %collective-permute-start.1 = (f32[2,16,4,128]{3,2,1,0:T(4,128)S(1)}, f32[2,16,4,128]{3,2,1,0:T(4,128)S(1)}, u32[]{:S(2)}, u32[]{:S(2)}) collective-permute-start(f32[2,16,4,128]{3,2,1,0:T(4,128)S(1)} %get-tuple-element.20), channel_id=1, source_target_pairs={{4,0},{8,4},{12,8},{5,1},{9,5},{13,9},{6,2},{10,6},{14,10},{7,3},{... | collective-permute-start | bytes 196616 | tf_op jit(solution)/shard_map/ppermute | solution.py:30
  8.8 1.8 %fusion.64 = (f32[1,1]{1,0:T(1,128)}, f32[1,1]{1,0:T(1,128)}, f32[1,1]{1,0:T(1,128)}, f32[1,1]{1,0:T(1,128)}, f32[1,1]{1,0:T(1,128)}, /*index=5*/f32[1,1]{1,0:T(...) fusion(f32[3,4]{1,0:T(4,128)} %param.8), kind=kLoop, calls=%fused_computation.129 | loop fusion | bytes 96 | tf_op jit(solution)/shard_map/slice | solution.py:65
  10.7 3.0 %collective-permute-done.1 = f32[2,16,4,128]{3,2,1,0:T(4,128)S(1)} collective-permute-done((f32[2,16,4,128]{3,2,1,0:T(4,128)S(1)}, f32[2,16,4,128]{3,2,1,0:T(4,128)S(1)}, u32[]{:S(2)}, u32[]{:S(2)}) %collective-permute-start.1) | collective-permute-done | bytes 65568 | tf_op jit(solution)/shard_map/ppermute | solution.py:30
  13.7 1.0 pad_maximum_fusion.2
  15.5 1.3 %collective-permute-start.3 = (f32[2,16,40,4]{2,1,3,0:T(8,128)S(1)}, f32[2,16,40,4]{2,1,3,0:T(8,128)S(1)}, u32[]{:S(2)}, u32[]{:S(2)}) collective-permute-start(f32[2,16,40,4]{2,1,3,0:T(8,128)S(1)} %copy.19), channel_id=1, source_target_pairs={{2,0},{3,1},{6,4},{7,5},{10,8},{11,9},{14,12},{15,13},{18,16},{19,... | collective-permute-start | bytes 61448 | tf_op jit(solution)/shard_map/ppermute | solution.py:30
  16.8 4.5 %collective-permute-start.2 = (f32[2,16,40,4]{2,1,3,0:T(8,128)S(1)}, f32[2,16,40,4]{2,1,3,0:T(8,128)S(1)}, u32[]{:S(2)}, u32[]{:S(2)}) collective-permute-start(f32[2,16,40,4]{2,1,3,0:T(8,128)S(1)} %copy.18), channel_id=1, source_target_pairs={{0,2},{1,3},{4,6},{5,7},{8,10},{9,11},{12,14},{13,15},{16,18},{17,... | collective-permute-start | bytes 61448 | tf_op jit(solution)/shard_map/ppermute | solution.py:28
  21.4 1.9 %collective-permute-done.2 = f32[2,16,40,4]{2,1,3,0:T(8,128)S(1)} collective-permute-done((f32[2,16,40,4]{2,1,3,0:T(8,128)S(1)}, f32[2,16,40,4]{2,1,3,0:T(8,128)S(1)}, u32[]{:S(2)}, u32[]{:S(2)}) %collective-permute-start.2) | collective-permute-done | bytes 20512 | tf_op jit(solution)/shard_map/ppermute | solution.py:28
  24.3 1.3 %collective-permute-start.4 = (f32[2,4,40,136]{3,2,1,0:T(8,128)S(1)}, f32[2,4,40,136]{3,2,1,0:T(8,128)S(1)}, u32[]{:S(2)}, u32[]{:S(2)}) collective-permute-start(f32[2,4,40,136]{3,2,1,0:T(8,128)S(1)} %get-tuple-element.15), channel_id=1, source_target_pairs={{0,1},{2,3},{4,5},{6,7},{8,9},{10,11},{12,13},{14,15},{16,17},{18,... | collective-permute-start | bytes 522248 | tf_op jit(solution)/shard_map/ppermute | solution.py:28
  25.6 1.3 %collective-permute-start.5 = (f32[2,4,40,136]{3,2,1,0:T(8,128)S(1)}, f32[2,4,40,136]{3,2,1,0:T(8,128)S(1)}, u32[]{:S(2)}, u32[]{:S(2)}) collective-permute-start(f32[2,4,40,136]{3,2,1,0:T(8,128)S(1)} %get-tuple-element.16), channel_id=1, source_target_pairs={{1,0},{3,2},{5,4},{7,6},{9,8},{11,10},{13,12},{15,14},{17,16},{19,... | collective-permute-start | bytes 522248 | tf_op jit(solution)/shard_map/ppermute | solution.py:30
  26.9 2.1 %collective-permute-done.5 = f32[2,4,40,136]{3,2,1,0:T(8,128)S(1)} collective-permute-done((f32[2,4,40,136]{3,2,1,0:T(8,128)S(1)}, f32[2,4,40,136]{3,2,1,0:T(8,128)S(1)}, u32[]{:S(2)}, u32[]{:S(2)}) %collective-permute-start.5) | collective-permute-done | bytes 174112 | tf_op jit(solution)/shard_map/ppermute | solution.py:30
  29.8 6.1 %add_add_fusion.1 = (f32[1,24,40,136]{3,2,1,0:T(8,128)S(1)}, f32[1,24,40,136]{3,2,1,0:T(8,128)S(1)}, pred[1,24,40,136]{3,2,1,0:T(8,128)(4,1)S(1)}, pred[1,24,40,...) fusion(f32[]{:T(128)} %bitcast.12, f32[]{:T(128)} %bitcast.11, ...), kind=kLoop, calls=%fused_computation.23 | loop fusion | flops 2611200 | bytes 2611232 | tf_op jit(solution)/shard_map/add | solution.py:66
  35.9 3.1 %add_add_fusion = (f32[1,24,40,136]{3,2,1,0:T(8,128)S(1)}, f32[1,24,40,136]{3,2,1,0:T(8,128)S(1)}) fusion(f32[1,24,40,136]{3,2,1,0:T(8,128)S(1)} %get-tuple-element.10, pred[1,24,40,136]{3,2,1,0:T(8,128)(4,1)S(1)} %get-tuple-element.14, pred[1,24,40,136]{3,2,1,0:T(8,128)(4,1)S(1)} %get-tuple-element.13, pred[1,24,40,136]{3,2,1,0:T(8,128)(4,1)S(1)} %get-tuple-element.12, ...), kind=kLoop, calls=%fused_computation.22 | loop fusion | flops 1175040 | bytes 2093360 | tf_op jit(solution)/shard_map/add | solution.py:66
  42.0 4.8 %pad.4.w_ref = f32[8,4,16,40,128]{4,3,2,1,0:T(8,128)} pad(f32[8,4,16,40,40]{4,3,2,1,0:T(8,128)S(1)} %fusion, f32[]{:T(128)} %constant.15.clone.1), padding=0_0x0_0x0_0x0_0x0_88 | pad | bytes 13762564 | tf_op jit(solution)/shard_map/jit(_pad)/pad | solution.py:278
  46.8 16.9 %shard_map.77 = f32[8,8,128]{2,1,0:T(8,128)} custom-call(f32[8,4,16,40,128]{4,3,2,1,0:T(8,128)} %pad.4.w_ref), custom_call_target="tpu_custom_call" | custom-call | tf_op jit(solution)/shard_map/pallas_call | solution.py:280
  65.7 1.3 %collective-permute-start.7 = (f32[5,2,1,4]{3,1,2,0:T(2,128)S(1)}, f32[5,2,1,4]{3,1,2,0:T(2,128)S(1)}, u32[]{:S(2)}, u32[]{:S(2)}) collective-permute-start(f32[5,2,1,4]{3,1,2,0:T(2,128)S(1)} %constant_dynamic-update-slice_fusion), channel_id=1, source_target_pairs={{4,0},{8,4},{12,8},{5,1},{9,5},{13,9},{6,2},{10,6},{14,10},{7,3},{... | collective-permute-start | bytes 488 | tf_op jit(solution)/shard_map/ppermute | solution.py:346
  67.0 4.5 %collective-permute-start.6 = (f32[5,2,1,4]{3,1,2,0:T(2,128)S(1)}, f32[5,2,1,4]{3,1,2,0:T(2,128)S(1)}, u32[]{:S(2)}, u32[]{:S(2)}) collective-permute-start(f32[5,2,1,4]{3,1,2,0:T(2,128)S(1)} %constant_dynamic-update-slice_fusion), channel_id=1, source_target_pairs={{0,4},{4,8},{8,12},{1,5},{5,9},{9,13},{2,6},{6,10},{10,14},{3,7},{... | collective-permute-start | bytes 488 | tf_op jit(solution)/shard_map/ppermute | solution.py:345
  71.8 1.5 %collective-permute-start.10 = (f32[5,1,1,4]{3,1,2,0:T(1,128)S(1)}, f32[5,1,1,4]{3,1,2,0:T(1,128)S(1)}, u32[]{:S(2)}, u32[]{:S(2)}) collective-permute-start(f32[5,1,1,4]{3,1,2,0:T(1,128)S(1)} %get-tuple-element.21), channel_id=1, source_target_pairs={{0,1},{2,3},{4,5},{6,7},{8,9},{10,11},{12,13},{14,15},{16,17},{18,... | collective-permute-start | bytes 248 | tf_op jit(solution)/shard_map/ppermute | solution.py:345
  73.2 1.3 %collective-permute-start.11 = (f32[5,1,1,4]{3,1,2,0:T(1,128)S(1)}, f32[5,1,1,4]{3,1,2,0:T(1,128)S(1)}, u32[]{:S(2)}, u32[]{:S(2)}) collective-permute-start(f32[5,1,1,4]{3,1,2,0:T(1,128)S(1)} %get-tuple-element.22), channel_id=1, source_target_pairs={{1,0},{3,2},{5,4},{7,6},{9,8},{11,10},{13,12},{15,14},{17,16},{19,... | collective-permute-start | bytes 248 | tf_op jit(solution)/shard_map/ppermute | solution.py:346
  74.5 4.3 %collective-permute-start.8 = (f32[5,2,1,1]{3,1,2,0:T(2,128)S(1)}, f32[5,2,1,1]{3,1,2,0:T(2,128)S(1)}, u32[]{:S(2)}, u32[]{:S(2)}) collective-permute-start(f32[5,2,1,1]{3,1,2,0:T(2,128)S(1)} %get-tuple-element.23), channel_id=1, source_target_pairs={{0,2},{1,3},{4,6},{5,7},{8,10},{9,11},{12,14},{13,15},{16,18},{17,... | collective-permute-start | bytes 128 | tf_op jit(solution)/shard_map/ppermute | solution.py:345
  78.8 1.3 %collective-permute-done.8 = f32[5,2,1,1]{3,1,2,0:T(2,128)S(1)} collective-permute-done((f32[5,2,1,1]{3,1,2,0:T(2,128)S(1)}, f32[5,2,1,1]{3,1,2,0:T(2,128)S(1)}, u32[]{:S(2)}, u32[]{:S(2)}) %collective-permute-start.8) | collective-permute-done | bytes 72 | tf_op jit(solution)/shard_map/ppermute | solution.py:345
  80.1 1.3 %collective-permute-start.9 = (f32[5,2,1,1]{3,1,2,0:T(2,128)S(1)}, f32[5,2,1,1]{3,1,2,0:T(2,128)S(1)}, u32[]{:S(2)}, u32[]{:S(2)}) collective-permute-start(f32[5,2,1,1]{3,1,2,0:T(2,128)S(1)} %get-tuple-element.24), channel_id=1, source_target_pairs={{2,0},{3,1},{6,4},{7,5},{10,8},{11,9},{14,12},{15,13},{18,16},{19,... | collective-permute-start | bytes 128 | tf_op jit(solution)/shard_map/ppermute | solution.py:346
  81.4 4.2 %collective-permute-done.9 = f32[5,2,1,1]{3,1,2,0:T(2,128)S(1)} collective-permute-done((f32[5,2,1,1]{3,1,2,0:T(2,128)S(1)}, f32[5,2,1,1]{3,1,2,0:T(2,128)S(1)}, u32[]{:S(2)}, u32[]{:S(2)}) %collective-permute-start.9) | collective-permute-done | bytes 72 | tf_op jit(solution)/shard_map/ppermute | solution.py:346
  85.9 1.3 %collective-permute-start.13 = (f32[2,1,4]{2,0,1:T(2,128)S(1)}, f32[2,1,4]{2,0,1:T(2,128)S(1)}, u32[]{:S(2)}, u32[]{:S(2)}) collective-permute-start(f32[2,1,4]{2,0,1:T(2,128)S(1)} %fusion.14), channel_id=1, source_target_pairs={{4,0},{8,4},{12,8},{5,1},{9,5},{13,9},{6,2},{10,6},{14,10},{7,3},{... | collective-permute-start | bytes 104 | tf_op jit(solution)/shard_map/ppermute | solution.py:346
  87.2 4.5 %collective-permute-start.12 = (f32[2,1,4]{2,0,1:T(2,128)S(1)}, f32[2,1,4]{2,0,1:T(2,128)S(1)}, u32[]{:S(2)}, u32[]{:S(2)}) collective-permute-start(f32[2,1,4]{2,0,1:T(2,128)S(1)} %fusion.14), channel_id=1, source_target_pairs={{0,4},{4,8},{8,12},{1,5},{5,9},{9,13},{2,6},{6,10},{10,14},{3,7},{... | collective-permute-start | bytes 104 | tf_op jit(solution)/shard_map/ppermute | solution.py:345
  91.8 1.3 %collective-permute-start.16 = (f32[1,1,4]{2,0,1:T(1,128)S(1)}, f32[1,1,4]{2,0,1:T(1,128)S(1)}, u32[]{:S(2)}, u32[]{:S(2)}) collective-permute-start(f32[1,1,4]{2,0,1:T(1,128)S(1)} %get-tuple-element.42), channel_id=1, source_target_pairs={{0,1},{2,3},{4,5},{6,7},{8,9},{10,11},{12,13},{14,15},{16,17},{18,... | collective-permute-start | bytes 56 | tf_op jit(solution)/shard_map/ppermute | solution.py:345
  93.1 1.3 %collective-permute-start.17 = (f32[1,1,4]{2,0,1:T(1,128)S(1)}, f32[1,1,4]{2,0,1:T(1,128)S(1)}, u32[]{:S(2)}, u32[]{:S(2)}) collective-permute-start(f32[1,1,4]{2,0,1:T(1,128)S(1)} %get-tuple-element.43), channel_id=1, source_target_pairs={{1,0},{3,2},{5,4},{7,6},{9,8},{11,10},{13,12},{15,14},{17,16},{19,... | collective-permute-start | bytes 56 | tf_op jit(solution)/shard_map/ppermute | solution.py:346
  94.4 1.3 %collective-permute-start.15 = (f32[2,1,1]{2,0,1:T(2,128)S(1)}, f32[2,1,1]{2,0,1:T(2,128)S(1)}, u32[]{:S(2)}, u32[]{:S(2)}) collective-permute-start(f32[2,1,1]{2,0,1:T(2,128)S(1)} %get-tuple-element.46), channel_id=1, source_target_pairs={{2,0},{3,1},{6,4},{7,5},{10,8},{11,9},{14,12},{15,13},{18,16},{19,... | collective-permute-start | bytes 32 | tf_op jit(solution)/shard_map/ppermute | solution.py:346
  95.7 4.2 %collective-permute-done.15 = f32[2,1,1]{2,0,1:T(2,128)S(1)} collective-permute-done((f32[2,1,1]{2,0,1:T(2,128)S(1)}, f32[2,1,1]{2,0,1:T(2,128)S(1)}, u32[]{:S(2)}, u32[]{:S(2)}) %collective-permute-start.15) | collective-permute-done | bytes 40 | tf_op jit(solution)/shard_map/ppermute | solution.py:346
  99.8 1.6 %collective-permute-start.14 = (f32[2,1,1]{2,0,1:T(2,128)S(1)}, f32[2,1,1]{2,0,1:T(2,128)S(1)}, u32[]{:S(2)}, u32[]{:S(2)}) collective-permute-start(f32[2,1,1]{2,0,1:T(2,128)S(1)} %get-tuple-element.47), channel_id=1, source_target_pairs={{0,2},{1,3},{4,6},{5,7},{8,10},{9,11},{12,14},{13,15},{16,18},{17,... | collective-permute-start | bytes 32 | tf_op jit(solution)/shard_map/ppermute | solution.py:345
  101.5 1.3 %collective-permute-done.14 = f32[2,1,1]{2,0,1:T(2,128)S(1)} collective-permute-done((f32[2,1,1]{2,0,1:T(2,128)S(1)}, f32[2,1,1]{2,0,1:T(2,128)S(1)}, u32[]{:S(2)}, u32[]{:S(2)}) %collective-permute-start.14) | collective-permute-done | bytes 40 | tf_op jit(solution)/shard_map/ppermute | solution.py:345
  (63 shorter events, 9.6 us)
Async XLA Ops:
  0.6 23.2 %copy-start = (f32[16,32,128]{2,1,0:T(8,128)S(1)}, f32[16,32,128]{2,1,0:T(8,128)}, u32[]{:S(2)}) copy-start(f32[16,32,128]{2,1,0:T(8,128)} %param.6) | copy-start | bytes 786436
  2.6 8.1 %collective-permute-start = (f32[2,16,4,128]{3,2,1,0:T(4,128)S(1)}, f32[2,16,4,128]{3,2,1,0:T(4,128)S(1)}, u32[]{:S(2)}, u32[]{:S(2)}) collective-permute-start(f32[2,16,4,128]{3,2,1,0:T(4,128)S(1)} %get-tuple-element.19), channel_id=1, source_target_pairs={{0,4},{4,8},{8,12},{1,5},{5,9},{9,13},{2,6},{6,10},{10,14},{3,7},{... | collective-permute-start | bytes 196616 | tf_op jit(solution)/shard_map/ppermute | solution.py:28
  7.5 6.2 %collective-permute-start.1 = (f32[2,16,4,128]{3,2,1,0:T(4,128)S(1)}, f32[2,16,4,128]{3,2,1,0:T(4,128)S(1)}, u32[]{:S(2)}, u32[]{:S(2)}) collective-permute-start(f32[2,16,4,128]{3,2,1,0:T(4,128)S(1)} %get-tuple-element.20), channel_id=1, source_target_pairs={{4,0},{8,4},{12,8},{5,1},{9,5},{13,9},{6,2},{10,6},{14,10},{7,3},{... | collective-permute-start | bytes 196616 | tf_op jit(solution)/shard_map/ppermute | solution.py:30
  15.5 8.1 %collective-permute-start.3 = (f32[2,16,40,4]{2,1,3,0:T(8,128)S(1)}, f32[2,16,40,4]{2,1,3,0:T(8,128)S(1)}, u32[]{:S(2)}, u32[]{:S(2)}) collective-permute-start(f32[2,16,40,4]{2,1,3,0:T(8,128)S(1)} %copy.19), channel_id=1, source_target_pairs={{2,0},{3,1},{6,4},{7,5},{10,8},{11,9},{14,12},{15,13},{18,16},{19,... | collective-permute-start | bytes 61448 | tf_op jit(solution)/shard_map/ppermute | solution.py:30
  16.8 6.4 %collective-permute-start.2 = (f32[2,16,40,4]{2,1,3,0:T(8,128)S(1)}, f32[2,16,40,4]{2,1,3,0:T(8,128)S(1)}, u32[]{:S(2)}, u32[]{:S(2)}) collective-permute-start(f32[2,16,40,4]{2,1,3,0:T(8,128)S(1)} %copy.18), channel_id=1, source_target_pairs={{0,2},{1,3},{4,6},{5,7},{8,10},{9,11},{12,14},{13,15},{16,18},{17,... | collective-permute-start | bytes 61448 | tf_op jit(solution)/shard_map/ppermute | solution.py:28
  24.3 2.7 %collective-permute-start.4 = (f32[2,4,40,136]{3,2,1,0:T(8,128)S(1)}, f32[2,4,40,136]{3,2,1,0:T(8,128)S(1)}, u32[]{:S(2)}, u32[]{:S(2)}) collective-permute-start(f32[2,4,40,136]{3,2,1,0:T(8,128)S(1)} %get-tuple-element.15), channel_id=1, source_target_pairs={{0,1},{2,3},{4,5},{6,7},{8,9},{10,11},{12,13},{14,15},{16,17},{18,... | collective-permute-start | bytes 522248 | tf_op jit(solution)/shard_map/ppermute | solution.py:28
  25.6 3.5 %collective-permute-start.5 = (f32[2,4,40,136]{3,2,1,0:T(8,128)S(1)}, f32[2,4,40,136]{3,2,1,0:T(8,128)S(1)}, u32[]{:S(2)}, u32[]{:S(2)}) collective-permute-start(f32[2,4,40,136]{3,2,1,0:T(8,128)S(1)} %get-tuple-element.16), channel_id=1, source_target_pairs={{1,0},{3,2},{5,4},{7,6},{9,8},{11,10},{13,12},{15,14},{17,16},{19,... | collective-permute-start | bytes 522248 | tf_op jit(solution)/shard_map/ppermute | solution.py:30
  46.8 18.7 %copy-start.1 = (f32[2,1,4]{2,1,0:T(1,128)S(1)}, f32[2,1,4]{2,1,0:T(1,128)}, u32[]{:S(2)}) copy-start(f32[2,1,4]{2,1,0:T(1,128)} %param.9) | copy-start | bytes 100
  46.8 38.9 %copy-start.2 = (f32[2,1,4]{2,1,0:T(1,128)S(1)}, f32[2,1,4]{2,1,0:T(1,128)}, u32[]{:S(2)}) copy-start(f32[2,1,4]{2,1,0:T(1,128)} %param.10) | copy-start | bytes 100
  46.8 38.9 %copy-start.3 = (f32[2,1,4]{2,1,0:T(1,128)S(1)}, f32[2,1,4]{2,1,0:T(1,128)}, u32[]{:S(2)}) copy-start(f32[2,1,4]{2,1,0:T(1,128)} %param.11) | copy-start | bytes 100
  65.7 20.0 %collective-permute-start.7 = (f32[5,2,1,4]{3,1,2,0:T(2,128)S(1)}, f32[5,2,1,4]{3,1,2,0:T(2,128)S(1)}, u32[]{:S(2)}, u32[]{:S(2)}) collective-permute-start(f32[5,2,1,4]{3,1,2,0:T(2,128)S(1)} %constant_dynamic-update-slice_fusion), channel_id=1, source_target_pairs={{4,0},{8,4},{12,8},{5,1},{9,5},{13,9},{6,2},{10,6},{14,10},{7,3},{... | collective-permute-start | bytes 488 | tf_op jit(solution)/shard_map/ppermute | solution.py:346
  67.0 18.7 %collective-permute-start.6 = (f32[5,2,1,4]{3,1,2,0:T(2,128)S(1)}, f32[5,2,1,4]{3,1,2,0:T(2,128)S(1)}, u32[]{:S(2)}, u32[]{:S(2)}) collective-permute-start(f32[5,2,1,4]{3,1,2,0:T(2,128)S(1)} %constant_dynamic-update-slice_fusion), channel_id=1, source_target_pairs={{0,4},{4,8},{8,12},{1,5},{5,9},{9,13},{2,6},{6,10},{10,14},{3,7},{... | collective-permute-start | bytes 488 | tf_op jit(solution)/shard_map/ppermute | solution.py:345
  71.8 13.9 %collective-permute-start.10 = (f32[5,1,1,4]{3,1,2,0:T(1,128)S(1)}, f32[5,1,1,4]{3,1,2,0:T(1,128)S(1)}, u32[]{:S(2)}, u32[]{:S(2)}) collective-permute-start(f32[5,1,1,4]{3,1,2,0:T(1,128)S(1)} %get-tuple-element.21), channel_id=1, source_target_pairs={{0,1},{2,3},{4,5},{6,7},{8,9},{10,11},{12,13},{14,15},{16,17},{18,... | collective-permute-start | bytes 248 | tf_op jit(solution)/shard_map/ppermute | solution.py:345
  73.2 12.4 %collective-permute-start.11 = (f32[5,1,1,4]{3,1,2,0:T(1,128)S(1)}, f32[5,1,1,4]{3,1,2,0:T(1,128)S(1)}, u32[]{:S(2)}, u32[]{:S(2)}) collective-permute-start(f32[5,1,1,4]{3,1,2,0:T(1,128)S(1)} %get-tuple-element.22), channel_id=1, source_target_pairs={{1,0},{3,2},{5,4},{7,6},{9,8},{11,10},{13,12},{15,14},{17,16},{19,... | collective-permute-start | bytes 248 | tf_op jit(solution)/shard_map/ppermute | solution.py:346
  74.5 5.6 %collective-permute-start.8 = (f32[5,2,1,1]{3,1,2,0:T(2,128)S(1)}, f32[5,2,1,1]{3,1,2,0:T(2,128)S(1)}, u32[]{:S(2)}, u32[]{:S(2)}) collective-permute-start(f32[5,2,1,1]{3,1,2,0:T(2,128)S(1)} %get-tuple-element.23), channel_id=1, source_target_pairs={{0,2},{1,3},{4,6},{5,7},{8,10},{9,11},{12,14},{13,15},{16,18},{17,... | collective-permute-start | bytes 128 | tf_op jit(solution)/shard_map/ppermute | solution.py:345
  80.1 5.5 %collective-permute-start.9 = (f32[5,2,1,1]{3,1,2,0:T(2,128)S(1)}, f32[5,2,1,1]{3,1,2,0:T(2,128)S(1)}, u32[]{:S(2)}, u32[]{:S(2)}) collective-permute-start(f32[5,2,1,1]{3,1,2,0:T(2,128)S(1)} %get-tuple-element.24), channel_id=1, source_target_pairs={{2,0},{3,1},{6,4},{7,5},{10,8},{11,9},{14,12},{15,13},{18,16},{19,... | collective-permute-start | bytes 128 | tf_op jit(solution)/shard_map/ppermute | solution.py:346
  85.9 16.9 %collective-permute-start.13 = (f32[2,1,4]{2,0,1:T(2,128)S(1)}, f32[2,1,4]{2,0,1:T(2,128)S(1)}, u32[]{:S(2)}, u32[]{:S(2)}) collective-permute-start(f32[2,1,4]{2,0,1:T(2,128)S(1)} %fusion.14), channel_id=1, source_target_pairs={{4,0},{8,4},{12,8},{5,1},{9,5},{13,9},{6,2},{10,6},{14,10},{7,3},{... | collective-permute-start | bytes 104 | tf_op jit(solution)/shard_map/ppermute | solution.py:346
  87.2 15.6 %collective-permute-start.12 = (f32[2,1,4]{2,0,1:T(2,128)S(1)}, f32[2,1,4]{2,0,1:T(2,128)S(1)}, u32[]{:S(2)}, u32[]{:S(2)}) collective-permute-start(f32[2,1,4]{2,0,1:T(2,128)S(1)} %fusion.14), channel_id=1, source_target_pairs={{0,4},{4,8},{8,12},{1,5},{5,9},{9,13},{2,6},{6,10},{10,14},{3,7},{... | collective-permute-start | bytes 104 | tf_op jit(solution)/shard_map/ppermute | solution.py:345
  91.8 11.0 %collective-permute-start.16 = (f32[1,1,4]{2,0,1:T(1,128)S(1)}, f32[1,1,4]{2,0,1:T(1,128)S(1)}, u32[]{:S(2)}, u32[]{:S(2)}) collective-permute-start(f32[1,1,4]{2,0,1:T(1,128)S(1)} %get-tuple-element.42), channel_id=1, source_target_pairs={{0,1},{2,3},{4,5},{6,7},{8,9},{10,11},{12,13},{14,15},{16,17},{18,... | collective-permute-start | bytes 56 | tf_op jit(solution)/shard_map/ppermute | solution.py:345
  93.1 9.7 %collective-permute-start.17 = (f32[1,1,4]{2,0,1:T(1,128)S(1)}, f32[1,1,4]{2,0,1:T(1,128)S(1)}, u32[]{:S(2)}, u32[]{:S(2)}) collective-permute-start(f32[1,1,4]{2,0,1:T(1,128)S(1)} %get-tuple-element.43), channel_id=1, source_target_pairs={{1,0},{3,2},{5,4},{7,6},{9,8},{11,10},{13,12},{15,14},{17,16},{19,... | collective-permute-start | bytes 56 | tf_op jit(solution)/shard_map/ppermute | solution.py:346
  94.4 5.5 %collective-permute-start.15 = (f32[2,1,1]{2,0,1:T(2,128)S(1)}, f32[2,1,1]{2,0,1:T(2,128)S(1)}, u32[]{:S(2)}, u32[]{:S(2)}) collective-permute-start(f32[2,1,1]{2,0,1:T(2,128)S(1)} %get-tuple-element.46), channel_id=1, source_target_pairs={{2,0},{3,1},{6,4},{7,5},{10,8},{11,9},{14,12},{15,13},{18,16},{19,... | collective-permute-start | bytes 32 | tf_op jit(solution)/shard_map/ppermute | solution.py:346
  99.8 2.9 %collective-permute-start.14 = (f32[2,1,1]{2,0,1:T(2,128)S(1)}, f32[2,1,1]{2,0,1:T(2,128)S(1)}, u32[]{:S(2)}, u32[]{:S(2)}) collective-permute-start(f32[2,1,1]{2,0,1:T(2,128)S(1)} %get-tuple-element.47), channel_id=1, source_target_pairs={{0,2},{1,3},{4,6},{5,7},{8,10},{9,11},{12,14},{13,15},{16,18},{17,... | collective-permute-start | bytes 32 | tf_op jit(solution)/shard_map/ppermute | solution.py:345
where the time goes:
time: 104 us; the launch traced here: 103 us
  starting transfers between devices  40.2 us (39%)
  waiting for transfers between devices  18 us (17%)
  Pallas kernels  16.9 us (16%)
  other arithmetic  14.4 us (14%)
  local copies, waits for them, and re-layouts  13.1 us (13%)
    ppermute x6, starting transfers between devices, faces(): lower = lax.ppermute(tail, axis, [(i, i + 1) for i in range(ends)])  17.8 us
    pallas_call x1, Pallas kernels, upscale_windows(): pl.pallas_call(window_kernel, grid=(count,), in_specs=[pl.BlockSpec((1, 4...  16.9 us
    ppermute x3, starting transfers between devices, extended(): lax.ppermute(tail, axis, [(i, (i + 1) % count) for i in range(ends)])  10.8 us
    add x2, other arithmetic, log_fields(): return (base_log, base_log + extra_y, base_log + extra_z)  9.19 us
    ppermute x6, waiting for transfers between devices, faces(): upper = lax.ppermute(head, axis, [(i + 1, i) for i in range(ends)])  8.39 us
    ppermute x6, starting transfers between devices, faces(): upper = lax.ppermute(head, axis, [(i + 1, i) for i in range(ends)])  7.73 us
    ppermute x3, waiting for transfers between devices, extended(): lax.ppermute(head, axis, [((i + 1) % count, i) for i in range(ends)])  5.15 us
    pad x1, local copies, waits for them, and re-layouts, upscale_windows(): windows = jnp.pad(windows, ((0, 0),) * 4 + ((0, LANES - span_y),))  4.85 us
  transfers between devices with their start and end apart: 18, of which 7 were waited for; matrix products, arithmetic and copies ran while one was open for 2% of the time, Pallas kernels for 0%

commit v1 on v0

--- a/solution.py
+++ b/solution.py
@@ -390,19 +390,24 @@
     mask_y = span_mask(anchor_y, log_x.shape[2] - 2 * RIM, cols_len * size_y, RIM)
     inside = mask_z[:, None, None] * mask_x[None, :, None] * mask_y[None, None, :]
     upscaled = upscale_windows(jnp.stack([log_x, log_y, log_z, inside]))
-    fixed = accumulation * pressure_old + source
-    ones = jnp.ones_like(pressure_old)
-    bundle = jnp.stack([upscaled[0], upscaled[1], upscaled[2], pressure_old, ones])
-    sides = (("gx", 2), ("gy", 3), ("gz", 1))
-    dim_of = (2, 3, 1)
-    views = neighbour_views(bundle, faces(bundle, sides), dim_of)
-    inside_views = [(below[4], above[4]) for below, above in views]
-    perm_views = [(below[:3], above[:3]) for below, above in views]
-    press_views = [(below[3], above[3]) for below, above in views]
-    pressure = coarse_step(upscaled, perm_views, inside_views, press_views, accumulation, fixed)
-    got = faces(pressure, (("gx", 1), ("gy", 2), ("gz", 0)))
-    press_views = neighbour_views(pressure, got, (1, 2, 0))
-    pressure = coarse_step(upscaled, perm_views, inside_views, press_views, accumulation, fixed)
+    coarse_z, coarse_x, coarse_y = pressure_old.shape
+    bundle = jnp.stack([upscaled[0], upscaled[1], upscaled[2], pressure_old, accumulation, source])
+    every = lax.all_gather(bundle, ("gz", "gx", "gy"), axis=0, tiled=False)
+    every = every.reshape((size_z, size_x, size_y) + bundle.shape)
+    every = every.transpose(3, 0, 4, 1, 5, 2, 6).reshape(
+        (bundle.shape[0], size_z * coarse_z, size_x * coarse_x, size_y * coarse_y)
+    )
+    perm_pad = jnp.pad(every[:3], ((0, 0), (1, 1), (1, 1), (1, 1)))
+    old_all = every[3]
+    acc_all = every[4]
+    fixed_all = acc_all * old_all + every[5]
+    inside_pad = jnp.pad(jnp.ones(old_all.shape, jnp.float32), 1)
+    pressure = old_all
+    for sweep_index in range(2):
+        pressure = coarse_sweep(perm_pad, jnp.pad(pressure, 1), inside_pad, acc_all, fixed_all)
+    pressure = lax.dynamic_slice(
+        pressure, (index_z * coarse_z, index_x * coarse_x, index_y * coarse_y), (coarse_z, coarse_x, coarse_y)
+    )
     return (pressure, upscaled)
 
 

time: 104 us -> 98.5 us (0.947)
  blocking collectives: 0 us -> 29.4 us
  starting transfers between devices: 40.2 us -> 13.5 us
  waiting for transfers between devices: 18 us -> 9.69 us
    all_gather x0 -> x1, blocking collectives: none -> 29.4 us  [local(): every = lax.all_gather(bundle, ('gz', 'gx', 'gy'), axis=0, tiled=False)]
    ppermute x12 -> x0, starting transfers between devices: 25.5 us -> none  [the longest x6 17.8 us: faces(): lower = lax.ppermute(tail, axis, [(i, i + 1) for i in range(ends)])]
    ppermute x12 -> x0, waiting for transfers between devices: 11 us -> none  [the longest x6 8.39 us: faces(): upper = lax.ppermute(head, axis, [(i + 1, i) for i in range(ends)])]
    ppermute x3, waiting for transfers between devices: 5.15 us -> 9.4 us  [extended(): lax.ppermute(head, axis, [((i + 1) % count, i) for i in range(ends)])]
    ppermute x3, waiting for transfers between devices: 1.87 us -> 0.29 us  [extended(): lax.ppermute(tail, axis, [(i, (i + 1) % count) for i in range(ends)])]
    ppermute x3, starting transfers between devices: 10.8 us -> 9.64 us  [extended(): lax.ppermute(tail, axis, [(i, (i + 1) % count) for i in range(ends)])]
    unnamed x19 -> x20, local copies, waits for them, and re-layouts: 2.24 us -> 2.25 us
  transfers between devices with their start and end apart: 18 -> 6, of which waited for: 7 -> 4; matrix products, arithmetic and copies ran while one was open for 2% -> 3% of each run, Pallas kernels for 0% -> 0%
where the time goes in v1:
time: 98.5 us; the launch traced here: 97.9 us
  blocking collectives  29.4 us (30%)
  Pallas kernels  16.9 us (17%)
  other arithmetic  14.5 us (15%)
  starting transfers between devices  13.5 us (14%)
  local copies, waits for them, and re-layouts  13 us (13%)
  waiting for transfers between devices  9.69 us (10%)
    all_gather x1, blocking collectives, local(): every = lax.all_gather(bundle, ('gz', 'gx', 'gy'), axis=0, tiled=False)  29.4 us
    pallas_call x1, Pallas kernels, upscale_windows(): pl.pallas_call(window_kernel, grid=(count,), in_specs=[pl.BlockSpec((1, 4...  16.9 us
    ppermute x3, starting transfers between devices, extended(): lax.ppermute(tail, axis, [(i, (i + 1) % count) for i in range(ends)])  9.64 us
    ppermute x3, waiting for transfers between devices, extended(): lax.ppermute(head, axis, [((i + 1) % count, i) for i in range(ends)])  9.4 us
    add x2, other arithmetic, log_fields(): return (base_log, base_log + extra_y, base_log + extra_z)  9.14 us
    pad x1, local copies, waits for them, and re-layouts, upscale_windows(): windows = jnp.pad(windows, ((0, 0),) * 4 + ((0, LANES - span_y),))  4.8 us
    ppermute x3, starting transfers between devices, extended(): lax.ppermute(head, axis, [((i + 1) % count, i) for i in range(ends)])  3.88 us
    unnamed x20, local copies, waits for them, and re-layouts  2.25 us
  transfers between devices with their start and end apart: 6, of which 4 were waited for; matrix products, arithmetic and copies ran while one was open for 3% of the time, Pallas kernels for 0%

profile of v1, /device:TPU:0, one launch (start us, length us, event | category | flops | bytes accessed | tf_op | source)
XLA Modules:
  0.0 97.9 jit_solution(4567136189501222470)
XLA Ops:
  0.6 1.0 %convert_bitcast_fusion = f32[1,16,32,128]{3,2,1,0:T(8,128)S(1)} fusion(s32[16,32,128]{2,1,0:T(8,128)} %param.7), kind=kLoop, calls=%fused_computation.36 | loop fusion | flops 65536 | bytes 524288 | tf_op jit(solution)/shard_map/stack | solution.py:382
  1.7 0.9 pad_maximum_fusion.10
  2.6 4.9 %collective-permute-start = (f32[2,16,4,128]{3,2,1,0:T(4,128)S(1)}, f32[2,16,4,128]{3,2,1,0:T(4,128)S(1)}, u32[]{:S(2)}, u32[]{:S(2)}) collective-permute-start(f32[2,16,4,128]{3,2,1,0:T(4,128)S(1)} %get-tuple-element.24), channel_id=1, source_target_pairs={{0,4},{4,8},{8,12},{1,5},{5,9},{9,13},{2,6},{6,10},{10,14},{3,7},{... | collective-permute-start | bytes 196616 | tf_op jit(solution)/shard_map/ppermute | solution.py:28
  7.5 1.3 %collective-permute-start.1 = (f32[2,16,4,128]{3,2,1,0:T(4,128)S(1)}, f32[2,16,4,128]{3,2,1,0:T(4,128)S(1)}, u32[]{:S(2)}, u32[]{:S(2)}) collective-permute-start(f32[2,16,4,128]{3,2,1,0:T(4,128)S(1)} %get-tuple-element.25), channel_id=1, source_target_pairs={{4,0},{8,4},{12,8},{5,1},{9,5},{13,9},{6,2},{10,6},{14,10},{7,3},{... | collective-permute-start | bytes 196616 | tf_op jit(solution)/shard_map/ppermute | solution.py:30
  8.8 1.8 %fusion.53 = (f32[1,1]{1,0:T(1,128)}, f32[1,1]{1,0:T(1,128)}, f32[1,1]{1,0:T(1,128)}, f32[1,1]{1,0:T(1,128)}, f32[1,1]{1,0:T(1,128)}, /*index=5*/f32[1,1]{1,0:T(...) fusion(f32[3,4]{1,0:T(4,128)} %param.8), kind=kLoop, calls=%fused_computation.125 | loop fusion | bytes 96 | tf_op jit(solution)/shard_map/slice | solution.py:65
  10.6 3.0 %collective-permute-done.1 = f32[2,16,4,128]{3,2,1,0:T(4,128)S(1)} collective-permute-done((f32[2,16,4,128]{3,2,1,0:T(4,128)S(1)}, f32[2,16,4,128]{3,2,1,0:T(4,128)S(1)}, u32[]{:S(2)}, u32[]{:S(2)}) %collective-permute-start.1) | collective-permute-done | bytes 65568 | tf_op jit(solution)/shard_map/ppermute | solution.py:30
  13.7 1.0 %pad_maximum_fusion.2 = f32[2,16,40,128]{3,2,1,0:T(8,128)S(1)} fusion(f32[2,16,4,128]{3,2,1,0:T(4,128)S(1)} %collective-permute-done.1, f32[1,16,32,128]{3,2,1,0:T(8,128)S(1)} %convert_bitcast_fusion, f32[1,16,32,128]{3,2,1,0:T(8,128)} %bitcast.73, f32[2,16,4,128]{3,2,1,0:T(4,128)S(1)} %collective-permute-done), kind=kLoop, calls=%fused_computation.28 | loop fusion | flops 491520 | bytes 1310720 | tf_op jit(solution)/shard_map/concatenate | solution.py:26
  15.2 3.4 %collective-permute-start.2 = (f32[2,16,40,4]{2,1,3,0:T(8,128)S(1)}, f32[2,16,40,4]{2,1,3,0:T(8,128)S(1)}, u32[]{:S(2)}, u32[]{:S(2)}) collective-permute-start(f32[2,16,40,4]{2,1,3,0:T(8,128)S(1)} %copy.11), channel_id=1, source_target_pairs={{0,2},{1,3},{4,6},{5,7},{8,10},{9,11},{12,14},{13,15},{16,18},{17,... | collective-permute-start | bytes 61448 | tf_op jit(solution)/shard_map/ppermute | solution.py:28
  18.9 1.3 %collective-permute-start.3 = (f32[2,16,40,4]{2,1,3,0:T(8,128)S(1)}, f32[2,16,40,4]{2,1,3,0:T(8,128)S(1)}, u32[]{:S(2)}, u32[]{:S(2)}) collective-permute-start(f32[2,16,40,4]{2,1,3,0:T(8,128)S(1)} %copy.12), channel_id=1, source_target_pairs={{2,0},{3,1},{6,4},{7,5},{10,8},{11,9},{14,12},{15,13},{18,16},{19,... | collective-permute-start | bytes 61448 | tf_op jit(solution)/shard_map/ppermute | solution.py:30
  20.5 0.3 copy.13
  20.8 4.2 %collective-permute-done.3 = f32[2,16,40,4]{2,1,3,0:T(8,128)S(1)} collective-permute-done((f32[2,16,40,4]{2,1,3,0:T(8,128)S(1)}, f32[2,16,40,4]{2,1,3,0:T(8,128)S(1)}, u32[]{:S(2)}, u32[]{:S(2)}) %collective-permute-start.3) | collective-permute-done | bytes 20512 | tf_op jit(solution)/shard_map/ppermute | solution.py:30
  25.0 0.3 copy.14
  25.4 0.4 pad_maximum_fusion.8
  25.8 1.3 %collective-permute-start.4 = (f32[2,4,40,136]{3,2,1,0:T(8,128)S(1)}, f32[2,4,40,136]{3,2,1,0:T(8,128)S(1)}, u32[]{:S(2)}, u32[]{:S(2)}) collective-permute-start(f32[2,4,40,136]{3,2,1,0:T(8,128)S(1)} %get-tuple-element.20), channel_id=1, source_target_pairs={{0,1},{2,3},{4,5},{6,7},{8,9},{10,11},{12,13},{14,15},{16,17},{18,... | collective-permute-start | bytes 522248 | tf_op jit(solution)/shard_map/ppermute | solution.py:28
  27.1 1.3 %collective-permute-start.5 = (f32[2,4,40,136]{3,2,1,0:T(8,128)S(1)}, f32[2,4,40,136]{3,2,1,0:T(8,128)S(1)}, u32[]{:S(2)}, u32[]{:S(2)}) collective-permute-start(f32[2,4,40,136]{3,2,1,0:T(8,128)S(1)} %get-tuple-element.21), channel_id=1, source_target_pairs={{1,0},{3,2},{5,4},{7,6},{9,8},{11,10},{13,12},{15,14},{17,16},{19,... | collective-permute-start | bytes 522248 | tf_op jit(solution)/shard_map/ppermute | solution.py:30
  28.5 2.1 %collective-permute-done.5 = f32[2,4,40,136]{3,2,1,0:T(8,128)S(1)} collective-permute-done((f32[2,4,40,136]{3,2,1,0:T(8,128)S(1)}, f32[2,4,40,136]{3,2,1,0:T(8,128)S(1)}, u32[]{:S(2)}, u32[]{:S(2)}) %collective-permute-start.5) | collective-permute-done | bytes 174112 | tf_op jit(solution)/shard_map/ppermute | solution.py:30
  30.6 0.7 pad_maximum_fusion.1
  31.3 5.9 %add_add_fusion.1 = (f32[1,24,40,136]{3,2,1,0:T(8,128)S(1)}, f32[1,24,40,136]{3,2,1,0:T(8,128)S(1)}, pred[1,24,40,136]{3,2,1,0:T(8,128)(4,1)S(1)}, pred[1,24,40,...) fusion(f32[]{:T(128)} %bitcast.9, f32[]{:T(128)} %bitcast.8, ...), kind=kLoop, calls=%fused_computation.23 | loop fusion | flops 2611200 | bytes 2611232 | tf_op jit(solution)/shard_map/add | solution.py:66
  37.3 3.2 %add_add_fusion = (f32[1,24,40,136]{3,2,1,0:T(8,128)S(1)}, f32[1,24,40,136]{3,2,1,0:T(8,128)S(1)}) fusion(f32[1,24,40,136]{3,2,1,0:T(8,128)S(1)} %get-tuple-element.15, pred[1,24,40,136]{3,2,1,0:T(8,128)(4,1)S(1)} %get-tuple-element.19, pred[1,24,40,136]{3,2,1,0:T(8,128)(4,1)S(1)} %get-tuple-element.18, pred[1,24,40,136]{3,2,1,0:T(8,128)(4,1)S(1)} %get-tuple-element.17, ...), kind=kLoop, calls=%fused_computation.22 | loop fusion | flops 1175040 | bytes 2093360 | tf_op jit(solution)/shard_map/add | solution.py:66
  40.5 0.3 pad_maximum_fusion
  40.9 0.4 fusion.6
  41.3 0.4 fusion.5
  41.7 0.4 fusion.4
  42.2 0.4 fusion.2
  42.6 0.4 fusion.1
  43.0 0.4 fusion
  43.4 4.8 %pad.18.w_ref = f32[8,4,16,40,128]{4,3,2,1,0:T(8,128)} pad(f32[8,4,16,40,40]{4,3,2,1,0:T(8,128)S(1)} %fusion, f32[]{:T(128)} %constant.18.clone.1), padding=0_0x0_0x0_0x0_0x0_88 | pad | bytes 13762564 | tf_op jit(solution)/shard_map/jit(_pad)/pad | solution.py:278
  48.2 16.9 %shard_map.77 = f32[8,8,128]{2,1,0:T(8,128)} custom-call(f32[8,4,16,40,128]{4,3,2,1,0:T(8,128)} %pad.18.w_ref), custom_call_target="tpu_custom_call" | custom-call | tf_op jit(solution)/shard_map/pallas_call | solution.py:280
  65.1 0.8 slice.337
  66.3 29.4 %all-gather = f32[96,2,1,4]{3,1,2,0:T(2,128)S(1)} all-gather(f32[6,2,1,4]{3,1,2,0:T(2,128)S(1)} %constant_dynamic-update-slice_fusion), channel_id=2, replica_groups=mesh['real'=2,'gx'=4,'gy'=2,'gz'=2] {'gz','gx','gy'}, dimensions={0}, use_global_device_ids=true | all-gather | bytes 3264 | tf_op jit(solution)/shard_map/all_gather | solution.py:395
  95.8 0.7 reshape.81
  97.2 0.7 dynamic-slice_divide_fusion
  (43 shorter events, 2.6 us)
Async XLA Ops:
  0.6 24.7 %copy-start = (f32[16,32,128]{2,1,0:T(8,128)S(1)}, f32[16,32,128]{2,1,0:T(8,128)}, u32[]{:S(2)}) copy-start(f32[16,32,128]{2,1,0:T(8,128)} %param.6) | copy-start | bytes 786436
  2.6 8.1 %collective-permute-start = (f32[2,16,4,128]{3,2,1,0:T(4,128)S(1)}, f32[2,16,4,128]{3,2,1,0:T(4,128)S(1)}, u32[]{:S(2)}, u32[]{:S(2)}) collective-permute-start(f32[2,16,4,128]{3,2,1,0:T(4,128)S(1)} %get-tuple-element.24), channel_id=1, source_target_pairs={{0,4},{4,8},{8,12},{1,5},{5,9},{9,13},{2,6},{6,10},{10,14},{3,7},{... | collective-permute-start | bytes 196616 | tf_op jit(solution)/shard_map/ppermute | solution.py:28
  7.5 6.2 %collective-permute-start.1 = (f32[2,16,4,128]{3,2,1,0:T(4,128)S(1)}, f32[2,16,4,128]{3,2,1,0:T(4,128)S(1)}, u32[]{:S(2)}, u32[]{:S(2)}) collective-permute-start(f32[2,16,4,128]{3,2,1,0:T(4,128)S(1)} %get-tuple-element.25), channel_id=1, source_target_pairs={{4,0},{8,4},{12,8},{5,1},{9,5},{13,9},{6,2},{10,6},{14,10},{7,3},{... | collective-permute-start | bytes 196616 | tf_op jit(solution)/shard_map/ppermute | solution.py:30
  15.2 5.3 %collective-permute-start.2 = (f32[2,16,40,4]{2,1,3,0:T(8,128)S(1)}, f32[2,16,40,4]{2,1,3,0:T(8,128)S(1)}, u32[]{:S(2)}, u32[]{:S(2)}) collective-permute-start(f32[2,16,40,4]{2,1,3,0:T(8,128)S(1)} %copy.11), channel_id=1, source_target_pairs={{0,2},{1,3},{4,6},{5,7},{8,10},{9,11},{12,14},{13,15},{16,18},{17,... | collective-permute-start | bytes 61448 | tf_op jit(solution)/shard_map/ppermute | solution.py:28
  18.9 6.2 %collective-permute-start.3 = (f32[2,16,40,4]{2,1,3,0:T(8,128)S(1)}, f32[2,16,40,4]{2,1,3,0:T(8,128)S(1)}, u32[]{:S(2)}, u32[]{:S(2)}) collective-permute-start(f32[2,16,40,4]{2,1,3,0:T(8,128)S(1)} %copy.12), channel_id=1, source_target_pairs={{2,0},{3,1},{6,4},{7,5},{10,8},{11,9},{14,12},{15,13},{18,16},{19,... | collective-permute-start | bytes 61448 | tf_op jit(solution)/shard_map/ppermute | solution.py:30
  25.8 2.7 %collective-permute-start.4 = (f32[2,4,40,136]{3,2,1,0:T(8,128)S(1)}, f32[2,4,40,136]{3,2,1,0:T(8,128)S(1)}, u32[]{:S(2)}, u32[]{:S(2)}) collective-permute-start(f32[2,4,40,136]{3,2,1,0:T(8,128)S(1)} %get-tuple-element.20), channel_id=1, source_target_pairs={{0,1},{2,3},{4,5},{6,7},{8,9},{10,11},{12,13},{14,15},{16,17},{18,... | collective-permute-start | bytes 522248 | tf_op jit(solution)/shard_map/ppermute | solution.py:28
  27.1 3.5 %collective-permute-start.5 = (f32[2,4,40,136]{3,2,1,0:T(8,128)S(1)}, f32[2,4,40,136]{3,2,1,0:T(8,128)S(1)}, u32[]{:S(2)}, u32[]{:S(2)}) collective-permute-start(f32[2,4,40,136]{3,2,1,0:T(8,128)S(1)} %get-tuple-element.21), channel_id=1, source_target_pairs={{1,0},{3,2},{5,4},{7,6},{9,8},{11,10},{13,12},{15,14},{17,16},{19,... | collective-permute-start | bytes 522248 | tf_op jit(solution)/shard_map/ppermute | solution.py:30
  48.2 18.0 %copy-start.1 = (f32[2,1,4]{2,1,0:T(1,128)S(1)}, f32[2,1,4]{2,1,0:T(1,128)}, u32[]{:S(2)}) copy-start(f32[2,1,4]{2,1,0:T(1,128)} %param.9) | copy-start | bytes 100
  48.2 18.1 %copy-start.2 = (f32[2,1,4]{2,1,0:T(1,128)S(1)}, f32[2,1,4]{2,1,0:T(1,128)}, u32[]{:S(2)}) copy-start(f32[2,1,4]{2,1,0:T(1,128)} %param.10) | copy-start | bytes 100
  48.2 18.1 %copy-start.3 = (f32[2,1,4]{2,1,0:T(1,128)S(1)}, f32[2,1,4]{2,1,0:T(1,128)}, u32[]{:S(2)}) copy-start(f32[2,1,4]{2,1,0:T(1,128)} %param.11) | copy-start | bytes 100

commit v2 on v1

--- a/solution.py
+++ b/solution.py
@@ -392,11 +392,9 @@
     upscaled = upscale_windows(jnp.stack([log_x, log_y, log_z, inside]))
     coarse_z, coarse_x, coarse_y = pressure_old.shape
     bundle = jnp.stack([upscaled[0], upscaled[1], upscaled[2], pressure_old, accumulation, source])
-    every = lax.all_gather(bundle, ("gz", "gx", "gy"), axis=0, tiled=False)
-    every = every.reshape((size_z, size_x, size_y) + bundle.shape)
-    every = every.transpose(3, 0, 4, 1, 5, 2, 6).reshape(
-        (bundle.shape[0], size_z * coarse_z, size_x * coarse_x, size_y * coarse_y)
-    )
+    every = lax.all_gather(bundle, "gy", axis=3, tiled=True)
+    every = lax.all_gather(every, "gx", axis=2, tiled=True)
+    every = lax.all_gather(every, "gz", axis=1, tiled=True)
     perm_pad = jnp.pad(every[:3], ((0, 0), (1, 1), (1, 1), (1, 1)))
     old_all = every[3]
     acc_all = every[4]

time: 98.5 us -> 84.5 us (0.86)
  blocking collectives: 29.4 us -> 15.6 us
    all_gather x1 -> x3, blocking collectives: 29.4 us -> 15.6 us  [the longest x1 9.49 us: local(): every = lax.all_gather(every, 'gx', axis=2, tiled=True)]
where the time goes in v2:
time: 84.5 us; the launch traced here: 83.9 us
  Pallas kernels  16.9 us (20%)
  blocking collectives  15.6 us (18%)
  other arithmetic  14.5 us (17%)
  starting transfers between devices  13.5 us (16%)
  local copies, waits for them, and re-layouts  12.8 us (15%)
  waiting for transfers between devices  9.7 us (11%)
  between operations  0.86 us (1%)
    pallas_call x1, Pallas kernels, upscale_windows(): pl.pallas_call(window_kernel, grid=(count,), in_specs=[pl.BlockSpec((1, 4...  16.9 us
    ppermute x3, starting transfers between devices, extended(): lax.ppermute(tail, axis, [(i, (i + 1) % count) for i in range(ends)])  9.64 us
    all_gather x1, blocking collectives, local(): every = lax.all_gather(every, 'gx', axis=2, tiled=True)  9.49 us
    ppermute x3, waiting for transfers between devices, extended(): lax.ppermute(head, axis, [((i + 1) % count, i) for i in range(ends)])  9.41 us
    add x2, other arithmetic, log_fields(): return (base_log, base_log + extra_y, base_log + extra_z)  9.14 us
    pad x1, local copies, waits for them, and re-layouts, upscale_windows(): windows = jnp.pad(windows, ((0, 0),) * 4 + ((0, LANES - span_y),))  4.81 us
    all_gather x1, blocking collectives, local(): every = lax.all_gather(bundle, 'gy', axis=3, tiled=True)  4.33 us
    ppermute x3, starting transfers between devices, extended(): lax.ppermute(head, axis, [((i + 1) % count, i) for i in range(ends)])  3.88 us
  transfers between devices with their start and end apart: 6, of which 4 were waited for; matrix products, arithmetic and copies ran while one was open for 3% of the time, Pallas kernels for 0%

profile of v2, /device:TPU:0, one launch (start us, length us, event | category | flops | bytes accessed | tf_op | source)
XLA Modules:
  0.0 83.9 jit_solution(8229369174785266145)
XLA Ops:
  0.6 1.0 %convert_bitcast_fusion = f32[1,16,32,128]{3,2,1,0:T(8,128)S(1)} fusion(s32[16,32,128]{2,1,0:T(8,128)} %param.7), kind=kLoop, calls=%fused_computation.36 | loop fusion | flops 65536 | bytes 524288 | tf_op jit(solution)/shard_map/stack | solution.py:382
  1.7 0.9 %pad_maximum_fusion.10 = (f32[2,16,4,128]{3,2,1,0:T(4,128)S(1)}, f32[2,16,4,128]{3,2,1,0:T(4,128)S(1)}) fusion(f32[1,16,32,128]{3,2,1,0:T(8,128)S(1)} %convert_bitcast_fusion, f32[1,16,32,128]{3,2,1,0:T(8,128)} %bitcast.88), kind=kLoop, calls=%fused_computation.47 | loop fusion | flops 32768 | bytes 655360 | tf_op jit(solution)/shard_map/slice | solution.py:25
  2.6 4.9 %collective-permute-start = (f32[2,16,4,128]{3,2,1,0:T(4,128)S(1)}, f32[2,16,4,128]{3,2,1,0:T(4,128)S(1)}, u32[]{:S(2)}, u32[]{:S(2)}) collective-permute-start(f32[2,16,4,128]{3,2,1,0:T(4,128)S(1)} %get-tuple-element.24), channel_id=1, source_target_pairs={{0,4},{4,8},{8,12},{1,5},{5,9},{9,13},{2,6},{6,10},{10,14},{3,7},{... | collective-permute-start | bytes 196616 | tf_op jit(solution)/shard_map/ppermute | solution.py:28
  7.5 1.3 %collective-permute-start.1 = (f32[2,16,4,128]{3,2,1,0:T(4,128)S(1)}, f32[2,16,4,128]{3,2,1,0:T(4,128)S(1)}, u32[]{:S(2)}, u32[]{:S(2)}) collective-permute-start(f32[2,16,4,128]{3,2,1,0:T(4,128)S(1)} %get-tuple-element.25), channel_id=1, source_target_pairs={{4,0},{8,4},{12,8},{5,1},{9,5},{13,9},{6,2},{10,6},{14,10},{7,3},{... | collective-permute-start | bytes 196616 | tf_op jit(solution)/shard_map/ppermute | solution.py:30
  8.8 1.8 %fusion.53 = (f32[1,1]{1,0:T(1,128)}, f32[1,1]{1,0:T(1,128)}, f32[1,1]{1,0:T(1,128)}, f32[1,1]{1,0:T(1,128)}, f32[1,1]{1,0:T(1,128)}, /*index=5*/f32[1,1]{1,0:T(...) fusion(f32[3,4]{1,0:T(4,128)} %param.8), kind=kLoop, calls=%fused_computation.126 | loop fusion | bytes 96 | tf_op jit(solution)/shard_map/slice | solution.py:65
  10.6 3.0 %collective-permute-done.1 = f32[2,16,4,128]{3,2,1,0:T(4,128)S(1)} collective-permute-done((f32[2,16,4,128]{3,2,1,0:T(4,128)S(1)}, f32[2,16,4,128]{3,2,1,0:T(4,128)S(1)}, u32[]{:S(2)}, u32[]{:S(2)}) %collective-permute-start.1) | collective-permute-done | bytes 65568 | tf_op jit(solution)/shard_map/ppermute | solution.py:30
  13.7 1.0 %pad_maximum_fusion.2 = f32[2,16,40,128]{3,2,1,0:T(8,128)S(1)} fusion(f32[2,16,4,128]{3,2,1,0:T(4,128)S(1)} %collective-permute-done.1, f32[1,16,32,128]{3,2,1,0:T(8,128)S(1)} %convert_bitcast_fusion, f32[1,16,32,128]{3,2,1,0:T(8,128)} %bitcast.89, f32[2,16,4,128]{3,2,1,0:T(4,128)S(1)} %collective-permute-done), kind=kLoop, calls=%fused_computation.28 | loop fusion | flops 491520 | bytes 1310720 | tf_op jit(solution)/shard_map/concatenate | solution.py:26
  15.2 3.4 %collective-permute-start.2 = (f32[2,16,40,4]{2,1,3,0:T(8,128)S(1)}, f32[2,16,40,4]{2,1,3,0:T(8,128)S(1)}, u32[]{:S(2)}, u32[]{:S(2)}) collective-permute-start(f32[2,16,40,4]{2,1,3,0:T(8,128)S(1)} %copy.19), channel_id=1, source_target_pairs={{0,2},{1,3},{4,6},{5,7},{8,10},{9,11},{12,14},{13,15},{16,18},{17,... | collective-permute-start | bytes 61448 | tf_op jit(solution)/shard_map/ppermute | solution.py:28
  18.9 1.3 %collective-permute-start.3 = (f32[2,16,40,4]{2,1,3,0:T(8,128)S(1)}, f32[2,16,40,4]{2,1,3,0:T(8,128)S(1)}, u32[]{:S(2)}, u32[]{:S(2)}) collective-permute-start(f32[2,16,40,4]{2,1,3,0:T(8,128)S(1)} %copy.20), channel_id=1, source_target_pairs={{2,0},{3,1},{6,4},{7,5},{10,8},{11,9},{14,12},{15,13},{18,16},{19,... | collective-permute-start | bytes 61448 | tf_op jit(solution)/shard_map/ppermute | solution.py:30
  20.5 0.3 copy.21
  20.8 4.2 %collective-permute-done.3 = f32[2,16,40,4]{2,1,3,0:T(8,128)S(1)} collective-permute-done((f32[2,16,40,4]{2,1,3,0:T(8,128)S(1)}, f32[2,16,40,4]{2,1,3,0:T(8,128)S(1)}, u32[]{:S(2)}, u32[]{:S(2)}) %collective-permute-start.3) | collective-permute-done | bytes 20512 | tf_op jit(solution)/shard_map/ppermute | solution.py:30
  25.4 0.4 pad_maximum_fusion.8
  25.8 1.3 %collective-permute-start.4 = (f32[2,4,40,136]{3,2,1,0:T(8,128)S(1)}, f32[2,4,40,136]{3,2,1,0:T(8,128)S(1)}, u32[]{:S(2)}, u32[]{:S(2)}) collective-permute-start(f32[2,4,40,136]{3,2,1,0:T(8,128)S(1)} %get-tuple-element.20), channel_id=1, source_target_pairs={{0,1},{2,3},{4,5},{6,7},{8,9},{10,11},{12,13},{14,15},{16,17},{18,... | collective-permute-start | bytes 522248 | tf_op jit(solution)/shard_map/ppermute | solution.py:28
  27.1 1.3 %collective-permute-start.5 = (f32[2,4,40,136]{3,2,1,0:T(8,128)S(1)}, f32[2,4,40,136]{3,2,1,0:T(8,128)S(1)}, u32[]{:S(2)}, u32[]{:S(2)}) collective-permute-start(f32[2,4,40,136]{3,2,1,0:T(8,128)S(1)} %get-tuple-element.21), channel_id=1, source_target_pairs={{1,0},{3,2},{5,4},{7,6},{9,8},{11,10},{13,12},{15,14},{17,16},{19,... | collective-permute-start | bytes 522248 | tf_op jit(solution)/shard_map/ppermute | solution.py:30
  28.5 2.1 %collective-permute-done.5 = f32[2,4,40,136]{3,2,1,0:T(8,128)S(1)} collective-permute-done((f32[2,4,40,136]{3,2,1,0:T(8,128)S(1)}, f32[2,4,40,136]{3,2,1,0:T(8,128)S(1)}, u32[]{:S(2)}, u32[]{:S(2)}) %collective-permute-start.5) | collective-permute-done | bytes 174112 | tf_op jit(solution)/shard_map/ppermute | solution.py:30
  30.6 0.7 pad_maximum_fusion.1
  31.3 6.0 %add_add_fusion.1 = (f32[1,24,40,136]{3,2,1,0:T(8,128)S(1)}, f32[1,24,40,136]{3,2,1,0:T(8,128)S(1)}, pred[1,24,40,136]{3,2,1,0:T(8,128)(4,1)S(1)}, pred[1,24,40,...) fusion(f32[]{:T(128)} %bitcast.9, f32[]{:T(128)} %bitcast.8, ...), kind=kLoop, calls=%fused_computation.23 | loop fusion | flops 2611200 | bytes 2611232 | tf_op jit(solution)/shard_map/add | solution.py:66
  37.3 3.1 %add_add_fusion = (f32[1,24,40,136]{3,2,1,0:T(8,128)S(1)}, f32[1,24,40,136]{3,2,1,0:T(8,128)S(1)}) fusion(f32[1,24,40,136]{3,2,1,0:T(8,128)S(1)} %get-tuple-element.15, pred[1,24,40,136]{3,2,1,0:T(8,128)(4,1)S(1)} %get-tuple-element.19, pred[1,24,40,136]{3,2,1,0:T(8,128)(4,1)S(1)} %get-tuple-element.18, pred[1,24,40,136]{3,2,1,0:T(8,128)(4,1)S(1)} %get-tuple-element.17, ...), kind=kLoop, calls=%fused_computation.22 | loop fusion | flops 1175040 | bytes 2093360 | tf_op jit(solution)/shard_map/add | solution.py:66
  40.9 0.4 fusion.6
  41.3 0.4 fusion.5
  41.7 0.4 fusion.4
  42.2 0.4 fusion.2
  42.6 0.4 fusion.1
  43.0 0.4 fusion
  43.4 4.8 %pad.18.w_ref = f32[8,4,16,40,128]{4,3,2,1,0:T(8,128)} pad(f32[8,4,16,40,40]{4,3,2,1,0:T(8,128)S(1)} %fusion, f32[]{:T(128)} %constant.18.clone.1), padding=0_0x0_0x0_0x0_0x0_88 | pad | bytes 13762564 | tf_op jit(solution)/shard_map/jit(_pad)/pad | solution.py:278
  48.2 16.9 %shard_map.77 = f32[8,8,128]{2,1,0:T(8,128)} custom-call(f32[8,4,16,40,128]{4,3,2,1,0:T(8,128)} %pad.18.w_ref), custom_call_target="tpu_custom_call" | custom-call | tf_op jit(solution)/shard_map/pallas_call | solution.py:280
  65.1 0.8 slice.330
  66.4 4.3 %all_gather.9 = f32[6,2,1,8]{0,1,2,3:T(2,128)S(1)} all-gather(f32[6,2,1,4]{0,1,2,3:T(2,128)S(1)} %copy.24), channel_id=1, replica_groups=mesh['real'=2,'gx'=4,'gy'=2,'gz'=2] {'gy'}, dimensions={3}, use_global_device_ids=true | all-gather | bytes 576 | tf_op jit(solution)/shard_map/all_gather | solution.py:395
  70.7 9.5 %all_gather.10 = f32[6,2,4,8]{0,1,2,3:T(2,128)S(1)} all-gather(f32[6,2,1,8]{0,1,2,3:T(2,128)S(1)} %all_gather.9), channel_id=1, replica_groups=mesh['real'=2,'gx'=4,'gy'=2,'gz'=2] {'gx'}, dimensions={2}, use_global_device_ids=true | all-gather | bytes 1920 | tf_op jit(solution)/shard_map/all_gather | solution.py:396
  80.3 1.8 %all_gather.11 = f32[6,4,4,8]{3,2,0,1:T(4,128)S(1)} all-gather(f32[6,2,4,8]{3,2,0,1:T(4,128)S(1)} %copy.25), channel_id=1, replica_groups=mesh['real'=2,'gx'=4,'gy'=2,'gz'=2] {'gz'}, dimensions={1}, use_global_device_ids=true | all-gather | bytes 4608 | tf_op jit(solution)/shard_map/all_gather | solution.py:397
  82.3 0.7 reshape.69
  83.2 0.7 dynamic-slice_divide_fusion
  (41 shorter events, 3.0 us)
Async XLA Ops:
  0.6 24.7 %copy-start = (f32[16,32,128]{2,1,0:T(8,128)S(1)}, f32[16,32,128]{2,1,0:T(8,128)}, u32[]{:S(2)}) copy-start(f32[16,32,128]{2,1,0:T(8,128)} %param.6) | copy-start | bytes 786436
  2.6 8.1 %collective-permute-start = (f32[2,16,4,128]{3,2,1,0:T(4,128)S(1)}, f32[2,16,4,128]{3,2,1,0:T(4,128)S(1)}, u32[]{:S(2)}, u32[]{:S(2)}) collective-permute-start(f32[2,16,4,128]{3,2,1,0:T(4,128)S(1)} %get-tuple-element.24), channel_id=1, source_target_pairs={{0,4},{4,8},{8,12},{1,5},{5,9},{9,13},{2,6},{6,10},{10,14},{3,7},{... | collective-permute-start | bytes 196616 | tf_op jit(solution)/shard_map/ppermute | solution.py:28
  7.5 6.2 %collective-permute-start.1 = (f32[2,16,4,128]{3,2,1,0:T(4,128)S(1)}, f32[2,16,4,128]{3,2,1,0:T(4,128)S(1)}, u32[]{:S(2)}, u32[]{:S(2)}) collective-permute-start(f32[2,16,4,128]{3,2,1,0:T(4,128)S(1)} %get-tuple-element.25), channel_id=1, source_target_pairs={{4,0},{8,4},{12,8},{5,1},{9,5},{13,9},{6,2},{10,6},{14,10},{7,3},{... | collective-permute-start | bytes 196616 | tf_op jit(solution)/shard_map/ppermute | solution.py:30
  15.2 5.3 %collective-permute-start.2 = (f32[2,16,40,4]{2,1,3,0:T(8,128)S(1)}, f32[2,16,40,4]{2,1,3,0:T(8,128)S(1)}, u32[]{:S(2)}, u32[]{:S(2)}) collective-permute-start(f32[2,16,40,4]{2,1,3,0:T(8,128)S(1)} %copy.19), channel_id=1, source_target_pairs={{0,2},{1,3},{4,6},{5,7},{8,10},{9,11},{12,14},{13,15},{16,18},{17,... | collective-permute-start | bytes 61448 | tf_op jit(solution)/shard_map/ppermute | solution.py:28
  18.9 6.2 %collective-permute-start.3 = (f32[2,16,40,4]{2,1,3,0:T(8,128)S(1)}, f32[2,16,40,4]{2,1,3,0:T(8,128)S(1)}, u32[]{:S(2)}, u32[]{:S(2)}) collective-permute-start(f32[2,16,40,4]{2,1,3,0:T(8,128)S(1)} %copy.20), channel_id=1, source_target_pairs={{2,0},{3,1},{6,4},{7,5},{10,8},{11,9},{14,12},{15,13},{18,16},{19,... | collective-permute-start | bytes 61448 | tf_op jit(solution)/shard_map/ppermute | solution.py:30
  25.8 2.7 %collective-permute-start.4 = (f32[2,4,40,136]{3,2,1,0:T(8,128)S(1)}, f32[2,4,40,136]{3,2,1,0:T(8,128)S(1)}, u32[]{:S(2)}, u32[]{:S(2)}) collective-permute-start(f32[2,4,40,136]{3,2,1,0:T(8,128)S(1)} %get-tuple-element.20), channel_id=1, source_target_pairs={{0,1},{2,3},{4,5},{6,7},{8,9},{10,11},{12,13},{14,15},{16,17},{18,... | collective-permute-start | bytes 522248 | tf_op jit(solution)/shard_map/ppermute | solution.py:28
  27.1 3.5 %collective-permute-start.5 = (f32[2,4,40,136]{3,2,1,0:T(8,128)S(1)}, f32[2,4,40,136]{3,2,1,0:T(8,128)S(1)}, u32[]{:S(2)}, u32[]{:S(2)}) collective-permute-start(f32[2,4,40,136]{3,2,1,0:T(8,128)S(1)} %get-tuple-element.21), channel_id=1, source_target_pairs={{1,0},{3,2},{5,4},{7,6},{9,8},{11,10},{13,12},{15,14},{17,16},{19,... | collective-permute-start | bytes 522248 | tf_op jit(solution)/shard_map/ppermute | solution.py:30
  48.2 18.0 %copy-start.1 = (f32[2,1,4]{2,1,0:T(1,128)S(1)}, f32[2,1,4]{2,1,0:T(1,128)}, u32[]{:S(2)}) copy-start(f32[2,1,4]{2,1,0:T(1,128)} %param.9) | copy-start | bytes 100
  48.2 18.0 %copy-start.2 = (f32[2,1,4]{2,1,0:T(1,128)S(1)}, f32[2,1,4]{2,1,0:T(1,128)}, u32[]{:S(2)}) copy-start(f32[2,1,4]{2,1,0:T(1,128)} %param.10) | copy-start | bytes 100
  48.2 18.1 %copy-start.3 = (f32[2,1,4]{2,1,0:T(1,128)S(1)}, f32[2,1,4]{2,1,0:T(1,128)}, u32[]{:S(2)}) copy-start(f32[2,1,4]{2,1,0:T(1,128)} %param.11) | copy-start | bytes 100

commit v3 on v2

--- a/solution.py
+++ b/solution.py
@@ -160,18 +160,37 @@
 LANES = 128
 
 
-def window_kernel(w_ref, o_ref):
+def window_kernel(table_ref, raw_ref, o_ref):
     span_z = CCZ + 2 * RIM
     span_x = CCX + 2 * RIM
     span_y = CCY + 2 * RIM
     shape = (span_z, span_x, LANES)
-    log_x = w_ref[0, 0]
-    log_y = w_ref[0, 1]
-    log_z = w_ref[0, 2]
-    inside = w_ref[0, 3]
+    block_z = pl.program_id(0)
+    block_x = pl.program_id(1)
+    block_y = pl.program_id(2)
+    wide = raw_ref.shape[-1]
+    shift = (wide - block_y * CCY) % wide
+
+    def cut(field):
+        slab = raw_ref[field, pl.ds(block_z * CCZ, span_z), pl.ds(block_x * CCX, span_x), :]
+        return pltpu.roll(slab, shift, 2)[:, :, :LANES]
+
+    noise = cut(0)
+    codes = cut(1)
     depth_pos = lax.broadcasted_iota(jnp.int32, shape, 0)
     column_pos = lax.broadcasted_iota(jnp.int32, shape, 1)
     row_pos = lax.broadcasted_iota(jnp.int32, shape, 2)
+    inside = jnp.where(row_pos < span_y, cut(2), 0.0)
+
+    def lookup(row):
+        value = jnp.zeros(shape, jnp.float32)
+        for code_value in range(NFAC):
+            value = jnp.where(codes == code_value, table_ref[row, code_value], value)
+        return value
+
+    log_x = noise + lookup(0)
+    log_y = log_x + lookup(1)
+    log_z = log_x + lookup(2)
     perm_x = jnp.exp(log_x)
     perm_y = jnp.exp(log_y)
     perm_z = jnp.exp(log_z)
@@ -256,34 +275,26 @@
     o_ref[0] = jnp.concatenate(rows, axis=0)
 
 
-def upscale_windows(fields):
-    span_z = CCZ + 2 * RIM
-    span_x = CCX + 2 * RIM
+def upscale_windows(raw, facies_table):
     span_y = CCY + 2 * RIM
-    count_z = (fields.shape[1] - 2 * RIM) // CCZ
-    count_x = (fields.shape[2] - 2 * RIM) // CCX
-    count_y = (fields.shape[3] - 2 * RIM) // CCY
-    pieces = []
-    for block_z in range(count_z):
-        for block_x in range(count_x):
-            for block_y in range(count_y):
-                piece = fields[
-                    :,
-                    block_z * CCZ : block_z * CCZ + span_z,
-                    block_x * CCX : block_x * CCX + span_x,
-                    block_y * CCY : block_y * CCY + span_y,
-                ]
-                pieces.append(piece)
-    windows = jnp.stack(pieces)
-    windows = jnp.pad(windows, ((0, 0),) * 4 + ((0, LANES - span_y),))
-    count = windows.shape[0]
+    count_z = (raw.shape[1] - 2 * RIM) // CCZ
+    count_x = (raw.shape[2] - 2 * RIM) // CCX
+    count_y = (raw.shape[3] - 2 * RIM) // CCY
+    wide = -(-(raw.shape[3] + LANES) // LANES) * LANES
+    raw = jnp.pad(raw, ((0, 0),) * 3 + ((0, wide - raw.shape[3]),))
+    count = count_z * count_x * count_y
     sums = pl.pallas_call(
         window_kernel,
-        grid=(count,),
-        in_specs=[pl.BlockSpec((1, 4, span_z, span_x, LANES), lambda i: (i, 0, 0, 0, 0))],
-        out_specs=pl.BlockSpec((1, 8, LANES), lambda i: (i, 0, 0)),
+        grid=(count_z, count_x, count_y),
+        in_specs=[
+            pl.BlockSpec(memory_space=pltpu.SMEM),
+            pl.BlockSpec(raw.shape, lambda z, x, y: (0, 0, 0, 0)),
+        ],
+        out_specs=pl.BlockSpec(
+            (1, 8, LANES), lambda z, x, y: (z * count_x * count_y + x * count_y + y, 0, 0)
+        ),
         out_shape=jax.ShapeDtypeStruct((count, 8, LANES), jnp.float32),
-    )(windows)
+    )(facies_table, raw)
     return sums[:, :3, 0].T.reshape((3, count_z, count_x, count_y))
 
 
@@ -381,15 +392,14 @@
     index_y = lax.axis_index("gy")
     raw = jnp.stack([log_noise, facies.astype(jnp.float32)])
     raw = extended(raw, (("gx", 2), ("gy", 3), ("gz", 1)), RIM)
-    log_x, log_y, log_z = log_fields(raw[0], raw[1], facies_table)
     anchor_z = index_z * depth_len
     anchor_y = index_y * cols_len
     anchor_x = index_x * rows_len
-    mask_z = span_mask(anchor_z, log_x.shape[0] - 2 * RIM, depth_len * size_z, RIM)
-    mask_x = span_mask(anchor_x, log_x.shape[1] - 2 * RIM, rows_len * size_x, RIM)
-    mask_y = span_mask(anchor_y, log_x.shape[2] - 2 * RIM, cols_len * size_y, RIM)
+    mask_z = span_mask(anchor_z, depth_len, depth_len * size_z, RIM)
+    mask_x = span_mask(anchor_x, rows_len, rows_len * size_x, RIM)
+    mask_y = span_mask(anchor_y, cols_len, cols_len * size_y, RIM)
     inside = mask_z[:, None, None] * mask_x[None, :, None] * mask_y[None, None, :]
-    upscaled = upscale_windows(jnp.stack([log_x, log_y, log_z, inside]))
+    upscaled = upscale_windows(jnp.concatenate([raw, inside[None]]), facies_table)
     coarse_z, coarse_x, coarse_y = pressure_old.shape
     bundle = jnp.stack([upscaled[0], upscaled[1], upscaled[2], pressure_old, accumulation, source])
     every = lax.all_gather(bundle, "gy", axis=3, tiled=True)

time: 84.5 us -> 79.4 us (0.940)
  Pallas kernels: 16.9 us -> 25.2 us
  other arithmetic: 14.5 us -> 6.56 us
  local copies, waits for them, and re-layouts: 12.8 us -> 5.86 us
  waiting for transfers between devices: 9.7 us -> 11.3 us
    add x2 -> x0, other arithmetic: 9.14 us -> none  [log_fields(): return (base_log, base_log + extra_y, base_log + extra_z)]
    pallas_call x1, Pallas kernels: 16.9 us -> 25.2 us  [upscale_windows(): pl.pallas_call(window_kernel, grid=(count_z, count_x, count_y), in_specs=...]
    pad x1, local copies, waits for them, and re-layouts: 4.81 us -> 2.29 us  [upscale_windows(): raw = jnp.pad(raw, ((0, 0),) * 3 + ((0, wide - raw.shape[3]),))]
    unnamed x20 -> x13, local copies, waits for them, and re-layouts: 2.25 us -> 0.05 us
    concatenate x0 -> x1, other arithmetic: none -> 2.03 us  [local(): jnp.concatenate([raw, inside[None]])]
    slice x1 -> x0, local copies, waits for them, and re-layouts: 1.79 us -> none  [log_fields(): facies_table[2, code_value]]
    ppermute x3, waiting for transfers between devices: 9.41 us -> 10.5 us  [extended(): lax.ppermute(head, axis, [((i + 1) % count, i) for i in range(ends)])]
    concatenate x2 -> x1, other arithmetic: 1.74 us -> 1.03 us  [extended(): jnp.concatenate([lax.ppermute(tail, axis, [(i, (i + 1) % count) for i in...]
  transfers between devices with their start and end apart: 6 -> 6, of which waited for: 4 -> 5; matrix products, arithmetic and copies ran while one was open for 3% -> 1% of each run, Pallas kernels for 0% -> 0%
where the time goes in v3:
time: 79.4 us; the launch traced here: 78.9 us
  Pallas kernels  25.2 us (32%)
  blocking collectives  15.6 us (20%)
  starting transfers between devices  13.5 us (17%)
  waiting for transfers between devices  11.3 us (14%)
  other arithmetic  6.56 us (8%)
  local copies, waits for them, and re-layouts  5.86 us (7%)
  between operations  0.82 us (1%)
    pallas_call x1, Pallas kernels, upscale_windows(): pl.pallas_call(window_kernel, grid=(count_z, count_x, count_y), in_specs=...  25.2 us
    ppermute x3, waiting for transfers between devices, extended(): lax.ppermute(head, axis, [((i + 1) % count, i) for i in range(ends)])  10.5 us
    ppermute x3, starting transfers between devices, extended(): lax.ppermute(tail, axis, [(i, (i + 1) % count) for i in range(ends)])  9.64 us
    all_gather x1, blocking collectives, local(): every = lax.all_gather(every, 'gx', axis=2, tiled=True)  9.49 us
    all_gather x1, blocking collectives, local(): every = lax.all_gather(bundle, 'gy', axis=3, tiled=True)  4.33 us
    ppermute x3, starting transfers between devices, extended(): lax.ppermute(head, axis, [((i + 1) % count, i) for i in range(ends)])  3.88 us
    pad x1, local copies, waits for them, and re-layouts, upscale_windows(): raw = jnp.pad(raw, ((0, 0),) * 3 + ((0, wide - raw.shape[3]),))  2.29 us
    concatenate x1, other arithmetic, local(): jnp.concatenate([raw, inside[None]])  2.03 us
  transfers between devices with their start and end apart: 6, of which 5 were waited for; matrix products, arithmetic and copies ran while one was open for 1% of the time, Pallas kernels for 0%

profile of v3, /device:TPU:0, one launch (start us, length us, event | category | flops | bytes accessed | tf_op | source)
XLA Modules:
  0.0 78.9 jit_solution(17499293196954481574)
XLA Ops:
  0.6 1.0 %convert_bitcast_fusion = f32[1,16,32,128]{3,2,1,0:T(8,128)S(1)} fusion(s32[16,32,128]{2,1,0:T(8,128)} %param.7), kind=kLoop, calls=%fused_computation.9 | loop fusion | flops 65536 | bytes 524288 | tf_op jit(solution)/shard_map/stack | solution.py:393
  1.6 0.9 %pad_maximum_fusion.9 = (f32[2,16,4,128]{3,2,1,0:T(4,128)S(1)}, f32[2,16,4,128]{3,2,1,0:T(4,128)S(1)}) fusion(f32[1,16,32,128]{3,2,1,0:T(8,128)S(1)} %convert_bitcast_fusion, f32[1,16,32,128]{3,2,1,0:T(8,128)} %bitcast.44), kind=kLoop, calls=%fused_computation.20 | loop fusion | flops 32768 | bytes 655360 | tf_op jit(solution)/shard_map/slice | solution.py:25
  2.5 4.9 %collective-permute-start = (f32[2,16,4,128]{3,2,1,0:T(4,128)S(1)}, f32[2,16,4,128]{3,2,1,0:T(4,128)S(1)}, u32[]{:S(2)}, u32[]{:S(2)}) collective-permute-start(f32[2,16,4,128]{3,2,1,0:T(4,128)S(1)} %get-tuple-element.18), channel_id=1, source_target_pairs={{0,4},{4,8},{8,12},{1,5},{5,9},{9,13},{2,6},{6,10},{10,14},{3,7},{... | collective-permute-start | bytes 196616 | tf_op jit(solution)/shard_map/ppermute | solution.py:28
  7.4 1.3 %collective-permute-start.1 = (f32[2,16,4,128]{3,2,1,0:T(4,128)S(1)}, f32[2,16,4,128]{3,2,1,0:T(4,128)S(1)}, u32[]{:S(2)}, u32[]{:S(2)}) collective-permute-start(f32[2,16,4,128]{3,2,1,0:T(4,128)S(1)} %get-tuple-element.19), channel_id=1, source_target_pairs={{4,0},{8,4},{12,8},{5,1},{9,5},{13,9},{6,2},{10,6},{14,10},{7,3},{... | collective-permute-start | bytes 196616 | tf_op jit(solution)/shard_map/ppermute | solution.py:30
  8.9 0.5 collective-permute-done
  9.3 4.3 %collective-permute-done.1 = f32[2,16,4,128]{3,2,1,0:T(4,128)S(1)} collective-permute-done((f32[2,16,4,128]{3,2,1,0:T(4,128)S(1)}, f32[2,16,4,128]{3,2,1,0:T(4,128)S(1)}, u32[]{:S(2)}, u32[]{:S(2)}) %collective-permute-start.1) | collective-permute-done | bytes 65568 | tf_op jit(solution)/shard_map/ppermute | solution.py:30
  13.6 1.0 %pad_maximum_fusion.1 = f32[2,16,40,128]{3,2,1,0:T(8,128)S(1)} fusion(f32[2,16,4,128]{3,2,1,0:T(4,128)S(1)} %collective-permute-done.1, f32[1,16,32,128]{3,2,1,0:T(8,128)S(1)} %convert_bitcast_fusion, f32[1,16,32,128]{3,2,1,0:T(8,128)} %bitcast.45, f32[2,16,4,128]{3,2,1,0:T(4,128)S(1)} %collective-permute-done), kind=kLoop, calls=%fused_computation.1 | loop fusion | flops 491520 | bytes 1310720 | tf_op jit(solution)/shard_map/concatenate | solution.py:26
  14.6 0.2 fusion.40
  14.9 0.3 copy.19
  15.2 3.4 %collective-permute-start.2 = (f32[2,16,40,4]{2,1,3,0:T(8,128)S(1)}, f32[2,16,40,4]{2,1,3,0:T(8,128)S(1)}, u32[]{:S(2)}, u32[]{:S(2)}) collective-permute-start(f32[2,16,40,4]{2,1,3,0:T(8,128)S(1)} %copy.19), channel_id=1, source_target_pairs={{0,2},{1,3},{4,6},{5,7},{8,10},{9,11},{12,14},{13,15},{16,18},{17,... | collective-permute-start | bytes 61448 | tf_op jit(solution)/shard_map/ppermute | solution.py:28
  18.6 0.3 copy.20
  18.8 1.3 %collective-permute-start.3 = (f32[2,16,40,4]{2,1,3,0:T(8,128)S(1)}, f32[2,16,40,4]{2,1,3,0:T(8,128)S(1)}, u32[]{:S(2)}, u32[]{:S(2)}) collective-permute-start(f32[2,16,40,4]{2,1,3,0:T(8,128)S(1)} %copy.20), channel_id=1, source_target_pairs={{2,0},{3,1},{6,4},{7,5},{10,8},{11,9},{14,12},{15,13},{18,16},{19,... | collective-permute-start | bytes 61448 | tf_op jit(solution)/shard_map/ppermute | solution.py:30
  20.2 0.3 collective-permute-done.2
  20.5 0.3 copy.21
  20.8 4.2 %collective-permute-done.3 = f32[2,16,40,4]{2,1,3,0:T(8,128)S(1)} collective-permute-done((f32[2,16,40,4]{2,1,3,0:T(8,128)S(1)}, f32[2,16,40,4]{2,1,3,0:T(8,128)S(1)}, u32[]{:S(2)}, u32[]{:S(2)}) %collective-permute-start.3) | collective-permute-done | bytes 20512 | tf_op jit(solution)/shard_map/ppermute | solution.py:30
  25.0 0.3 copy.22
  25.3 0.4 pad_maximum_fusion.7
  25.7 1.3 %collective-permute-start.4 = (f32[2,4,40,136]{3,2,1,0:T(8,128)S(1)}, f32[2,4,40,136]{3,2,1,0:T(8,128)S(1)}, u32[]{:S(2)}, u32[]{:S(2)}) collective-permute-start(f32[2,4,40,136]{3,2,1,0:T(8,128)S(1)} %get-tuple-element.14), channel_id=1, source_target_pairs={{0,1},{2,3},{4,5},{6,7},{8,9},{10,11},{12,13},{14,15},{16,17},{18,... | collective-permute-start | bytes 522248 | tf_op jit(solution)/shard_map/ppermute | solution.py:28
  27.0 1.3 %collective-permute-start.5 = (f32[2,4,40,136]{3,2,1,0:T(8,128)S(1)}, f32[2,4,40,136]{3,2,1,0:T(8,128)S(1)}, u32[]{:S(2)}, u32[]{:S(2)}) collective-permute-start(f32[2,4,40,136]{3,2,1,0:T(8,128)S(1)} %get-tuple-element.15), channel_id=1, source_target_pairs={{1,0},{3,2},{5,4},{7,6},{9,8},{11,10},{13,12},{15,14},{17,16},{19,... | collective-permute-start | bytes 522248 | tf_op jit(solution)/shard_map/ppermute | solution.py:30
  28.3 0.2 broadcast_multiply_fusion
  28.5 2.0 %collective-permute-done.5 = f32[2,4,40,136]{3,2,1,0:T(8,128)S(1)} collective-permute-done((f32[2,4,40,136]{3,2,1,0:T(8,128)S(1)}, f32[2,4,40,136]{3,2,1,0:T(8,128)S(1)}, u32[]{:S(2)}, u32[]{:S(2)}) %collective-permute-start.5) | collective-permute-done | bytes 174112 | tf_op jit(solution)/shard_map/ppermute | solution.py:30
  30.6 2.0 %pad_maximum_fusion = f32[3,24,40,136]{3,2,1,0:T(8,128)S(1)} fusion(f32[1,24,40,136]{3,2,1,0:T(8,128)S(1)} %broadcast_multiply_fusion, f32[2,4,40,136]{3,2,1,0:T(8,128)S(1)} %collective-permute-done.5, f32[2,16,40,4]{3,2,1,0:T(8,128)S(1)} %copy.22, f32[2,16,4,128]{3,2,1,0:T(4,128)S(1)} %collective-permute-done.1, ...), kind=kLoop, calls=%fused_computation | loop fusion | flops 3133440 | bytes 3133440 | tf_op jit(solution)/shard_map/concatenate | solution.py:402
  32.6 2.3 %pad.18.raw_ref = f32[3,24,40,384]{3,2,1,0:T(8,128)} pad(f32[3,24,40,136]{3,2,1,0:T(8,128)S(1)} %pad_maximum_fusion, f32[]{:T(128)} %constant.15.clone.1), padding=0_0x0_0x0_0x0_248 | pad | bytes 5990404 | tf_op jit(solution)/shard_map/jit(_pad)/pad | solution.py:284
  34.9 25.2 %shard_map.77 = f32[8,8,128]{2,1,0:T(8,128)} custom-call(f32[3,4]{1,0:T(4,128)} %table_ref.1, f32[3,24,40,384]{3,2,1,0:T(8,128)} %pad.18.raw_ref), custom_call_target="tpu_custom_call" | custom-call | tf_op jit(solution)/shard_map/pallas_call | solution.py:286
  60.1 0.8 slice.232
  61.4 4.3 %all_gather.9 = f32[6,2,1,8]{0,1,2,3:T(2,128)S(1)} all-gather(f32[6,2,1,4]{0,1,2,3:T(2,128)S(1)} %copy.24), channel_id=1, replica_groups=mesh['real'=2,'gx'=4,'gy'=2,'gz'=2] {'gy'}, dimensions={3}, use_global_device_ids=true | all-gather | bytes 576 | tf_op jit(solution)/shard_map/all_gather | solution.py:405
  65.8 9.5 %all_gather.10 = f32[6,2,4,8]{0,1,2,3:T(2,128)S(1)} all-gather(f32[6,2,1,8]{0,1,2,3:T(2,128)S(1)} %all_gather.9), channel_id=1, replica_groups=mesh['real'=2,'gx'=4,'gy'=2,'gz'=2] {'gx'}, dimensions={2}, use_global_device_ids=true | all-gather | bytes 1920 | tf_op jit(solution)/shard_map/all_gather | solution.py:406
  75.2 0.1 copy.25
  75.4 1.8 %all_gather.11 = f32[6,4,4,8]{3,2,0,1:T(4,128)S(1)} all-gather(f32[6,2,4,8]{3,2,0,1:T(4,128)S(1)} %copy.25), channel_id=1, replica_groups=mesh['real'=2,'gx'=4,'gy'=2,'gz'=2] {'gz'}, dimensions={1}, use_global_device_ids=true | all-gather | bytes 4608 | tf_op jit(solution)/shard_map/all_gather | solution.py:407
  77.3 0.7 reshape.69
  78.0 0.1 fusion.10
  78.3 0.7 dynamic-slice_divide_fusion
  (30 shorter events, 0.9 us)
Async XLA Ops:
  2.5 6.8 %collective-permute-start = (f32[2,16,4,128]{3,2,1,0:T(4,128)S(1)}, f32[2,16,4,128]{3,2,1,0:T(4,128)S(1)}, u32[]{:S(2)}, u32[]{:S(2)}) collective-permute-start(f32[2,16,4,128]{3,2,1,0:T(4,128)S(1)} %get-tuple-element.18), channel_id=1, source_target_pairs={{0,4},{4,8},{8,12},{1,5},{5,9},{9,13},{2,6},{6,10},{10,14},{3,7},{... | collective-permute-start | bytes 196616 | tf_op jit(solution)/shard_map/ppermute | solution.py:28
  7.4 6.2 %collective-permute-start.1 = (f32[2,16,4,128]{3,2,1,0:T(4,128)S(1)}, f32[2,16,4,128]{3,2,1,0:T(4,128)S(1)}, u32[]{:S(2)}, u32[]{:S(2)}) collective-permute-start(f32[2,16,4,128]{3,2,1,0:T(4,128)S(1)} %get-tuple-element.19), channel_id=1, source_target_pairs={{4,0},{8,4},{12,8},{5,1},{9,5},{13,9},{6,2},{10,6},{14,10},{7,3},{... | collective-permute-start | bytes 196616 | tf_op jit(solution)/shard_map/ppermute | solution.py:30
  14.6 10.7 %copy-start = (f32[16,32,128]{2,1,0:T(8,128)S(1)}, f32[16,32,128]{2,1,0:T(8,128)}, u32[]{:S(2)}) copy-start(f32[16,32,128]{2,1,0:T(8,128)} %param.6) | copy-start | bytes 786436
  15.2 5.3 %collective-permute-start.2 = (f32[2,16,40,4]{2,1,3,0:T(8,128)S(1)}, f32[2,16,40,4]{2,1,3,0:T(8,128)S(1)}, u32[]{:S(2)}, u32[]{:S(2)}) collective-permute-start(f32[2,16,40,4]{2,1,3,0:T(8,128)S(1)} %copy.19), channel_id=1, source_target_pairs={{0,2},{1,3},{4,6},{5,7},{8,10},{9,11},{12,14},{13,15},{16,18},{17,... | collective-permute-start | bytes 61448 | tf_op jit(solution)/shard_map/ppermute | solution.py:28
  18.8 6.2 %collective-permute-start.3 = (f32[2,16,40,4]{2,1,3,0:T(8,128)S(1)}, f32[2,16,40,4]{2,1,3,0:T(8,128)S(1)}, u32[]{:S(2)}, u32[]{:S(2)}) collective-permute-start(f32[2,16,40,4]{2,1,3,0:T(8,128)S(1)} %copy.20), channel_id=1, source_target_pairs={{2,0},{3,1},{6,4},{7,5},{10,8},{11,9},{14,12},{15,13},{18,16},{19,... | collective-permute-start | bytes 61448 | tf_op jit(solution)/shard_map/ppermute | solution.py:30
  25.7 2.8 %collective-permute-start.4 = (f32[2,4,40,136]{3,2,1,0:T(8,128)S(1)}, f32[2,4,40,136]{3,2,1,0:T(8,128)S(1)}, u32[]{:S(2)}, u32[]{:S(2)}) collective-permute-start(f32[2,4,40,136]{3,2,1,0:T(8,128)S(1)} %get-tuple-element.14), channel_id=1, source_target_pairs={{0,1},{2,3},{4,5},{6,7},{8,9},{10,11},{12,13},{14,15},{16,17},{18,... | collective-permute-start | bytes 522248 | tf_op jit(solution)/shard_map/ppermute | solution.py:28
  27.0 3.5 %collective-permute-start.5 = (f32[2,4,40,136]{3,2,1,0:T(8,128)S(1)}, f32[2,4,40,136]{3,2,1,0:T(8,128)S(1)}, u32[]{:S(2)}, u32[]{:S(2)}) collective-permute-start(f32[2,4,40,136]{3,2,1,0:T(8,128)S(1)} %get-tuple-element.15), channel_id=1, source_target_pairs={{1,0},{3,2},{5,4},{7,6},{9,8},{11,10},{13,12},{15,14},{17,16},{19,... | collective-permute-start | bytes 522248 | tf_op jit(solution)/shard_map/ppermute | solution.py:30
  34.9 26.4 %copy-start.1 = (f32[2,1,4]{2,1,0:T(1,128)S(1)}, f32[2,1,4]{2,1,0:T(1,128)}, u32[]{:S(2)}) copy-start(f32[2,1,4]{2,1,0:T(1,128)} %param.9) | copy-start | bytes 100
  34.9 26.4 %copy-start.2 = (f32[2,1,4]{2,1,0:T(1,128)S(1)}, f32[2,1,4]{2,1,0:T(1,128)}, u32[]{:S(2)}) copy-start(f32[2,1,4]{2,1,0:T(1,128)} %param.10) | copy-start | bytes 100
  34.9 26.4 %copy-start.3 = (f32[2,1,4]{2,1,0:T(1,128)S(1)}, f32[2,1,4]{2,1,0:T(1,128)}, u32[]{:S(2)}) copy-start(f32[2,1,4]{2,1,0:T(1,128)} %param.11) | copy-start | bytes 100

commit v4 on v3

--- a/solution.py
+++ b/solution.py
@@ -1,3 +1,5 @@
+import functools
+
 import jax
 import jax.numpy as jnp
 from jax import lax
@@ -160,27 +162,41 @@
 LANES = 128
 
 
-def window_kernel(table_ref, raw_ref, o_ref):
+def window_kernel(table_ref, raw_ref, o_ref, *, count_x, count_y, count):
     span_z = CCZ + 2 * RIM
     span_x = CCX + 2 * RIM
     span_y = CCY + 2 * RIM
+    segments = LANES // span_y
     shape = (span_z, span_x, LANES)
-    block_z = pl.program_id(0)
-    block_x = pl.program_id(1)
-    block_y = pl.program_id(2)
+    pack = pl.program_id(0)
     wide = raw_ref.shape[-1]
-    shift = (wide - block_y * CCY) % wide
-
-    def cut(field):
-        slab = raw_ref[field, pl.ds(block_z * CCZ, span_z), pl.ds(block_x * CCX, span_x), :]
-        return pltpu.roll(slab, shift, 2)[:, :, :LANES]
-
-    noise = cut(0)
-    codes = cut(1)
     depth_pos = lax.broadcasted_iota(jnp.int32, shape, 0)
     column_pos = lax.broadcasted_iota(jnp.int32, shape, 1)
-    row_pos = lax.broadcasted_iota(jnp.int32, shape, 2)
-    inside = jnp.where(row_pos < span_y, cut(2), 0.0)
+    lane = lax.broadcasted_iota(jnp.int32, shape, 2)
+    segment = jnp.zeros(shape, jnp.int32)
+    for bound in range(1, segments + 1):
+        segment = segment + (lane >= bound * span_y).astype(jnp.int32)
+    row_pos = lane - span_y * segment
+    noise = jnp.zeros(shape, jnp.float32)
+    codes = jnp.zeros(shape, jnp.float32)
+    inside = jnp.zeros(shape, jnp.float32)
+    for slot in range(segments):
+        window = pack * segments + slot
+        valid = window < count
+        window = jnp.minimum(window, count - 1)
+        block_z = window // (count_x * count_y)
+        block_x = (window // count_y) % count_x
+        block_y = window % count_y
+        shift = (slot * span_y - block_y * CCY + wide) % wide
+        here = segment == slot
+
+        def cut(field):
+            slab = raw_ref[field, pl.ds(block_z * CCZ, span_z), pl.ds(block_x * CCX, span_x), :]
+            return pltpu.roll(slab, shift, 2)[:, :, :LANES]
+
+        noise = jnp.where(here, cut(0), noise)
+        codes = jnp.where(here, cut(1), codes)
+        inside = jnp.where(here & valid, cut(2), inside)
 
     def lookup(row):
         value = jnp.zeros(shape, jnp.float32)
@@ -249,13 +265,13 @@
     ramp_z = ((span_z - 1) / 2.0 - depth_pos).astype(jnp.float32)
     cheb_ratio = BOUND_MID / BOUND_HALF
     cases = (
-        (ramp_x, link_x, face_x, CCY * CCZ, up_x),
-        (ramp_y, link_y, face_y, CCX * CCZ, up_y),
-        (ramp_z, link_z, face_z, CCX * CCY, up_z),
+        (ramp_x, link_x, face_x, CCY * CCZ, up_x, down_x),
+        (ramp_y, link_y, face_y, CCX * CCZ, up_y, down_y),
+        (ramp_z, link_z, face_z, CCX * CCY, up_z, down_z),
     )
     rows = []
-    for ramp, link, face, area, upper_of in cases:
-        source_term = -unknown * apply_operator(ramp)
+    for ramp, link, face, area, upper_of, lower_of in cases:
+        source_term = -unknown * (link - lower_of(link))
         update = scaling * source_term / BOUND_MID
         solution = update
         rho_old = 1.0 / cheb_ratio
@@ -269,8 +285,7 @@
         flux = jnp.where(face, link * (pressure - upper_of(pressure)), 0.0)
         total = jnp.sum(flux, axis=0)
         total = jnp.sum(total, axis=0, keepdims=True)
-        total = jnp.sum(total, axis=1, keepdims=True)
-        rows.append(jnp.broadcast_to(total * (0.5 / area), (1, LANES)))
+        rows.append(total * (0.5 / area))
     rows.append(jnp.zeros((8 - len(rows), LANES), jnp.float32))
     o_ref[0] = jnp.concatenate(rows, axis=0)
 
@@ -283,19 +298,22 @@
     wide = -(-(raw.shape[3] + LANES) // LANES) * LANES
     raw = jnp.pad(raw, ((0, 0),) * 3 + ((0, wide - raw.shape[3]),))
     count = count_z * count_x * count_y
+    segments = LANES // span_y
+    packs = -(-count // segments)
+    kernel = functools.partial(window_kernel, count_x=count_x, count_y=count_y, count=count)
     sums = pl.pallas_call(
-        window_kernel,
-        grid=(count_z, count_x, count_y),
+        kernel,
+        grid=(packs,),
         in_specs=[
             pl.BlockSpec(memory_space=pltpu.SMEM),
-            pl.BlockSpec(raw.shape, lambda z, x, y: (0, 0, 0, 0)),
+            pl.BlockSpec(raw.shape, lambda p: (0, 0, 0, 0)),
         ],
-        out_specs=pl.BlockSpec(
-            (1, 8, LANES), lambda z, x, y: (z * count_x * count_y + x * count_y + y, 0, 0)
-        ),
-        out_shape=jax.ShapeDtypeStruct((count, 8, LANES), jnp.float32),
+        out_specs=pl.BlockSpec((1, 8, LANES), lambda p: (p, 0, 0)),
+        out_shape=jax.ShapeDtypeStruct((packs, 8, LANES), jnp.float32),
     )(facies_table, raw)
-    return sums[:, :3, 0].T.reshape((3, count_z, count_x, count_y))
+    sums = sums[:, :3, : segments * span_y].reshape(packs, 3, segments, span_y).sum(axis=3)
+    sums = sums.transpose(1, 0, 2).reshape(3, packs * segments)[:, :count]
+    return sums.reshape((3, count_z, count_x, count_y))
 
 
 def coarse_sweep(perm_pad, press_pad, inside_pad, accumulation, fixed):

time: 79.4 us -> 69.1 us (0.87)
  Pallas kernels: 25.2 us -> 14.8 us
    pallas_call x1, Pallas kernels: 25.2 us -> 14.8 us  [upscale_windows(): pl.pallas_call(kernel, grid=(packs,), in_specs=[pl.BlockSpec(memory_space...]
where the time goes in v4:
time: 69.1 us; the launch traced here: 68.7 us
  blocking collectives  15.6 us (23%)
  Pallas kernels  14.8 us (21%)
  starting transfers between devices  13.5 us (20%)
  waiting for transfers between devices  11.3 us (16%)
  other arithmetic  6.67 us (10%)
  local copies, waits for them, and re-layouts  5.89 us (9%)
  between operations  0.84 us (1%)
    pallas_call x1, Pallas kernels, upscale_windows(): pl.pallas_call(kernel, grid=(packs,), in_specs=[pl.BlockSpec(memory_space...  14.8 us
    ppermute x3, waiting for transfers between devices, extended(): lax.ppermute(head, axis, [((i + 1) % count, i) for i in range(ends)])  10.5 us
    ppermute x3, starting transfers between devices, extended(): lax.ppermute(tail, axis, [(i, (i + 1) % count) for i in range(ends)])  9.64 us
    all_gather x1, blocking collectives, local(): every = lax.all_gather(every, 'gx', axis=2, tiled=True)  9.49 us
    all_gather x1, blocking collectives, local(): every = lax.all_gather(bundle, 'gy', axis=3, tiled=True)  4.33 us
    ppermute x3, starting transfers between devices, extended(): lax.ppermute(head, axis, [((i + 1) % count, i) for i in range(ends)])  3.88 us
    pad x1, local copies, waits for them, and re-layouts, upscale_windows(): raw = jnp.pad(raw, ((0, 0),) * 3 + ((0, wide - raw.shape[3]),))  2.3 us
    concatenate x1, other arithmetic, local(): jnp.concatenate([raw, inside[None]])  2.04 us
  transfers between devices with their start and end apart: 6, of which 5 were waited for; matrix products, arithmetic and copies ran while one was open for 1% of the time, Pallas kernels for 0%

profile of v4, /device:TPU:0, one launch (start us, length us, event | category | flops | bytes accessed | tf_op | source)
XLA Modules:
  0.0 68.7 jit_solution(4629328792196558434)
XLA Ops:
  0.6 1.0 %convert_bitcast_fusion = f32[1,16,32,128]{3,2,1,0:T(8,128)S(1)} fusion(s32[16,32,128]{2,1,0:T(8,128)} %param.7), kind=kLoop, calls=%fused_computation.9 | loop fusion | flops 65536 | bytes 524288 | tf_op jit(solution)/shard_map/stack | solution.py:411
  1.6 0.9 %pad_maximum_fusion.9 = (f32[2,16,4,128]{3,2,1,0:T(4,128)S(1)}, f32[2,16,4,128]{3,2,1,0:T(4,128)S(1)}) fusion(f32[1,16,32,128]{3,2,1,0:T(8,128)S(1)} %convert_bitcast_fusion, f32[1,16,32,128]{3,2,1,0:T(8,128)} %bitcast.43), kind=kLoop, calls=%fused_computation.20 | loop fusion | flops 32768 | bytes 655360 | tf_op jit(solution)/shard_map/slice | solution.py:27
  2.5 4.9 %collective-permute-start = (f32[2,16,4,128]{3,2,1,0:T(4,128)S(1)}, f32[2,16,4,128]{3,2,1,0:T(4,128)S(1)}, u32[]{:S(2)}, u32[]{:S(2)}) collective-permute-start(f32[2,16,4,128]{3,2,1,0:T(4,128)S(1)} %get-tuple-element.18), channel_id=1, source_target_pairs={{0,4},{4,8},{8,12},{1,5},{5,9},{9,13},{2,6},{6,10},{10,14},{3,7},{... | collective-permute-start | bytes 196616 | tf_op jit(solution)/shard_map/ppermute | solution.py:30
  7.4 1.3 %collective-permute-start.1 = (f32[2,16,4,128]{3,2,1,0:T(4,128)S(1)}, f32[2,16,4,128]{3,2,1,0:T(4,128)S(1)}, u32[]{:S(2)}, u32[]{:S(2)}) collective-permute-start(f32[2,16,4,128]{3,2,1,0:T(4,128)S(1)} %get-tuple-element.19), channel_id=1, source_target_pairs={{4,0},{8,4},{12,8},{5,1},{9,5},{13,9},{6,2},{10,6},{14,10},{7,3},{... | collective-permute-start | bytes 196616 | tf_op jit(solution)/shard_map/ppermute | solution.py:32
  8.9 0.5 collective-permute-done
  9.3 4.3 %collective-permute-done.1 = f32[2,16,4,128]{3,2,1,0:T(4,128)S(1)} collective-permute-done((f32[2,16,4,128]{3,2,1,0:T(4,128)S(1)}, f32[2,16,4,128]{3,2,1,0:T(4,128)S(1)}, u32[]{:S(2)}, u32[]{:S(2)}) %collective-permute-start.1) | collective-permute-done | bytes 65568 | tf_op jit(solution)/shard_map/ppermute | solution.py:32
  13.6 1.0 %pad_maximum_fusion.1 = f32[2,16,40,128]{3,2,1,0:T(8,128)S(1)} fusion(f32[2,16,4,128]{3,2,1,0:T(4,128)S(1)} %collective-permute-done.1, f32[1,16,32,128]{3,2,1,0:T(8,128)S(1)} %convert_bitcast_fusion, f32[1,16,32,128]{3,2,1,0:T(8,128)} %bitcast.44, f32[2,16,4,128]{3,2,1,0:T(4,128)S(1)} %collective-permute-done), kind=kLoop, calls=%fused_computation.1 | loop fusion | flops 491520 | bytes 1310720 | tf_op jit(solution)/shard_map/concatenate | solution.py:28
  14.6 0.2 fusion.40
  14.9 0.3 copy.18
  15.2 3.4 %collective-permute-start.2 = (f32[2,16,40,4]{2,1,3,0:T(8,128)S(1)}, f32[2,16,40,4]{2,1,3,0:T(8,128)S(1)}, u32[]{:S(2)}, u32[]{:S(2)}) collective-permute-start(f32[2,16,40,4]{2,1,3,0:T(8,128)S(1)} %copy.18), channel_id=1, source_target_pairs={{0,2},{1,3},{4,6},{5,7},{8,10},{9,11},{12,14},{13,15},{16,18},{17,... | collective-permute-start | bytes 61448 | tf_op jit(solution)/shard_map/ppermute | solution.py:30
  18.6 0.3 copy.19
  18.8 1.3 %collective-permute-start.3 = (f32[2,16,40,4]{2,1,3,0:T(8,128)S(1)}, f32[2,16,40,4]{2,1,3,0:T(8,128)S(1)}, u32[]{:S(2)}, u32[]{:S(2)}) collective-permute-start(f32[2,16,40,4]{2,1,3,0:T(8,128)S(1)} %copy.19), channel_id=1, source_target_pairs={{2,0},{3,1},{6,4},{7,5},{10,8},{11,9},{14,12},{15,13},{18,16},{19,... | collective-permute-start | bytes 61448 | tf_op jit(solution)/shard_map/ppermute | solution.py:32
  20.2 0.3 collective-permute-done.2
  20.5 0.3 copy.20
  20.8 4.2 %collective-permute-done.3 = f32[2,16,40,4]{2,1,3,0:T(8,128)S(1)} collective-permute-done((f32[2,16,40,4]{2,1,3,0:T(8,128)S(1)}, f32[2,16,40,4]{2,1,3,0:T(8,128)S(1)}, u32[]{:S(2)}, u32[]{:S(2)}) %collective-permute-start.3) | collective-permute-done | bytes 20512 | tf_op jit(solution)/shard_map/ppermute | solution.py:32
  25.0 0.3 copy.21
  25.3 0.4 pad_maximum_fusion.7
  25.7 1.3 %collective-permute-start.4 = (f32[2,4,40,136]{3,2,1,0:T(8,128)S(1)}, f32[2,4,40,136]{3,2,1,0:T(8,128)S(1)}, u32[]{:S(2)}, u32[]{:S(2)}) collective-permute-start(f32[2,4,40,136]{3,2,1,0:T(8,128)S(1)} %get-tuple-element.14), channel_id=1, source_target_pairs={{0,1},{2,3},{4,5},{6,7},{8,9},{10,11},{12,13},{14,15},{16,17},{18,... | collective-permute-start | bytes 522248 | tf_op jit(solution)/shard_map/ppermute | solution.py:30
  27.0 1.3 %collective-permute-start.5 = (f32[2,4,40,136]{3,2,1,0:T(8,128)S(1)}, f32[2,4,40,136]{3,2,1,0:T(8,128)S(1)}, u32[]{:S(2)}, u32[]{:S(2)}) collective-permute-start(f32[2,4,40,136]{3,2,1,0:T(8,128)S(1)} %get-tuple-element.15), channel_id=1, source_target_pairs={{1,0},{3,2},{5,4},{7,6},{9,8},{11,10},{13,12},{15,14},{17,16},{19,... | collective-permute-start | bytes 522248 | tf_op jit(solution)/shard_map/ppermute | solution.py:32
  28.3 0.2 broadcast_multiply_fusion
  28.5 2.0 %collective-permute-done.5 = f32[2,4,40,136]{3,2,1,0:T(8,128)S(1)} collective-permute-done((f32[2,4,40,136]{3,2,1,0:T(8,128)S(1)}, f32[2,4,40,136]{3,2,1,0:T(8,128)S(1)}, u32[]{:S(2)}, u32[]{:S(2)}) %collective-permute-start.5) | collective-permute-done | bytes 174112 | tf_op jit(solution)/shard_map/ppermute | solution.py:32
  30.6 2.0 %pad_maximum_fusion = f32[3,24,40,136]{3,2,1,0:T(8,128)S(1)} fusion(f32[1,24,40,136]{3,2,1,0:T(8,128)S(1)} %broadcast_multiply_fusion, f32[2,4,40,136]{3,2,1,0:T(8,128)S(1)} %collective-permute-done.5, f32[2,16,40,4]{3,2,1,0:T(8,128)S(1)} %copy.21, f32[2,16,4,128]{3,2,1,0:T(4,128)S(1)} %collective-permute-done.1, ...), kind=kLoop, calls=%fused_computation | loop fusion | flops 3133440 | bytes 3133440 | tf_op jit(solution)/shard_map/concatenate | solution.py:420
  32.6 2.3 %pad.18.raw_ref = f32[3,24,40,384]{3,2,1,0:T(8,128)} pad(f32[3,24,40,136]{3,2,1,0:T(8,128)S(1)} %pad_maximum_fusion, f32[]{:T(128)} %constant.14.clone.1), padding=0_0x0_0x0_0x0_248 | pad | bytes 5990404 | tf_op jit(solution)/shard_map/jit(_pad)/pad | solution.py:299
  34.9 14.8 %shard_map.77 = f32[3,8,128]{2,1,0:T(8,128)} custom-call(f32[3,4]{1,0:T(4,128)} %table_ref.1, f32[3,24,40,384]{3,2,1,0:T(8,128)} %pad.18.raw_ref), custom_call_target="tpu_custom_call" | custom-call | tf_op jit(solution)/shard_map/pallas_call | solution.py:304
  49.8 0.7 %slice.239 = f32[3,3,120]{2,1,0:T(4,128)S(1)} slice(f32[3,8,128]{2,1,0:T(8,128)} %shard_map.77), slice={[0:3], [0:3], [0:120]} | slice | bytes 8640 | tf_op jit(solution)/shard_map/slice | solution.py:314
  51.2 4.3 %all_gather.9 = f32[6,2,1,8]{0,1,2,3:T(2,128)S(1)} all-gather(f32[6,2,1,4]{0,1,2,3:T(2,128)S(1)} %copy.23), channel_id=1, replica_groups=mesh['real'=2,'gx'=4,'gy'=2,'gz'=2] {'gy'}, dimensions={3}, use_global_device_ids=true | all-gather | bytes 576 | tf_op jit(solution)/shard_map/all_gather | solution.py:423
  55.5 9.5 %all_gather.10 = f32[6,2,4,8]{0,1,2,3:T(2,128)S(1)} all-gather(f32[6,2,1,8]{0,1,2,3:T(2,128)S(1)} %all_gather.9), channel_id=1, replica_groups=mesh['real'=2,'gx'=4,'gy'=2,'gz'=2] {'gx'}, dimensions={2}, use_global_device_ids=true | all-gather | bytes 1920 | tf_op jit(solution)/shard_map/all_gather | solution.py:424
  65.0 0.1 copy.24
  65.2 1.8 %all_gather.11 = f32[6,4,4,8]{3,2,0,1:T(4,128)S(1)} all-gather(f32[6,2,4,8]{3,2,0,1:T(4,128)S(1)} %copy.24), channel_id=1, replica_groups=mesh['real'=2,'gx'=4,'gy'=2,'gz'=2] {'gz'}, dimensions={1}, use_global_device_ids=true | all-gather | bytes 4608 | tf_op jit(solution)/shard_map/all_gather | solution.py:425
  67.1 0.1 fusion.10
  67.3 0.7 reshape.77
  68.0 0.7 dynamic-slice_divide_fusion
  (33 shorter events, 1.0 us)
Async XLA Ops:
  2.5 6.8 %collective-permute-start = (f32[2,16,4,128]{3,2,1,0:T(4,128)S(1)}, f32[2,16,4,128]{3,2,1,0:T(4,128)S(1)}, u32[]{:S(2)}, u32[]{:S(2)}) collective-permute-start(f32[2,16,4,128]{3,2,1,0:T(4,128)S(1)} %get-tuple-element.18), channel_id=1, source_target_pairs={{0,4},{4,8},{8,12},{1,5},{5,9},{9,13},{2,6},{6,10},{10,14},{3,7},{... | collective-permute-start | bytes 196616 | tf_op jit(solution)/shard_map/ppermute | solution.py:30
  7.4 6.2 %collective-permute-start.1 = (f32[2,16,4,128]{3,2,1,0:T(4,128)S(1)}, f32[2,16,4,128]{3,2,1,0:T(4,128)S(1)}, u32[]{:S(2)}, u32[]{:S(2)}) collective-permute-start(f32[2,16,4,128]{3,2,1,0:T(4,128)S(1)} %get-tuple-element.19), channel_id=1, source_target_pairs={{4,0},{8,4},{12,8},{5,1},{9,5},{13,9},{6,2},{10,6},{14,10},{7,3},{... | collective-permute-start | bytes 196616 | tf_op jit(solution)/shard_map/ppermute | solution.py:32
  14.6 10.7 %copy-start = (f32[16,32,128]{2,1,0:T(8,128)S(1)}, f32[16,32,128]{2,1,0:T(8,128)}, u32[]{:S(2)}) copy-start(f32[16,32,128]{2,1,0:T(8,128)} %param.6) | copy-start | bytes 786436
  15.2 5.3 %collective-permute-start.2 = (f32[2,16,40,4]{2,1,3,0:T(8,128)S(1)}, f32[2,16,40,4]{2,1,3,0:T(8,128)S(1)}, u32[]{:S(2)}, u32[]{:S(2)}) collective-permute-start(f32[2,16,40,4]{2,1,3,0:T(8,128)S(1)} %copy.18), channel_id=1, source_target_pairs={{0,2},{1,3},{4,6},{5,7},{8,10},{9,11},{12,14},{13,15},{16,18},{17,... | collective-permute-start | bytes 61448 | tf_op jit(solution)/shard_map/ppermute | solution.py:30
  18.8 6.2 %collective-permute-start.3 = (f32[2,16,40,4]{2,1,3,0:T(8,128)S(1)}, f32[2,16,40,4]{2,1,3,0:T(8,128)S(1)}, u32[]{:S(2)}, u32[]{:S(2)}) collective-permute-start(f32[2,16,40,4]{2,1,3,0:T(8,128)S(1)} %copy.19), channel_id=1, source_target_pairs={{2,0},{3,1},{6,4},{7,5},{10,8},{11,9},{14,12},{15,13},{18,16},{19,... | collective-permute-start | bytes 61448 | tf_op jit(solution)/shard_map/ppermute | solution.py:32
  25.7 2.8 %collective-permute-start.4 = (f32[2,4,40,136]{3,2,1,0:T(8,128)S(1)}, f32[2,4,40,136]{3,2,1,0:T(8,128)S(1)}, u32[]{:S(2)}, u32[]{:S(2)}) collective-permute-start(f32[2,4,40,136]{3,2,1,0:T(8,128)S(1)} %get-tuple-element.14), channel_id=1, source_target_pairs={{0,1},{2,3},{4,5},{6,7},{8,9},{10,11},{12,13},{14,15},{16,17},{18,... | collective-permute-start | bytes 522248 | tf_op jit(solution)/shard_map/ppermute | solution.py:30
  27.0 3.5 %collective-permute-start.5 = (f32[2,4,40,136]{3,2,1,0:T(8,128)S(1)}, f32[2,4,40,136]{3,2,1,0:T(8,128)S(1)}, u32[]{:S(2)}, u32[]{:S(2)}) collective-permute-start(f32[2,4,40,136]{3,2,1,0:T(8,128)S(1)} %get-tuple-element.15), channel_id=1, source_target_pairs={{1,0},{3,2},{5,4},{7,6},{9,8},{11,10},{13,12},{15,14},{17,16},{19,... | collective-permute-start | bytes 522248 | tf_op jit(solution)/shard_map/ppermute | solution.py:32
  34.9 16.1 %copy-start.1 = (f32[2,1,4]{2,1,0:T(1,128)S(1)}, f32[2,1,4]{2,1,0:T(1,128)}, u32[]{:S(2)}) copy-start(f32[2,1,4]{2,1,0:T(1,128)} %param.9) | copy-start | bytes 100
  34.9 16.1 %copy-start.2 = (f32[2,1,4]{2,1,0:T(1,128)S(1)}, f32[2,1,4]{2,1,0:T(1,128)}, u32[]{:S(2)}) copy-start(f32[2,1,4]{2,1,0:T(1,128)} %param.10) | copy-start | bytes 100
  34.9 16.2 %copy-start.3 = (f32[2,1,4]{2,1,0:T(1,128)S(1)}, f32[2,1,4]{2,1,0:T(1,128)}, u32[]{:S(2)}) copy-start(f32[2,1,4]{2,1,0:T(1,128)} %param.11) | copy-start | bytes 100

commit v5 on v4

--- a/solution.py
+++ b/solution.py
@@ -1,4 +1,5 @@
 import functools
+import itertools
 
 import jax
 import jax.numpy as jnp
@@ -34,6 +35,76 @@
             axis=dim,
         )
     return cells
+
+
+def halo_all(block, width):
+    names = ("gx", "gy", "gz")
+    dims = (2, 3, 1)
+    sizes = [lax.axis_size(name) for name in names]
+    coords = [lax.axis_index(name) for name in names]
+
+    def linear(point):
+        return (point[0] * sizes[1] + point[1]) * sizes[2] + point[2]
+
+    def region(values, dim, offset, lower_first):
+        length = values.shape[dim]
+        first = lax.slice_in_dim(values, 0, width, axis=dim)
+        last = lax.slice_in_dim(values, length - width, length, axis=dim)
+        if offset == "P":
+            return jnp.where(lower_first, last, first)
+        return last if offset == -1 else first
+
+    received = {}
+
+    def fetch(key):
+        if key in received:
+            return received[key]
+        slab = block
+        for axis in range(3):
+            if key[axis] != 0:
+                slab = region(slab, dims[axis], key[axis], coords[axis] == 0)
+        pairs = []
+        for source in itertools.product(*[range(size) for size in sizes]):
+            target = []
+            for axis in range(3):
+                if key[axis] == "P":
+                    target.append(1 - source[axis])
+                else:
+                    target.append(source[axis] - key[axis])
+            if all(0 <= target[axis] < sizes[axis] for axis in range(3)):
+                pairs.append((linear(source), linear(target)))
+        received[key] = lax.ppermute(slab, names, pairs) if pairs else jnp.zeros_like(slab)
+        return received[key]
+
+    pieces = {}
+    for offset in itertools.product((-1, 0, 1), repeat=3):
+        if offset == (0, 0, 0):
+            pieces[offset] = block
+            continue
+        key = []
+        keep = jnp.bool_(True)
+        for axis in range(3):
+            if offset[axis] != 0 and sizes[axis] == 2:
+                key.append("P")
+                keep = keep & (coords[axis] == (1 if offset[axis] == -1 else 0))
+            else:
+                key.append(offset[axis])
+        if any(abs(offset[axis]) == 1 and sizes[axis] == 1 for axis in range(3)):
+            slab = block
+            for axis in range(3):
+                if offset[axis] != 0:
+                    slab = lax.slice_in_dim(slab, 0, width, axis=dims[axis])
+            pieces[offset] = jnp.zeros_like(slab)
+            continue
+        got = fetch(tuple(key))
+        pieces[offset] = jnp.where(keep, got, 0.0)
+    planes = []
+    for oz in (-1, 0, 1):
+        rows = []
+        for ox in (-1, 0, 1):
+            rows.append(jnp.concatenate([pieces[(ox, oy, oz)] for oy in (-1, 0, 1)], axis=3))
+        planes.append(jnp.concatenate(rows, axis=2))
+    return jnp.concatenate(planes, axis=1)
 
 
 def raise_flat(values, offset):
@@ -409,7 +480,7 @@
     index_x = lax.axis_index("gx")
     index_y = lax.axis_index("gy")
     raw = jnp.stack([log_noise, facies.astype(jnp.float32)])
-    raw = extended(raw, (("gx", 2), ("gy", 3), ("gz", 1)), RIM)
+    raw = halo_all(raw, RIM)
     anchor_z = index_z * depth_len
     anchor_y = index_y * cols_len
     anchor_x = index_x * rows_len

time: 69.1 us -> 89.3 us (1.29)
  starting transfers between devices: 13.5 us -> 26.8 us
  other arithmetic: 6.67 us -> 13.4 us
  blocking collectives: 15.6 us -> 18.2 us
  local copies, waits for them, and re-layouts: 5.89 us -> 4.5 us
  waiting for transfers between devices: 11.3 us -> 9.95 us
    ppermute x6 -> x11, starting transfers between devices: 13.5 us -> 26.8 us  [fetch(): lax.ppermute(slab, names, pairs)]
    concatenate x1, other arithmetic: 2.04 us -> 7.54 us  [local(): jnp.concatenate([raw, inside[None]])]
    select_n x0 -> x16, other arithmetic: none -> 3.47 us  [the longest x7 3.18 us: region(): return jnp.where(lower_first, last, first)]
    all_gather x1, blocking collectives: 9.49 us -> 12.1 us  [local(): every = lax.all_gather(every, 'gx', axis=2, tiled=True)]
    ppermute x6 -> x11, waiting for transfers between devices: 11.3 us -> 9.95 us  [fetch(): lax.ppermute(slab, names, pairs)]
    slice x2 -> x0, other arithmetic: 1.29 us -> none  [extended(): lax.slice_in_dim(cells, cells.shape[dim] - width, cells.shape[dim], axis=...]
    concatenate x1 -> x0, other arithmetic: 1.03 us -> none  [extended(): jnp.concatenate([lax.ppermute(tail, axis, [(i, (i + 1) % count) for i in...]
  transfers between devices with their start and end apart: 6 -> 11, of which waited for: 5 -> 4; matrix products, arithmetic and copies ran while one was open for 1% -> 3% of each run, Pallas kernels for 0% -> 0%
where the time goes in v5:
time: 89.3 us; the launch traced here: 88.8 us
  starting transfers between devices  26.8 us (30%)
  blocking collectives  18.2 us (20%)
  Pallas kernels  14.8 us (17%)
  other arithmetic  13.4 us (15%)
  waiting for transfers between devices  9.95 us (11%)
  local copies, waits for them, and re-layouts  4.5 us (5%)
  between operations  1.02 us (1%)
    ppermute x11, starting transfers between devices, fetch(): lax.ppermute(slab, names, pairs)  26.8 us
    pallas_call x1, Pallas kernels, upscale_windows(): pl.pallas_call(kernel, grid=(packs,), in_specs=[pl.BlockSpec(memory_space...  14.8 us
    all_gather x1, blocking collectives, local(): every = lax.all_gather(every, 'gx', axis=2, tiled=True)  12.1 us
    ppermute x11, waiting for transfers between devices, fetch(): lax.ppermute(slab, names, pairs)  9.95 us
    concatenate x1, other arithmetic, local(): jnp.concatenate([raw, inside[None]])  7.54 us
    all_gather x1, blocking collectives, local(): every = lax.all_gather(bundle, 'gy', axis=3, tiled=True)  4.33 us
    select_n x7, other arithmetic, region(): return jnp.where(lower_first, last, first)  3.18 us
    pad x1, local copies, waits for them, and re-layouts, upscale_windows(): raw = jnp.pad(raw, ((0, 0),) * 3 + ((0, wide - raw.shape[3]),))  2.32 us
  transfers between devices with their start and end apart: 11, of which 4 were waited for; matrix products, arithmetic and copies ran while one was open for 3% of the time, Pallas kernels for 0%

profile of v5, /device:TPU:0, one launch (start us, length us, event | category | flops | bytes accessed | tf_op | source)
XLA Modules:
  0.0 88.8 jit_solution(15799463811969198376)
XLA Ops:
  0.6 1.0 %convert_bitcast_fusion = f32[1,16,32,128]{3,2,1,0:T(8,128)S(1)} fusion(s32[16,32,128]{2,1,0:T(8,128)} %param.7), kind=kLoop, calls=%fused_computation.33 | loop fusion | flops 65536 | bytes 524288 | tf_op jit(solution)/shard_map/stack | solution.py:482
  1.7 1.1 %fusion.8 = (f32[2,16,4,4]{3,2,1,0:T(4,128)S(1)}, f32[2,16,4,4]{3,2,1,0:T(4,128)S(1)}) fusion(f32[1,16,32,128]{3,2,1,0:T(8,128)} %bitcast.43, f32[1,16,32,128]{3,2,1,0:T(8,128)S(1)} %convert_bitcast_fusion, pred[]{:T(512)S(6)} %eq.11), kind=kLoop, calls=%fused_computation.49 | loop fusion | flops 3072 | bytes 528385 | tf_op jit(solution)/shard_map/jit(_where)/select_n | solution.py:54
  2.7 5.9 %collective-permute-start.6 = (f32[2,16,4,4]{3,2,1,0:T(4,128)S(1)}, f32[2,16,4,4]{3,2,1,0:T(4,128)S(1)}, u32[]{:S(2)}, u32[]{:S(2)}) collective-permute-start(f32[2,16,4,4]{3,2,1,0:T(4,128)S(1)} %get-tuple-element.20), channel_id=1, source_target_pairs={{0,6},{1,7},{2,4},{3,5},{4,10},{5,11},{6,8},{7,9},{8,14},{9,15},{1... | collective-permute-start | bytes 6152 | tf_op jit(solution)/shard_map/ppermute | solution.py:76
  8.6 2.6 %collective-permute-start = (f32[2,4,4,4]{3,2,1,0:T(4,128)S(1)}, f32[2,4,4,4]{3,2,1,0:T(4,128)S(1)}, u32[]{:S(2)}, u32[]{:S(2)}) collective-permute-start(f32[2,4,4,4]{3,2,1,0:T(4,128)S(1)} %slice_select_fusion.2), channel_id=1, source_target_pairs={{0,7},{1,6},{2,5},{3,4},{4,11},{5,10},{6,9},{7,8},{8,15},{9,14},{1... | collective-permute-start | bytes 1544 | tf_op jit(solution)/shard_map/ppermute | solution.py:76
  11.3 1.3 %collective-permute-start.9 = (f32[2,16,4,4]{3,2,1,0:T(4,128)S(1)}, f32[2,16,4,4]{3,2,1,0:T(4,128)S(1)}, u32[]{:S(2)}, u32[]{:S(2)}) collective-permute-start(f32[2,16,4,4]{3,2,1,0:T(4,128)S(1)} %get-tuple-element.21), channel_id=1, source_target_pairs={{4,2},{5,3},{6,0},{7,1},{8,6},{9,7},{10,4},{11,5},{12,10},{13,11},... | collective-permute-start | bytes 6152 | tf_op jit(solution)/shard_map/ppermute | solution.py:76
  12.6 1.3 %collective-permute-start.4 = (f32[2,4,4,4]{3,2,1,0:T(4,128)S(1)}, f32[2,4,4,4]{3,2,1,0:T(4,128)S(1)}, u32[]{:S(2)}, u32[]{:S(2)}) collective-permute-start(f32[2,4,4,4]{3,2,1,0:T(4,128)S(1)} %slice_select_fusion.1), channel_id=1, source_target_pairs={{4,3},{5,2},{6,1},{7,0},{8,7},{9,6},{10,5},{11,4},{12,11},{13,10},... | collective-permute-start | bytes 1544 | tf_op jit(solution)/shard_map/ppermute | solution.py:76
  13.9 1.3 %fusion.1 = f32[2,16,32,4]{3,2,1,0:T(8,128)S(1)} fusion(f32[1,16,32,128]{3,2,1,0:T(8,128)} %bitcast.44, f32[1,16,32,128]{3,2,1,0:T(8,128)S(1)} %convert_bitcast_fusion, pred[]{:T(512)S(6)} %eq.11), kind=kLoop, calls=%fused_computation.28 | loop fusion | flops 12288 | bytes 540673 | tf_op jit(solution)/shard_map/jit(_where)/select_n | solution.py:54
  15.1 1.6 %collective-permute-start.8 = (f32[2,16,32,4]{3,2,1,0:T(8,128)S(1)}, f32[2,16,32,4]{3,2,1,0:T(8,128)S(1)}, u32[]{:S(2)}, u32[]{:S(2)}) collective-permute-start(f32[2,16,32,4]{3,2,1,0:T(8,128)S(1)} %fusion.1), channel_id=1, source_target_pairs={{0,2},{1,3},{2,0},{3,1},{4,6},{5,7},{6,4},{7,5},{8,10},{9,11},{10,... | collective-permute-start | bytes 49160 | tf_op jit(solution)/shard_map/ppermute | solution.py:76
  16.7 0.8 fusion.21
  17.7 0.2 broadcast_multiply_fusion
  17.9 0.9 collective-permute-start.2
  18.8 1.2 %collective-permute-done.4 = f32[2,4,4,4]{3,2,1,0:T(4,128)S(1)} collective-permute-done((f32[2,4,4,4]{3,2,1,0:T(4,128)S(1)}, f32[2,4,4,4]{3,2,1,0:T(4,128)S(1)}, u32[]{:S(2)}, u32[]{:S(2)}) %collective-permute-start.4) | collective-permute-done | bytes 544 | tf_op jit(solution)/shard_map/ppermute | solution.py:76
  20.0 4.4 %collective-permute-start.1 = (f32[2,4,4,128]{3,2,1,0:T(4,128)S(1)}, f32[2,4,4,128]{3,2,1,0:T(4,128)S(1)}, u32[]{:S(2)}, u32[]{:S(2)}) collective-permute-start(f32[2,4,4,128]{3,2,1,0:T(4,128)S(1)} %get-tuple-element.18), channel_id=1, source_target_pairs={{0,5},{1,4},{2,7},{3,6},{4,9},{5,8},{6,11},{7,10},{8,13},{9,12},{1... | collective-permute-start | bytes 49160 | tf_op jit(solution)/shard_map/ppermute | solution.py:76
  24.4 1.3 %collective-permute-start.5 = (f32[2,4,4,128]{3,2,1,0:T(4,128)S(1)}, f32[2,4,4,128]{3,2,1,0:T(4,128)S(1)}, u32[]{:S(2)}, u32[]{:S(2)}) collective-permute-start(f32[2,4,4,128]{3,2,1,0:T(4,128)S(1)} %get-tuple-element.19), channel_id=1, source_target_pairs={{4,1},{5,0},{6,3},{7,2},{8,5},{9,4},{10,7},{11,6},{12,9},{13,8},{1... | collective-permute-start | bytes 49160 | tf_op jit(solution)/shard_map/ppermute | solution.py:76
  25.8 0.5 collective-permute-start.3
  26.3 7.1 %collective-permute-done.2 = f32[2,4,32,4]{3,2,1,0:T(8,128)S(1)} collective-permute-done((f32[2,4,32,4]{3,2,1,0:T(8,128)S(1)}, f32[2,4,32,4]{3,2,1,0:T(8,128)S(1)}, u32[]{:S(2)}, u32[]{:S(2)}) %collective-permute-start.2) | collective-permute-done | bytes 4128 | tf_op jit(solution)/shard_map/ppermute | solution.py:76
  33.4 1.3 %collective-permute-start.10 = (f32[2,16,4,128]{3,2,1,0:T(4,128)S(1)}, f32[2,16,4,128]{3,2,1,0:T(4,128)S(1)}, u32[]{:S(2)}, u32[]{:S(2)}) collective-permute-start(f32[2,16,4,128]{3,2,1,0:T(4,128)S(1)} %get-tuple-element.15), channel_id=1, source_target_pairs={{4,0},{5,1},{6,2},{7,3},{8,4},{9,5},{10,6},{11,7},{12,8},{13,9},{1... | collective-permute-start | bytes 196616 | tf_op jit(solution)/shard_map/ppermute | solution.py:76
  34.8 5.8 %collective-permute-start.7 = (f32[2,16,4,128]{3,2,1,0:T(4,128)S(1)}, f32[2,16,4,128]{3,2,1,0:T(4,128)S(1)}, u32[]{:S(2)}, u32[]{:S(2)}) collective-permute-start(f32[2,16,4,128]{3,2,1,0:T(4,128)S(1)} %get-tuple-element.14), channel_id=1, source_target_pairs={{0,4},{1,5},{2,6},{3,7},{4,8},{5,9},{6,10},{7,11},{8,12},{9,13},{1... | collective-permute-start | bytes 196616 | tf_op jit(solution)/shard_map/ppermute | solution.py:76
  40.6 0.1 broadcast_select_fusion.1
  40.8 0.1 collective-permute-done.10
  41.0 1.5 %collective-permute-done.7 = f32[2,16,4,128]{3,2,1,0:T(4,128)S(1)} collective-permute-done((f32[2,16,4,128]{3,2,1,0:T(4,128)S(1)}, f32[2,16,4,128]{3,2,1,0:T(4,128)S(1)}, u32[]{:S(2)}, u32[]{:S(2)}) %collective-permute-start.7) | collective-permute-done | bytes 65568 | tf_op jit(solution)/shard_map/ppermute | solution.py:76
  42.5 7.5 %pad_maximum_fusion = f32[3,24,40,136]{3,2,1,0:T(8,128)S(1)} fusion(f32[1,24,40,136]{3,2,1,0:T(8,128)S(1)} %broadcast_multiply_fusion, f32[2,4,4,4]{3,2,1,0:T(4,128)S(1)} %get-tuple-element.44, f32[2,4,4,128]{3,2,1,0:T(4,128)S(1)} %get-tuple-element.48, f32[2,4,4,4]{3,2,1,0:T(4,128)S(1)} %get-tuple-element.45, f32[2,4,32,4]{3,2,1,0:T(8,128)S(1)} %get-tuple-element.23, ...), kind=kLoop, calls=%fused_computation | loop fusion | flops 10967040 | bytes 3133440 | tf_op jit(solution)/shard_map/concatenate | solution.py:491
  50.0 2.3 %pad.18.raw_ref = f32[3,24,40,384]{3,2,1,0:T(8,128)} pad(f32[3,24,40,136]{3,2,1,0:T(8,128)S(1)} %pad_maximum_fusion, f32[]{:T(128)} %constant.20.clone.1), padding=0_0x0_0x0_0x0_248 | pad | bytes 5990404 | tf_op jit(solution)/shard_map/jit(_pad)/pad | solution.py:370
  52.4 14.8 %shard_map.77 = f32[3,8,128]{2,1,0:T(8,128)} custom-call(f32[3,4]{1,0:T(4,128)} %table_ref.1, f32[3,24,40,384]{3,2,1,0:T(8,128)} %pad.18.raw_ref), custom_call_target="tpu_custom_call" | custom-call | tf_op jit(solution)/shard_map/pallas_call | solution.py:375
  67.2 0.7 slice.345
  68.7 4.3 %all_gather.9 = f32[6,2,1,8]{0,1,2,3:T(2,128)S(1)} all-gather(f32[6,2,1,4]{0,1,2,3:T(2,128)S(1)} %copy.19), channel_id=1, replica_groups=mesh['real'=2,'gx'=4,'gy'=2,'gz'=2] {'gy'}, dimensions={3}, use_global_device_ids=true | all-gather | bytes 576 | tf_op jit(solution)/shard_map/all_gather | solution.py:494
  73.0 12.1 %all_gather.10 = f32[6,2,4,8]{0,1,2,3:T(2,128)S(1)} all-gather(f32[6,2,1,8]{0,1,2,3:T(2,128)S(1)} %all_gather.9), channel_id=1, replica_groups=mesh['real'=2,'gx'=4,'gy'=2,'gz'=2] {'gx'}, dimensions={2}, use_global_device_ids=true | all-gather | bytes 1920 | tf_op jit(solution)/shard_map/all_gather | solution.py:495
  85.1 0.1 copy.20
  85.2 1.8 %all_gather.11 = f32[6,4,4,8]{3,2,0,1:T(4,128)S(1)} all-gather(f32[6,2,4,8]{3,2,0,1:T(4,128)S(1)} %copy.20), channel_id=1, replica_groups=mesh['real'=2,'gx'=4,'gy'=2,'gz'=2] {'gz'}, dimensions={1}, use_global_device_ids=true | all-gather | bytes 4608 | tf_op jit(solution)/shard_map/all_gather | solution.py:496
  87.1 0.1 fusion.29
  87.3 0.7 reshape.77
  88.1 0.7 dynamic-slice_divide_fusion
  (52 shorter events, 1.3 us)
Async XLA Ops:
  0.6 16.9 %copy-start = (f32[16,32,128]{2,1,0:T(8,128)S(1)}, f32[16,32,128]{2,1,0:T(8,128)}, u32[]{:S(2)}) copy-start(f32[16,32,128]{2,1,0:T(8,128)} %param.6) | copy-start | bytes 786436
  2.7 21.7 %collective-permute-start.6 = (f32[2,16,4,4]{3,2,1,0:T(4,128)S(1)}, f32[2,16,4,4]{3,2,1,0:T(4,128)S(1)}, u32[]{:S(2)}, u32[]{:S(2)}) collective-permute-start(f32[2,16,4,4]{3,2,1,0:T(4,128)S(1)} %get-tuple-element.20), channel_id=1, source_target_pairs={{0,6},{1,7},{2,4},{3,5},{4,10},{5,11},{6,8},{7,9},{8,14},{9,15},{1... | collective-permute-start | bytes 6152 | tf_op jit(solution)/shard_map/ppermute | solution.py:76
  8.6 9.3 %collective-permute-start = (f32[2,4,4,4]{3,2,1,0:T(4,128)S(1)}, f32[2,4,4,4]{3,2,1,0:T(4,128)S(1)}, u32[]{:S(2)}, u32[]{:S(2)}) collective-permute-start(f32[2,4,4,4]{3,2,1,0:T(4,128)S(1)} %slice_select_fusion.2), channel_id=1, source_target_pairs={{0,7},{1,6},{2,5},{3,4},{4,11},{5,10},{6,9},{7,8},{8,15},{9,14},{1... | collective-permute-start | bytes 1544 | tf_op jit(solution)/shard_map/ppermute | solution.py:76
  11.3 14.5 %collective-permute-start.9 = (f32[2,16,4,4]{3,2,1,0:T(4,128)S(1)}, f32[2,16,4,4]{3,2,1,0:T(4,128)S(1)}, u32[]{:S(2)}, u32[]{:S(2)}) collective-permute-start(f32[2,16,4,4]{3,2,1,0:T(4,128)S(1)} %get-tuple-element.21), channel_id=1, source_target_pairs={{4,2},{5,3},{6,0},{7,1},{8,6},{9,7},{10,4},{11,5},{12,10},{13,11},... | collective-permute-start | bytes 6152 | tf_op jit(solution)/shard_map/ppermute | solution.py:76
  12.6 7.4 %collective-permute-start.4 = (f32[2,4,4,4]{3,2,1,0:T(4,128)S(1)}, f32[2,4,4,4]{3,2,1,0:T(4,128)S(1)}, u32[]{:S(2)}, u32[]{:S(2)}) collective-permute-start(f32[2,4,4,4]{3,2,1,0:T(4,128)S(1)} %slice_select_fusion.1), channel_id=1, source_target_pairs={{4,3},{5,2},{6,1},{7,0},{8,7},{9,6},{10,5},{11,4},{12,11},{13,10},... | collective-permute-start | bytes 1544 | tf_op jit(solution)/shard_map/ppermute | solution.py:76
  15.1 19.6 %collective-permute-start.8 = (f32[2,16,32,4]{3,2,1,0:T(8,128)S(1)}, f32[2,16,32,4]{3,2,1,0:T(8,128)S(1)}, u32[]{:S(2)}, u32[]{:S(2)}) collective-permute-start(f32[2,16,32,4]{3,2,1,0:T(8,128)S(1)} %fusion.1), channel_id=1, source_target_pairs={{0,2},{1,3},{2,0},{3,1},{4,6},{5,7},{6,4},{7,5},{8,10},{9,11},{10,... | collective-permute-start | bytes 49160 | tf_op jit(solution)/shard_map/ppermute | solution.py:76
  17.9 15.5 %collective-permute-start.2 = (f32[2,4,32,4]{3,2,1,0:T(8,128)S(1)}, f32[2,4,32,4]{3,2,1,0:T(8,128)S(1)}, u32[]{:S(2)}, u32[]{:S(2)}) collective-permute-start(f32[2,4,32,4]{3,2,1,0:T(8,128)S(1)} %slice_select_fusion), channel_id=1, source_target_pairs={{0,3},{1,2},{2,1},{3,0},{4,7},{5,6},{6,5},{7,4},{8,11},{9,10},{10,... | collective-permute-start | bytes 12296 | tf_op jit(solution)/shard_map/ppermute | solution.py:76
  20.0 20.8 %collective-permute-start.1 = (f32[2,4,4,128]{3,2,1,0:T(4,128)S(1)}, f32[2,4,4,128]{3,2,1,0:T(4,128)S(1)}, u32[]{:S(2)}, u32[]{:S(2)}) collective-permute-start(f32[2,4,4,128]{3,2,1,0:T(4,128)S(1)} %get-tuple-element.18), channel_id=1, source_target_pairs={{0,5},{1,4},{2,7},{3,6},{4,9},{5,8},{6,11},{7,10},{8,13},{9,12},{1... | collective-permute-start | bytes 49160 | tf_op jit(solution)/shard_map/ppermute | solution.py:76
  24.4 16.3 %collective-permute-start.5 = (f32[2,4,4,128]{3,2,1,0:T(4,128)S(1)}, f32[2,4,4,128]{3,2,1,0:T(4,128)S(1)}, u32[]{:S(2)}, u32[]{:S(2)}) collective-permute-start(f32[2,4,4,128]{3,2,1,0:T(4,128)S(1)} %get-tuple-element.19), channel_id=1, source_target_pairs={{4,1},{5,0},{6,3},{7,2},{8,5},{9,4},{10,7},{11,6},{12,9},{13,8},{1... | collective-permute-start | bytes 49160 | tf_op jit(solution)/shard_map/ppermute | solution.py:76
  25.8 15.0 %collective-permute-start.3 = (f32[2,4,32,128]{3,2,1,0:T(8,128)S(1)}, f32[2,4,32,128]{3,2,1,0:T(8,128)S(1)}, u32[]{:S(2)}, u32[]{:S(2)}) collective-permute-start(f32[2,4,32,128]{3,2,1,0:T(8,128)S(1)} %fusion.4), channel_id=1, source_target_pairs={{0,1},{1,0},{2,3},{3,2},{4,5},{5,4},{6,7},{7,6},{8,9},{9,8},{10,11... | collective-permute-start | bytes 393224 | tf_op jit(solution)/shard_map/ppermute | solution.py:76
  33.4 7.6 %collective-permute-start.10 = (f32[2,16,4,128]{3,2,1,0:T(4,128)S(1)}, f32[2,16,4,128]{3,2,1,0:T(4,128)S(1)}, u32[]{:S(2)}, u32[]{:S(2)}) collective-permute-start(f32[2,16,4,128]{3,2,1,0:T(4,128)S(1)} %get-tuple-element.15), channel_id=1, source_target_pairs={{4,0},{5,1},{6,2},{7,3},{8,4},{9,5},{10,6},{11,7},{12,8},{13,9},{1... | collective-permute-start | bytes 196616 | tf_op jit(solution)/shard_map/ppermute | solution.py:76
  34.8 7.7 %collective-permute-start.7 = (f32[2,16,4,128]{3,2,1,0:T(4,128)S(1)}, f32[2,16,4,128]{3,2,1,0:T(4,128)S(1)}, u32[]{:S(2)}, u32[]{:S(2)}) collective-permute-start(f32[2,16,4,128]{3,2,1,0:T(4,128)S(1)} %get-tuple-element.14), channel_id=1, source_target_pairs={{0,4},{1,5},{2,6},{3,7},{4,8},{5,9},{6,10},{7,11},{8,12},{9,13},{1... | collective-permute-start | bytes 196616 | tf_op jit(solution)/shard_map/ppermute | solution.py:76
  52.4 16.1 %copy-start.1 = (f32[2,1,4]{2,1,0:T(1,128)S(1)}, f32[2,1,4]{2,1,0:T(1,128)}, u32[]{:S(2)}) copy-start(f32[2,1,4]{2,1,0:T(1,128)} %param.9) | copy-start | bytes 100
  52.4 16.1 %copy-start.2 = (f32[2,1,4]{2,1,0:T(1,128)S(1)}, f32[2,1,4]{2,1,0:T(1,128)}, u32[]{:S(2)}) copy-start(f32[2,1,4]{2,1,0:T(1,128)} %param.10) | copy-start | bytes 100
  52.4 16.2 %copy-start.3 = (f32[2,1,4]{2,1,0:T(1,128)S(1)}, f32[2,1,4]{2,1,0:T(1,128)}, u32[]{:S(2)}) copy-start(f32[2,1,4]{2,1,0:T(1,128)} %param.11) | copy-start | bytes 100

commit v6 on v4

--- a/solution.py
+++ b/solution.py
@@ -25,14 +25,15 @@
         ends = count - 1
         head = lax.slice_in_dim(cells, 0, width, axis=dim)
         tail = lax.slice_in_dim(cells, cells.shape[dim] - width, cells.shape[dim], axis=dim)
-        cells = jnp.concatenate(
-            [
-                lax.ppermute(tail, axis, [(i, (i + 1) % count) for i in range(ends)]),
-                cells,
-                lax.ppermute(head, axis, [((i + 1) % count, i) for i in range(ends)]),
-            ],
-            axis=dim,
-        )
+        if count == 2:
+            lower_side = lax.axis_index(axis) == 0
+            got = lax.ppermute(jnp.where(lower_side, tail, head), axis, [(0, 1), (1, 0)])
+            below = jnp.where(lower_side, 0.0, got)
+            above = jnp.where(lower_side, got, 0.0)
+        else:
+            below = lax.ppermute(tail, axis, [(i, (i + 1) % count) for i in range(ends)])
+            above = lax.ppermute(head, axis, [((i + 1) % count, i) for i in range(ends)])
+        cells = jnp.concatenate([below, cells, above], axis=dim)
     return cells
 
 

time: 69.1 us -> 61 us (0.88)
  starting transfers between devices: 13.5 us -> 7.98 us
  waiting for transfers between devices: 11.3 us -> 8.93 us
    ppermute x3 -> x1, waiting for transfers between devices: 10.5 us -> 4.27 us  [extended(): lax.ppermute(head, axis, [((i + 1) % count, i) for i in range(ends)])]
    ppermute x3 -> x1, starting transfers between devices: 9.64 us -> 5.06 us  [extended(): lax.ppermute(tail, axis, [(i, (i + 1) % count) for i in range(ends)])]
    ppermute x0 -> x2, waiting for transfers between devices: none -> 4.18 us  [extended(): lax.ppermute(jnp.where(lower_side, tail, head), axis, [(0, 1), (1, 0)])]
    ppermute x3 -> x1, starting transfers between devices: 3.88 us -> 1.29 us  [extended(): lax.ppermute(head, axis, [((i + 1) % count, i) for i in range(ends)])]
    ppermute x0 -> x2, starting transfers between devices: none -> 1.62 us  [extended(): lax.ppermute(jnp.where(lower_side, tail, head), axis, [(0, 1), (1, 0)])]
    select_n x0 -> x3, local copies, waits for them, and re-layouts: none -> 0.89 us  [the longest x1 0.31 us: extended(): below = jnp.where(lower_side, 0.0, got)]
    slice x3 -> x0, local copies, waits for them, and re-layouts: 0.79 us -> none  [the longest x2 0.51 us: extended(): lax.slice_in_dim(cells, cells.shape[dim] - width, cells.shape[dim], axis=...]
  transfers between devices with their start and end apart: 6 -> 4, of which waited for: 5 -> 4; matrix products, arithmetic and copies ran while one was open for 1% -> 0% of each run, Pallas kernels for 0% -> 0%
where the time goes in v6:
time: 61 us; the launch traced here: 60.6 us
  blocking collectives  15.6 us (26%)
  Pallas kernels  14.9 us (24%)
  waiting for transfers between devices  8.93 us (15%)
  starting transfers between devices  7.98 us (13%)
  other arithmetic  6.99 us (11%)
  local copies, waits for them, and re-layouts  5.39 us (9%)
  between operations  0.81 us (1%)
    pallas_call x1, Pallas kernels, upscale_windows(): pl.pallas_call(kernel, grid=(packs,), in_specs=[pl.BlockSpec(memory_space...  14.9 us
    all_gather x1, blocking collectives, local(): every = lax.all_gather(every, 'gx', axis=2, tiled=True)  9.49 us
    ppermute x1, starting transfers between devices, extended(): lax.ppermute(tail, axis, [(i, (i + 1) % count) for i in range(ends)])  5.06 us
    all_gather x1, blocking collectives, local(): every = lax.all_gather(bundle, 'gy', axis=3, tiled=True)  4.33 us
    ppermute x1, waiting for transfers between devices, extended(): lax.ppermute(head, axis, [((i + 1) % count, i) for i in range(ends)])  4.27 us
    ppermute x2, waiting for transfers between devices, extended(): lax.ppermute(jnp.where(lower_side, tail, head), axis, [(0, 1), (1, 0)])  4.18 us
    pad x1, local copies, waits for them, and re-layouts, upscale_windows(): raw = jnp.pad(raw, ((0, 0),) * 3 + ((0, wide - raw.shape[3]),))  2.31 us
    concatenate x1, other arithmetic, local(): jnp.concatenate([raw, inside[None]])  2.07 us
  transfers between devices with their start and end apart: 4, of which 4 were waited for; matrix products, arithmetic and copies ran while one was open for 0% of the time, Pallas kernels for 0%

profile of v6, /device:TPU:0, one launch (start us, length us, event | category | flops | bytes accessed | tf_op | source)
XLA Modules:
  0.0 60.6 jit_solution(3758221751791710323)
XLA Ops:
  0.6 1.0 %convert_bitcast_fusion = f32[1,16,32,128]{3,2,1,0:T(8,128)S(1)} fusion(s32[16,32,128]{2,1,0:T(8,128)} %param.7), kind=kLoop, calls=%fused_computation.10 | loop fusion | flops 65536 | bytes 524288 | tf_op jit(solution)/shard_map/stack | solution.py:412
  1.6 0.9 %pad_maximum_fusion.8 = (f32[2,16,4,128]{3,2,1,0:T(4,128)S(1)}, f32[2,16,4,128]{3,2,1,0:T(4,128)S(1)}) fusion(f32[1,16,32,128]{3,2,1,0:T(8,128)S(1)} %convert_bitcast_fusion, f32[1,16,32,128]{3,2,1,0:T(8,128)} %bitcast.43), kind=kLoop, calls=%fused_computation.23 | loop fusion | flops 32768 | bytes 655360 | tf_op jit(solution)/shard_map/slice | solution.py:27
  2.5 5.1 %collective-permute-start = (f32[2,16,4,128]{3,2,1,0:T(4,128)S(1)}, f32[2,16,4,128]{3,2,1,0:T(4,128)S(1)}, u32[]{:S(2)}, u32[]{:S(2)}) collective-permute-start(f32[2,16,4,128]{3,2,1,0:T(4,128)S(1)} %get-tuple-element.16), channel_id=1, source_target_pairs={{0,4},{4,8},{8,12},{1,5},{5,9},{9,13},{2,6},{6,10},{10,14},{3,7},{... | collective-permute-start | bytes 196616 | tf_op jit(solution)/shard_map/ppermute | solution.py:34
  7.6 1.3 %collective-permute-start.1 = (f32[2,16,4,128]{3,2,1,0:T(4,128)S(1)}, f32[2,16,4,128]{3,2,1,0:T(4,128)S(1)}, u32[]{:S(2)}, u32[]{:S(2)}) collective-permute-start(f32[2,16,4,128]{3,2,1,0:T(4,128)S(1)} %get-tuple-element.17), channel_id=1, source_target_pairs={{4,0},{8,4},{12,8},{5,1},{9,5},{13,9},{6,2},{10,6},{14,10},{7,3},{... | collective-permute-start | bytes 196616 | tf_op jit(solution)/shard_map/ppermute | solution.py:35
  9.0 0.5 collective-permute-done
  9.5 4.3 %collective-permute-done.1 = f32[2,16,4,128]{3,2,1,0:T(4,128)S(1)} collective-permute-done((f32[2,16,4,128]{3,2,1,0:T(4,128)S(1)}, f32[2,16,4,128]{3,2,1,0:T(4,128)S(1)}, u32[]{:S(2)}, u32[]{:S(2)}) %collective-permute-start.1) | collective-permute-done | bytes 65568 | tf_op jit(solution)/shard_map/ppermute | solution.py:35
  13.7 1.0 %pad_maximum_fusion.1 = f32[2,16,40,128]{3,2,1,0:T(8,128)S(1)} fusion(f32[2,16,4,128]{3,2,1,0:T(4,128)S(1)} %collective-permute-done.1, f32[1,16,32,128]{3,2,1,0:T(8,128)S(1)} %convert_bitcast_fusion, f32[1,16,32,128]{3,2,1,0:T(8,128)} %bitcast.44, f32[2,16,4,128]{3,2,1,0:T(4,128)S(1)} %collective-permute-done), kind=kLoop, calls=%fused_computation.2 | loop fusion | flops 491520 | bytes 1310720 | tf_op jit(solution)/shard_map/concatenate | solution.py:36
  14.8 0.2 slice_select_fusion
  15.0 0.3 copy.30
  15.3 1.6 %collective-permute-start.2 = (f32[2,16,40,4]{2,1,3,0:T(8,128)S(1)}, f32[2,16,40,4]{2,1,3,0:T(8,128)S(1)}, u32[]{:S(2)}, u32[]{:S(2)}) collective-permute-start(f32[2,16,40,4]{2,1,3,0:T(8,128)S(1)} %copy.30), channel_id=1, source_target_pairs={{0,2},{2,0},{1,3},{3,1},{4,6},{6,4},{5,7},{7,5},{8,10},{10,8},{9,1... | collective-permute-start | bytes 61448 | tf_op jit(solution)/shard_map/ppermute | solution.py:30
  16.8 2.8 %collective-permute-done.2 = f32[2,16,40,4]{2,1,3,0:T(8,128)S(1)} collective-permute-done((f32[2,16,40,4]{2,1,3,0:T(8,128)S(1)}, f32[2,16,40,4]{2,1,3,0:T(8,128)S(1)}, u32[]{:S(2)}, u32[]{:S(2)}) %collective-permute-start.2) | collective-permute-done | bytes 20512 | tf_op jit(solution)/shard_map/ppermute | solution.py:30
  19.6 0.3 copy.33
  19.9 0.3 copy.34
  20.3 0.4 fusion
  20.7 0.2 broadcast_multiply_fusion
  20.9 1.4 %collective-permute-done.3 = f32[2,4,40,136]{3,2,1,0:T(8,128)S(1)} collective-permute-done((f32[2,4,40,136]{3,2,1,0:T(8,128)S(1)}, f32[2,4,40,136]{3,2,1,0:T(8,128)S(1)}, u32[]{:S(2)}, u32[]{:S(2)}) %collective-permute-start.3) | collective-permute-done | bytes 174112 | tf_op jit(solution)/shard_map/ppermute | solution.py:30
  22.4 2.1 %pad_maximum_fusion = f32[3,24,40,136]{3,2,1,0:T(8,128)S(1)} fusion(f32[1,24,40,136]{3,2,1,0:T(8,128)S(1)} %broadcast_multiply_fusion, f32[2,4,40,136]{3,2,1,0:T(8,128)S(1)} %get-tuple-element.19, f32[2,16,40,4]{3,2,1,0:T(8,128)S(1)} %copy.34, f32[2,16,4,128]{3,2,1,0:T(4,128)S(1)} %collective-permute-done.1, f32[1,16,32,128]{3,2,1,0:T(8,128)S(1)} %convert_bitcast_fusion, ...), kind=kLoop, calls=%fused_computation | loop fusion | flops 3133440 | bytes 3133440 | tf_op jit(solution)/shard_map/concatenate | solution.py:421
  24.5 2.3 %pad.18.raw_ref = f32[3,24,40,384]{3,2,1,0:T(8,128)} pad(f32[3,24,40,136]{3,2,1,0:T(8,128)S(1)} %pad_maximum_fusion, f32[]{:T(128)} %constant.18.clone.1), padding=0_0x0_0x0_0x0_248 | pad | bytes 5990404 | tf_op jit(solution)/shard_map/jit(_pad)/pad | solution.py:300
  26.8 14.9 %shard_map.77 = f32[3,8,128]{2,1,0:T(8,128)} custom-call(f32[3,4]{1,0:T(4,128)} %table_ref.1, f32[3,24,40,384]{3,2,1,0:T(8,128)} %pad.18.raw_ref), custom_call_target="tpu_custom_call" | custom-call | tf_op jit(solution)/shard_map/pallas_call | solution.py:305
  41.7 0.7 %slice.239 = f32[3,3,120]{2,1,0:T(4,128)S(1)} slice(f32[3,8,128]{2,1,0:T(8,128)} %shard_map.77), slice={[0:3], [0:3], [0:120]} | slice | bytes 8640 | tf_op jit(solution)/shard_map/slice | solution.py:315
  42.4 0.1 reshape.75
  42.5 0.1 reduce_sum.9
  42.7 0.1 slice.197
  43.0 0.1 copy.36
  43.1 4.3 %all_gather.9 = f32[6,2,1,8]{0,1,2,3:T(2,128)S(1)} all-gather(f32[6,2,1,4]{0,1,2,3:T(2,128)S(1)} %copy.36), channel_id=1, replica_groups=mesh['real'=2,'gx'=4,'gy'=2,'gz'=2] {'gy'}, dimensions={3}, use_global_device_ids=true | all-gather | bytes 576 | tf_op jit(solution)/shard_map/all_gather | solution.py:424
  47.4 9.5 %all_gather.10 = f32[6,2,4,8]{0,1,2,3:T(2,128)S(1)} all-gather(f32[6,2,1,8]{0,1,2,3:T(2,128)S(1)} %all_gather.9), channel_id=1, replica_groups=mesh['real'=2,'gx'=4,'gy'=2,'gz'=2] {'gx'}, dimensions={2}, use_global_device_ids=true | all-gather | bytes 1920 | tf_op jit(solution)/shard_map/all_gather | solution.py:425
  56.9 0.1 copy.37
  57.0 1.8 %all_gather.11 = f32[6,4,4,8]{3,2,0,1:T(4,128)S(1)} all-gather(f32[6,2,4,8]{3,2,0,1:T(4,128)S(1)} %copy.37), channel_id=1, replica_groups=mesh['real'=2,'gx'=4,'gy'=2,'gz'=2] {'gz'}, dimensions={1}, use_global_device_ids=true | all-gather | bytes 4608 | tf_op jit(solution)/shard_map/all_gather | solution.py:426
  59.0 0.1 fusion.11
  59.2 0.7 %reshape.77 = f32[3,2,1,4]{3,1,0,2:T(2,128)} reshape(f32[3,8]{1,0:T(4,128)S(1)} %bitcast.48) | data formatting | bytes 192 | tf_op jit(solution)/shard_map/reshape | solution.py:317
  59.8 0.1 fusion.18
  59.9 0.7 %dynamic-slice_divide_fusion = f32[2,1,4]{2,1,0:T(1,128)} fusion(f32[4,4,8]{2,1,0:T(4,128)S(1)} %get-tuple-element.21, s32[]{:T(128)S(6)} %select_n.57, s32[]{:T(128)S(6)} %select_n.58, s32[]{:T(128)S(6)} %select_n.59, f32[4,4,8]{2,1,0:T(4,128)S(1)} %get-tuple-element.31, f32[4,4,8]{2,1,0:T(4,128)S(1)} %get-tuple-element.15, ...), kind=kLoop, calls=%fused_computation.90 | loop fusion | flops 80 | bytes 396 | tf_op jit(solution)/shard_map/div | solution.py:338
  (30 shorter events, 0.7 us)
Async XLA Ops:
  2.5 17.7 %copy-start = (f32[16,32,128]{2,1,0:T(8,128)S(1)}, f32[16,32,128]{2,1,0:T(8,128)}, u32[]{:S(2)}) copy-start(f32[16,32,128]{2,1,0:T(8,128)} %param.6) | copy-start | bytes 786436
  2.5 7.0 %collective-permute-start = (f32[2,16,4,128]{3,2,1,0:T(4,128)S(1)}, f32[2,16,4,128]{3,2,1,0:T(4,128)S(1)}, u32[]{:S(2)}, u32[]{:S(2)}) collective-permute-start(f32[2,16,4,128]{3,2,1,0:T(4,128)S(1)} %get-tuple-element.16), channel_id=1, source_target_pairs={{0,4},{4,8},{8,12},{1,5},{5,9},{9,13},{2,6},{6,10},{10,14},{3,7},{... | collective-permute-start | bytes 196616 | tf_op jit(solution)/shard_map/ppermute | solution.py:34
  7.6 6.2 %collective-permute-start.1 = (f32[2,16,4,128]{3,2,1,0:T(4,128)S(1)}, f32[2,16,4,128]{3,2,1,0:T(4,128)S(1)}, u32[]{:S(2)}, u32[]{:S(2)}) collective-permute-start(f32[2,16,4,128]{3,2,1,0:T(4,128)S(1)} %get-tuple-element.17), channel_id=1, source_target_pairs={{4,0},{8,4},{12,8},{5,1},{9,5},{13,9},{6,2},{10,6},{14,10},{7,3},{... | collective-permute-start | bytes 196616 | tf_op jit(solution)/shard_map/ppermute | solution.py:35
  15.3 4.3 %collective-permute-start.2 = (f32[2,16,40,4]{2,1,3,0:T(8,128)S(1)}, f32[2,16,40,4]{2,1,3,0:T(8,128)S(1)}, u32[]{:S(2)}, u32[]{:S(2)}) collective-permute-start(f32[2,16,40,4]{2,1,3,0:T(8,128)S(1)} %copy.30), channel_id=1, source_target_pairs={{0,2},{2,0},{1,3},{3,1},{4,6},{6,4},{5,7},{7,5},{8,10},{10,8},{9,1... | collective-permute-start | bytes 61448 | tf_op jit(solution)/shard_map/ppermute | solution.py:30
  20.7 1.7 %collective-permute-start.3 = (f32[2,4,40,136]{3,2,1,0:T(8,128)S(1)}, f32[2,4,40,136]{3,2,1,0:T(8,128)S(1)}, u32[]{:S(2)}, u32[]{:S(2)}) collective-permute-start(f32[2,4,40,136]{3,2,1,0:T(8,128)S(1)} %fusion), channel_id=1, source_target_pairs={{0,1},{1,0},{2,3},{3,2},{4,5},{5,4},{6,7},{7,6},{8,9},{9,8},{10,11... | collective-permute-start | bytes 522248 | tf_op jit(solution)/shard_map/ppermute | solution.py:30
  26.8 16.1 %copy-start.1 = (f32[2,1,4]{2,1,0:T(1,128)S(1)}, f32[2,1,4]{2,1,0:T(1,128)}, u32[]{:S(2)}) copy-start(f32[2,1,4]{2,1,0:T(1,128)} %param.9) | copy-start | bytes 100
  26.8 16.1 %copy-start.2 = (f32[2,1,4]{2,1,0:T(1,128)S(1)}, f32[2,1,4]{2,1,0:T(1,128)}, u32[]{:S(2)}) copy-start(f32[2,1,4]{2,1,0:T(1,128)} %param.10) | copy-start | bytes 100
  26.8 16.2 %copy-start.3 = (f32[2,1,4]{2,1,0:T(1,128)S(1)}, f32[2,1,4]{2,1,0:T(1,128)}, u32[]{:S(2)}) copy-start(f32[2,1,4]{2,1,0:T(1,128)} %param.11) | copy-start | bytes 100

commit v7 on v6

--- a/solution.py
+++ b/solution.py
@@ -19,7 +19,7 @@
 BOUND_HALF = 0.9
 
 
-def extended(cells, sides, width):
+def extended(cells, sides, width, lanes=None):
     for axis, dim in sides:
         count = lax.axis_size(axis)
         ends = count - 1
@@ -33,7 +33,11 @@
         else:
             below = lax.ppermute(tail, axis, [(i, (i + 1) % count) for i in range(ends)])
             above = lax.ppermute(head, axis, [((i + 1) % count, i) for i in range(ends)])
-        cells = jnp.concatenate([below, cells, above], axis=dim)
+        parts = [below, cells, above]
+        if lanes is not None and dim == cells.ndim - 1:
+            extra = lanes - (cells.shape[dim] + 2 * width)
+            parts.append(jnp.zeros(cells.shape[:-1] + (extra,), cells.dtype))
+        cells = jnp.concatenate(parts, axis=dim)
     return cells
 
 
@@ -163,7 +167,7 @@
 LANES = 128
 
 
-def window_kernel(table_ref, raw_ref, o_ref, *, count_x, count_y, count):
+def window_kernel(table_ref, bounds_ref, raw_ref, o_ref, *, count_x, count_y, count):
     span_z = CCZ + 2 * RIM
     span_x = CCX + 2 * RIM
     span_y = CCY + 2 * RIM
@@ -195,9 +199,20 @@
             slab = raw_ref[field, pl.ds(block_z * CCZ, span_z), pl.ds(block_x * CCX, span_x), :]
             return pltpu.roll(slab, shift, 2)[:, :, :LANES]
 
+        depth_at = depth_pos + block_z * CCZ
+        column_at = column_pos + block_x * CCX
+        row_at = row_pos + block_y * CCY
+        held = (
+            (depth_at >= bounds_ref[0])
+            & (depth_at < bounds_ref[1])
+            & (column_at >= bounds_ref[2])
+            & (column_at < bounds_ref[3])
+            & (row_at >= bounds_ref[4])
+            & (row_at < bounds_ref[5])
+        )
         noise = jnp.where(here, cut(0), noise)
         codes = jnp.where(here, cut(1), codes)
-        inside = jnp.where(here & valid, cut(2), inside)
+        inside = jnp.where(here & valid & held, 1.0, inside)
 
     def lookup(row):
         value = jnp.zeros(shape, jnp.float32)
@@ -291,13 +306,11 @@
     o_ref[0] = jnp.concatenate(rows, axis=0)
 
 
-def upscale_windows(raw, facies_table):
+def upscale_windows(raw, facies_table, bounds, cols_len):
     span_y = CCY + 2 * RIM
     count_z = (raw.shape[1] - 2 * RIM) // CCZ
     count_x = (raw.shape[2] - 2 * RIM) // CCX
-    count_y = (raw.shape[3] - 2 * RIM) // CCY
-    wide = -(-(raw.shape[3] + LANES) // LANES) * LANES
-    raw = jnp.pad(raw, ((0, 0),) * 3 + ((0, wide - raw.shape[3]),))
+    count_y = cols_len // CCY
     count = count_z * count_x * count_y
     segments = LANES // span_y
     packs = -(-count // segments)
@@ -307,11 +320,12 @@
         grid=(packs,),
         in_specs=[
             pl.BlockSpec(memory_space=pltpu.SMEM),
+            pl.BlockSpec(memory_space=pltpu.SMEM),
             pl.BlockSpec(raw.shape, lambda p: (0, 0, 0, 0)),
         ],
         out_specs=pl.BlockSpec((1, 8, LANES), lambda p: (p, 0, 0)),
         out_shape=jax.ShapeDtypeStruct((packs, 8, LANES), jnp.float32),
-    )(facies_table, raw)
+    )(facies_table, bounds, raw)
     sums = sums[:, :3, : segments * span_y].reshape(packs, 3, segments, span_y).sum(axis=3)
     sums = sums.transpose(1, 0, 2).reshape(3, packs * segments)[:, :count]
     return sums.reshape((3, count_z, count_x, count_y))
@@ -410,15 +424,22 @@
     index_x = lax.axis_index("gx")
     index_y = lax.axis_index("gy")
     raw = jnp.stack([log_noise, facies.astype(jnp.float32)])
-    raw = extended(raw, (("gx", 2), ("gy", 3), ("gz", 1)), RIM)
+    wide = -(-(cols_len + 2 * RIM) // LANES) * LANES
+    raw = extended(raw, (("gx", 2), ("gz", 1), ("gy", 3)), RIM, wide)
     anchor_z = index_z * depth_len
     anchor_y = index_y * cols_len
     anchor_x = index_x * rows_len
-    mask_z = span_mask(anchor_z, depth_len, depth_len * size_z, RIM)
-    mask_x = span_mask(anchor_x, rows_len, rows_len * size_x, RIM)
-    mask_y = span_mask(anchor_y, cols_len, cols_len * size_y, RIM)
-    inside = mask_z[:, None, None] * mask_x[None, :, None] * mask_y[None, None, :]
-    upscaled = upscale_windows(jnp.concatenate([raw, inside[None]]), facies_table)
+    bounds = jnp.stack(
+        [
+            RIM - anchor_z,
+            depth_len * size_z + RIM - anchor_z,
+            RIM - anchor_x,
+            rows_len * size_x + RIM - anchor_x,
+            RIM - anchor_y,
+            cols_len * size_y + RIM - anchor_y,
+        ]
+    ).astype(jnp.int32)
+    upscaled = upscale_windows(raw, facies_table, bounds, cols_len)
     coarse_z, coarse_x, coarse_y = pressure_old.shape
     bundle = jnp.stack([upscaled[0], upscaled[1], upscaled[2], pressure_old, accumulation, source])
     every = lax.all_gather(bundle, "gy", axis=3, tiled=True)

time: 61 us -> 55.3 us (0.907)
  Pallas kernels: 14.9 us -> 11 us
  local copies, waits for them, and re-layouts: 5.39 us -> 4.15 us
    pallas_call x1, Pallas kernels: 14.9 us -> 11 us  [upscale_windows(): pl.pallas_call(kernel, grid=(packs,), in_specs=[pl.BlockSpec(memory_space...]
    pad x1 -> x0, local copies, waits for them, and re-layouts: 2.31 us -> none  [upscale_windows(): raw = jnp.pad(raw, ((0, 0),) * 3 + ((0, wide - raw.shape[3]),))]
    concatenate x2, other arithmetic: 3.09 us -> 2.37 us  [extended(): cells = jnp.concatenate(parts, axis=dim)]
    another operation x0 -> x1, local copies, waits for them, and re-layouts: none -> 0.68 us  [local(): jnp.stack([RIM - anchor_z, depth_len * size_z + RIM - anchor_z, RIM - anc...]
  transfers between devices with their start and end apart: 4 -> 4, of which waited for: 4 -> 4; matrix products, arithmetic and copies ran while one was open for 0% -> 1% of each run, Pallas kernels for 0% -> 0%
where the time goes in v7:
time: 55.3 us; the launch traced here: 54.9 us
  blocking collectives  15.6 us (28%)
  Pallas kernels  11 us (20%)
  waiting for transfers between devices  8.82 us (16%)
  starting transfers between devices  7.85 us (14%)
  other arithmetic  6.62 us (12%)
  local copies, waits for them, and re-layouts  4.15 us (8%)
  between operations  0.78 us (1%)
    pallas_call x1, Pallas kernels, upscale_windows(): pl.pallas_call(kernel, grid=(packs,), in_specs=[pl.BlockSpec(memory_space...  11 us
    all_gather x1, blocking collectives, local(): every = lax.all_gather(every, 'gx', axis=2, tiled=True)  9.49 us
    ppermute x1, starting transfers between devices, extended(): lax.ppermute(tail, axis, [(i, (i + 1) % count) for i in range(ends)])  4.93 us
    all_gather x1, blocking collectives, local(): every = lax.all_gather(bundle, 'gy', axis=3, tiled=True)  4.33 us
    ppermute x1, waiting for transfers between devices, extended(): lax.ppermute(head, axis, [((i + 1) % count, i) for i in range(ends)])  4.27 us
    ppermute x2, waiting for transfers between devices, extended(): lax.ppermute(jnp.where(lower_side, tail, head), axis, [(0, 1), (1, 0)])  3.97 us
    concatenate x2, other arithmetic, extended(): cells = jnp.concatenate(parts, axis=dim)  2.37 us
    all_gather x1, blocking collectives, local(): every = lax.all_gather(every, 'gz', axis=1, tiled=True)  1.83 us
  transfers between devices with their start and end apart: 4, of which 4 were waited for; matrix products, arithmetic and copies ran while one was open for 1% of the time, Pallas kernels for 0%

profile of v7, /device:TPU:0, one launch (start us, length us, event | category | flops | bytes accessed | tf_op | source)
XLA Modules:
  0.0 54.9 jit_solution(8097367574222280043)
XLA Ops:
  0.6 1.0 %convert_bitcast_fusion = f32[1,16,32,128]{3,2,1,0:T(8,128)S(1)} fusion(s32[16,32,128]{2,1,0:T(8,128)} %param.7), kind=kLoop, calls=%fused_computation.3 | loop fusion | flops 65536 | bytes 524288 | tf_op jit(solution)/shard_map/stack | solution.py:426
  1.7 0.9 %pad_maximum_fusion.5 = (f32[2,16,4,128]{3,2,1,0:T(4,128)S(1)}, f32[2,16,4,128]{3,2,1,0:T(4,128)S(1)}) fusion(f32[1,16,32,128]{3,2,1,0:T(8,128)S(1)} %convert_bitcast_fusion, f32[1,16,32,128]{3,2,1,0:T(8,128)} %bitcast.49), kind=kLoop, calls=%fused_computation.20 | loop fusion | flops 32768 | bytes 655360 | tf_op jit(solution)/shard_map/slice | solution.py:27
  2.6 4.9 %collective-permute-start = (f32[2,16,4,128]{3,2,1,0:T(4,128)S(1)}, f32[2,16,4,128]{3,2,1,0:T(4,128)S(1)}, u32[]{:S(2)}, u32[]{:S(2)}) collective-permute-start(f32[2,16,4,128]{3,2,1,0:T(4,128)S(1)} %get-tuple-element.16), channel_id=1, source_target_pairs={{0,4},{4,8},{8,12},{1,5},{5,9},{9,13},{2,6},{6,10},{10,14},{3,7},{... | collective-permute-start | bytes 196616 | tf_op jit(solution)/shard_map/ppermute | solution.py:34
  7.5 1.3 %collective-permute-start.1 = (f32[2,16,4,128]{3,2,1,0:T(4,128)S(1)}, f32[2,16,4,128]{3,2,1,0:T(4,128)S(1)}, u32[]{:S(2)}, u32[]{:S(2)}) collective-permute-start(f32[2,16,4,128]{3,2,1,0:T(4,128)S(1)} %get-tuple-element.17), channel_id=1, source_target_pairs={{4,0},{8,4},{12,8},{5,1},{9,5},{13,9},{6,2},{10,6},{14,10},{7,3},{... | collective-permute-start | bytes 196616 | tf_op jit(solution)/shard_map/ppermute | solution.py:35
  8.8 0.6 %collective-permute-done = f32[2,16,4,128]{3,2,1,0:T(4,128)S(1)} collective-permute-done((f32[2,16,4,128]{3,2,1,0:T(4,128)S(1)}, f32[2,16,4,128]{3,2,1,0:T(4,128)S(1)}, u32[]{:S(2)}, u32[]{:S(2)}) %collective-permute-start) | collective-permute-done | bytes 65568 | tf_op jit(solution)/shard_map/ppermute | solution.py:34
  9.4 4.3 %collective-permute-done.1 = f32[2,16,4,128]{3,2,1,0:T(4,128)S(1)} collective-permute-done((f32[2,16,4,128]{3,2,1,0:T(4,128)S(1)}, f32[2,16,4,128]{3,2,1,0:T(4,128)S(1)}, u32[]{:S(2)}, u32[]{:S(2)}) %collective-permute-start.1) | collective-permute-done | bytes 65568 | tf_op jit(solution)/shard_map/ppermute | solution.py:35
  13.7 0.9 %fusion = f32[2,4,40,128]{3,2,1,0:T(8,128)S(1)} fusion(f32[2,16,4,128]{3,2,1,0:T(4,128)S(1)} %collective-permute-done.1, f32[2,16,4,128]{3,2,1,0:T(4,128)S(1)} %collective-permute-done, f32[1,16,32,128]{3,2,1,0:T(8,128)S(1)} %convert_bitcast_fusion, f32[1,16,32,128]{3,2,1,0:T(8,128)} %bitcast.50, pred[]{:T(512)S(6)} %eq.7), kind=kLoop, calls=%fused_computation.5 | loop fusion | flops 286720 | bytes 819201 | tf_op jit(solution)/shard_map/jit(_where)/select_n | solution.py:30
  14.7 1.4 %collective-permute-done.2 = f32[2,4,40,128]{3,2,1,0:T(8,128)S(1)} collective-permute-done((f32[2,4,40,128]{3,2,1,0:T(8,128)S(1)}, f32[2,4,40,128]{3,2,1,0:T(8,128)S(1)}, u32[]{:S(2)}, u32[]{:S(2)}) %collective-permute-start.2) | collective-permute-done | bytes 163872 | tf_op jit(solution)/shard_map/ppermute | solution.py:30
  16.1 0.1 pad_maximum_fusion
  16.2 0.3 slice_select_fusion
  16.5 0.4 copy.30
  16.9 1.6 %collective-permute-start.3 = (f32[2,24,40,4]{2,1,3,0:T(8,128)S(1)}, f32[2,24,40,4]{2,1,3,0:T(8,128)S(1)}, u32[]{:S(2)}, u32[]{:S(2)}) collective-permute-start(f32[2,24,40,4]{2,1,3,0:T(8,128)S(1)} %copy.30), channel_id=1, source_target_pairs={{0,2},{2,0},{1,3},{3,1},{4,6},{6,4},{5,7},{7,5},{8,10},{10,8},{9,1... | collective-permute-start | bytes 92168 | tf_op jit(solution)/shard_map/ppermute | solution.py:30
  18.5 0.7 %stack.48.bounds_ref = s32[6]{0:T(128)} concatenate(s32[1]{0:T(128)} %bitcast, s32[1]{0:T(128)} %bitcast.1, s32[1]{0:T(128)} %bitcast.2, s32[1]{0:T(128)} %bitcast.3, s32[1]{0:T(128)} %bitcast.4, s32[1]{0:T(128)} %bitcast.5), dimensions={0} | concatenate | bytes 48 | tf_op jit(solution)/shard_map/stack | solution.py:432
  19.2 2.6 %collective-permute-done.3 = f32[2,24,40,4]{2,1,3,0:T(8,128)S(1)} collective-permute-done((f32[2,24,40,4]{2,1,3,0:T(8,128)S(1)}, f32[2,24,40,4]{2,1,3,0:T(8,128)S(1)}, u32[]{:S(2)}, u32[]{:S(2)}) %collective-permute-start.3) | collective-permute-done | bytes 30752 | tf_op jit(solution)/shard_map/ppermute | solution.py:30
  21.8 0.4 copy.33
  22.2 0.4 copy.34
  22.6 2.3 %maximum_maximum_fusion.raw_ref = f32[2,24,40,256]{3,2,1,0:T(8,128)} fusion(f32[2,24,40,4]{3,2,1,0:T(8,128)S(1)} %copy.34, f32[2,4,40,128]{3,2,1,0:T(8,128)S(1)} %get-tuple-element.19, f32[2,16,4,128]{3,2,1,0:T(4,128)S(1)} %collective-permute-done.1, f32[1,16,32,128]{3,2,1,0:T(8,128)S(1)} %convert_bitcast_fusion, f32[1,16,32,128]{3,2,1,0:T(8,128)S(1)} %bitcast.52, ...), kind=kLoop, calls=%fused_computation | loop fusion | flops 3932160 | bytes 3011584 | tf_op jit(solution)/shard_map/concatenate | solution.py:40
  24.9 11.0 %shard_map.77 = f32[3,8,128]{2,1,0:T(8,128)} custom-call(f32[3,4]{1,0:T(4,128)} %table_ref.1, s32[6]{0:T(128)} %stack.48.bounds_ref, f32[2,24,40,256]{3,2,1,0:T(8,128)} %maximum_maximum_fusion.raw_ref), custom_call_target="tpu_custom_call" | custom-call | tf_op jit(solution)/shard_map/pallas_call | solution.py:318
  36.0 0.7 %slice.239 = f32[3,3,120]{2,1,0:T(4,128)S(1)} slice(f32[3,8,128]{2,1,0:T(8,128)} %shard_map.77), slice={[0:3], [0:3], [0:120]} | slice | bytes 8640 | tf_op jit(solution)/shard_map/slice | solution.py:329
  36.7 0.1 reshape.16
  36.7 0.1 reduce_sum.9
  36.9 0.1 reshape.17
  37.0 0.1 slice.197
  37.3 0.1 copy.36
  37.4 4.3 %all_gather.9 = f32[6,2,1,8]{0,1,2,3:T(2,128)S(1)} all-gather(f32[6,2,1,4]{0,1,2,3:T(2,128)S(1)} %copy.36), channel_id=1, replica_groups=mesh['real'=2,'gx'=4,'gy'=2,'gz'=2] {'gy'}, dimensions={3}, use_global_device_ids=true | all-gather | bytes 576 | tf_op jit(solution)/shard_map/all_gather | solution.py:445
  41.7 9.5 %all_gather.10 = f32[6,2,4,8]{0,1,2,3:T(2,128)S(1)} all-gather(f32[6,2,1,8]{0,1,2,3:T(2,128)S(1)} %all_gather.9), channel_id=1, replica_groups=mesh['real'=2,'gx'=4,'gy'=2,'gz'=2] {'gx'}, dimensions={2}, use_global_device_ids=true | all-gather | bytes 1920 | tf_op jit(solution)/shard_map/all_gather | solution.py:446
  51.2 0.1 copy.37
  51.3 1.8 %all_gather.11 = f32[6,4,4,8]{3,2,0,1:T(4,128)S(1)} all-gather(f32[6,2,4,8]{3,2,0,1:T(4,128)S(1)} %copy.37), channel_id=1, replica_groups=mesh['real'=2,'gx'=4,'gy'=2,'gz'=2] {'gz'}, dimensions={1}, use_global_device_ids=true | all-gather | bytes 4608 | tf_op jit(solution)/shard_map/all_gather | solution.py:447
  53.3 0.1 fusion.11
  53.5 0.7 %reshape.18 = f32[3,2,1,4]{3,1,0,2:T(2,128)} reshape(f32[3,8]{1,0:T(4,128)S(1)} %bitcast.54) | data formatting | bytes 192 | tf_op jit(solution)/shard_map/reshape | solution.py:331
  54.1 0.1 fusion.18
  54.2 0.7 %dynamic-slice_divide_fusion = f32[2,1,4]{2,1,0:T(1,128)} fusion(f32[4,4,8]{2,1,0:T(4,128)S(1)} %get-tuple-element.23, s32[]{:T(128)S(6)} %select_n.57, s32[]{:T(128)S(6)} %select_n.58, s32[]{:T(128)S(6)} %select_n.59, f32[4,4,8]{2,1,0:T(4,128)S(1)} %get-tuple-element.31, f32[4,4,8]{2,1,0:T(4,128)S(1)} %get-tuple-element.15, ...), kind=kLoop, calls=%fused_computation.83 | loop fusion | flops 80 | bytes 396 | tf_op jit(solution)/shard_map/div | solution.py:352
  (27 shorter events, 0.6 us)
Async XLA Ops:
  0.6 15.4 %copy-start = (f32[16,32,128]{2,1,0:T(8,128)S(1)}, f32[16,32,128]{2,1,0:T(8,128)}, u32[]{:S(2)}) copy-start(f32[16,32,128]{2,1,0:T(8,128)} %param.6) | copy-start | bytes 786436
  2.6 6.8 %collective-permute-start = (f32[2,16,4,128]{3,2,1,0:T(4,128)S(1)}, f32[2,16,4,128]{3,2,1,0:T(4,128)S(1)}, u32[]{:S(2)}, u32[]{:S(2)}) collective-permute-start(f32[2,16,4,128]{3,2,1,0:T(4,128)S(1)} %get-tuple-element.16), channel_id=1, source_target_pairs={{0,4},{4,8},{8,12},{1,5},{5,9},{9,13},{2,6},{6,10},{10,14},{3,7},{... | collective-permute-start | bytes 196616 | tf_op jit(solution)/shard_map/ppermute | solution.py:34
  7.5 6.2 %collective-permute-start.1 = (f32[2,16,4,128]{3,2,1,0:T(4,128)S(1)}, f32[2,16,4,128]{3,2,1,0:T(4,128)S(1)}, u32[]{:S(2)}, u32[]{:S(2)}) collective-permute-start(f32[2,16,4,128]{3,2,1,0:T(4,128)S(1)} %get-tuple-element.17), channel_id=1, source_target_pairs={{4,0},{8,4},{12,8},{5,1},{9,5},{13,9},{6,2},{10,6},{14,10},{7,3},{... | collective-permute-start | bytes 196616 | tf_op jit(solution)/shard_map/ppermute | solution.py:35
  14.6 1.5 %collective-permute-start.2 = (f32[2,4,40,128]{3,2,1,0:T(8,128)S(1)}, f32[2,4,40,128]{3,2,1,0:T(8,128)S(1)}, u32[]{:S(2)}, u32[]{:S(2)}) collective-permute-start(f32[2,4,40,128]{3,2,1,0:T(8,128)S(1)} %fusion), channel_id=1, source_target_pairs={{0,1},{1,0},{2,3},{3,2},{4,5},{5,4},{6,7},{7,6},{8,9},{9,8},{10,11... | collective-permute-start | bytes 491528 | tf_op jit(solution)/shard_map/ppermute | solution.py:30
  16.9 4.9 %collective-permute-start.3 = (f32[2,24,40,4]{2,1,3,0:T(8,128)S(1)}, f32[2,24,40,4]{2,1,3,0:T(8,128)S(1)}, u32[]{:S(2)}, u32[]{:S(2)}) collective-permute-start(f32[2,24,40,4]{2,1,3,0:T(8,128)S(1)} %copy.30), channel_id=1, source_target_pairs={{0,2},{2,0},{1,3},{3,1},{4,6},{6,4},{5,7},{7,5},{8,10},{10,8},{9,1... | collective-permute-start | bytes 92168 | tf_op jit(solution)/shard_map/ppermute | solution.py:30
  24.9 12.3 %copy-start.1 = (f32[2,1,4]{2,1,0:T(1,128)S(1)}, f32[2,1,4]{2,1,0:T(1,128)}, u32[]{:S(2)}) copy-start(f32[2,1,4]{2,1,0:T(1,128)} %param.9) | copy-start | bytes 100
  24.9 12.3 %copy-start.2 = (f32[2,1,4]{2,1,0:T(1,128)S(1)}, f32[2,1,4]{2,1,0:T(1,128)}, u32[]{:S(2)}) copy-start(f32[2,1,4]{2,1,0:T(1,128)} %param.10) | copy-start | bytes 100
  24.9 12.3 %copy-start.3 = (f32[2,1,4]{2,1,0:T(1,128)S(1)}, f32[2,1,4]{2,1,0:T(1,128)}, u32[]{:S(2)}) copy-start(f32[2,1,4]{2,1,0:T(1,128)} %param.11) | copy-start | bytes 100

commit v8 on v7

--- a/solution.py
+++ b/solution.py
@@ -214,10 +214,12 @@
         codes = jnp.where(here, cut(1), codes)
         inside = jnp.where(here & valid & held, 1.0, inside)
 
+    matches = [codes == code_value for code_value in range(NFAC)]
+
     def lookup(row):
         value = jnp.zeros(shape, jnp.float32)
         for code_value in range(NFAC):
-            value = jnp.where(codes == code_value, table_ref[row, code_value], value)
+            value = jnp.where(matches[code_value], table_ref[row, code_value], value)
         return value
 
     log_x = noise + lookup(0)
@@ -442,9 +444,11 @@
     upscaled = upscale_windows(raw, facies_table, bounds, cols_len)
     coarse_z, coarse_x, coarse_y = pressure_old.shape
     bundle = jnp.stack([upscaled[0], upscaled[1], upscaled[2], pressure_old, accumulation, source])
-    every = lax.all_gather(bundle, "gy", axis=3, tiled=True)
+    fields = bundle.shape[0]
+    every = lax.all_gather(bundle, ("gy", "gz"), axis=0, tiled=False)
+    every = every.reshape((size_y, size_z) + bundle.shape).transpose(2, 1, 3, 4, 0, 5)
+    every = every.reshape((fields, size_z * coarse_z, coarse_x, size_y * coarse_y))
     every = lax.all_gather(every, "gx", axis=2, tiled=True)
-    every = lax.all_gather(every, "gz", axis=1, tiled=True)
     perm_pad = jnp.pad(every[:3], ((0, 0), (1, 1), (1, 1), (1, 1)))
     old_all = every[3]
     acc_all = every[4]

time: 55.3 us -> 58.1 us (1.051)
  blocking collectives: 15.6 us -> 18.5 us
    all_gather x1, blocking collectives: 9.49 us -> 13.3 us  [local(): every = lax.all_gather(every, 'gx', axis=2, tiled=True)]
    all_gather x2 -> x1, blocking collectives: 6.16 us -> 5.19 us  [local(): every = lax.all_gather(bundle, ('gy', 'gz'), axis=0, tiled=False)]
where the time goes in v8:
time: 58.1 us; the launch traced here: 57.8 us
  blocking collectives  18.5 us (32%)
  Pallas kernels  11 us (19%)
  waiting for transfers between devices  8.9 us (15%)
  starting transfers between devices  7.85 us (14%)
  other arithmetic  6.55 us (11%)
  local copies, waits for them, and re-layouts  4.17 us (7%)
  between operations  0.79 us (1%)
    all_gather x1, blocking collectives, local(): every = lax.all_gather(every, 'gx', axis=2, tiled=True)  13.3 us
    pallas_call x1, Pallas kernels, upscale_windows(): pl.pallas_call(kernel, grid=(packs,), in_specs=[pl.BlockSpec(memory_space...  11 us
    all_gather x1, blocking collectives, local(): every = lax.all_gather(bundle, ('gy', 'gz'), axis=0, tiled=False)  5.19 us
    ppermute x1, starting transfers between devices, extended(): lax.ppermute(tail, axis, [(i, (i + 1) % count) for i in range(ends)])  4.93 us
    ppermute x1, waiting for transfers between devices, extended(): lax.ppermute(head, axis, [((i + 1) % count, i) for i in range(ends)])  4.27 us
    ppermute x2, waiting for transfers between devices, extended(): lax.ppermute(jnp.where(lower_side, tail, head), axis, [(0, 1), (1, 0)])  4.05 us
    concatenate x2, other arithmetic, extended(): cells = jnp.concatenate(parts, axis=dim)  2.39 us
    ppermute x2, starting transfers between devices, extended(): lax.ppermute(jnp.where(lower_side, tail, head), axis, [(0, 1), (1, 0)])  1.63 us
  transfers between devices with their start and end apart: 4, of which 4 were waited for; matrix products, arithmetic and copies ran while one was open for 1% of the time, Pallas kernels for 0%

profile of v8, /device:TPU:0, one launch (start us, length us, event | category | flops | bytes accessed | tf_op | source)
XLA Modules:
  0.0 57.8 jit_solution(18202224351403735330)
XLA Ops:
  0.6 1.0 %convert_bitcast_fusion = f32[1,16,32,128]{3,2,1,0:T(8,128)S(1)} fusion(s32[16,32,128]{2,1,0:T(8,128)} %param.7), kind=kLoop, calls=%fused_computation.3 | loop fusion | flops 65536 | bytes 524288 | tf_op jit(solution)/shard_map/stack | solution.py:428
  1.7 0.9 %pad_maximum_fusion.5 = (f32[2,16,4,128]{3,2,1,0:T(4,128)S(1)}, f32[2,16,4,128]{3,2,1,0:T(4,128)S(1)}) fusion(f32[1,16,32,128]{3,2,1,0:T(8,128)S(1)} %convert_bitcast_fusion, f32[1,16,32,128]{3,2,1,0:T(8,128)} %bitcast.61), kind=kLoop, calls=%fused_computation.20 | loop fusion | flops 32768 | bytes 655360 | tf_op jit(solution)/shard_map/slice | solution.py:27
  2.6 4.9 %collective-permute-start = (f32[2,16,4,128]{3,2,1,0:T(4,128)S(1)}, f32[2,16,4,128]{3,2,1,0:T(4,128)S(1)}, u32[]{:S(2)}, u32[]{:S(2)}) collective-permute-start(f32[2,16,4,128]{3,2,1,0:T(4,128)S(1)} %get-tuple-element.24), channel_id=1, source_target_pairs={{0,4},{4,8},{8,12},{1,5},{5,9},{9,13},{2,6},{6,10},{10,14},{3,7},{... | collective-permute-start | bytes 196616 | tf_op jit(solution)/shard_map/ppermute | solution.py:34
  7.5 1.3 %collective-permute-start.1 = (f32[2,16,4,128]{3,2,1,0:T(4,128)S(1)}, f32[2,16,4,128]{3,2,1,0:T(4,128)S(1)}, u32[]{:S(2)}, u32[]{:S(2)}) collective-permute-start(f32[2,16,4,128]{3,2,1,0:T(4,128)S(1)} %get-tuple-element.25), channel_id=1, source_target_pairs={{4,0},{8,4},{12,8},{5,1},{9,5},{13,9},{6,2},{10,6},{14,10},{7,3},{... | collective-permute-start | bytes 196616 | tf_op jit(solution)/shard_map/ppermute | solution.py:35
  8.8 0.6 collective-permute-done
  9.4 4.3 %collective-permute-done.1 = f32[2,16,4,128]{3,2,1,0:T(4,128)S(1)} collective-permute-done((f32[2,16,4,128]{3,2,1,0:T(4,128)S(1)}, f32[2,16,4,128]{3,2,1,0:T(4,128)S(1)}, u32[]{:S(2)}, u32[]{:S(2)}) %collective-permute-start.1) | collective-permute-done | bytes 65568 | tf_op jit(solution)/shard_map/ppermute | solution.py:35
  13.7 0.9 %fusion = f32[2,4,40,128]{3,2,1,0:T(8,128)S(1)} fusion(f32[2,16,4,128]{3,2,1,0:T(4,128)S(1)} %collective-permute-done.1, f32[2,16,4,128]{3,2,1,0:T(4,128)S(1)} %collective-permute-done, f32[1,16,32,128]{3,2,1,0:T(8,128)S(1)} %convert_bitcast_fusion, f32[1,16,32,128]{3,2,1,0:T(8,128)} %bitcast.62, pred[]{:T(512)S(6)} %eq.7), kind=kLoop, calls=%fused_computation.5 | loop fusion | flops 286720 | bytes 819201 | tf_op jit(solution)/shard_map/jit(_where)/select_n | solution.py:30
  14.7 1.4 %collective-permute-done.2 = f32[2,4,40,128]{3,2,1,0:T(8,128)S(1)} collective-permute-done((f32[2,4,40,128]{3,2,1,0:T(8,128)S(1)}, f32[2,4,40,128]{3,2,1,0:T(8,128)S(1)}, u32[]{:S(2)}, u32[]{:S(2)}) %collective-permute-start.2) | collective-permute-done | bytes 163872 | tf_op jit(solution)/shard_map/ppermute | solution.py:30
  16.1 0.1 pad_maximum_fusion
  16.2 0.3 slice_select_fusion
  16.5 0.4 copy.81
  16.9 1.6 %collective-permute-start.3 = (f32[2,24,40,4]{2,1,3,0:T(8,128)S(1)}, f32[2,24,40,4]{2,1,3,0:T(8,128)S(1)}, u32[]{:S(2)}, u32[]{:S(2)}) collective-permute-start(f32[2,24,40,4]{2,1,3,0:T(8,128)S(1)} %copy.81), channel_id=1, source_target_pairs={{0,2},{2,0},{1,3},{3,1},{4,6},{6,4},{5,7},{7,5},{8,10},{10,8},{9,1... | collective-permute-start | bytes 92168 | tf_op jit(solution)/shard_map/ppermute | solution.py:30
  18.5 0.6 %stack.48.bounds_ref = s32[6]{0:T(128)} concatenate(s32[1]{0:T(128)} %bitcast, s32[1]{0:T(128)} %bitcast.1, s32[1]{0:T(128)} %bitcast.2, s32[1]{0:T(128)} %bitcast.3, s32[1]{0:T(128)} %bitcast.4, s32[1]{0:T(128)} %bitcast.5), dimensions={0} | concatenate | bytes 48 | tf_op jit(solution)/shard_map/stack | solution.py:434
  19.1 2.7 %collective-permute-done.3 = f32[2,24,40,4]{2,1,3,0:T(8,128)S(1)} collective-permute-done((f32[2,24,40,4]{2,1,3,0:T(8,128)S(1)}, f32[2,24,40,4]{2,1,3,0:T(8,128)S(1)}, u32[]{:S(2)}, u32[]{:S(2)}) %collective-permute-start.3) | collective-permute-done | bytes 30752 | tf_op jit(solution)/shard_map/ppermute | solution.py:30
  21.8 0.4 copy.84
  22.2 0.4 copy.85
  22.6 2.3 %maximum_maximum_fusion.raw_ref = f32[2,24,40,256]{3,2,1,0:T(8,128)} fusion(f32[2,24,40,4]{3,2,1,0:T(8,128)S(1)} %copy.85, f32[2,4,40,128]{3,2,1,0:T(8,128)S(1)} %get-tuple-element.27, f32[2,16,4,128]{3,2,1,0:T(4,128)S(1)} %collective-permute-done.1, f32[1,16,32,128]{3,2,1,0:T(8,128)S(1)} %convert_bitcast_fusion, f32[1,16,32,128]{3,2,1,0:T(8,128)S(1)} %bitcast.64, ...), kind=kLoop, calls=%fused_computation | loop fusion | flops 3932160 | bytes 3011584 | tf_op jit(solution)/shard_map/concatenate | solution.py:40
  24.9 11.0 %shard_map.77 = f32[3,8,128]{2,1,0:T(8,128)} custom-call(f32[3,4]{1,0:T(4,128)} %table_ref.1, s32[6]{0:T(128)} %stack.48.bounds_ref, f32[2,24,40,256]{3,2,1,0:T(8,128)} %maximum_maximum_fusion.raw_ref), custom_call_target="tpu_custom_call" | custom-call | tf_op jit(solution)/shard_map/pallas_call | solution.py:320
  36.0 0.7 %slice.239 = f32[3,3,120]{2,1,0:T(4,128)S(1)} slice(f32[3,8,128]{2,1,0:T(8,128)} %shard_map.77), slice={[0:3], [0:3], [0:120]} | slice | bytes 8640 | tf_op jit(solution)/shard_map/slice | solution.py:331
  36.7 0.1 reshape.22
  36.8 0.1 reduce_sum.9
  36.9 0.1 reshape.23
  37.0 0.1 slice.197
  37.3 5.2 %all-gather = f32[24,2,1,4]{3,1,2,0:T(2,128)S(1)} all-gather(f32[6,2,1,4]{3,1,2,0:T(2,128)S(1)} %constant_dynamic-update-slice_fusion), channel_id=2, replica_groups=mesh['real'=2,'gx'=4,'gy'=2,'gz'=2] {'gy','gz'}, dimensions={0}, use_global_device_ids=true | all-gather | bytes 960 | tf_op jit(solution)/shard_map/all_gather | solution.py:448
  42.5 0.1 copy.87
  42.6 0.1 copy.88
  42.7 13.3 %all_gather.11 = f32[6,4,4,8]{3,1,0,2:T(4,128)S(1)} all-gather(f32[6,4,1,8]{3,1,0,2:T(4,128)S(1)} %copy.88), channel_id=1, replica_groups=mesh['real'=2,'gx'=4,'gy'=2,'gz'=2] {'gx'}, dimensions={2}, use_global_device_ids=true | all-gather | bytes 3840 | tf_op jit(solution)/shard_map/all_gather | solution.py:451
  56.0 0.1 fusion.3
  56.1 0.1 fusion.11
  56.3 0.7 %reshape.26 = f32[3,2,1,4]{3,1,0,2:T(2,128)} reshape(f32[3,8]{1,0:T(4,128)S(1)} %bitcast.69) | data formatting | bytes 192 | tf_op jit(solution)/shard_map/reshape | solution.py:333
  57.0 0.1 fusion.18
  57.1 0.7 %dynamic-slice_divide_fusion = f32[2,1,4]{2,1,0:T(1,128)} fusion(f32[4,4,8]{2,1,0:T(4,128)S(1)} %get-tuple-element.34, s32[]{:T(128)S(6)} %select_n.57, s32[]{:T(128)S(6)} %select_n.58, s32[]{:T(128)S(6)} %select_n.59, f32[4,4,8]{2,1,0:T(4,128)S(1)} %get-tuple-element.42, f32[4,4,8]{2,1,0:T(4,128)S(1)} %get-tuple-element.23, ...), kind=kLoop, calls=%fused_computation.87 | loop fusion | flops 80 | bytes 396 | tf_op jit(solution)/shard_map/div | solution.py:354
  (29 shorter events, 0.5 us)
Async XLA Ops:
  0.6 15.4 %copy-start = (f32[16,32,128]{2,1,0:T(8,128)S(1)}, f32[16,32,128]{2,1,0:T(8,128)}, u32[]{:S(2)}) copy-start(f32[16,32,128]{2,1,0:T(8,128)} %param.6) | copy-start | bytes 786436
  2.6 6.8 %collective-permute-start = (f32[2,16,4,128]{3,2,1,0:T(4,128)S(1)}, f32[2,16,4,128]{3,2,1,0:T(4,128)S(1)}, u32[]{:S(2)}, u32[]{:S(2)}) collective-permute-start(f32[2,16,4,128]{3,2,1,0:T(4,128)S(1)} %get-tuple-element.24), channel_id=1, source_target_pairs={{0,4},{4,8},{8,12},{1,5},{5,9},{9,13},{2,6},{6,10},{10,14},{3,7},{... | collective-permute-start | bytes 196616 | tf_op jit(solution)/shard_map/ppermute | solution.py:34
  7.5 6.2 %collective-permute-start.1 = (f32[2,16,4,128]{3,2,1,0:T(4,128)S(1)}, f32[2,16,4,128]{3,2,1,0:T(4,128)S(1)}, u32[]{:S(2)}, u32[]{:S(2)}) collective-permute-start(f32[2,16,4,128]{3,2,1,0:T(4,128)S(1)} %get-tuple-element.25), channel_id=1, source_target_pairs={{4,0},{8,4},{12,8},{5,1},{9,5},{13,9},{6,2},{10,6},{14,10},{7,3},{... | collective-permute-start | bytes 196616 | tf_op jit(solution)/shard_map/ppermute | solution.py:35
  14.6 1.5 %collective-permute-start.2 = (f32[2,4,40,128]{3,2,1,0:T(8,128)S(1)}, f32[2,4,40,128]{3,2,1,0:T(8,128)S(1)}, u32[]{:S(2)}, u32[]{:S(2)}) collective-permute-start(f32[2,4,40,128]{3,2,1,0:T(8,128)S(1)} %fusion), channel_id=1, source_target_pairs={{0,1},{1,0},{2,3},{3,2},{4,5},{5,4},{6,7},{7,6},{8,9},{9,8},{10,11... | collective-permute-start | bytes 491528 | tf_op jit(solution)/shard_map/ppermute | solution.py:30
  16.9 4.9 %collective-permute-start.3 = (f32[2,24,40,4]{2,1,3,0:T(8,128)S(1)}, f32[2,24,40,4]{2,1,3,0:T(8,128)S(1)}, u32[]{:S(2)}, u32[]{:S(2)}) collective-permute-start(f32[2,24,40,4]{2,1,3,0:T(8,128)S(1)} %copy.81), channel_id=1, source_target_pairs={{0,2},{2,0},{1,3},{3,1},{4,6},{6,4},{5,7},{7,5},{8,10},{10,8},{9,1... | collective-permute-start | bytes 92168 | tf_op jit(solution)/shard_map/ppermute | solution.py:30
  24.9 12.3 %copy-start.1 = (f32[2,1,4]{2,1,0:T(1,128)S(1)}, f32[2,1,4]{2,1,0:T(1,128)}, u32[]{:S(2)}) copy-start(f32[2,1,4]{2,1,0:T(1,128)} %param.9) | copy-start | bytes 100
  24.9 12.3 %copy-start.2 = (f32[2,1,4]{2,1,0:T(1,128)S(1)}, f32[2,1,4]{2,1,0:T(1,128)}, u32[]{:S(2)}) copy-start(f32[2,1,4]{2,1,0:T(1,128)} %param.10) | copy-start | bytes 100
  24.9 12.3 %copy-start.3 = (f32[2,1,4]{2,1,0:T(1,128)S(1)}, f32[2,1,4]{2,1,0:T(1,128)}, u32[]{:S(2)}) copy-start(f32[2,1,4]{2,1,0:T(1,128)} %param.11) | copy-start | bytes 100

commit v9 on v7

--- a/solution.py
+++ b/solution.py
@@ -19,12 +19,16 @@
 BOUND_HALF = 0.9
 
 
-def extended(cells, sides, width, lanes=None):
+def extended(cells, sides, width, lanes=None, edges=None):
     for axis, dim in sides:
         count = lax.axis_size(axis)
         ends = count - 1
-        head = lax.slice_in_dim(cells, 0, width, axis=dim)
-        tail = lax.slice_in_dim(cells, cells.shape[dim] - width, cells.shape[dim], axis=dim)
+        if edges is not None:
+            head, tail = edges
+            edges = None
+        else:
+            head = lax.slice_in_dim(cells, 0, width, axis=dim)
+            tail = lax.slice_in_dim(cells, cells.shape[dim] - width, cells.shape[dim], axis=dim)
         if count == 2:
             lower_side = lax.axis_index(axis) == 0
             got = lax.ppermute(jnp.where(lower_side, tail, head), axis, [(0, 1), (1, 0)])
@@ -423,9 +427,14 @@
     index_z = lax.axis_index("gz")
     index_x = lax.axis_index("gx")
     index_y = lax.axis_index("gy")
-    raw = jnp.stack([log_noise, facies.astype(jnp.float32)])
+    sources = (log_noise, facies.astype(jnp.float32))
+    edges = (
+        jnp.stack([field[:, :RIM] for field in sources]),
+        jnp.stack([field[:, rows_len - RIM :] for field in sources]),
+    )
+    raw = jnp.stack(sources)
     wide = -(-(cols_len + 2 * RIM) // LANES) * LANES
-    raw = extended(raw, (("gx", 2), ("gz", 1), ("gy", 3)), RIM, wide)
+    raw = extended(raw, (("gx", 2), ("gz", 1), ("gy", 3)), RIM, wide, edges)
     anchor_z = index_z * depth_len
     anchor_y = index_y * cols_len
     anchor_x = index_x * rows_len

time: 55.3 us -> 55.3 us (level)
  other arithmetic: 6.62 us -> 5.78 us
  local copies, waits for them, and re-layouts: 4.15 us -> 4.97 us
    another operation x0 -> x1, local copies, waits for them, and re-layouts: none -> 0.9 us  [local(): jnp.stack([field[:, rows_len - RIM:] for field in sources])]
    slice x1 -> x0, other arithmetic: 0.9 us -> none  [extended(): lax.slice_in_dim(cells, cells.shape[dim] - width, cells.shape[dim], axis=...]
where the time goes in v9:
time: 55.3 us; the launch traced here: 55 us
  blocking collectives  15.6 us (28%)
  Pallas kernels  11 us (20%)
  waiting for transfers between devices  8.9 us (16%)
  starting transfers between devices  7.85 us (14%)
  other arithmetic  5.78 us (10%)
  local copies, waits for them, and re-layouts  4.97 us (9%)
  between operations  0.79 us (1%)
    pallas_call x1, Pallas kernels, upscale_windows(): pl.pallas_call(kernel, grid=(packs,), in_specs=[pl.BlockSpec(memory_space...  11 us
    all_gather x1, blocking collectives, local(): every = lax.all_gather(every, 'gx', axis=2, tiled=True)  9.49 us
    ppermute x1, starting transfers between devices, extended(): lax.ppermute(tail, axis, [(i, (i + 1) % count) for i in range(ends)])  4.93 us
    all_gather x1, blocking collectives, local(): every = lax.all_gather(bundle, 'gy', axis=3, tiled=True)  4.33 us
    ppermute x1, waiting for transfers between devices, extended(): lax.ppermute(head, axis, [((i + 1) % count, i) for i in range(ends)])  4.3 us
    ppermute x2, waiting for transfers between devices, extended(): lax.ppermute(jnp.where(lower_side, tail, head), axis, [(0, 1), (1, 0)])  4.05 us
    concatenate x2, other arithmetic, extended(): cells = jnp.concatenate(parts, axis=dim)  2.39 us
    all_gather x1, blocking collectives, local(): every = lax.all_gather(every, 'gz', axis=1, tiled=True)  1.83 us
  transfers between devices with their start and end apart: 4, of which 4 were waited for; matrix products, arithmetic and copies ran while one was open for 1% of the time, Pallas kernels for 0%

profile of v9, /device:TPU:0, one launch (start us, length us, event | category | flops | bytes accessed | tf_op | source)
XLA Modules:
  0.0 55.0 jit_solution(17648456128144481424)
XLA Ops:
  0.6 1.0 %convert_bitcast_fusion = (f32[1,16,32,128]{3,2,1,0:T(8,128)S(1)}, f32[16,32,128]{2,1,0:T(8,128)S(1)}) fusion(s32[16,32,128]{2,1,0:T(8,128)} %param.7), kind=kLoop, calls=%fused_computation.99 | loop fusion | flops 65536 | bytes 786432 | tf_op jit(solution)/shard_map/stack | solution.py:435
  1.7 0.9 %slice_bitcast_fusion.1 = (f32[1,16,4,128]{3,2,1,0:T(4,128)S(1)}, f32[1,16,4,128]{3,2,1,0:T(4,128)S(1)}, f32[1,16,4,128]{3,2,1,0:T(4,128)S(1)}, f32[1,16,4,128]{3,2,1,0:T(4,128)S(1)}) fusion(f32[16,32,128]{2,1,0:T(8,128)S(1)} %get-tuple-element.17, f32[16,32,128]{2,1,0:T(8,128)} %param.6), kind=kLoop, calls=%fused_computation.35 | loop fusion | bytes 262144 | tf_op jit(solution)/shard_map/stack | solution.py:433
  2.6 4.9 %collective-permute-start = (f32[2,16,4,128]{3,2,1,0:T(4,128)S(1)}, f32[2,16,4,128]{3,2,1,0:T(4,128)S(1)}, u32[]{:S(2)}, u32[]{:S(2)}) collective-permute-start(f32[2,16,4,128]{3,2,1,0:T(4,128)S(1)} %pad_maximum_fusion.4), channel_id=1, source_target_pairs={{0,4},{4,8},{8,12},{1,5},{5,9},{9,13},{2,6},{6,10},{10,14},{3,7},{... | collective-permute-start | bytes 196616 | tf_op jit(solution)/shard_map/ppermute | solution.py:38
  7.6 1.3 %collective-permute-start.1 = (f32[2,16,4,128]{3,2,1,0:T(4,128)S(1)}, f32[2,16,4,128]{3,2,1,0:T(4,128)S(1)}, u32[]{:S(2)}, u32[]{:S(2)}) collective-permute-start(f32[2,16,4,128]{3,2,1,0:T(4,128)S(1)} %pad_maximum_fusion.5), channel_id=1, source_target_pairs={{4,0},{8,4},{12,8},{5,1},{9,5},{13,9},{6,2},{10,6},{14,10},{7,3},{... | collective-permute-start | bytes 196616 | tf_op jit(solution)/shard_map/ppermute | solution.py:39
  8.9 0.6 %collective-permute-done = f32[2,16,4,128]{3,2,1,0:T(4,128)S(1)} collective-permute-done((f32[2,16,4,128]{3,2,1,0:T(4,128)S(1)}, f32[2,16,4,128]{3,2,1,0:T(4,128)S(1)}, u32[]{:S(2)}, u32[]{:S(2)}) %collective-permute-start) | collective-permute-done | bytes 65568 | tf_op jit(solution)/shard_map/ppermute | solution.py:38
  9.4 4.3 %collective-permute-done.1 = f32[2,16,4,128]{3,2,1,0:T(4,128)S(1)} collective-permute-done((f32[2,16,4,128]{3,2,1,0:T(4,128)S(1)}, f32[2,16,4,128]{3,2,1,0:T(4,128)S(1)}, u32[]{:S(2)}, u32[]{:S(2)}) %collective-permute-start.1) | collective-permute-done | bytes 65568 | tf_op jit(solution)/shard_map/ppermute | solution.py:39
  13.7 0.9 %fusion = f32[2,4,40,128]{3,2,1,0:T(8,128)S(1)} fusion(f32[2,16,4,128]{3,2,1,0:T(4,128)S(1)} %collective-permute-done.1, f32[2,16,4,128]{3,2,1,0:T(4,128)S(1)} %collective-permute-done, f32[1,16,32,128]{3,2,1,0:T(8,128)S(1)} %get-tuple-element.16, f32[1,16,32,128]{3,2,1,0:T(8,128)} %bitcast.57, pred[]{:T(512)S(6)} %eq.7), kind=kLoop, calls=%fused_computation.4 | loop fusion | flops 286720 | bytes 819201 | tf_op jit(solution)/shard_map/jit(_where)/select_n | solution.py:34
  14.7 1.4 %collective-permute-done.2 = f32[2,4,40,128]{3,2,1,0:T(8,128)S(1)} collective-permute-done((f32[2,4,40,128]{3,2,1,0:T(8,128)S(1)}, f32[2,4,40,128]{3,2,1,0:T(8,128)S(1)}, u32[]{:S(2)}, u32[]{:S(2)}) %collective-permute-start.2) | collective-permute-done | bytes 163872 | tf_op jit(solution)/shard_map/ppermute | solution.py:34
  16.1 0.1 pad_maximum_fusion
  16.3 0.3 slice_select_fusion
  16.6 0.4 copy.30
  17.0 1.6 %collective-permute-start.3 = (f32[2,24,40,4]{2,1,3,0:T(8,128)S(1)}, f32[2,24,40,4]{2,1,3,0:T(8,128)S(1)}, u32[]{:S(2)}, u32[]{:S(2)}) collective-permute-start(f32[2,24,40,4]{2,1,3,0:T(8,128)S(1)} %copy.30), channel_id=1, source_target_pairs={{0,2},{2,0},{1,3},{3,1},{4,6},{6,4},{5,7},{7,5},{8,10},{10,8},{9,1... | collective-permute-start | bytes 92168 | tf_op jit(solution)/shard_map/ppermute | solution.py:34
  18.6 0.6 %stack.66.bounds_ref = s32[6]{0:T(128)} concatenate(s32[1]{0:T(128)} %bitcast, s32[1]{0:T(128)} %bitcast.1, s32[1]{0:T(128)} %bitcast.2, s32[1]{0:T(128)} %bitcast.3, s32[1]{0:T(128)} %bitcast.4, s32[1]{0:T(128)} %bitcast.5), dimensions={0} | concatenate | bytes 48 | tf_op jit(solution)/shard_map/stack | solution.py:441
  19.2 2.7 %collective-permute-done.3 = f32[2,24,40,4]{2,1,3,0:T(8,128)S(1)} collective-permute-done((f32[2,24,40,4]{2,1,3,0:T(8,128)S(1)}, f32[2,24,40,4]{2,1,3,0:T(8,128)S(1)}, u32[]{:S(2)}, u32[]{:S(2)}) %collective-permute-start.3) | collective-permute-done | bytes 30752 | tf_op jit(solution)/shard_map/ppermute | solution.py:34
  21.9 0.4 copy.33
  22.3 0.4 copy.34
  22.7 2.3 %maximum_maximum_fusion.raw_ref = f32[2,24,40,256]{3,2,1,0:T(8,128)} fusion(f32[2,24,40,4]{3,2,1,0:T(8,128)S(1)} %copy.34, f32[2,4,40,128]{3,2,1,0:T(8,128)S(1)} %get-tuple-element.23, f32[2,16,4,128]{3,2,1,0:T(4,128)S(1)} %collective-permute-done.1, f32[1,16,32,128]{3,2,1,0:T(8,128)S(1)} %get-tuple-element.16, f32[1,16,32,128]{3,2,1,0:T(8,128)S(1)} %bitcast.59, ...), kind=kLoop, calls=%fused_computation | loop fusion | flops 3932160 | bytes 3011584 | tf_op jit(solution)/shard_map/concatenate | solution.py:44
  25.0 11.0 %shard_map.77 = f32[3,8,128]{2,1,0:T(8,128)} custom-call(f32[3,4]{1,0:T(4,128)} %table_ref.1, s32[6]{0:T(128)} %stack.66.bounds_ref, f32[2,24,40,256]{3,2,1,0:T(8,128)} %maximum_maximum_fusion.raw_ref), custom_call_target="tpu_custom_call" | custom-call | tf_op jit(solution)/shard_map/pallas_call | solution.py:322
  36.0 0.7 %slice.249 = f32[3,3,120]{2,1,0:T(4,128)S(1)} slice(f32[3,8,128]{2,1,0:T(8,128)} %shard_map.77), slice={[0:3], [0:3], [0:120]} | slice | bytes 8640 | tf_op jit(solution)/shard_map/slice | solution.py:333
  36.7 0.1 reshape.16
  36.8 0.1 reduce_sum.9
  36.9 0.1 reshape.17
  37.0 0.1 slice.205
  37.4 0.1 copy.36
  37.5 4.3 %all_gather.9 = f32[6,2,1,8]{0,1,2,3:T(2,128)S(1)} all-gather(f32[6,2,1,4]{0,1,2,3:T(2,128)S(1)} %copy.36), channel_id=1, replica_groups=mesh['real'=2,'gx'=4,'gy'=2,'gz'=2] {'gy'}, dimensions={3}, use_global_device_ids=true | all-gather | bytes 576 | tf_op jit(solution)/shard_map/all_gather | solution.py:454
  41.8 9.5 %all_gather.10 = f32[6,2,4,8]{0,1,2,3:T(2,128)S(1)} all-gather(f32[6,2,1,8]{0,1,2,3:T(2,128)S(1)} %all_gather.9), channel_id=1, replica_groups=mesh['real'=2,'gx'=4,'gy'=2,'gz'=2] {'gx'}, dimensions={2}, use_global_device_ids=true | all-gather | bytes 1920 | tf_op jit(solution)/shard_map/all_gather | solution.py:455
  51.3 0.1 copy.37
  51.4 1.8 %all_gather.11 = f32[6,4,4,8]{3,2,0,1:T(4,128)S(1)} all-gather(f32[6,2,4,8]{3,2,0,1:T(4,128)S(1)} %copy.37), channel_id=1, replica_groups=mesh['real'=2,'gx'=4,'gy'=2,'gz'=2] {'gz'}, dimensions={1}, use_global_device_ids=true | all-gather | bytes 4608 | tf_op jit(solution)/shard_map/all_gather | solution.py:456
  53.3 0.1 fusion.11
  53.5 0.7 %reshape.18 = f32[3,2,1,4]{3,1,0,2:T(2,128)} reshape(f32[3,8]{1,0:T(4,128)S(1)} %bitcast.61) | data formatting | bytes 192 | tf_op jit(solution)/shard_map/reshape | solution.py:335
  54.2 0.1 fusion.18
  54.3 0.7 %dynamic-slice_divide_fusion = f32[2,1,4]{2,1,0:T(1,128)} fusion(f32[4,4,8]{2,1,0:T(4,128)S(1)} %get-tuple-element.27, s32[]{:T(128)S(6)} %select_n.57, s32[]{:T(128)S(6)} %select_n.58, s32[]{:T(128)S(6)} %select_n.59, f32[4,4,8]{2,1,0:T(4,128)S(1)} %get-tuple-element.35, f32[4,4,8]{2,1,0:T(4,128)S(1)} %get-tuple-element.15, ...), kind=kLoop, calls=%fused_computation.86 | loop fusion | flops 80 | bytes 396 | tf_op jit(solution)/shard_map/div | solution.py:356
  (29 shorter events, 0.6 us)
Async XLA Ops:
  0.6 15.5 %copy-start = (f32[16,32,128]{2,1,0:T(8,128)S(1)}, f32[16,32,128]{2,1,0:T(8,128)}, u32[]{:S(2)}) copy-start(f32[16,32,128]{2,1,0:T(8,128)} %param.6) | copy-start | bytes 786436
  2.6 6.8 %collective-permute-start = (f32[2,16,4,128]{3,2,1,0:T(4,128)S(1)}, f32[2,16,4,128]{3,2,1,0:T(4,128)S(1)}, u32[]{:S(2)}, u32[]{:S(2)}) collective-permute-start(f32[2,16,4,128]{3,2,1,0:T(4,128)S(1)} %pad_maximum_fusion.4), channel_id=1, source_target_pairs={{0,4},{4,8},{8,12},{1,5},{5,9},{9,13},{2,6},{6,10},{10,14},{3,7},{... | collective-permute-start | bytes 196616 | tf_op jit(solution)/shard_map/ppermute | solution.py:38
  7.6 6.2 %collective-permute-start.1 = (f32[2,16,4,128]{3,2,1,0:T(4,128)S(1)}, f32[2,16,4,128]{3,2,1,0:T(4,128)S(1)}, u32[]{:S(2)}, u32[]{:S(2)}) collective-permute-start(f32[2,16,4,128]{3,2,1,0:T(4,128)S(1)} %pad_maximum_fusion.5), channel_id=1, source_target_pairs={{4,0},{8,4},{12,8},{5,1},{9,5},{13,9},{6,2},{10,6},{14,10},{7,3},{... | collective-permute-start | bytes 196616 | tf_op jit(solution)/shard_map/ppermute | solution.py:39
  14.6 1.5 %collective-permute-start.2 = (f32[2,4,40,128]{3,2,1,0:T(8,128)S(1)}, f32[2,4,40,128]{3,2,1,0:T(8,128)S(1)}, u32[]{:S(2)}, u32[]{:S(2)}) collective-permute-start(f32[2,4,40,128]{3,2,1,0:T(8,128)S(1)} %fusion), channel_id=1, source_target_pairs={{0,1},{1,0},{2,3},{3,2},{4,5},{5,4},{6,7},{7,6},{8,9},{9,8},{10,11... | collective-permute-start | bytes 491528 | tf_op jit(solution)/shard_map/ppermute | solution.py:34
  17.0 4.9 %collective-permute-start.3 = (f32[2,24,40,4]{2,1,3,0:T(8,128)S(1)}, f32[2,24,40,4]{2,1,3,0:T(8,128)S(1)}, u32[]{:S(2)}, u32[]{:S(2)}) collective-permute-start(f32[2,24,40,4]{2,1,3,0:T(8,128)S(1)} %copy.30), channel_id=1, source_target_pairs={{0,2},{2,0},{1,3},{3,1},{4,6},{6,4},{5,7},{7,5},{8,10},{10,8},{9,1... | collective-permute-start | bytes 92168 | tf_op jit(solution)/shard_map/ppermute | solution.py:34
  25.0 12.3 %copy-start.1 = (f32[2,1,4]{2,1,0:T(1,128)S(1)}, f32[2,1,4]{2,1,0:T(1,128)}, u32[]{:S(2)}) copy-start(f32[2,1,4]{2,1,0:T(1,128)} %param.9) | copy-start | bytes 100
  25.0 12.3 %copy-start.2 = (f32[2,1,4]{2,1,0:T(1,128)S(1)}, f32[2,1,4]{2,1,0:T(1,128)}, u32[]{:S(2)}) copy-start(f32[2,1,4]{2,1,0:T(1,128)} %param.10) | copy-start | bytes 100
  25.0 12.3 %copy-start.3 = (f32[2,1,4]{2,1,0:T(1,128)S(1)}, f32[2,1,4]{2,1,0:T(1,128)}, u32[]{:S(2)}) copy-start(f32[2,1,4]{2,1,0:T(1,128)} %param.11) | copy-start | bytes 100

commit v10 on v7

--- a/solution.py
+++ b/solution.py
@@ -175,13 +175,25 @@
     shape = (span_z, span_x, LANES)
     pack = pl.program_id(0)
     wide = raw_ref.shape[-1]
-    depth_pos = lax.broadcasted_iota(jnp.int32, shape, 0)
-    column_pos = lax.broadcasted_iota(jnp.int32, shape, 1)
-    lane = lax.broadcasted_iota(jnp.int32, shape, 2)
-    segment = jnp.zeros(shape, jnp.int32)
+    plane = (span_x, LANES)
+    column_pos = lax.broadcasted_iota(jnp.int32, plane, 0)
+    lane = lax.broadcasted_iota(jnp.int32, plane, 1)
+    segment = jnp.zeros(plane, jnp.int32)
     for bound in range(1, segments + 1):
         segment = segment + (lane >= bound * span_y).astype(jnp.int32)
     row_pos = lane - span_y * segment
+    zero_plane = jnp.zeros(plane, jnp.float32)
+    one_plane = jnp.ones(plane, jnp.float32)
+
+    def deep(make):
+        return jnp.stack([make(depth) for depth in range(span_z)])
+
+    def flat(values):
+        return jnp.broadcast_to(values[None], shape)
+
+    def as_float(mask):
+        return mask.astype(jnp.float32)
+
     noise = jnp.zeros(shape, jnp.float32)
     codes = jnp.zeros(shape, jnp.float32)
     inside = jnp.zeros(shape, jnp.float32)
@@ -199,20 +211,24 @@
             slab = raw_ref[field, pl.ds(block_z * CCZ, span_z), pl.ds(block_x * CCX, span_x), :]
             return pltpu.roll(slab, shift, 2)[:, :, :LANES]
 
-        depth_at = depth_pos + block_z * CCZ
         column_at = column_pos + block_x * CCX
         row_at = row_pos + block_y * CCY
-        held = (
-            (depth_at >= bounds_ref[0])
-            & (depth_at < bounds_ref[1])
+        held = as_float(
+            here
             & (column_at >= bounds_ref[2])
             & (column_at < bounds_ref[3])
             & (row_at >= bounds_ref[4])
             & (row_at < bounds_ref[5])
-        )
-        noise = jnp.where(here, cut(0), noise)
-        codes = jnp.where(here, cut(1), codes)
-        inside = jnp.where(here & valid & held, 1.0, inside)
+        ) * jnp.where(valid, 1.0, 0.0)
+
+        def layer(depth):
+            depth_at = depth + block_z * CCZ
+            keep = (depth_at >= bounds_ref[0]) & (depth_at < bounds_ref[1])
+            return held * jnp.where(keep, 1.0, 0.0)
+
+        noise = jnp.where(here[None], cut(0), noise)
+        codes = jnp.where(here[None], cut(1), codes)
+        inside = inside + deep(layer)
 
     def lookup(row):
         value = jnp.zeros(shape, jnp.float32)
@@ -246,12 +262,13 @@
         return jnp.concatenate([v[-1:], v[:-1]], axis=0)
 
     def links(perm, other_perm, other_inside, valid):
-        value = inside * other_inside * 2.0 * perm * other_perm / (perm + other_perm)
-        return jnp.where(valid, value, 0.0)
-
-    link_x = links(perm_x, up_x(perm_x), up_x(inside), column_pos < span_x - 1)
-    link_y = links(perm_y, up_y(perm_y), up_y(inside), row_pos < span_y - 1)
-    link_z = links(perm_z, up_z(perm_z), up_z(inside), depth_pos < span_z - 1)
+        return inside * other_inside * 2.0 * perm * other_perm / (perm + other_perm) * valid
+
+    link_x = links(perm_x, up_x(perm_x), up_x(inside), flat(as_float(column_pos < span_x - 1)))
+    link_y = links(perm_y, up_y(perm_y), up_y(inside), flat(as_float(row_pos < span_y - 1)))
+    link_z = links(
+        perm_z, up_z(perm_z), up_z(inside), deep(lambda depth: one_plane if depth < span_z - 1 else zero_plane)
+    )
     diagonal = link_x + down_x(link_x) + link_y + down_y(link_y) + link_z + down_z(link_z)
 
     def apply_operator(field):
@@ -260,25 +277,22 @@
         beside = beside + link_z * up_z(field) + down_z(link_z * field)
         return diagonal * field - beside
 
-    interior = (
-        (depth_pos >= 1)
-        & (depth_pos <= span_z - 2)
-        & (column_pos >= 1)
-        & (column_pos <= span_x - 2)
-        & (row_pos >= 1)
-        & (row_pos <= span_y - 2)
-    )
-    unknown = jnp.where(interior, inside, 0.0)
+    interior_plane = as_float(
+        (column_pos >= 1) & (column_pos <= span_x - 2) & (row_pos >= 1) & (row_pos <= span_y - 2)
+    )
+    unknown = inside * deep(lambda depth: interior_plane if 1 <= depth <= span_z - 2 else zero_plane)
     scaling = unknown / (diagonal + 1.0 - unknown)
-    core_z = (depth_pos >= RIM) & (depth_pos < RIM + CCZ)
     core_x = (column_pos >= RIM) & (column_pos < RIM + CCX)
     core_y = (row_pos >= RIM) & (row_pos < RIM + CCY)
-    face_x = ((column_pos == RIM - 1) | (column_pos == RIM + CCX - 1)) & core_z & core_y
-    face_y = ((row_pos == RIM - 1) | (row_pos == RIM + CCY - 1)) & core_z & core_x
-    face_z = ((depth_pos == RIM - 1) | (depth_pos == RIM + CCZ - 1)) & core_x & core_y
-    ramp_x = ((span_x - 1) / 2.0 - column_pos).astype(jnp.float32)
-    ramp_y = ((span_y - 1) / 2.0 - row_pos).astype(jnp.float32)
-    ramp_z = ((span_z - 1) / 2.0 - depth_pos).astype(jnp.float32)
+    face_x_plane = as_float(((column_pos == RIM - 1) | (column_pos == RIM + CCX - 1)) & core_y)
+    face_y_plane = as_float(((row_pos == RIM - 1) | (row_pos == RIM + CCY - 1)) & core_x)
+    face_z_plane = as_float(core_x & core_y)
+    face_x = deep(lambda depth: face_x_plane if RIM <= depth < RIM + CCZ else zero_plane)
+    face_y = deep(lambda depth: face_y_plane if RIM <= depth < RIM + CCZ else zero_plane)
+    face_z = deep(lambda depth: face_z_plane if depth in (RIM - 1, RIM + CCZ - 1) else zero_plane)
+    ramp_x = flat(((span_x - 1) / 2.0 - column_pos).astype(jnp.float32))
+    ramp_y = flat(((span_y - 1) / 2.0 - row_pos).astype(jnp.float32))
+    ramp_z = deep(lambda depth: jnp.full(plane, (span_z - 1) / 2.0 - depth, jnp.float32))
     cheb_ratio = BOUND_MID / BOUND_HALF
     cases = (
         (ramp_x, link_x, face_x, CCY * CCZ, up_x, down_x),
@@ -298,7 +312,7 @@
             solution = solution + update
             rho_old = rho_new
         pressure = ramp + solution
-        flux = jnp.where(face, link * (pressure - upper_of(pressure)), 0.0)
+        flux = link * (pressure - upper_of(pressure)) * face
         total = jnp.sum(flux, axis=0)
         total = jnp.sum(total, axis=0, keepdims=True)
         rows.append(total * (0.5 / area))

time: 55.3 us -> 58.2 us (1.052)
  Pallas kernels: 11 us -> 13.9 us
    pallas_call x1, Pallas kernels: 11 us -> 13.9 us  [upscale_windows(): pl.pallas_call(kernel, grid=(packs,), in_specs=[pl.BlockSpec(memory_space...]
where the time goes in v10:
time: 58.2 us; the launch traced here: 57.8 us
  blocking collectives  15.6 us (27%)
  Pallas kernels  13.9 us (24%)
  waiting for transfers between devices  8.82 us (15%)
  starting transfers between devices  7.85 us (13%)
  other arithmetic  6.62 us (11%)
  local copies, waits for them, and re-layouts  4.15 us (7%)
  between operations  0.78 us (1%)
    pallas_call x1, Pallas kernels, upscale_windows(): pl.pallas_call(kernel, grid=(packs,), in_specs=[pl.BlockSpec(memory_space...  13.9 us
    all_gather x1, blocking collectives, local(): every = lax.all_gather(every, 'gx', axis=2, tiled=True)  9.49 us
    ppermute x1, starting transfers between devices, extended(): lax.ppermute(tail, axis, [(i, (i + 1) % count) for i in range(ends)])  4.93 us
    all_gather x1, blocking collectives, local(): every = lax.all_gather(bundle, 'gy', axis=3, tiled=True)  4.33 us
    ppermute x1, waiting for transfers between devices, extended(): lax.ppermute(head, axis, [((i + 1) % count, i) for i in range(ends)])  4.27 us
    ppermute x2, waiting for transfers between devices, extended(): lax.ppermute(jnp.where(lower_side, tail, head), axis, [(0, 1), (1, 0)])  3.97 us
    concatenate x2, other arithmetic, extended(): cells = jnp.concatenate(parts, axis=dim)  2.37 us
    all_gather x1, blocking collectives, local(): every = lax.all_gather(every, 'gz', axis=1, tiled=True)  1.83 us
  transfers between devices with their start and end apart: 4, of which 4 were waited for; matrix products, arithmetic and copies ran while one was open for 1% of the time, Pallas kernels for 0%

profile of v10, /device:TPU:0, one launch (start us, length us, event | category | flops | bytes accessed | tf_op | source)
XLA Modules:
  0.0 57.8 jit_solution(2942513219607913756)
XLA Ops:
  0.6 1.0 %convert_bitcast_fusion = f32[1,16,32,128]{3,2,1,0:T(8,128)S(1)} fusion(s32[16,32,128]{2,1,0:T(8,128)} %param.7), kind=kLoop, calls=%fused_computation.3 | loop fusion | flops 65536 | bytes 524288 | tf_op jit(solution)/shard_map/stack | solution.py:440
  1.7 0.9 %pad_maximum_fusion.5 = (f32[2,16,4,128]{3,2,1,0:T(4,128)S(1)}, f32[2,16,4,128]{3,2,1,0:T(4,128)S(1)}) fusion(f32[1,16,32,128]{3,2,1,0:T(8,128)S(1)} %convert_bitcast_fusion, f32[1,16,32,128]{3,2,1,0:T(8,128)} %bitcast.49), kind=kLoop, calls=%fused_computation.20 | loop fusion | flops 32768 | bytes 655360 | tf_op jit(solution)/shard_map/slice | solution.py:27
  2.6 4.9 %collective-permute-start = (f32[2,16,4,128]{3,2,1,0:T(4,128)S(1)}, f32[2,16,4,128]{3,2,1,0:T(4,128)S(1)}, u32[]{:S(2)}, u32[]{:S(2)}) collective-permute-start(f32[2,16,4,128]{3,2,1,0:T(4,128)S(1)} %get-tuple-element.16), channel_id=1, source_target_pairs={{0,4},{4,8},{8,12},{1,5},{5,9},{9,13},{2,6},{6,10},{10,14},{3,7},{... | collective-permute-start | bytes 196616 | tf_op jit(solution)/shard_map/ppermute | solution.py:34
  7.5 1.3 %collective-permute-start.1 = (f32[2,16,4,128]{3,2,1,0:T(4,128)S(1)}, f32[2,16,4,128]{3,2,1,0:T(4,128)S(1)}, u32[]{:S(2)}, u32[]{:S(2)}) collective-permute-start(f32[2,16,4,128]{3,2,1,0:T(4,128)S(1)} %get-tuple-element.17), channel_id=1, source_target_pairs={{4,0},{8,4},{12,8},{5,1},{9,5},{13,9},{6,2},{10,6},{14,10},{7,3},{... | collective-permute-start | bytes 196616 | tf_op jit(solution)/shard_map/ppermute | solution.py:35
  8.8 0.6 collective-permute-done
  9.4 4.3 %collective-permute-done.1 = f32[2,16,4,128]{3,2,1,0:T(4,128)S(1)} collective-permute-done((f32[2,16,4,128]{3,2,1,0:T(4,128)S(1)}, f32[2,16,4,128]{3,2,1,0:T(4,128)S(1)}, u32[]{:S(2)}, u32[]{:S(2)}) %collective-permute-start.1) | collective-permute-done | bytes 65568 | tf_op jit(solution)/shard_map/ppermute | solution.py:35
  13.7 0.9 %fusion = f32[2,4,40,128]{3,2,1,0:T(8,128)S(1)} fusion(f32[2,16,4,128]{3,2,1,0:T(4,128)S(1)} %collective-permute-done.1, f32[2,16,4,128]{3,2,1,0:T(4,128)S(1)} %collective-permute-done, f32[1,16,32,128]{3,2,1,0:T(8,128)S(1)} %convert_bitcast_fusion, f32[1,16,32,128]{3,2,1,0:T(8,128)} %bitcast.50, pred[]{:T(512)S(6)} %eq.7), kind=kLoop, calls=%fused_computation.5 | loop fusion | flops 286720 | bytes 819201 | tf_op jit(solution)/shard_map/jit(_where)/select_n | solution.py:30
  14.7 1.4 %collective-permute-done.2 = f32[2,4,40,128]{3,2,1,0:T(8,128)S(1)} collective-permute-done((f32[2,4,40,128]{3,2,1,0:T(8,128)S(1)}, f32[2,4,40,128]{3,2,1,0:T(8,128)S(1)}, u32[]{:S(2)}, u32[]{:S(2)}) %collective-permute-start.2) | collective-permute-done | bytes 163872 | tf_op jit(solution)/shard_map/ppermute | solution.py:30
  16.1 0.1 pad_maximum_fusion
  16.2 0.3 slice_select_fusion
  16.5 0.4 copy.30
  16.9 1.6 %collective-permute-start.3 = (f32[2,24,40,4]{2,1,3,0:T(8,128)S(1)}, f32[2,24,40,4]{2,1,3,0:T(8,128)S(1)}, u32[]{:S(2)}, u32[]{:S(2)}) collective-permute-start(f32[2,24,40,4]{2,1,3,0:T(8,128)S(1)} %copy.30), channel_id=1, source_target_pairs={{0,2},{2,0},{1,3},{3,1},{4,6},{6,4},{5,7},{7,5},{8,10},{10,8},{9,1... | collective-permute-start | bytes 92168 | tf_op jit(solution)/shard_map/ppermute | solution.py:30
  18.5 0.7 %stack.48.bounds_ref = s32[6]{0:T(128)} concatenate(s32[1]{0:T(128)} %bitcast, s32[1]{0:T(128)} %bitcast.1, s32[1]{0:T(128)} %bitcast.2, s32[1]{0:T(128)} %bitcast.3, s32[1]{0:T(128)} %bitcast.4, s32[1]{0:T(128)} %bitcast.5), dimensions={0} | concatenate | bytes 48 | tf_op jit(solution)/shard_map/stack | solution.py:446
  19.2 2.6 %collective-permute-done.3 = f32[2,24,40,4]{2,1,3,0:T(8,128)S(1)} collective-permute-done((f32[2,24,40,4]{2,1,3,0:T(8,128)S(1)}, f32[2,24,40,4]{2,1,3,0:T(8,128)S(1)}, u32[]{:S(2)}, u32[]{:S(2)}) %collective-permute-start.3) | collective-permute-done | bytes 30752 | tf_op jit(solution)/shard_map/ppermute | solution.py:30
  21.8 0.4 copy.33
  22.2 0.4 copy.34
  22.6 2.3 %maximum_maximum_fusion.raw_ref = f32[2,24,40,256]{3,2,1,0:T(8,128)} fusion(f32[2,24,40,4]{3,2,1,0:T(8,128)S(1)} %copy.34, f32[2,4,40,128]{3,2,1,0:T(8,128)S(1)} %get-tuple-element.19, f32[2,16,4,128]{3,2,1,0:T(4,128)S(1)} %collective-permute-done.1, f32[1,16,32,128]{3,2,1,0:T(8,128)S(1)} %convert_bitcast_fusion, f32[1,16,32,128]{3,2,1,0:T(8,128)S(1)} %bitcast.52, ...), kind=kLoop, calls=%fused_computation | loop fusion | flops 3932160 | bytes 3011584 | tf_op jit(solution)/shard_map/concatenate | solution.py:40
  24.9 13.9 %shard_map.77 = f32[3,8,128]{2,1,0:T(8,128)} custom-call(f32[3,4]{1,0:T(4,128)} %table_ref.1, s32[6]{0:T(128)} %stack.48.bounds_ref, f32[2,24,40,256]{3,2,1,0:T(8,128)} %maximum_maximum_fusion.raw_ref), custom_call_target="tpu_custom_call" | custom-call | tf_op jit(solution)/shard_map/pallas_call | solution.py:332
  38.9 0.7 %slice.239 = f32[3,3,120]{2,1,0:T(4,128)S(1)} slice(f32[3,8,128]{2,1,0:T(8,128)} %shard_map.77), slice={[0:3], [0:3], [0:120]} | slice | bytes 8640 | tf_op jit(solution)/shard_map/slice | solution.py:343
  39.6 0.1 reshape.16
  39.7 0.1 reduce_sum.9
  39.8 0.1 reshape.17
  39.9 0.1 slice.197
  40.2 0.1 copy.36
  40.3 4.3 %all_gather.9 = f32[6,2,1,8]{0,1,2,3:T(2,128)S(1)} all-gather(f32[6,2,1,4]{0,1,2,3:T(2,128)S(1)} %copy.36), channel_id=1, replica_groups=mesh['real'=2,'gx'=4,'gy'=2,'gz'=2] {'gy'}, dimensions={3}, use_global_device_ids=true | all-gather | bytes 576 | tf_op jit(solution)/shard_map/all_gather | solution.py:459
  44.6 9.5 %all_gather.10 = f32[6,2,4,8]{0,1,2,3:T(2,128)S(1)} all-gather(f32[6,2,1,8]{0,1,2,3:T(2,128)S(1)} %all_gather.9), channel_id=1, replica_groups=mesh['real'=2,'gx'=4,'gy'=2,'gz'=2] {'gx'}, dimensions={2}, use_global_device_ids=true | all-gather | bytes 1920 | tf_op jit(solution)/shard_map/all_gather | solution.py:460
  54.1 0.1 copy.37
  54.2 1.8 %all_gather.11 = f32[6,4,4,8]{3,2,0,1:T(4,128)S(1)} all-gather(f32[6,2,4,8]{3,2,0,1:T(4,128)S(1)} %copy.37), channel_id=1, replica_groups=mesh['real'=2,'gx'=4,'gy'=2,'gz'=2] {'gz'}, dimensions={1}, use_global_device_ids=true | all-gather | bytes 4608 | tf_op jit(solution)/shard_map/all_gather | solution.py:461
  56.2 0.1 fusion.11
  56.4 0.7 %reshape.18 = f32[3,2,1,4]{3,1,0,2:T(2,128)} reshape(f32[3,8]{1,0:T(4,128)S(1)} %bitcast.54) | data formatting | bytes 192 | tf_op jit(solution)/shard_map/reshape | solution.py:345
  57.0 0.1 fusion.18
  57.1 0.7 %dynamic-slice_divide_fusion = f32[2,1,4]{2,1,0:T(1,128)} fusion(f32[4,4,8]{2,1,0:T(4,128)S(1)} %get-tuple-element.23, s32[]{:T(128)S(6)} %select_n.57, s32[]{:T(128)S(6)} %select_n.58, s32[]{:T(128)S(6)} %select_n.59, f32[4,4,8]{2,1,0:T(4,128)S(1)} %get-tuple-element.31, f32[4,4,8]{2,1,0:T(4,128)S(1)} %get-tuple-element.15, ...), kind=kLoop, calls=%fused_computation.83 | loop fusion | flops 80 | bytes 396 | tf_op jit(solution)/shard_map/div | solution.py:366
  (27 shorter events, 0.6 us)
Async XLA Ops:
  0.6 15.4 %copy-start = (f32[16,32,128]{2,1,0:T(8,128)S(1)}, f32[16,32,128]{2,1,0:T(8,128)}, u32[]{:S(2)}) copy-start(f32[16,32,128]{2,1,0:T(8,128)} %param.6) | copy-start | bytes 786436
  2.6 6.8 %collective-permute-start = (f32[2,16,4,128]{3,2,1,0:T(4,128)S(1)}, f32[2,16,4,128]{3,2,1,0:T(4,128)S(1)}, u32[]{:S(2)}, u32[]{:S(2)}) collective-permute-start(f32[2,16,4,128]{3,2,1,0:T(4,128)S(1)} %get-tuple-element.16), channel_id=1, source_target_pairs={{0,4},{4,8},{8,12},{1,5},{5,9},{9,13},{2,6},{6,10},{10,14},{3,7},{... | collective-permute-start | bytes 196616 | tf_op jit(solution)/shard_map/ppermute | solution.py:34
  7.5 6.2 %collective-permute-start.1 = (f32[2,16,4,128]{3,2,1,0:T(4,128)S(1)}, f32[2,16,4,128]{3,2,1,0:T(4,128)S(1)}, u32[]{:S(2)}, u32[]{:S(2)}) collective-permute-start(f32[2,16,4,128]{3,2,1,0:T(4,128)S(1)} %get-tuple-element.17), channel_id=1, source_target_pairs={{4,0},{8,4},{12,8},{5,1},{9,5},{13,9},{6,2},{10,6},{14,10},{7,3},{... | collective-permute-start | bytes 196616 | tf_op jit(solution)/shard_map/ppermute | solution.py:35
  14.6 1.5 %collective-permute-start.2 = (f32[2,4,40,128]{3,2,1,0:T(8,128)S(1)}, f32[2,4,40,128]{3,2,1,0:T(8,128)S(1)}, u32[]{:S(2)}, u32[]{:S(2)}) collective-permute-start(f32[2,4,40,128]{3,2,1,0:T(8,128)S(1)} %fusion), channel_id=1, source_target_pairs={{0,1},{1,0},{2,3},{3,2},{4,5},{5,4},{6,7},{7,6},{8,9},{9,8},{10,11... | collective-permute-start | bytes 491528 | tf_op jit(solution)/shard_map/ppermute | solution.py:30
  16.9 4.9 %collective-permute-start.3 = (f32[2,24,40,4]{2,1,3,0:T(8,128)S(1)}, f32[2,24,40,4]{2,1,3,0:T(8,128)S(1)}, u32[]{:S(2)}, u32[]{:S(2)}) collective-permute-start(f32[2,24,40,4]{2,1,3,0:T(8,128)S(1)} %copy.30), channel_id=1, source_target_pairs={{0,2},{2,0},{1,3},{3,1},{4,6},{6,4},{5,7},{7,5},{8,10},{10,8},{9,1... | collective-permute-start | bytes 92168 | tf_op jit(solution)/shard_map/ppermute | solution.py:30
  24.9 15.2 %copy-start.1 = (f32[2,1,4]{2,1,0:T(1,128)S(1)}, f32[2,1,4]{2,1,0:T(1,128)}, u32[]{:S(2)}) copy-start(f32[2,1,4]{2,1,0:T(1,128)} %param.9) | copy-start | bytes 100
  24.9 15.2 %copy-start.2 = (f32[2,1,4]{2,1,0:T(1,128)S(1)}, f32[2,1,4]{2,1,0:T(1,128)}, u32[]{:S(2)}) copy-start(f32[2,1,4]{2,1,0:T(1,128)} %param.10) | copy-start | bytes 100
  24.9 15.3 %copy-start.3 = (f32[2,1,4]{2,1,0:T(1,128)S(1)}, f32[2,1,4]{2,1,0:T(1,128)}, u32[]{:S(2)}) copy-start(f32[2,1,4]{2,1,0:T(1,128)} %param.11) | copy-start | bytes 100

commit v11 on v7

--- a/solution.py
+++ b/solution.py
@@ -33,10 +33,11 @@
         else:
             below = lax.ppermute(tail, axis, [(i, (i + 1) % count) for i in range(ends)])
             above = lax.ppermute(head, axis, [((i + 1) % count, i) for i in range(ends)])
-        parts = [below, cells, above]
         if lanes is not None and dim == cells.ndim - 1:
             extra = lanes - (cells.shape[dim] + 2 * width)
-            parts.append(jnp.zeros(cells.shape[:-1] + (extra,), cells.dtype))
+            parts = [cells, above, jnp.zeros(cells.shape[:-1] + (extra,), cells.dtype), below]
+        else:
+            parts = [below, cells, above]
         cells = jnp.concatenate(parts, axis=dim)
     return cells
 
@@ -192,7 +193,7 @@
         block_z = window // (count_x * count_y)
         block_x = (window // count_y) % count_x
         block_y = window % count_y
-        shift = (slot * span_y - block_y * CCY + wide) % wide
+        shift = (slot * span_y - block_y * CCY + RIM + wide) % wide
         here = segment == slot
 
         def cut(field):

time: 55.3 us -> 54.7 us (0.989)
  other arithmetic: 6.62 us -> 6.02 us
    concatenate x2, other arithmetic: 2.37 us -> 1.77 us  [extended(): cells = jnp.concatenate(parts, axis=dim)]
where the time goes in v11:
time: 54.7 us; the launch traced here: 54.3 us
  blocking collectives  15.6 us (29%)
  Pallas kernels  11 us (20%)
  waiting for transfers between devices  8.82 us (16%)
  starting transfers between devices  7.85 us (14%)
  other arithmetic  6.02 us (11%)
  local copies, waits for them, and re-layouts  4.15 us (8%)
  between operations  0.78 us (1%)
    pallas_call x1, Pallas kernels, upscale_windows(): pl.pallas_call(kernel, grid=(packs,), in_specs=[pl.BlockSpec(memory_space...  11 us
    all_gather x1, blocking collectives, local(): every = lax.all_gather(every, 'gx', axis=2, tiled=True)  9.49 us
    ppermute x1, starting transfers between devices, extended(): lax.ppermute(tail, axis, [(i, (i + 1) % count) for i in range(ends)])  4.93 us
    all_gather x1, blocking collectives, local(): every = lax.all_gather(bundle, 'gy', axis=3, tiled=True)  4.33 us
    ppermute x1, waiting for transfers between devices, extended(): lax.ppermute(head, axis, [((i + 1) % count, i) for i in range(ends)])  4.27 us
    ppermute x2, waiting for transfers between devices, extended(): lax.ppermute(jnp.where(lower_side, tail, head), axis, [(0, 1), (1, 0)])  3.97 us
    all_gather x1, blocking collectives, local(): every = lax.all_gather(every, 'gz', axis=1, tiled=True)  1.83 us
    concatenate x2, other arithmetic, extended(): cells = jnp.concatenate(parts, axis=dim)  1.77 us
  transfers between devices with their start and end apart: 4, of which 4 were waited for; matrix products, arithmetic and copies ran while one was open for 1% of the time, Pallas kernels for 0%

profile of v11, /device:TPU:0, one launch (start us, length us, event | category | flops | bytes accessed | tf_op | source)
XLA Modules:
  0.0 54.3 jit_solution(359479818657465233)
XLA Ops:
  0.6 1.0 %convert_bitcast_fusion = f32[1,16,32,128]{3,2,1,0:T(8,128)S(1)} fusion(s32[16,32,128]{2,1,0:T(8,128)} %param.7), kind=kLoop, calls=%fused_computation.3 | loop fusion | flops 65536 | bytes 524288 | tf_op jit(solution)/shard_map/stack | solution.py:427
  1.7 0.9 %pad_maximum_fusion.6 = (f32[2,16,4,128]{3,2,1,0:T(4,128)S(1)}, f32[2,16,4,128]{3,2,1,0:T(4,128)S(1)}) fusion(f32[1,16,32,128]{3,2,1,0:T(8,128)S(1)} %convert_bitcast_fusion, f32[1,16,32,128]{3,2,1,0:T(8,128)} %bitcast.49), kind=kLoop, calls=%fused_computation.20 | loop fusion | flops 32768 | bytes 655360 | tf_op jit(solution)/shard_map/slice | solution.py:27
  2.6 4.9 %collective-permute-start = (f32[2,16,4,128]{3,2,1,0:T(4,128)S(1)}, f32[2,16,4,128]{3,2,1,0:T(4,128)S(1)}, u32[]{:S(2)}, u32[]{:S(2)}) collective-permute-start(f32[2,16,4,128]{3,2,1,0:T(4,128)S(1)} %get-tuple-element.16), channel_id=1, source_target_pairs={{0,4},{4,8},{8,12},{1,5},{5,9},{9,13},{2,6},{6,10},{10,14},{3,7},{... | collective-permute-start | bytes 196616 | tf_op jit(solution)/shard_map/ppermute | solution.py:34
  7.5 1.3 %collective-permute-start.1 = (f32[2,16,4,128]{3,2,1,0:T(4,128)S(1)}, f32[2,16,4,128]{3,2,1,0:T(4,128)S(1)}, u32[]{:S(2)}, u32[]{:S(2)}) collective-permute-start(f32[2,16,4,128]{3,2,1,0:T(4,128)S(1)} %get-tuple-element.17), channel_id=1, source_target_pairs={{4,0},{8,4},{12,8},{5,1},{9,5},{13,9},{6,2},{10,6},{14,10},{7,3},{... | collective-permute-start | bytes 196616 | tf_op jit(solution)/shard_map/ppermute | solution.py:35
  8.8 0.6 %collective-permute-done = f32[2,16,4,128]{3,2,1,0:T(4,128)S(1)} collective-permute-done((f32[2,16,4,128]{3,2,1,0:T(4,128)S(1)}, f32[2,16,4,128]{3,2,1,0:T(4,128)S(1)}, u32[]{:S(2)}, u32[]{:S(2)}) %collective-permute-start) | collective-permute-done | bytes 65568 | tf_op jit(solution)/shard_map/ppermute | solution.py:34
  9.4 4.3 %collective-permute-done.1 = f32[2,16,4,128]{3,2,1,0:T(4,128)S(1)} collective-permute-done((f32[2,16,4,128]{3,2,1,0:T(4,128)S(1)}, f32[2,16,4,128]{3,2,1,0:T(4,128)S(1)}, u32[]{:S(2)}, u32[]{:S(2)}) %collective-permute-start.1) | collective-permute-done | bytes 65568 | tf_op jit(solution)/shard_map/ppermute | solution.py:35
  13.7 0.9 %fusion = f32[2,4,40,128]{3,2,1,0:T(8,128)S(1)} fusion(f32[2,16,4,128]{3,2,1,0:T(4,128)S(1)} %collective-permute-done.1, f32[2,16,4,128]{3,2,1,0:T(4,128)S(1)} %collective-permute-done, f32[1,16,32,128]{3,2,1,0:T(8,128)S(1)} %convert_bitcast_fusion, f32[1,16,32,128]{3,2,1,0:T(8,128)} %bitcast.50, pred[]{:T(512)S(6)} %eq.6), kind=kLoop, calls=%fused_computation.5 | loop fusion | flops 286720 | bytes 819201 | tf_op jit(solution)/shard_map/jit(_where)/select_n | solution.py:30
  14.7 1.4 %collective-permute-done.2 = f32[2,4,40,128]{3,2,1,0:T(8,128)S(1)} collective-permute-done((f32[2,4,40,128]{3,2,1,0:T(8,128)S(1)}, f32[2,4,40,128]{3,2,1,0:T(8,128)S(1)}, u32[]{:S(2)}, u32[]{:S(2)}) %collective-permute-start.2) | collective-permute-done | bytes 163872 | tf_op jit(solution)/shard_map/ppermute | solution.py:30
  16.1 0.1 pad_maximum_fusion.1
  16.2 0.3 slice_select_fusion
  16.5 0.4 copy.30
  16.9 1.6 %collective-permute-start.3 = (f32[2,24,40,4]{2,1,3,0:T(8,128)S(1)}, f32[2,24,40,4]{2,1,3,0:T(8,128)S(1)}, u32[]{:S(2)}, u32[]{:S(2)}) collective-permute-start(f32[2,24,40,4]{2,1,3,0:T(8,128)S(1)} %copy.30), channel_id=1, source_target_pairs={{0,2},{2,0},{1,3},{3,1},{4,6},{6,4},{5,7},{7,5},{8,10},{10,8},{9,1... | collective-permute-start | bytes 92168 | tf_op jit(solution)/shard_map/ppermute | solution.py:30
  18.5 0.7 %stack.48.bounds_ref = s32[6]{0:T(128)} concatenate(s32[1]{0:T(128)} %bitcast, s32[1]{0:T(128)} %bitcast.1, s32[1]{0:T(128)} %bitcast.2, s32[1]{0:T(128)} %bitcast.3, s32[1]{0:T(128)} %bitcast.4, s32[1]{0:T(128)} %bitcast.5), dimensions={0} | concatenate | bytes 48 | tf_op jit(solution)/shard_map/stack | solution.py:433
  19.2 2.6 %collective-permute-done.3 = f32[2,24,40,4]{2,1,3,0:T(8,128)S(1)} collective-permute-done((f32[2,24,40,4]{2,1,3,0:T(8,128)S(1)}, f32[2,24,40,4]{2,1,3,0:T(8,128)S(1)}, u32[]{:S(2)}, u32[]{:S(2)}) %collective-permute-start.3) | collective-permute-done | bytes 30752 | tf_op jit(solution)/shard_map/ppermute | solution.py:30
  21.8 0.4 copy.33
  22.2 0.4 copy.34
  22.6 1.7 %pad_maximum_fusion.raw_ref = f32[2,24,40,256]{3,2,1,0:T(8,128)} fusion(f32[2,24,40,4]{3,2,1,0:T(8,128)S(1)} %copy.34, f32[2,24,40,4]{3,2,1,0:T(8,128)S(1)} %copy.33, f32[2,4,40,128]{3,2,1,0:T(8,128)S(1)} %get-tuple-element.19, f32[2,16,4,128]{3,2,1,0:T(4,128)S(1)} %collective-permute-done.1, f32[1,16,32,128]{3,2,1,0:T(8,128)S(1)} %convert_bitcast_fusion, ...), kind=kLoop, calls=%fused_computation | loop fusion | flops 3932160 | bytes 3011584 | tf_op jit(solution)/shard_map/concatenate | solution.py:41
  24.3 11.0 %shard_map.77 = f32[3,8,128]{2,1,0:T(8,128)} custom-call(f32[3,4]{1,0:T(4,128)} %table_ref.1, s32[6]{0:T(128)} %stack.48.bounds_ref, f32[2,24,40,256]{3,2,1,0:T(8,128)} %pad_maximum_fusion.raw_ref), custom_call_target="tpu_custom_call" | custom-call | tf_op jit(solution)/shard_map/pallas_call | solution.py:319
  35.4 0.7 %slice.239 = f32[3,3,120]{2,1,0:T(4,128)S(1)} slice(f32[3,8,128]{2,1,0:T(8,128)} %shard_map.77), slice={[0:3], [0:3], [0:120]} | slice | bytes 8640 | tf_op jit(solution)/shard_map/slice | solution.py:330
  36.1 0.1 reshape.16
  36.1 0.1 reduce_sum.9
  36.3 0.1 reshape.17
  36.4 0.1 slice.197
  36.7 0.1 copy.36
  36.8 4.3 %all_gather.9 = f32[6,2,1,8]{0,1,2,3:T(2,128)S(1)} all-gather(f32[6,2,1,4]{0,1,2,3:T(2,128)S(1)} %copy.36), channel_id=1, replica_groups=mesh['real'=2,'gx'=4,'gy'=2,'gz'=2] {'gy'}, dimensions={3}, use_global_device_ids=true | all-gather | bytes 576 | tf_op jit(solution)/shard_map/all_gather | solution.py:446
  41.1 9.5 %all_gather.10 = f32[6,2,4,8]{0,1,2,3:T(2,128)S(1)} all-gather(f32[6,2,1,8]{0,1,2,3:T(2,128)S(1)} %all_gather.9), channel_id=1, replica_groups=mesh['real'=2,'gx'=4,'gy'=2,'gz'=2] {'gx'}, dimensions={2}, use_global_device_ids=true | all-gather | bytes 1920 | tf_op jit(solution)/shard_map/all_gather | solution.py:447
  50.6 0.1 copy.37
  50.7 1.8 %all_gather.11 = f32[6,4,4,8]{3,2,0,1:T(4,128)S(1)} all-gather(f32[6,2,4,8]{3,2,0,1:T(4,128)S(1)} %copy.37), channel_id=1, replica_groups=mesh['real'=2,'gx'=4,'gy'=2,'gz'=2] {'gz'}, dimensions={1}, use_global_device_ids=true | all-gather | bytes 4608 | tf_op jit(solution)/shard_map/all_gather | solution.py:448
  52.7 0.1 fusion.11
  52.9 0.7 %reshape.18 = f32[3,2,1,4]{3,1,0,2:T(2,128)} reshape(f32[3,8]{1,0:T(4,128)S(1)} %bitcast.54) | data formatting | bytes 192 | tf_op jit(solution)/shard_map/reshape | solution.py:332
  53.5 0.1 fusion.18
  53.6 0.7 %dynamic-slice_divide_fusion = f32[2,1,4]{2,1,0:T(1,128)} fusion(f32[4,4,8]{2,1,0:T(4,128)S(1)} %get-tuple-element.23, s32[]{:T(128)S(6)} %select_n.57, s32[]{:T(128)S(6)} %select_n.58, s32[]{:T(128)S(6)} %select_n.59, f32[4,4,8]{2,1,0:T(4,128)S(1)} %get-tuple-element.31, f32[4,4,8]{2,1,0:T(4,128)S(1)} %get-tuple-element.15, ...), kind=kLoop, calls=%fused_computation.83 | loop fusion | flops 80 | bytes 396 | tf_op jit(solution)/shard_map/div | solution.py:353
  (27 shorter events, 0.6 us)
Async XLA Ops:
  0.6 15.4 %copy-start = (f32[16,32,128]{2,1,0:T(8,128)S(1)}, f32[16,32,128]{2,1,0:T(8,128)}, u32[]{:S(2)}) copy-start(f32[16,32,128]{2,1,0:T(8,128)} %param.6) | copy-start | bytes 786436
  2.6 6.8 %collective-permute-start = (f32[2,16,4,128]{3,2,1,0:T(4,128)S(1)}, f32[2,16,4,128]{3,2,1,0:T(4,128)S(1)}, u32[]{:S(2)}, u32[]{:S(2)}) collective-permute-start(f32[2,16,4,128]{3,2,1,0:T(4,128)S(1)} %get-tuple-element.16), channel_id=1, source_target_pairs={{0,4},{4,8},{8,12},{1,5},{5,9},{9,13},{2,6},{6,10},{10,14},{3,7},{... | collective-permute-start | bytes 196616 | tf_op jit(solution)/shard_map/ppermute | solution.py:34
  7.5 6.2 %collective-permute-start.1 = (f32[2,16,4,128]{3,2,1,0:T(4,128)S(1)}, f32[2,16,4,128]{3,2,1,0:T(4,128)S(1)}, u32[]{:S(2)}, u32[]{:S(2)}) collective-permute-start(f32[2,16,4,128]{3,2,1,0:T(4,128)S(1)} %get-tuple-element.17), channel_id=1, source_target_pairs={{4,0},{8,4},{12,8},{5,1},{9,5},{13,9},{6,2},{10,6},{14,10},{7,3},{... | collective-permute-start | bytes 196616 | tf_op jit(solution)/shard_map/ppermute | solution.py:35
  14.6 1.5 %collective-permute-start.2 = (f32[2,4,40,128]{3,2,1,0:T(8,128)S(1)}, f32[2,4,40,128]{3,2,1,0:T(8,128)S(1)}, u32[]{:S(2)}, u32[]{:S(2)}) collective-permute-start(f32[2,4,40,128]{3,2,1,0:T(8,128)S(1)} %fusion), channel_id=1, source_target_pairs={{0,1},{1,0},{2,3},{3,2},{4,5},{5,4},{6,7},{7,6},{8,9},{9,8},{10,11... | collective-permute-start | bytes 491528 | tf_op jit(solution)/shard_map/ppermute | solution.py:30
  16.9 4.9 %collective-permute-start.3 = (f32[2,24,40,4]{2,1,3,0:T(8,128)S(1)}, f32[2,24,40,4]{2,1,3,0:T(8,128)S(1)}, u32[]{:S(2)}, u32[]{:S(2)}) collective-permute-start(f32[2,24,40,4]{2,1,3,0:T(8,128)S(1)} %copy.30), channel_id=1, source_target_pairs={{0,2},{2,0},{1,3},{3,1},{4,6},{6,4},{5,7},{7,5},{8,10},{10,8},{9,1... | collective-permute-start | bytes 92168 | tf_op jit(solution)/shard_map/ppermute | solution.py:30
  24.3 12.3 %copy-start.1 = (f32[2,1,4]{2,1,0:T(1,128)S(1)}, f32[2,1,4]{2,1,0:T(1,128)}, u32[]{:S(2)}) copy-start(f32[2,1,4]{2,1,0:T(1,128)} %param.9) | copy-start | bytes 100
  24.3 12.3 %copy-start.2 = (f32[2,1,4]{2,1,0:T(1,128)S(1)}, f32[2,1,4]{2,1,0:T(1,128)}, u32[]{:S(2)}) copy-start(f32[2,1,4]{2,1,0:T(1,128)} %param.10) | copy-start | bytes 100
  24.3 12.3 %copy-start.3 = (f32[2,1,4]{2,1,0:T(1,128)S(1)}, f32[2,1,4]{2,1,0:T(1,128)}, u32[]{:S(2)}) copy-start(f32[2,1,4]{2,1,0:T(1,128)} %param.11) | copy-start | bytes 100

commit v12 on v11

--- a/solution.py
+++ b/solution.py
@@ -301,10 +301,22 @@
         pressure = ramp + solution
         flux = jnp.where(face, link * (pressure - upper_of(pressure)), 0.0)
         total = jnp.sum(flux, axis=0)
-        total = jnp.sum(total, axis=0, keepdims=True)
-        rows.append(total * (0.5 / area))
-    rows.append(jnp.zeros((8 - len(rows), LANES), jnp.float32))
-    o_ref[0] = jnp.concatenate(rows, axis=0)
+        rows.append(jnp.sum(total, axis=0, keepdims=True) * (0.5 / area))
+    out_row = lax.broadcasted_iota(jnp.int32, (8, LANES), 0)
+    out_lane = lax.broadcasted_iota(jnp.int32, (8, LANES), 1)
+    first_segment = segment[0, 0:1, :]
+    gathered = jnp.zeros((8, LANES), jnp.float32)
+    for direction in range(3):
+        for slot in range(segments):
+            value = jnp.sum(jnp.where(first_segment == slot, rows[direction], 0.0))
+            spot = (out_row == direction) & (out_lane == pack * segments + slot)
+            gathered = jnp.where(spot, value, gathered)
+
+    @pl.when(pack == 0)
+    def _():
+        o_ref[...] = jnp.zeros((8, LANES), jnp.float32)
+
+    o_ref[...] = o_ref[...] + gathered
 
 
 def upscale_windows(raw, facies_table, bounds, cols_len):
@@ -324,12 +336,10 @@
             pl.BlockSpec(memory_space=pltpu.SMEM),
             pl.BlockSpec(raw.shape, lambda p: (0, 0, 0, 0)),
         ],
-        out_specs=pl.BlockSpec((1, 8, LANES), lambda p: (p, 0, 0)),
-        out_shape=jax.ShapeDtypeStruct((packs, 8, LANES), jnp.float32),
+        out_specs=pl.BlockSpec((8, LANES), lambda p: (0, 0)),
+        out_shape=jax.ShapeDtypeStruct((8, LANES), jnp.float32),
     )(facies_table, bounds, raw)
-    sums = sums[:, :3, : segments * span_y].reshape(packs, 3, segments, span_y).sum(axis=3)
-    sums = sums.transpose(1, 0, 2).reshape(3, packs * segments)[:, :count]
-    return sums.reshape((3, count_z, count_x, count_y))
+    return sums[:3, :count].reshape((3, count_z, count_x, count_y))
 
 
 def coarse_sweep(perm_pad, press_pad, inside_pad, accumulation, fixed):

time: 54.7 us -> 55.5 us (1.015)
    slice x2, local copies, waits for them, and re-layouts: 0.1 us -> 0.9 us  [local(): upscaled[2]]
where the time goes in v12:
time: 55.5 us; the launch traced here: 55.1 us
  blocking collectives  15.6 us (28%)
  Pallas kernels  11.4 us (21%)
  waiting for transfers between devices  8.87 us (16%)
  starting transfers between devices  7.85 us (14%)
  other arithmetic  5.94 us (11%)
  local copies, waits for them, and re-layouts  4.7 us (8%)
  between operations  0.76 us (1%)
    pallas_call x1, Pallas kernels, upscale_windows(): pl.pallas_call(kernel, grid=(packs,), in_specs=[pl.BlockSpec(memory_space...  11.4 us
    all_gather x1, blocking collectives, local(): every = lax.all_gather(every, 'gx', axis=2, tiled=True)  9.49 us
    ppermute x1, starting transfers between devices, extended(): lax.ppermute(tail, axis, [(i, (i + 1) % count) for i in range(ends)])  4.93 us
    all_gather x1, blocking collectives, local(): every = lax.all_gather(bundle, 'gy', axis=3, tiled=True)  4.33 us
    ppermute x1, waiting for transfers between devices, extended(): lax.ppermute(head, axis, [((i + 1) % count, i) for i in range(ends)])  4.27 us
    ppermute x2, waiting for transfers between devices, extended(): lax.ppermute(jnp.where(lower_side, tail, head), axis, [(0, 1), (1, 0)])  4.02 us
    all_gather x1, blocking collectives, local(): every = lax.all_gather(every, 'gz', axis=1, tiled=True)  1.83 us
    concatenate x2, other arithmetic, extended(): cells = jnp.concatenate(parts, axis=dim)  1.79 us
  transfers between devices with their start and end apart: 4, of which 4 were waited for; matrix products, arithmetic and copies ran while one was open for 1% of the time, Pallas kernels for 0%

profile of v12, /device:TPU:0, one launch (start us, length us, event | category | flops | bytes accessed | tf_op | source)
XLA Modules:
  0.0 55.1 jit_solution(3942060554094976623)
XLA Ops:
  0.6 1.0 %convert_bitcast_fusion = f32[1,16,32,128]{3,2,1,0:T(8,128)S(1)} fusion(s32[16,32,128]{2,1,0:T(8,128)} %param.7), kind=kLoop, calls=%fused_computation.3 | loop fusion | flops 65536 | bytes 524288 | tf_op jit(solution)/shard_map/stack | solution.py:437
  1.7 0.9 %pad_maximum_fusion.6 = (f32[2,16,4,128]{3,2,1,0:T(4,128)S(1)}, f32[2,16,4,128]{3,2,1,0:T(4,128)S(1)}) fusion(f32[1,16,32,128]{3,2,1,0:T(8,128)S(1)} %convert_bitcast_fusion, f32[1,16,32,128]{3,2,1,0:T(8,128)} %bitcast.47), kind=kLoop, calls=%fused_computation.20 | loop fusion | flops 32768 | bytes 655360 | tf_op jit(solution)/shard_map/slice | solution.py:27
  2.6 4.9 %collective-permute-start = (f32[2,16,4,128]{3,2,1,0:T(4,128)S(1)}, f32[2,16,4,128]{3,2,1,0:T(4,128)S(1)}, u32[]{:S(2)}, u32[]{:S(2)}) collective-permute-start(f32[2,16,4,128]{3,2,1,0:T(4,128)S(1)} %get-tuple-element.16), channel_id=1, source_target_pairs={{0,4},{4,8},{8,12},{1,5},{5,9},{9,13},{2,6},{6,10},{10,14},{3,7},{... | collective-permute-start | bytes 196616 | tf_op jit(solution)/shard_map/ppermute | solution.py:34
  7.5 1.3 %collective-permute-start.1 = (f32[2,16,4,128]{3,2,1,0:T(4,128)S(1)}, f32[2,16,4,128]{3,2,1,0:T(4,128)S(1)}, u32[]{:S(2)}, u32[]{:S(2)}) collective-permute-start(f32[2,16,4,128]{3,2,1,0:T(4,128)S(1)} %get-tuple-element.17), channel_id=1, source_target_pairs={{4,0},{8,4},{12,8},{5,1},{9,5},{13,9},{6,2},{10,6},{14,10},{7,3},{... | collective-permute-start | bytes 196616 | tf_op jit(solution)/shard_map/ppermute | solution.py:35
  8.8 0.6 %collective-permute-done = f32[2,16,4,128]{3,2,1,0:T(4,128)S(1)} collective-permute-done((f32[2,16,4,128]{3,2,1,0:T(4,128)S(1)}, f32[2,16,4,128]{3,2,1,0:T(4,128)S(1)}, u32[]{:S(2)}, u32[]{:S(2)}) %collective-permute-start) | collective-permute-done | bytes 65568 | tf_op jit(solution)/shard_map/ppermute | solution.py:34
  9.4 4.3 %collective-permute-done.1 = f32[2,16,4,128]{3,2,1,0:T(4,128)S(1)} collective-permute-done((f32[2,16,4,128]{3,2,1,0:T(4,128)S(1)}, f32[2,16,4,128]{3,2,1,0:T(4,128)S(1)}, u32[]{:S(2)}, u32[]{:S(2)}) %collective-permute-start.1) | collective-permute-done | bytes 65568 | tf_op jit(solution)/shard_map/ppermute | solution.py:35
  13.7 0.9 %fusion = f32[2,4,40,128]{3,2,1,0:T(8,128)S(1)} fusion(f32[2,16,4,128]{3,2,1,0:T(4,128)S(1)} %collective-permute-done.1, f32[2,16,4,128]{3,2,1,0:T(4,128)S(1)} %collective-permute-done, f32[1,16,32,128]{3,2,1,0:T(8,128)S(1)} %convert_bitcast_fusion, f32[1,16,32,128]{3,2,1,0:T(8,128)} %bitcast.48, pred[]{:T(512)S(6)} %eq.6), kind=kLoop, calls=%fused_computation.5 | loop fusion | flops 286720 | bytes 819201 | tf_op jit(solution)/shard_map/jit(_where)/select_n | solution.py:30
  14.7 1.4 %collective-permute-done.2 = f32[2,4,40,128]{3,2,1,0:T(8,128)S(1)} collective-permute-done((f32[2,4,40,128]{3,2,1,0:T(8,128)S(1)}, f32[2,4,40,128]{3,2,1,0:T(8,128)S(1)}, u32[]{:S(2)}, u32[]{:S(2)}) %collective-permute-start.2) | collective-permute-done | bytes 163872 | tf_op jit(solution)/shard_map/ppermute | solution.py:30
  16.1 0.1 pad_maximum_fusion.1
  16.2 0.3 slice_select_fusion
  16.5 0.4 copy.29
  16.9 1.6 %collective-permute-start.3 = (f32[2,24,40,4]{2,1,3,0:T(8,128)S(1)}, f32[2,24,40,4]{2,1,3,0:T(8,128)S(1)}, u32[]{:S(2)}, u32[]{:S(2)}) collective-permute-start(f32[2,24,40,4]{2,1,3,0:T(8,128)S(1)} %copy.29), channel_id=1, source_target_pairs={{0,2},{2,0},{1,3},{3,1},{4,6},{6,4},{5,7},{7,5},{8,10},{10,8},{9,1... | collective-permute-start | bytes 92168 | tf_op jit(solution)/shard_map/ppermute | solution.py:30
  18.5 0.6 %stack.48.bounds_ref = s32[6]{0:T(128)} concatenate(s32[1]{0:T(128)} %bitcast, s32[1]{0:T(128)} %bitcast.1, s32[1]{0:T(128)} %bitcast.2, s32[1]{0:T(128)} %bitcast.3, s32[1]{0:T(128)} %bitcast.4, s32[1]{0:T(128)} %bitcast.5), dimensions={0} | concatenate | bytes 48 | tf_op jit(solution)/shard_map/stack | solution.py:443
  19.2 2.6 %collective-permute-done.3 = f32[2,24,40,4]{2,1,3,0:T(8,128)S(1)} collective-permute-done((f32[2,24,40,4]{2,1,3,0:T(8,128)S(1)}, f32[2,24,40,4]{2,1,3,0:T(8,128)S(1)}, u32[]{:S(2)}, u32[]{:S(2)}) %collective-permute-start.3) | collective-permute-done | bytes 30752 | tf_op jit(solution)/shard_map/ppermute | solution.py:30
  21.8 0.4 copy.32
  22.2 0.4 copy.33
  22.6 1.7 %pad_maximum_fusion.raw_ref = f32[2,24,40,256]{3,2,1,0:T(8,128)} fusion(f32[2,24,40,4]{3,2,1,0:T(8,128)S(1)} %copy.33, f32[2,24,40,4]{3,2,1,0:T(8,128)S(1)} %copy.32, f32[2,4,40,128]{3,2,1,0:T(8,128)S(1)} %get-tuple-element.19, f32[2,16,4,128]{3,2,1,0:T(4,128)S(1)} %collective-permute-done.1, f32[1,16,32,128]{3,2,1,0:T(8,128)S(1)} %convert_bitcast_fusion, ...), kind=kLoop, calls=%fused_computation | loop fusion | flops 3932160 | bytes 3011584 | tf_op jit(solution)/shard_map/concatenate | solution.py:41
  24.3 11.4 %shard_map.77 = f32[8,128]{1,0:T(8,128)} custom-call(f32[3,4]{1,0:T(4,128)} %table_ref.1, s32[6]{0:T(128)} %stack.48.bounds_ref, f32[2,24,40,256]{3,2,1,0:T(8,128)} %pad_maximum_fusion.raw_ref), custom_call_target="tpu_custom_call" | custom-call | tf_op jit(solution)/shard_map/pallas_call | solution.py:331
  35.7 0.8 %slice_reduce_fusion = (f32[8]{0:T(128)S(1)}, f32[8]{0:T(128)S(1)}, f32[8]{0:T(128)S(1)}) fusion(f32[8,128]{1,0:T(8,128)} %shard_map.77), kind=kLoop, calls=%fused_computation.93 | loop fusion | bytes 192 | tf_op jit(solution)/shard_map/slice | solution.py:455
  36.5 0.1 slice.193
  36.8 0.1 copy.34
  36.9 4.3 %all_gather.9 = f32[6,2,1,8]{0,1,2,3:T(2,128)S(1)} all-gather(f32[6,2,1,4]{0,1,2,3:T(2,128)S(1)} %copy.34), channel_id=1, replica_groups=mesh['real'=2,'gx'=4,'gy'=2,'gz'=2] {'gy'}, dimensions={3}, use_global_device_ids=true | all-gather | bytes 576 | tf_op jit(solution)/shard_map/all_gather | solution.py:456
  41.3 9.5 %all_gather.10 = f32[6,2,4,8]{0,1,2,3:T(2,128)S(1)} all-gather(f32[6,2,1,8]{0,1,2,3:T(2,128)S(1)} %all_gather.9), channel_id=1, replica_groups=mesh['real'=2,'gx'=4,'gy'=2,'gz'=2] {'gx'}, dimensions={2}, use_global_device_ids=true | all-gather | bytes 1920 | tf_op jit(solution)/shard_map/all_gather | solution.py:457
  50.8 0.1 copy.35
  50.9 1.8 %all_gather.11 = f32[6,4,4,8]{3,2,0,1:T(4,128)S(1)} all-gather(f32[6,2,4,8]{3,2,0,1:T(4,128)S(1)} %copy.35), channel_id=1, replica_groups=mesh['real'=2,'gx'=4,'gy'=2,'gz'=2] {'gz'}, dimensions={1}, use_global_device_ids=true | all-gather | bytes 4608 | tf_op jit(solution)/shard_map/all_gather | solution.py:458
  52.7 0.1 fusion.3
  52.8 0.7 %slice.232 = f32[3,8]{1,0:T(4,128)S(1)} slice(f32[8,128]{1,0:T(8,128)} %shard_map.77), slice={[0:3], [0:8]} | slice | bytes 192 | tf_op jit(solution)/shard_map/slice | solution.py:342
  53.5 0.1 fusion.11
  53.6 0.1 fusion.19
  53.7 0.7 %reshape.10 = f32[3,2,1,4]{3,1,0,2:T(2,128)} reshape(f32[3,8]{1,0:T(4,128)S(1)} %slice.232) | data formatting | bytes 192 | tf_op jit(solution)/shard_map/reshape | solution.py:342
  54.4 0.1 fusion.18
  54.5 0.7 %dynamic-slice_divide_fusion = f32[2,1,4]{2,1,0:T(1,128)} fusion(f32[4,4,8]{2,1,0:T(4,128)S(1)} %get-tuple-element.23, s32[]{:T(128)S(6)} %select_n.57, s32[]{:T(128)S(6)} %select_n.58, s32[]{:T(128)S(6)} %select_n.59, f32[4,4,8]{2,1,0:T(4,128)S(1)} %get-tuple-element.31, f32[4,4,8]{2,1,0:T(4,128)S(1)} %get-tuple-element.15, ...), kind=kLoop, calls=%fused_computation.83 | loop fusion | flops 80 | bytes 396 | tf_op jit(solution)/shard_map/div | solution.py:363
  (23 shorter events, 0.4 us)
Async XLA Ops:
  0.6 15.4 %copy-start = (f32[16,32,128]{2,1,0:T(8,128)S(1)}, f32[16,32,128]{2,1,0:T(8,128)}, u32[]{:S(2)}) copy-start(f32[16,32,128]{2,1,0:T(8,128)} %param.6) | copy-start | bytes 786436
  2.6 6.8 %collective-permute-start = (f32[2,16,4,128]{3,2,1,0:T(4,128)S(1)}, f32[2,16,4,128]{3,2,1,0:T(4,128)S(1)}, u32[]{:S(2)}, u32[]{:S(2)}) collective-permute-start(f32[2,16,4,128]{3,2,1,0:T(4,128)S(1)} %get-tuple-element.16), channel_id=1, source_target_pairs={{0,4},{4,8},{8,12},{1,5},{5,9},{9,13},{2,6},{6,10},{10,14},{3,7},{... | collective-permute-start | bytes 196616 | tf_op jit(solution)/shard_map/ppermute | solution.py:34
  7.5 6.2 %collective-permute-start.1 = (f32[2,16,4,128]{3,2,1,0:T(4,128)S(1)}, f32[2,16,4,128]{3,2,1,0:T(4,128)S(1)}, u32[]{:S(2)}, u32[]{:S(2)}) collective-permute-start(f32[2,16,4,128]{3,2,1,0:T(4,128)S(1)} %get-tuple-element.17), channel_id=1, source_target_pairs={{4,0},{8,4},{12,8},{5,1},{9,5},{13,9},{6,2},{10,6},{14,10},{7,3},{... | collective-permute-start | bytes 196616 | tf_op jit(solution)/shard_map/ppermute | solution.py:35
  14.6 1.5 %collective-permute-start.2 = (f32[2,4,40,128]{3,2,1,0:T(8,128)S(1)}, f32[2,4,40,128]{3,2,1,0:T(8,128)S(1)}, u32[]{:S(2)}, u32[]{:S(2)}) collective-permute-start(f32[2,4,40,128]{3,2,1,0:T(8,128)S(1)} %fusion), channel_id=1, source_target_pairs={{0,1},{1,0},{2,3},{3,2},{4,5},{5,4},{6,7},{7,6},{8,9},{9,8},{10,11... | collective-permute-start | bytes 491528 | tf_op jit(solution)/shard_map/ppermute | solution.py:30
  16.9 4.9 %collective-permute-start.3 = (f32[2,24,40,4]{2,1,3,0:T(8,128)S(1)}, f32[2,24,40,4]{2,1,3,0:T(8,128)S(1)}, u32[]{:S(2)}, u32[]{:S(2)}) collective-permute-start(f32[2,24,40,4]{2,1,3,0:T(8,128)S(1)} %copy.29), channel_id=1, source_target_pairs={{0,2},{2,0},{1,3},{3,1},{4,6},{6,4},{5,7},{7,5},{8,10},{10,8},{9,1... | collective-permute-start | bytes 92168 | tf_op jit(solution)/shard_map/ppermute | solution.py:30
  24.3 12.5 %copy-start.1 = (f32[2,1,4]{2,1,0:T(1,128)S(1)}, f32[2,1,4]{2,1,0:T(1,128)}, u32[]{:S(2)}) copy-start(f32[2,1,4]{2,1,0:T(1,128)} %param.9) | copy-start | bytes 100
  24.3 12.5 %copy-start.2 = (f32[2,1,4]{2,1,0:T(1,128)S(1)}, f32[2,1,4]{2,1,0:T(1,128)}, u32[]{:S(2)}) copy-start(f32[2,1,4]{2,1,0:T(1,128)} %param.10) | copy-start | bytes 100
  24.3 12.5 %copy-start.3 = (f32[2,1,4]{2,1,0:T(1,128)S(1)}, f32[2,1,4]{2,1,0:T(1,128)}, u32[]{:S(2)}) copy-start(f32[2,1,4]{2,1,0:T(1,128)} %param.11) | copy-start | bytes 100

commit v13 on v11

--- a/solution.py
+++ b/solution.py
@@ -40,6 +40,22 @@
             parts = [below, cells, above]
         cells = jnp.concatenate(parts, axis=dim)
     return cells
+
+
+def doubling_gather(values, axis, dim):
+    count = lax.axis_size(axis)
+    if count & (count - 1):
+        return lax.all_gather(values, axis, axis=dim, tiled=True)
+    index = lax.axis_index(axis)
+    step = 1
+    while step < count:
+        got = lax.ppermute(values, axis, [(i, i ^ step) for i in range(count)])
+        lower = (index // step) % 2 == 0
+        values = jnp.where(
+            lower, jnp.concatenate([values, got], axis=dim), jnp.concatenate([got, values], axis=dim)
+        )
+        step *= 2
+    return values
 
 
 def raise_flat(values, offset):
@@ -444,7 +460,7 @@
     coarse_z, coarse_x, coarse_y = pressure_old.shape
     bundle = jnp.stack([upscaled[0], upscaled[1], upscaled[2], pressure_old, accumulation, source])
     every = lax.all_gather(bundle, "gy", axis=3, tiled=True)
-    every = lax.all_gather(every, "gx", axis=2, tiled=True)
+    every = doubling_gather(every, "gx", 2)
     every = lax.all_gather(every, "gz", axis=1, tiled=True)
     perm_pad = jnp.pad(every[:3], ((0, 0), (1, 1), (1, 1), (1, 1)))
     old_all = every[3]

time: 54.7 us -> 52.9 us (0.967)
  blocking collectives: 15.6 us -> 6.16 us
  starting transfers between devices: 7.85 us -> 12.1 us
  waiting for transfers between devices: 8.82 us -> 12.4 us
    all_gather x1 -> x0, blocking collectives: 9.49 us -> none  [local(): every = lax.all_gather(every, 'gx', axis=2, tiled=True)]
    ppermute x0 -> x2, starting transfers between devices: none -> 4.23 us  [doubling_gather(): got = lax.ppermute(values, axis, [(i, i ^ step) for i in range(count)])]
    ppermute x0 -> x2, waiting for transfers between devices: none -> 3.46 us  [doubling_gather(): got = lax.ppermute(values, axis, [(i, i ^ step) for i in range(count)])]
  transfers between devices with their start and end apart: 4 -> 6, of which waited for: 4 -> 6; matrix products, arithmetic and copies ran while one was open for 1% -> 3% of each run, Pallas kernels for 0% -> 0%
where the time goes in v13:
time: 52.9 us; the launch traced here: 52.6 us
  waiting for transfers between devices  12.4 us (23%)
  starting transfers between devices  12.1 us (23%)
  Pallas kernels  11 us (21%)
  blocking collectives  6.16 us (12%)
  other arithmetic  6.08 us (11%)
  local copies, waits for them, and re-layouts  4.08 us (8%)
  between operations  0.79 us (1%)
    pallas_call x1, Pallas kernels, upscale_windows(): pl.pallas_call(kernel, grid=(packs,), in_specs=[pl.BlockSpec(memory_space...  11 us
    ppermute x1, starting transfers between devices, extended(): lax.ppermute(tail, axis, [(i, (i + 1) % count) for i in range(ends)])  4.93 us
    all_gather x1, blocking collectives, local(): every = lax.all_gather(bundle, 'gy', axis=3, tiled=True)  4.33 us
    ppermute x1, waiting for transfers between devices, extended(): lax.ppermute(head, axis, [((i + 1) % count, i) for i in range(ends)])  4.27 us
    ppermute x2, starting transfers between devices, doubling_gather(): got = lax.ppermute(values, axis, [(i, i ^ step) for i in range(count)])  4.23 us
    ppermute x2, waiting for transfers between devices, extended(): lax.ppermute(jnp.where(lower_side, tail, head), axis, [(0, 1), (1, 0)])  4.04 us
    ppermute x2, waiting for transfers between devices, doubling_gather(): got = lax.ppermute(values, axis, [(i, i ^ step) for i in range(count)])  3.46 us
    all_gather x1, blocking collectives, local(): every = lax.all_gather(every, 'gz', axis=1, tiled=True)  1.83 us
  transfers between devices with their start and end apart: 6, of which 6 were waited for; matrix products, arithmetic and copies ran while one was open for 3% of the time, Pallas kernels for 0%

profile of v13, /device:TPU:0, one launch (start us, length us, event | category | flops | bytes accessed | tf_op | source)
XLA Modules:
  0.0 52.6 jit_solution(12716737470036493235)
XLA Ops:
  0.6 1.0 %convert_bitcast_fusion = f32[1,16,32,128]{3,2,1,0:T(8,128)S(1)} fusion(s32[16,32,128]{2,1,0:T(8,128)} %param.7), kind=kLoop, calls=%fused_computation.3 | loop fusion | flops 65536 | bytes 524288 | tf_op jit(solution)/shard_map/stack | solution.py:443
  1.7 0.9 %pad_maximum_fusion.6 = (f32[2,16,4,128]{3,2,1,0:T(4,128)S(1)}, f32[2,16,4,128]{3,2,1,0:T(4,128)S(1)}) fusion(f32[1,16,32,128]{3,2,1,0:T(8,128)S(1)} %convert_bitcast_fusion, f32[1,16,32,128]{3,2,1,0:T(8,128)} %bitcast.49), kind=kLoop, calls=%fused_computation.20 | loop fusion | flops 32768 | bytes 655360 | tf_op jit(solution)/shard_map/slice | solution.py:27
  2.6 4.9 %collective-permute-start = (f32[2,16,4,128]{3,2,1,0:T(4,128)S(1)}, f32[2,16,4,128]{3,2,1,0:T(4,128)S(1)}, u32[]{:S(2)}, u32[]{:S(2)}) collective-permute-start(f32[2,16,4,128]{3,2,1,0:T(4,128)S(1)} %get-tuple-element.16), channel_id=1, source_target_pairs={{0,4},{4,8},{8,12},{1,5},{5,9},{9,13},{2,6},{6,10},{10,14},{3,7},{... | collective-permute-start | bytes 196616 | tf_op jit(solution)/shard_map/ppermute | solution.py:34
  7.5 1.3 %collective-permute-start.1 = (f32[2,16,4,128]{3,2,1,0:T(4,128)S(1)}, f32[2,16,4,128]{3,2,1,0:T(4,128)S(1)}, u32[]{:S(2)}, u32[]{:S(2)}) collective-permute-start(f32[2,16,4,128]{3,2,1,0:T(4,128)S(1)} %get-tuple-element.17), channel_id=1, source_target_pairs={{4,0},{8,4},{12,8},{5,1},{9,5},{13,9},{6,2},{10,6},{14,10},{7,3},{... | collective-permute-start | bytes 196616 | tf_op jit(solution)/shard_map/ppermute | solution.py:35
  8.8 0.6 %collective-permute-done = f32[2,16,4,128]{3,2,1,0:T(4,128)S(1)} collective-permute-done((f32[2,16,4,128]{3,2,1,0:T(4,128)S(1)}, f32[2,16,4,128]{3,2,1,0:T(4,128)S(1)}, u32[]{:S(2)}, u32[]{:S(2)}) %collective-permute-start) | collective-permute-done | bytes 65568 | tf_op jit(solution)/shard_map/ppermute | solution.py:34
  9.4 4.3 %collective-permute-done.1 = f32[2,16,4,128]{3,2,1,0:T(4,128)S(1)} collective-permute-done((f32[2,16,4,128]{3,2,1,0:T(4,128)S(1)}, f32[2,16,4,128]{3,2,1,0:T(4,128)S(1)}, u32[]{:S(2)}, u32[]{:S(2)}) %collective-permute-start.1) | collective-permute-done | bytes 65568 | tf_op jit(solution)/shard_map/ppermute | solution.py:35
  13.7 0.9 %fusion = f32[2,4,40,128]{3,2,1,0:T(8,128)S(1)} fusion(f32[2,16,4,128]{3,2,1,0:T(4,128)S(1)} %collective-permute-done.1, f32[2,16,4,128]{3,2,1,0:T(4,128)S(1)} %collective-permute-done, f32[1,16,32,128]{3,2,1,0:T(8,128)S(1)} %convert_bitcast_fusion, f32[1,16,32,128]{3,2,1,0:T(8,128)} %bitcast.50, pred[]{:T(512)S(6)} %eq.17), kind=kLoop, calls=%fused_computation.5 | loop fusion | flops 286720 | bytes 819201 | tf_op jit(solution)/shard_map/jit(_where)/select_n | solution.py:30
  14.7 1.4 %collective-permute-done.2 = f32[2,4,40,128]{3,2,1,0:T(8,128)S(1)} collective-permute-done((f32[2,4,40,128]{3,2,1,0:T(8,128)S(1)}, f32[2,4,40,128]{3,2,1,0:T(8,128)S(1)}, u32[]{:S(2)}, u32[]{:S(2)}) %collective-permute-start.2) | collective-permute-done | bytes 163872 | tf_op jit(solution)/shard_map/ppermute | solution.py:30
  16.1 0.1 pad_maximum_fusion.1
  16.2 0.3 slice_select_fusion
  16.5 0.4 copy.30
  16.9 1.6 %collective-permute-start.3 = (f32[2,24,40,4]{2,1,3,0:T(8,128)S(1)}, f32[2,24,40,4]{2,1,3,0:T(8,128)S(1)}, u32[]{:S(2)}, u32[]{:S(2)}) collective-permute-start(f32[2,24,40,4]{2,1,3,0:T(8,128)S(1)} %copy.30), channel_id=1, source_target_pairs={{0,2},{2,0},{1,3},{3,1},{4,6},{6,4},{5,7},{7,5},{8,10},{10,8},{9,1... | collective-permute-start | bytes 92168 | tf_op jit(solution)/shard_map/ppermute | solution.py:30
  18.5 0.6 %stack.48.bounds_ref = s32[6]{0:T(128)} concatenate(s32[1]{0:T(128)} %bitcast, s32[1]{0:T(128)} %bitcast.1, s32[1]{0:T(128)} %bitcast.2, s32[1]{0:T(128)} %bitcast.3, s32[1]{0:T(128)} %bitcast.4, s32[1]{0:T(128)} %bitcast.5), dimensions={0} | concatenate | bytes 48 | tf_op jit(solution)/shard_map/stack | solution.py:449
  19.1 2.7 %collective-permute-done.3 = f32[2,24,40,4]{2,1,3,0:T(8,128)S(1)} collective-permute-done((f32[2,24,40,4]{2,1,3,0:T(8,128)S(1)}, f32[2,24,40,4]{2,1,3,0:T(8,128)S(1)}, u32[]{:S(2)}, u32[]{:S(2)}) %collective-permute-start.3) | collective-permute-done | bytes 30752 | tf_op jit(solution)/shard_map/ppermute | solution.py:30
  21.8 0.4 copy.33
  22.2 0.4 copy.34
  22.6 1.7 %pad_maximum_fusion.raw_ref = f32[2,24,40,256]{3,2,1,0:T(8,128)} fusion(f32[2,24,40,4]{3,2,1,0:T(8,128)S(1)} %copy.34, f32[2,24,40,4]{3,2,1,0:T(8,128)S(1)} %copy.33, f32[2,4,40,128]{3,2,1,0:T(8,128)S(1)} %get-tuple-element.19, f32[2,16,4,128]{3,2,1,0:T(4,128)S(1)} %collective-permute-done.1, f32[1,16,32,128]{3,2,1,0:T(8,128)S(1)} %convert_bitcast_fusion, ...), kind=kLoop, calls=%fused_computation | loop fusion | flops 3932160 | bytes 3011584 | tf_op jit(solution)/shard_map/concatenate | solution.py:41
  24.3 11.0 %shard_map.77 = f32[3,8,128]{2,1,0:T(8,128)} custom-call(f32[3,4]{1,0:T(4,128)} %table_ref.1, s32[6]{0:T(128)} %stack.48.bounds_ref, f32[2,24,40,256]{3,2,1,0:T(8,128)} %pad_maximum_fusion.raw_ref), custom_call_target="tpu_custom_call" | custom-call | tf_op jit(solution)/shard_map/pallas_call | solution.py:335
  35.4 0.7 %slice.239 = f32[3,3,120]{2,1,0:T(4,128)S(1)} slice(f32[3,8,128]{2,1,0:T(8,128)} %shard_map.77), slice={[0:3], [0:3], [0:120]} | slice | bytes 8640 | tf_op jit(solution)/shard_map/slice | solution.py:346
  36.2 0.1 reduce_sum.9
  36.7 0.1 copy.36
  36.8 4.3 %all_gather.6 = f32[6,2,1,8]{0,1,2,3:T(2,128)S(1)} all-gather(f32[6,2,1,4]{0,1,2,3:T(2,128)S(1)} %copy.36), channel_id=1, replica_groups=mesh['real'=2,'gx'=4,'gy'=2,'gz'=2] {'gy'}, dimensions={3}, use_global_device_ids=true | all-gather | bytes 576 | tf_op jit(solution)/shard_map/all_gather | solution.py:462
  41.1 1.6 %collective-permute-start.4 = (f32[6,2,1,8]{0,1,2,3:T(2,128)S(1)}, f32[6,2,1,8]{0,1,2,3:T(2,128)S(1)}, u32[]{:S(2)}, u32[]{:S(2)}) collective-permute-start(f32[6,2,1,8]{0,1,2,3:T(2,128)S(1)} %all_gather.6), channel_id=1, source_target_pairs={{0,4},{4,0},{8,12},{12,8},{1,5},{5,1},{9,13},{13,9},{2,6},{6,2},{1... | collective-permute-start | bytes 1160 | tf_op jit(solution)/shard_map/ppermute | solution.py:52
  42.7 2.1 %collective-permute-done.4 = f32[6,2,1,8]{0,1,2,3:T(2,128)S(1)} collective-permute-done((f32[6,2,1,8]{0,1,2,3:T(2,128)S(1)}, f32[6,2,1,8]{0,1,2,3:T(2,128)S(1)}, u32[]{:S(2)}, u32[]{:S(2)}) %collective-permute-start.4) | collective-permute-done | bytes 416 | tf_op jit(solution)/shard_map/ppermute | solution.py:52
  44.8 2.7 %collective-permute-start.5 = (f32[6,2,2,8]{0,1,2,3:T(2,128)S(1)}, f32[6,2,2,8]{0,1,2,3:T(2,128)S(1)}, u32[]{:S(2)}, u32[]{:S(2)}) collective-permute-start(f32[6,2,2,8]{0,1,2,3:T(2,128)S(1)} %maximum_select_fusion.1), channel_id=1, source_target_pairs={{0,8},{4,12},{8,0},{12,4},{1,9},{5,13},{9,1},{13,5},{2,10},{6,14},... | collective-permute-start | bytes 2312 | tf_op jit(solution)/shard_map/ppermute | solution.py:52
  47.5 0.7 %reshape.18 = f32[3,2,1,4]{3,1,0,2:T(2,128)} reshape(f32[3,8]{1,0:T(4,128)S(1)} %bitcast.54) | data formatting | bytes 192 | tf_op jit(solution)/shard_map/reshape | solution.py:348
  48.1 1.4 %collective-permute-done.5 = f32[6,2,2,8]{0,1,2,3:T(2,128)S(1)} collective-permute-done((f32[6,2,2,8]{0,1,2,3:T(2,128)S(1)}, f32[6,2,2,8]{0,1,2,3:T(2,128)S(1)}, u32[]{:S(2)}, u32[]{:S(2)}) %collective-permute-start.5) | collective-permute-done | bytes 800 | tf_op jit(solution)/shard_map/ppermute | solution.py:52
  49.5 0.1 copy.37
  49.7 1.8 %all_gather.7 = f32[6,4,4,8]{3,2,0,1:T(4,128)S(1)} all-gather(f32[6,2,4,8]{3,2,0,1:T(4,128)S(1)} %copy.37), channel_id=1, replica_groups=mesh['real'=2,'gx'=4,'gy'=2,'gz'=2] {'gz'}, dimensions={1}, use_global_device_ids=true | all-gather | bytes 4608 | tf_op jit(solution)/shard_map/all_gather | solution.py:464
  51.6 0.1 fusion.11
  51.8 0.1 fusion.18
  51.9 0.7 %dynamic-slice_divide_fusion = f32[2,1,4]{2,1,0:T(1,128)} fusion(f32[4,4,8]{2,1,0:T(4,128)S(1)} %get-tuple-element.23, s32[]{:T(128)S(6)} %select_n.96, s32[]{:T(128)S(6)} %select_n.97, s32[]{:T(128)S(6)} %select_n.98, f32[4,4,8]{2,1,0:T(4,128)S(1)} %get-tuple-element.31, f32[4,4,8]{2,1,0:T(4,128)S(1)} %get-tuple-element.15, ...), kind=kLoop, calls=%fused_computation.85 | loop fusion | flops 80 | bytes 396 | tf_op jit(solution)/shard_map/div | solution.py:369
  (32 shorter events, 0.9 us)
Async XLA Ops:
  0.6 15.4 %copy-start = (f32[16,32,128]{2,1,0:T(8,128)S(1)}, f32[16,32,128]{2,1,0:T(8,128)}, u32[]{:S(2)}) copy-start(f32[16,32,128]{2,1,0:T(8,128)} %param.6) | copy-start | bytes 786436
  2.6 6.8 %collective-permute-start = (f32[2,16,4,128]{3,2,1,0:T(4,128)S(1)}, f32[2,16,4,128]{3,2,1,0:T(4,128)S(1)}, u32[]{:S(2)}, u32[]{:S(2)}) collective-permute-start(f32[2,16,4,128]{3,2,1,0:T(4,128)S(1)} %get-tuple-element.16), channel_id=1, source_target_pairs={{0,4},{4,8},{8,12},{1,5},{5,9},{9,13},{2,6},{6,10},{10,14},{3,7},{... | collective-permute-start | bytes 196616 | tf_op jit(solution)/shard_map/ppermute | solution.py:34
  7.5 6.2 %collective-permute-start.1 = (f32[2,16,4,128]{3,2,1,0:T(4,128)S(1)}, f32[2,16,4,128]{3,2,1,0:T(4,128)S(1)}, u32[]{:S(2)}, u32[]{:S(2)}) collective-permute-start(f32[2,16,4,128]{3,2,1,0:T(4,128)S(1)} %get-tuple-element.17), channel_id=1, source_target_pairs={{4,0},{8,4},{12,8},{5,1},{9,5},{13,9},{6,2},{10,6},{14,10},{7,3},{... | collective-permute-start | bytes 196616 | tf_op jit(solution)/shard_map/ppermute | solution.py:35
  14.6 1.5 %collective-permute-start.2 = (f32[2,4,40,128]{3,2,1,0:T(8,128)S(1)}, f32[2,4,40,128]{3,2,1,0:T(8,128)S(1)}, u32[]{:S(2)}, u32[]{:S(2)}) collective-permute-start(f32[2,4,40,128]{3,2,1,0:T(8,128)S(1)} %fusion), channel_id=1, source_target_pairs={{0,1},{1,0},{2,3},{3,2},{4,5},{5,4},{6,7},{7,6},{8,9},{9,8},{10,11... | collective-permute-start | bytes 491528 | tf_op jit(solution)/shard_map/ppermute | solution.py:30
  16.9 4.9 %collective-permute-start.3 = (f32[2,24,40,4]{2,1,3,0:T(8,128)S(1)}, f32[2,24,40,4]{2,1,3,0:T(8,128)S(1)}, u32[]{:S(2)}, u32[]{:S(2)}) collective-permute-start(f32[2,24,40,4]{2,1,3,0:T(8,128)S(1)} %copy.30), channel_id=1, source_target_pairs={{0,2},{2,0},{1,3},{3,1},{4,6},{6,4},{5,7},{7,5},{8,10},{10,8},{9,1... | collective-permute-start | bytes 92168 | tf_op jit(solution)/shard_map/ppermute | solution.py:30
  24.3 12.3 %copy-start.1 = (f32[2,1,4]{2,1,0:T(1,128)S(1)}, f32[2,1,4]{2,1,0:T(1,128)}, u32[]{:S(2)}) copy-start(f32[2,1,4]{2,1,0:T(1,128)} %param.9) | copy-start | bytes 100
  24.3 12.3 %copy-start.2 = (f32[2,1,4]{2,1,0:T(1,128)S(1)}, f32[2,1,4]{2,1,0:T(1,128)}, u32[]{:S(2)}) copy-start(f32[2,1,4]{2,1,0:T(1,128)} %param.10) | copy-start | bytes 100
  24.3 12.3 %copy-start.3 = (f32[2,1,4]{2,1,0:T(1,128)S(1)}, f32[2,1,4]{2,1,0:T(1,128)}, u32[]{:S(2)}) copy-start(f32[2,1,4]{2,1,0:T(1,128)} %param.11) | copy-start | bytes 100
  41.1 3.7 %collective-permute-start.4 = (f32[6,2,1,8]{0,1,2,3:T(2,128)S(1)}, f32[6,2,1,8]{0,1,2,3:T(2,128)S(1)}, u32[]{:S(2)}, u32[]{:S(2)}) collective-permute-start(f32[6,2,1,8]{0,1,2,3:T(2,128)S(1)} %all_gather.6), channel_id=1, source_target_pairs={{0,4},{4,0},{8,12},{12,8},{1,5},{5,1},{9,13},{13,9},{2,6},{6,2},{1... | collective-permute-start | bytes 1160 | tf_op jit(solution)/shard_map/ppermute | solution.py:52
  44.8 4.7 %collective-permute-start.5 = (f32[6,2,2,8]{0,1,2,3:T(2,128)S(1)}, f32[6,2,2,8]{0,1,2,3:T(2,128)S(1)}, u32[]{:S(2)}, u32[]{:S(2)}) collective-permute-start(f32[6,2,2,8]{0,1,2,3:T(2,128)S(1)} %maximum_select_fusion.1), channel_id=1, source_target_pairs={{0,8},{4,12},{8,0},{12,4},{1,9},{5,13},{9,1},{13,5},{2,10},{6,14},... | collective-permute-start | bytes 2312 | tf_op jit(solution)/shard_map/ppermute | solution.py:52

commit v14 on v13

--- a/solution.py
+++ b/solution.py
@@ -459,9 +459,9 @@
     upscaled = upscale_windows(raw, facies_table, bounds, cols_len)
     coarse_z, coarse_x, coarse_y = pressure_old.shape
     bundle = jnp.stack([upscaled[0], upscaled[1], upscaled[2], pressure_old, accumulation, source])
-    every = lax.all_gather(bundle, "gy", axis=3, tiled=True)
+    every = doubling_gather(bundle, "gy", 3)
     every = doubling_gather(every, "gx", 2)
-    every = lax.all_gather(every, "gz", axis=1, tiled=True)
+    every = doubling_gather(every, "gz", 1)
     perm_pad = jnp.pad(every[:3], ((0, 0), (1, 1), (1, 1), (1, 1)))
     old_all = every[3]
     acc_all = every[4]

time: 52.9 us -> 51.6 us (0.975)
  blocking collectives: 6.16 us -> 0 us
  waiting for transfers between devices: 12.4 us -> 15.6 us
  starting transfers between devices: 12.1 us -> 13.8 us
    all_gather x2 -> x0, blocking collectives: 6.16 us -> none  [the longest x1 4.33 us: local(): every = lax.all_gather(bundle, 'gy', axis=3, tiled=True)]
    ppermute x2 -> x4, waiting for transfers between devices: 3.46 us -> 6.7 us  [doubling_gather(): got = lax.ppermute(values, axis, [(i, i ^ step) for i in range(count)])]
    ppermute x2 -> x4, starting transfers between devices: 4.23 us -> 5.92 us  [doubling_gather(): got = lax.ppermute(values, axis, [(i, i ^ step) for i in range(count)])]
  transfers between devices with their start and end apart: 6 -> 8, of which waited for: 6 -> 8; matrix products, arithmetic and copies ran while one was open for 3% -> 3% of each run, Pallas kernels for 0% -> 0%
where the time goes in v14:
time: 51.6 us; the launch traced here: 51.3 us
  waiting for transfers between devices  15.6 us (30%)
  starting transfers between devices  13.8 us (27%)
  Pallas kernels  11 us (21%)
  other arithmetic  6.19 us (12%)
  local copies, waits for them, and re-layouts  3.85 us (7%)
  between operations  0.82 us (2%)
    pallas_call x1, Pallas kernels, upscale_windows(): pl.pallas_call(kernel, grid=(packs,), in_specs=[pl.BlockSpec(memory_space...  11 us
    ppermute x4, waiting for transfers between devices, doubling_gather(): got = lax.ppermute(values, axis, [(i, i ^ step) for i in range(count)])  6.7 us
    ppermute x4, starting transfers between devices, doubling_gather(): got = lax.ppermute(values, axis, [(i, i ^ step) for i in range(count)])  5.92 us
    ppermute x1, starting transfers between devices, extended(): lax.ppermute(tail, axis, [(i, (i + 1) % count) for i in range(ends)])  4.93 us
    ppermute x1, waiting for transfers between devices, extended(): lax.ppermute(head, axis, [((i + 1) % count, i) for i in range(ends)])  4.27 us
    ppermute x2, waiting for transfers between devices, extended(): lax.ppermute(jnp.where(lower_side, tail, head), axis, [(0, 1), (1, 0)])  4.04 us
    concatenate x2, other arithmetic, extended(): cells = jnp.concatenate(parts, axis=dim)  1.79 us
    ppermute x2, starting transfers between devices, extended(): lax.ppermute(jnp.where(lower_side, tail, head), axis, [(0, 1), (1, 0)])  1.63 us
  transfers between devices with their start and end apart: 8, of which 8 were waited for; matrix products, arithmetic and copies ran while one was open for 3% of the time, Pallas kernels for 0%

profile of v14, /device:TPU:0, one launch (start us, length us, event | category | flops | bytes accessed | tf_op | source)
XLA Modules:
  0.0 51.3 jit_solution(5947461406704087996)
XLA Ops:
  0.6 1.0 %convert_bitcast_fusion = f32[1,16,32,128]{3,2,1,0:T(8,128)S(1)} fusion(s32[16,32,128]{2,1,0:T(8,128)} %param.7), kind=kLoop, calls=%fused_computation.3 | loop fusion | flops 65536 | bytes 524288 | tf_op jit(solution)/shard_map/stack | solution.py:443
  1.7 0.9 %pad_maximum_fusion.6 = (f32[2,16,4,128]{3,2,1,0:T(4,128)S(1)}, f32[2,16,4,128]{3,2,1,0:T(4,128)S(1)}) fusion(f32[1,16,32,128]{3,2,1,0:T(8,128)S(1)} %convert_bitcast_fusion, f32[1,16,32,128]{3,2,1,0:T(8,128)} %bitcast.50), kind=kLoop, calls=%fused_computation.20 | loop fusion | flops 32768 | bytes 655360 | tf_op jit(solution)/shard_map/slice | solution.py:27
  2.6 4.9 %collective-permute-start = (f32[2,16,4,128]{3,2,1,0:T(4,128)S(1)}, f32[2,16,4,128]{3,2,1,0:T(4,128)S(1)}, u32[]{:S(2)}, u32[]{:S(2)}) collective-permute-start(f32[2,16,4,128]{3,2,1,0:T(4,128)S(1)} %get-tuple-element.16), channel_id=1, source_target_pairs={{0,4},{4,8},{8,12},{1,5},{5,9},{9,13},{2,6},{6,10},{10,14},{3,7},{... | collective-permute-start | bytes 196616 | tf_op jit(solution)/shard_map/ppermute | solution.py:34
  7.5 1.3 %collective-permute-start.1 = (f32[2,16,4,128]{3,2,1,0:T(4,128)S(1)}, f32[2,16,4,128]{3,2,1,0:T(4,128)S(1)}, u32[]{:S(2)}, u32[]{:S(2)}) collective-permute-start(f32[2,16,4,128]{3,2,1,0:T(4,128)S(1)} %get-tuple-element.17), channel_id=1, source_target_pairs={{4,0},{8,4},{12,8},{5,1},{9,5},{13,9},{6,2},{10,6},{14,10},{7,3},{... | collective-permute-start | bytes 196616 | tf_op jit(solution)/shard_map/ppermute | solution.py:35
  8.8 0.6 %collective-permute-done = f32[2,16,4,128]{3,2,1,0:T(4,128)S(1)} collective-permute-done((f32[2,16,4,128]{3,2,1,0:T(4,128)S(1)}, f32[2,16,4,128]{3,2,1,0:T(4,128)S(1)}, u32[]{:S(2)}, u32[]{:S(2)}) %collective-permute-start) | collective-permute-done | bytes 65568 | tf_op jit(solution)/shard_map/ppermute | solution.py:34
  9.4 4.3 %collective-permute-done.1 = f32[2,16,4,128]{3,2,1,0:T(4,128)S(1)} collective-permute-done((f32[2,16,4,128]{3,2,1,0:T(4,128)S(1)}, f32[2,16,4,128]{3,2,1,0:T(4,128)S(1)}, u32[]{:S(2)}, u32[]{:S(2)}) %collective-permute-start.1) | collective-permute-done | bytes 65568 | tf_op jit(solution)/shard_map/ppermute | solution.py:35
  13.7 0.9 %fusion = f32[2,4,40,128]{3,2,1,0:T(8,128)S(1)} fusion(f32[2,16,4,128]{3,2,1,0:T(4,128)S(1)} %collective-permute-done.1, f32[2,16,4,128]{3,2,1,0:T(4,128)S(1)} %collective-permute-done, f32[1,16,32,128]{3,2,1,0:T(8,128)S(1)} %convert_bitcast_fusion, f32[1,16,32,128]{3,2,1,0:T(8,128)} %bitcast.51, pred[]{:T(512)S(6)} %eq.27), kind=kLoop, calls=%fused_computation.5 | loop fusion | flops 286720 | bytes 819201 | tf_op jit(solution)/shard_map/jit(_where)/select_n | solution.py:30
  14.7 1.4 %collective-permute-done.2 = f32[2,4,40,128]{3,2,1,0:T(8,128)S(1)} collective-permute-done((f32[2,4,40,128]{3,2,1,0:T(8,128)S(1)}, f32[2,4,40,128]{3,2,1,0:T(8,128)S(1)}, u32[]{:S(2)}, u32[]{:S(2)}) %collective-permute-start.2) | collective-permute-done | bytes 163872 | tf_op jit(solution)/shard_map/ppermute | solution.py:30
  16.1 0.1 pad_maximum_fusion.1
  16.2 0.3 slice_select_fusion
  16.5 0.4 copy.36
  16.9 1.6 %collective-permute-start.3 = (f32[2,24,40,4]{2,1,3,0:T(8,128)S(1)}, f32[2,24,40,4]{2,1,3,0:T(8,128)S(1)}, u32[]{:S(2)}, u32[]{:S(2)}) collective-permute-start(f32[2,24,40,4]{2,1,3,0:T(8,128)S(1)} %copy.36), channel_id=1, source_target_pairs={{0,2},{2,0},{1,3},{3,1},{4,6},{6,4},{5,7},{7,5},{8,10},{10,8},{9,1... | collective-permute-start | bytes 92168 | tf_op jit(solution)/shard_map/ppermute | solution.py:30
  18.5 0.6 %stack.48.bounds_ref = s32[6]{0:T(128)} concatenate(s32[1]{0:T(128)} %bitcast, s32[1]{0:T(128)} %bitcast.1, s32[1]{0:T(128)} %bitcast.2, s32[1]{0:T(128)} %bitcast.3, s32[1]{0:T(128)} %bitcast.4, s32[1]{0:T(128)} %bitcast.5), dimensions={0} | concatenate | bytes 48 | tf_op jit(solution)/shard_map/stack | solution.py:449
  19.1 2.7 %collective-permute-done.3 = f32[2,24,40,4]{2,1,3,0:T(8,128)S(1)} collective-permute-done((f32[2,24,40,4]{2,1,3,0:T(8,128)S(1)}, f32[2,24,40,4]{2,1,3,0:T(8,128)S(1)}, u32[]{:S(2)}, u32[]{:S(2)}) %collective-permute-start.3) | collective-permute-done | bytes 30752 | tf_op jit(solution)/shard_map/ppermute | solution.py:30
  21.8 0.4 copy.39
  22.2 0.4 copy.40
  22.6 1.7 %pad_maximum_fusion.raw_ref = f32[2,24,40,256]{3,2,1,0:T(8,128)} fusion(f32[2,24,40,4]{3,2,1,0:T(8,128)S(1)} %copy.40, f32[2,24,40,4]{3,2,1,0:T(8,128)S(1)} %copy.39, f32[2,4,40,128]{3,2,1,0:T(8,128)S(1)} %get-tuple-element.19, f32[2,16,4,128]{3,2,1,0:T(4,128)S(1)} %collective-permute-done.1, f32[1,16,32,128]{3,2,1,0:T(8,128)S(1)} %convert_bitcast_fusion, ...), kind=kLoop, calls=%fused_computation | loop fusion | flops 3932160 | bytes 3011584 | tf_op jit(solution)/shard_map/concatenate | solution.py:41
  24.3 11.0 %shard_map.77 = f32[3,8,128]{2,1,0:T(8,128)} custom-call(f32[3,4]{1,0:T(4,128)} %table_ref.1, s32[6]{0:T(128)} %stack.48.bounds_ref, f32[2,24,40,256]{3,2,1,0:T(8,128)} %pad_maximum_fusion.raw_ref), custom_call_target="tpu_custom_call" | custom-call | tf_op jit(solution)/shard_map/pallas_call | solution.py:335
  35.4 0.7 %slice.239 = f32[3,3,120]{2,1,0:T(4,128)S(1)} slice(f32[3,8,128]{2,1,0:T(8,128)} %shard_map.77), slice={[0:3], [0:3], [0:120]} | slice | bytes 8640 | tf_op jit(solution)/shard_map/slice | solution.py:346
  36.1 0.1 reshape.68
  36.2 0.1 reduce_sum.9
  36.7 1.6 %collective-permute-start.4 = (f32[6,2,1,4]{3,1,2,0:T(2,128)S(1)}, f32[6,2,1,4]{3,1,2,0:T(2,128)S(1)}, u32[]{:S(2)}, u32[]{:S(2)}) collective-permute-start(f32[6,2,1,4]{3,1,2,0:T(2,128)S(1)} %constant_dynamic-update-slice_fusion), channel_id=1, source_target_pairs={{0,2},{2,0},{1,3},{3,1},{4,6},{6,4},{5,7},{7,5},{8,10},{10,8},{9,1... | collective-permute-start | bytes 584 | tf_op jit(solution)/shard_map/ppermute | solution.py:52
  38.3 2.1 %collective-permute-done.4 = f32[6,2,1,4]{3,1,2,0:T(2,128)S(1)} collective-permute-done((f32[6,2,1,4]{3,1,2,0:T(2,128)S(1)}, f32[6,2,1,4]{3,1,2,0:T(2,128)S(1)}, u32[]{:S(2)}, u32[]{:S(2)}) %collective-permute-start.4) | collective-permute-done | bytes 224 | tf_op jit(solution)/shard_map/ppermute | solution.py:52
  40.5 1.6 %collective-permute-start.5 = (f32[6,2,1,8]{3,1,2,0:T(2,128)S(1)}, f32[6,2,1,8]{3,1,2,0:T(2,128)S(1)}, u32[]{:S(2)}, u32[]{:S(2)}) collective-permute-start(f32[6,2,1,8]{3,1,2,0:T(2,128)S(1)} %maximum_select_fusion.3), channel_id=1, source_target_pairs={{0,4},{4,0},{8,12},{12,8},{1,5},{5,1},{9,13},{13,9},{2,6},{6,2},{1... | collective-permute-start | bytes 1160 | tf_op jit(solution)/shard_map/ppermute | solution.py:52
  42.1 2.1 %collective-permute-done.5 = f32[6,2,1,8]{3,1,2,0:T(2,128)S(1)} collective-permute-done((f32[6,2,1,8]{3,1,2,0:T(2,128)S(1)}, f32[6,2,1,8]{3,1,2,0:T(2,128)S(1)}, u32[]{:S(2)}, u32[]{:S(2)}) %collective-permute-start.5) | collective-permute-done | bytes 416 | tf_op jit(solution)/shard_map/ppermute | solution.py:52
  44.2 2.7 %collective-permute-start.6 = (f32[6,2,2,8]{3,1,2,0:T(2,128)S(1)}, f32[6,2,2,8]{3,1,2,0:T(2,128)S(1)}, u32[]{:S(2)}, u32[]{:S(2)}) collective-permute-start(f32[6,2,2,8]{3,1,2,0:T(2,128)S(1)} %maximum_select_fusion.2), channel_id=1, source_target_pairs={{0,8},{4,12},{8,0},{12,4},{1,9},{5,13},{9,1},{13,5},{2,10},{6,14},... | collective-permute-start | bytes 2312 | tf_op jit(solution)/shard_map/ppermute | solution.py:52
  46.8 2.0 %collective-permute-done.6 = f32[6,2,2,8]{3,1,2,0:T(2,128)S(1)} collective-permute-done((f32[6,2,2,8]{3,1,2,0:T(2,128)S(1)}, f32[6,2,2,8]{3,1,2,0:T(2,128)S(1)}, u32[]{:S(2)}, u32[]{:S(2)}) %collective-permute-start.6) | collective-permute-done | bytes 800 | tf_op jit(solution)/shard_map/ppermute | solution.py:52
  49.0 0.7 %reshape.70 = f32[3,2,1,4]{3,1,0,2:T(2,128)} reshape(f32[3,8]{1,0:T(4,128)S(1)} %bitcast.55) | data formatting | bytes 192 | tf_op jit(solution)/shard_map/reshape | solution.py:348
  49.6 0.5 collective-permute-done.7
  50.3 0.1 fusion.11
  50.5 0.1 fusion.18
  50.6 0.7 %dynamic-slice_divide_fusion = f32[2,1,4]{2,0,1:T(2,128)} fusion(f32[4,4,8]{2,0,1:T(4,128)S(1)} %get-tuple-element.23, s32[]{:T(128)S(6)} %select_n.136, s32[]{:T(128)S(6)} %select_n.137, s32[]{:T(128)S(6)} %select_n.138, f32[4,4,8]{2,0,1:T(4,128)S(1)} %get-tuple-element.31, f32[4,4,8]{2,0,1:T(4,128)S(1)} %get-tuple-element.15, ...), kind=kLoop, calls=%fused_computation.87 | loop fusion | flops 80 | bytes 396 | tf_op jit(solution)/shard_map/div | solution.py:369
  (35 shorter events, 1.0 us)
Async XLA Ops:
  0.6 15.4 %copy-start = (f32[16,32,128]{2,1,0:T(8,128)S(1)}, f32[16,32,128]{2,1,0:T(8,128)}, u32[]{:S(2)}) copy-start(f32[16,32,128]{2,1,0:T(8,128)} %param.6) | copy-start | bytes 786436
  2.6 6.8 %collective-permute-start = (f32[2,16,4,128]{3,2,1,0:T(4,128)S(1)}, f32[2,16,4,128]{3,2,1,0:T(4,128)S(1)}, u32[]{:S(2)}, u32[]{:S(2)}) collective-permute-start(f32[2,16,4,128]{3,2,1,0:T(4,128)S(1)} %get-tuple-element.16), channel_id=1, source_target_pairs={{0,4},{4,8},{8,12},{1,5},{5,9},{9,13},{2,6},{6,10},{10,14},{3,7},{... | collective-permute-start | bytes 196616 | tf_op jit(solution)/shard_map/ppermute | solution.py:34
  7.5 6.2 %collective-permute-start.1 = (f32[2,16,4,128]{3,2,1,0:T(4,128)S(1)}, f32[2,16,4,128]{3,2,1,0:T(4,128)S(1)}, u32[]{:S(2)}, u32[]{:S(2)}) collective-permute-start(f32[2,16,4,128]{3,2,1,0:T(4,128)S(1)} %get-tuple-element.17), channel_id=1, source_target_pairs={{4,0},{8,4},{12,8},{5,1},{9,5},{13,9},{6,2},{10,6},{14,10},{7,3},{... | collective-permute-start | bytes 196616 | tf_op jit(solution)/shard_map/ppermute | solution.py:35
  14.6 1.5 %collective-permute-start.2 = (f32[2,4,40,128]{3,2,1,0:T(8,128)S(1)}, f32[2,4,40,128]{3,2,1,0:T(8,128)S(1)}, u32[]{:S(2)}, u32[]{:S(2)}) collective-permute-start(f32[2,4,40,128]{3,2,1,0:T(8,128)S(1)} %fusion), channel_id=1, source_target_pairs={{0,1},{1,0},{2,3},{3,2},{4,5},{5,4},{6,7},{7,6},{8,9},{9,8},{10,11... | collective-permute-start | bytes 491528 | tf_op jit(solution)/shard_map/ppermute | solution.py:30
  16.9 4.9 %collective-permute-start.3 = (f32[2,24,40,4]{2,1,3,0:T(8,128)S(1)}, f32[2,24,40,4]{2,1,3,0:T(8,128)S(1)}, u32[]{:S(2)}, u32[]{:S(2)}) collective-permute-start(f32[2,24,40,4]{2,1,3,0:T(8,128)S(1)} %copy.36), channel_id=1, source_target_pairs={{0,2},{2,0},{1,3},{3,1},{4,6},{6,4},{5,7},{7,5},{8,10},{10,8},{9,1... | collective-permute-start | bytes 92168 | tf_op jit(solution)/shard_map/ppermute | solution.py:30
  24.3 12.3 %copy-start.1 = (f32[2,1,4]{2,1,0:T(1,128)S(1)}, f32[2,1,4]{2,1,0:T(1,128)}, u32[]{:S(2)}) copy-start(f32[2,1,4]{2,1,0:T(1,128)} %param.9) | copy-start | bytes 100
  24.3 12.3 %copy-start.2 = (f32[2,1,4]{2,1,0:T(1,128)S(1)}, f32[2,1,4]{2,1,0:T(1,128)}, u32[]{:S(2)}) copy-start(f32[2,1,4]{2,1,0:T(1,128)} %param.10) | copy-start | bytes 100
  24.3 12.3 %copy-start.3 = (f32[2,1,4]{2,1,0:T(1,128)S(1)}, f32[2,1,4]{2,1,0:T(1,128)}, u32[]{:S(2)}) copy-start(f32[2,1,4]{2,1,0:T(1,128)} %param.11) | copy-start | bytes 100
  36.7 3.7 %collective-permute-start.4 = (f32[6,2,1,4]{3,1,2,0:T(2,128)S(1)}, f32[6,2,1,4]{3,1,2,0:T(2,128)S(1)}, u32[]{:S(2)}, u32[]{:S(2)}) collective-permute-start(f32[6,2,1,4]{3,1,2,0:T(2,128)S(1)} %constant_dynamic-update-slice_fusion), channel_id=1, source_target_pairs={{0,2},{2,0},{1,3},{3,1},{4,6},{6,4},{5,7},{7,5},{8,10},{10,8},{9,1... | collective-permute-start | bytes 584 | tf_op jit(solution)/shard_map/ppermute | solution.py:52
  40.5 3.7 %collective-permute-start.5 = (f32[6,2,1,8]{3,1,2,0:T(2,128)S(1)}, f32[6,2,1,8]{3,1,2,0:T(2,128)S(1)}, u32[]{:S(2)}, u32[]{:S(2)}) collective-permute-start(f32[6,2,1,8]{3,1,2,0:T(2,128)S(1)} %maximum_select_fusion.3), channel_id=1, source_target_pairs={{0,4},{4,0},{8,12},{12,8},{1,5},{5,1},{9,13},{13,9},{2,6},{6,2},{1... | collective-permute-start | bytes 1160 | tf_op jit(solution)/shard_map/ppermute | solution.py:52
  44.2 4.7 %collective-permute-start.6 = (f32[6,2,2,8]{3,1,2,0:T(2,128)S(1)}, f32[6,2,2,8]{3,1,2,0:T(2,128)S(1)}, u32[]{:S(2)}, u32[]{:S(2)}) collective-permute-start(f32[6,2,2,8]{3,1,2,0:T(2,128)S(1)} %maximum_select_fusion.2), channel_id=1, source_target_pairs={{0,8},{4,12},{8,0},{12,4},{1,9},{5,13},{9,1},{13,5},{2,10},{6,14},... | collective-permute-start | bytes 2312 | tf_op jit(solution)/shard_map/ppermute | solution.py:52
  48.9 1.3 %collective-permute-start.7 = (f32[6,2,4,8]{3,1,2,0:T(2,128)S(1)}, f32[6,2,4,8]{3,1,2,0:T(2,128)S(1)}, u32[]{:S(2)}, u32[]{:S(2)}) collective-permute-start(f32[6,2,4,8]{3,1,2,0:T(2,128)S(1)} %maximum_select_fusion.1), channel_id=1, source_target_pairs={{0,1},{1,0},{2,3},{3,2},{4,5},{5,4},{6,7},{7,6},{8,9},{9,8},{10,11... | collective-permute-start | bytes 4616 | tf_op jit(solution)/shard_map/ppermute | solution.py:52

commit v15 on v14

--- a/solution.py
+++ b/solution.py
@@ -28,8 +28,8 @@
         if count == 2:
             lower_side = lax.axis_index(axis) == 0
             got = lax.ppermute(jnp.where(lower_side, tail, head), axis, [(0, 1), (1, 0)])
-            below = jnp.where(lower_side, 0.0, got)
-            above = jnp.where(lower_side, got, 0.0)
+            below = got
+            above = got
         else:
             below = lax.ppermute(tail, axis, [(i, (i + 1) % count) for i in range(ends)])
             above = lax.ppermute(head, axis, [((i + 1) % count, i) for i in range(ends)])

time: 51.6 us -> 51.1 us (level)
    select_n x2 -> x0, local copies, waits for them, and re-layouts: 0.82 us -> none  [the longest x1 0.41 us: extended(): above = jnp.where(lower_side, got, 0.0)]
where the time goes in v15:
time: 51.1 us; the launch traced here: 50.8 us
  waiting for transfers between devices  15.6 us (31%)
  starting transfers between devices  13.8 us (27%)
  Pallas kernels  11 us (22%)
  other arithmetic  6.14 us (12%)
  local copies, waits for them, and re-layouts  3.44 us (7%)
  between operations  0.8 us (2%)
    pallas_call x1, Pallas kernels, upscale_windows(): pl.pallas_call(kernel, grid=(packs,), in_specs=[pl.BlockSpec(memory_space...  11 us
    ppermute x4, waiting for transfers between devices, doubling_gather(): got = lax.ppermute(values, axis, [(i, i ^ step) for i in range(count)])  6.7 us
    ppermute x4, starting transfers between devices, doubling_gather(): got = lax.ppermute(values, axis, [(i, i ^ step) for i in range(count)])  5.92 us
    ppermute x1, starting transfers between devices, extended(): lax.ppermute(tail, axis, [(i, (i + 1) % count) for i in range(ends)])  4.93 us
    ppermute x1, waiting for transfers between devices, extended(): lax.ppermute(head, axis, [((i + 1) % count, i) for i in range(ends)])  4.27 us
    ppermute x2, waiting for transfers between devices, extended(): lax.ppermute(jnp.where(lower_side, tail, head), axis, [(0, 1), (1, 0)])  4.04 us
    concatenate x2, other arithmetic, extended(): cells = jnp.concatenate(parts, axis=dim)  1.78 us
    ppermute x2, starting transfers between devices, extended(): lax.ppermute(jnp.where(lower_side, tail, head), axis, [(0, 1), (1, 0)])  1.63 us
  transfers between devices with their start and end apart: 8, of which 8 were waited for; matrix products, arithmetic and copies ran while one was open for 3% of the time, Pallas kernels for 0%

profile of v15, /device:TPU:0, one launch (start us, length us, event | category | flops | bytes accessed | tf_op | source)
XLA Modules:
  0.0 50.8 jit_solution(7473848844334020877)
XLA Ops:
  0.6 1.0 %convert_bitcast_fusion = f32[1,16,32,128]{3,2,1,0:T(8,128)S(1)} fusion(s32[16,32,128]{2,1,0:T(8,128)} %param.7), kind=kLoop, calls=%fused_computation.3 | loop fusion | flops 65536 | bytes 524288 | tf_op jit(solution)/shard_map/stack | solution.py:443
  1.7 0.9 %pad_maximum_fusion.6 = (f32[2,16,4,128]{3,2,1,0:T(4,128)S(1)}, f32[2,16,4,128]{3,2,1,0:T(4,128)S(1)}) fusion(f32[1,16,32,128]{3,2,1,0:T(8,128)S(1)} %convert_bitcast_fusion, f32[1,16,32,128]{3,2,1,0:T(8,128)} %bitcast.50), kind=kLoop, calls=%fused_computation.18 | loop fusion | flops 32768 | bytes 655360 | tf_op jit(solution)/shard_map/slice | solution.py:27
  2.6 4.9 %collective-permute-start = (f32[2,16,4,128]{3,2,1,0:T(4,128)S(1)}, f32[2,16,4,128]{3,2,1,0:T(4,128)S(1)}, u32[]{:S(2)}, u32[]{:S(2)}) collective-permute-start(f32[2,16,4,128]{3,2,1,0:T(4,128)S(1)} %get-tuple-element.14), channel_id=1, source_target_pairs={{0,4},{4,8},{8,12},{1,5},{5,9},{9,13},{2,6},{6,10},{10,14},{3,7},{... | collective-permute-start | bytes 196616 | tf_op jit(solution)/shard_map/ppermute | solution.py:34
  7.5 1.3 %collective-permute-start.1 = (f32[2,16,4,128]{3,2,1,0:T(4,128)S(1)}, f32[2,16,4,128]{3,2,1,0:T(4,128)S(1)}, u32[]{:S(2)}, u32[]{:S(2)}) collective-permute-start(f32[2,16,4,128]{3,2,1,0:T(4,128)S(1)} %get-tuple-element.15), channel_id=1, source_target_pairs={{4,0},{8,4},{12,8},{5,1},{9,5},{13,9},{6,2},{10,6},{14,10},{7,3},{... | collective-permute-start | bytes 196616 | tf_op jit(solution)/shard_map/ppermute | solution.py:35
  8.8 0.6 %collective-permute-done = f32[2,16,4,128]{3,2,1,0:T(4,128)S(1)} collective-permute-done((f32[2,16,4,128]{3,2,1,0:T(4,128)S(1)}, f32[2,16,4,128]{3,2,1,0:T(4,128)S(1)}, u32[]{:S(2)}, u32[]{:S(2)}) %collective-permute-start) | collective-permute-done | bytes 65568 | tf_op jit(solution)/shard_map/ppermute | solution.py:34
  9.4 4.3 %collective-permute-done.1 = f32[2,16,4,128]{3,2,1,0:T(4,128)S(1)} collective-permute-done((f32[2,16,4,128]{3,2,1,0:T(4,128)S(1)}, f32[2,16,4,128]{3,2,1,0:T(4,128)S(1)}, u32[]{:S(2)}, u32[]{:S(2)}) %collective-permute-start.1) | collective-permute-done | bytes 65568 | tf_op jit(solution)/shard_map/ppermute | solution.py:35
  13.7 0.9 %fusion = f32[2,4,40,128]{3,2,1,0:T(8,128)S(1)} fusion(f32[2,16,4,128]{3,2,1,0:T(4,128)S(1)} %collective-permute-done.1, f32[2,16,4,128]{3,2,1,0:T(4,128)S(1)} %collective-permute-done, f32[1,16,32,128]{3,2,1,0:T(8,128)S(1)} %convert_bitcast_fusion, f32[1,16,32,128]{3,2,1,0:T(8,128)} %bitcast.51, pred[]{:T(512)S(6)} %eq.27), kind=kLoop, calls=%fused_computation.5 | loop fusion | flops 286720 | bytes 819201 | tf_op jit(solution)/shard_map/jit(_where)/select_n | solution.py:30
  14.7 1.4 %collective-permute-done.2 = f32[2,4,40,128]{3,2,1,0:T(8,128)S(1)} collective-permute-done((f32[2,4,40,128]{3,2,1,0:T(8,128)S(1)}, f32[2,4,40,128]{3,2,1,0:T(8,128)S(1)}, u32[]{:S(2)}, u32[]{:S(2)}) %collective-permute-start.2) | collective-permute-done | bytes 163872 | tf_op jit(solution)/shard_map/ppermute | solution.py:30
  16.0 0.1 pad_maximum_fusion.1
  16.1 0.3 slice_select_fusion
  16.5 0.4 copy.18
  16.8 1.6 %collective-permute-start.3 = (f32[2,24,40,4]{2,1,3,0:T(8,128)S(1)}, f32[2,24,40,4]{2,1,3,0:T(8,128)S(1)}, u32[]{:S(2)}, u32[]{:S(2)}) collective-permute-start(f32[2,24,40,4]{2,1,3,0:T(8,128)S(1)} %copy.18), channel_id=1, source_target_pairs={{0,2},{2,0},{1,3},{3,1},{4,6},{6,4},{5,7},{7,5},{8,10},{10,8},{9,1... | collective-permute-start | bytes 92168 | tf_op jit(solution)/shard_map/ppermute | solution.py:30
  18.5 0.6 %stack.48.bounds_ref = s32[6]{0:T(128)} concatenate(s32[1]{0:T(128)} %bitcast, s32[1]{0:T(128)} %bitcast.1, s32[1]{0:T(128)} %bitcast.2, s32[1]{0:T(128)} %bitcast.3, s32[1]{0:T(128)} %bitcast.4, s32[1]{0:T(128)} %bitcast.5), dimensions={0} | concatenate | bytes 48 | tf_op jit(solution)/shard_map/stack | solution.py:449
  19.1 2.7 %collective-permute-done.3 = f32[2,24,40,4]{2,1,3,0:T(8,128)S(1)} collective-permute-done((f32[2,24,40,4]{2,1,3,0:T(8,128)S(1)}, f32[2,24,40,4]{2,1,3,0:T(8,128)S(1)}, u32[]{:S(2)}, u32[]{:S(2)}) %collective-permute-start.3) | collective-permute-done | bytes 30752 | tf_op jit(solution)/shard_map/ppermute | solution.py:30
  21.7 0.4 copy.19
  22.2 1.7 %pad_maximum_fusion.raw_ref = f32[2,24,40,256]{3,2,1,0:T(8,128)} fusion(f32[2,24,40,4]{3,2,1,0:T(8,128)S(1)} %copy.19, f32[2,4,40,128]{3,2,1,0:T(8,128)S(1)} %collective-permute-done.2, f32[2,16,4,128]{3,2,1,0:T(4,128)S(1)} %collective-permute-done.1, f32[1,16,32,128]{3,2,1,0:T(8,128)S(1)} %convert_bitcast_fusion, f32[1,16,32,128]{3,2,1,0:T(8,128)S(1)} %bitcast.53, ...), kind=kLoop, calls=%fused_computation | loop fusion | flops 3932160 | bytes 2817024 | tf_op jit(solution)/shard_map/concatenate | solution.py:41
  23.9 11.0 %shard_map.77 = f32[3,8,128]{2,1,0:T(8,128)} custom-call(f32[3,4]{1,0:T(4,128)} %table_ref.1, s32[6]{0:T(128)} %stack.48.bounds_ref, f32[2,24,40,256]{3,2,1,0:T(8,128)} %pad_maximum_fusion.raw_ref), custom_call_target="tpu_custom_call" | custom-call | tf_op jit(solution)/shard_map/pallas_call | solution.py:335
  34.9 0.7 %slice.239 = f32[3,3,120]{2,1,0:T(4,128)S(1)} slice(f32[3,8,128]{2,1,0:T(8,128)} %shard_map.77), slice={[0:3], [0:3], [0:120]} | slice | bytes 8640 | tf_op jit(solution)/shard_map/slice | solution.py:346
  35.6 0.1 reshape.68
  35.7 0.1 reduce_sum.9
  35.9 0.1 slice.197
  36.2 1.6 %collective-permute-start.4 = (f32[6,2,1,4]{3,1,2,0:T(2,128)S(1)}, f32[6,2,1,4]{3,1,2,0:T(2,128)S(1)}, u32[]{:S(2)}, u32[]{:S(2)}) collective-permute-start(f32[6,2,1,4]{3,1,2,0:T(2,128)S(1)} %constant_dynamic-update-slice_fusion), channel_id=1, source_target_pairs={{0,2},{2,0},{1,3},{3,1},{4,6},{6,4},{5,7},{7,5},{8,10},{10,8},{9,1... | collective-permute-start | bytes 584 | tf_op jit(solution)/shard_map/ppermute | solution.py:52
  37.8 2.1 %collective-permute-done.4 = f32[6,2,1,4]{3,1,2,0:T(2,128)S(1)} collective-permute-done((f32[6,2,1,4]{3,1,2,0:T(2,128)S(1)}, f32[6,2,1,4]{3,1,2,0:T(2,128)S(1)}, u32[]{:S(2)}, u32[]{:S(2)}) %collective-permute-start.4) | collective-permute-done | bytes 224 | tf_op jit(solution)/shard_map/ppermute | solution.py:52
  40.0 1.6 %collective-permute-start.5 = (f32[6,2,1,8]{3,1,2,0:T(2,128)S(1)}, f32[6,2,1,8]{3,1,2,0:T(2,128)S(1)}, u32[]{:S(2)}, u32[]{:S(2)}) collective-permute-start(f32[6,2,1,8]{3,1,2,0:T(2,128)S(1)} %maximum_select_fusion.3), channel_id=1, source_target_pairs={{0,4},{4,0},{8,12},{12,8},{1,5},{5,1},{9,13},{13,9},{2,6},{6,2},{1... | collective-permute-start | bytes 1160 | tf_op jit(solution)/shard_map/ppermute | solution.py:52
  41.6 2.1 %collective-permute-done.5 = f32[6,2,1,8]{3,1,2,0:T(2,128)S(1)} collective-permute-done((f32[6,2,1,8]{3,1,2,0:T(2,128)S(1)}, f32[6,2,1,8]{3,1,2,0:T(2,128)S(1)}, u32[]{:S(2)}, u32[]{:S(2)}) %collective-permute-start.5) | collective-permute-done | bytes 416 | tf_op jit(solution)/shard_map/ppermute | solution.py:52
  43.7 2.7 %collective-permute-start.6 = (f32[6,2,2,8]{3,1,2,0:T(2,128)S(1)}, f32[6,2,2,8]{3,1,2,0:T(2,128)S(1)}, u32[]{:S(2)}, u32[]{:S(2)}) collective-permute-start(f32[6,2,2,8]{3,1,2,0:T(2,128)S(1)} %maximum_select_fusion.2), channel_id=1, source_target_pairs={{0,8},{4,12},{8,0},{12,4},{1,9},{5,13},{9,1},{13,5},{2,10},{6,14},... | collective-permute-start | bytes 2312 | tf_op jit(solution)/shard_map/ppermute | solution.py:52
  46.4 2.0 %collective-permute-done.6 = f32[6,2,2,8]{3,1,2,0:T(2,128)S(1)} collective-permute-done((f32[6,2,2,8]{3,1,2,0:T(2,128)S(1)}, f32[6,2,2,8]{3,1,2,0:T(2,128)S(1)}, u32[]{:S(2)}, u32[]{:S(2)}) %collective-permute-start.6) | collective-permute-done | bytes 800 | tf_op jit(solution)/shard_map/ppermute | solution.py:52
  48.5 0.7 %reshape.70 = f32[3,2,1,4]{3,1,0,2:T(2,128)} reshape(f32[3,8]{1,0:T(4,128)S(1)} %bitcast.55) | data formatting | bytes 192 | tf_op jit(solution)/shard_map/reshape | solution.py:348
  49.1 0.5 %collective-permute-done.7 = f32[6,2,4,8]{3,1,2,0:T(2,128)S(1)} collective-permute-done((f32[6,2,4,8]{3,1,2,0:T(2,128)S(1)}, f32[6,2,4,8]{3,1,2,0:T(2,128)S(1)}, u32[]{:S(2)}, u32[]{:S(2)}) %collective-permute-start.7) | collective-permute-done | bytes 1568 | tf_op jit(solution)/shard_map/ppermute | solution.py:52
  49.8 0.1 fusion.11
  50.0 0.1 fusion.18
  50.1 0.7 %dynamic-slice_divide_fusion = f32[2,1,4]{2,0,1:T(2,128)} fusion(f32[4,4,8]{2,0,1:T(4,128)S(1)} %get-tuple-element.17, s32[]{:T(128)S(6)} %select_n.108, s32[]{:T(128)S(6)} %select_n.109, s32[]{:T(128)S(6)} %select_n.110, f32[4,4,8]{2,0,1:T(4,128)S(1)} %get-tuple-element.25, f32[4,4,8]{2,0,1:T(4,128)S(1)} %get-tuple-element.13, ...), kind=kLoop, calls=%fused_computation.83 | loop fusion | flops 80 | bytes 396 | tf_op jit(solution)/shard_map/div | solution.py:369
  (32 shorter events, 0.9 us)
Async XLA Ops:
  0.6 15.4 %copy-start = (f32[16,32,128]{2,1,0:T(8,128)S(1)}, f32[16,32,128]{2,1,0:T(8,128)}, u32[]{:S(2)}) copy-start(f32[16,32,128]{2,1,0:T(8,128)} %param.6) | copy-start | bytes 786436
  2.6 6.8 %collective-permute-start = (f32[2,16,4,128]{3,2,1,0:T(4,128)S(1)}, f32[2,16,4,128]{3,2,1,0:T(4,128)S(1)}, u32[]{:S(2)}, u32[]{:S(2)}) collective-permute-start(f32[2,16,4,128]{3,2,1,0:T(4,128)S(1)} %get-tuple-element.14), channel_id=1, source_target_pairs={{0,4},{4,8},{8,12},{1,5},{5,9},{9,13},{2,6},{6,10},{10,14},{3,7},{... | collective-permute-start | bytes 196616 | tf_op jit(solution)/shard_map/ppermute | solution.py:34
  7.5 6.2 %collective-permute-start.1 = (f32[2,16,4,128]{3,2,1,0:T(4,128)S(1)}, f32[2,16,4,128]{3,2,1,0:T(4,128)S(1)}, u32[]{:S(2)}, u32[]{:S(2)}) collective-permute-start(f32[2,16,4,128]{3,2,1,0:T(4,128)S(1)} %get-tuple-element.15), channel_id=1, source_target_pairs={{4,0},{8,4},{12,8},{5,1},{9,5},{13,9},{6,2},{10,6},{14,10},{7,3},{... | collective-permute-start | bytes 196616 | tf_op jit(solution)/shard_map/ppermute | solution.py:35
  14.6 1.5 %collective-permute-start.2 = (f32[2,4,40,128]{3,2,1,0:T(8,128)S(1)}, f32[2,4,40,128]{3,2,1,0:T(8,128)S(1)}, u32[]{:S(2)}, u32[]{:S(2)}) collective-permute-start(f32[2,4,40,128]{3,2,1,0:T(8,128)S(1)} %fusion), channel_id=1, source_target_pairs={{0,1},{1,0},{2,3},{3,2},{4,5},{5,4},{6,7},{7,6},{8,9},{9,8},{10,11... | collective-permute-start | bytes 491528 | tf_op jit(solution)/shard_map/ppermute | solution.py:30
  16.8 4.9 %collective-permute-start.3 = (f32[2,24,40,4]{2,1,3,0:T(8,128)S(1)}, f32[2,24,40,4]{2,1,3,0:T(8,128)S(1)}, u32[]{:S(2)}, u32[]{:S(2)}) collective-permute-start(f32[2,24,40,4]{2,1,3,0:T(8,128)S(1)} %copy.18), channel_id=1, source_target_pairs={{0,2},{2,0},{1,3},{3,1},{4,6},{6,4},{5,7},{7,5},{8,10},{10,8},{9,1... | collective-permute-start | bytes 92168 | tf_op jit(solution)/shard_map/ppermute | solution.py:30
  23.9 12.3 %copy-start.1 = (f32[2,1,4]{2,1,0:T(1,128)S(1)}, f32[2,1,4]{2,1,0:T(1,128)}, u32[]{:S(2)}) copy-start(f32[2,1,4]{2,1,0:T(1,128)} %param.9) | copy-start | bytes 100
  23.9 12.3 %copy-start.2 = (f32[2,1,4]{2,1,0:T(1,128)S(1)}, f32[2,1,4]{2,1,0:T(1,128)}, u32[]{:S(2)}) copy-start(f32[2,1,4]{2,1,0:T(1,128)} %param.10) | copy-start | bytes 100
  23.9 12.3 %copy-start.3 = (f32[2,1,4]{2,1,0:T(1,128)S(1)}, f32[2,1,4]{2,1,0:T(1,128)}, u32[]{:S(2)}) copy-start(f32[2,1,4]{2,1,0:T(1,128)} %param.11) | copy-start | bytes 100
  36.2 3.7 %collective-permute-start.4 = (f32[6,2,1,4]{3,1,2,0:T(2,128)S(1)}, f32[6,2,1,4]{3,1,2,0:T(2,128)S(1)}, u32[]{:S(2)}, u32[]{:S(2)}) collective-permute-start(f32[6,2,1,4]{3,1,2,0:T(2,128)S(1)} %constant_dynamic-update-slice_fusion), channel_id=1, source_target_pairs={{0,2},{2,0},{1,3},{3,1},{4,6},{6,4},{5,7},{7,5},{8,10},{10,8},{9,1... | collective-permute-start | bytes 584 | tf_op jit(solution)/shard_map/ppermute | solution.py:52
  40.0 3.7 %collective-permute-start.5 = (f32[6,2,1,8]{3,1,2,0:T(2,128)S(1)}, f32[6,2,1,8]{3,1,2,0:T(2,128)S(1)}, u32[]{:S(2)}, u32[]{:S(2)}) collective-permute-start(f32[6,2,1,8]{3,1,2,0:T(2,128)S(1)} %maximum_select_fusion.3), channel_id=1, source_target_pairs={{0,4},{4,0},{8,12},{12,8},{1,5},{5,1},{9,13},{13,9},{2,6},{6,2},{1... | collective-permute-start | bytes 1160 | tf_op jit(solution)/shard_map/ppermute | solution.py:52
  43.7 4.7 %collective-permute-start.6 = (f32[6,2,2,8]{3,1,2,0:T(2,128)S(1)}, f32[6,2,2,8]{3,1,2,0:T(2,128)S(1)}, u32[]{:S(2)}, u32[]{:S(2)}) collective-permute-start(f32[6,2,2,8]{3,1,2,0:T(2,128)S(1)} %maximum_select_fusion.2), channel_id=1, source_target_pairs={{0,8},{4,12},{8,0},{12,4},{1,9},{5,13},{9,1},{13,5},{2,10},{6,14},... | collective-permute-start | bytes 2312 | tf_op jit(solution)/shard_map/ppermute | solution.py:52
  48.4 1.3 %collective-permute-start.7 = (f32[6,2,4,8]{3,1,2,0:T(2,128)S(1)}, f32[6,2,4,8]{3,1,2,0:T(2,128)S(1)}, u32[]{:S(2)}, u32[]{:S(2)}) collective-permute-start(f32[6,2,4,8]{3,1,2,0:T(2,128)S(1)} %maximum_select_fusion.1), channel_id=1, source_target_pairs={{0,1},{1,0},{2,3},{3,2},{4,5},{5,4},{6,7},{7,6},{8,9},{9,8},{10,11... | collective-permute-start | bytes 4616 | tf_op jit(solution)/shard_map/ppermute | solution.py:52

commit v16 on v15

--- a/solution.py
+++ b/solution.py
@@ -442,7 +442,7 @@
     index_y = lax.axis_index("gy")
     raw = jnp.stack([log_noise, facies.astype(jnp.float32)])
     wide = -(-(cols_len + 2 * RIM) // LANES) * LANES
-    raw = extended(raw, (("gx", 2), ("gz", 1), ("gy", 3)), RIM, wide)
+    raw = extended(raw, (("gz", 1), ("gx", 2), ("gy", 3)), RIM, wide)
     anchor_z = index_z * depth_len
     anchor_y = index_y * cols_len
     anchor_x = index_x * rows_len

time: 51.1 us -> 51.3 us (level)
    ppermute x2, waiting for transfers between devices: 4.04 us -> 3.42 us  [extended(): lax.ppermute(jnp.where(lower_side, tail, head), axis, [(0, 1), (1, 0)])]
where the time goes in v16:
time: 51.3 us; the launch traced here: 50.9 us
  waiting for transfers between devices  15.3 us (30%)
  starting transfers between devices  14.1 us (27%)
  Pallas kernels  11 us (21%)
  other arithmetic  6.17 us (12%)
  local copies, waits for them, and re-layouts  3.44 us (7%)
  between operations  0.8 us (2%)
    pallas_call x1, Pallas kernels, upscale_windows(): pl.pallas_call(kernel, grid=(packs,), in_specs=[pl.BlockSpec(memory_space...  11 us
    ppermute x4, waiting for transfers between devices, doubling_gather(): got = lax.ppermute(values, axis, [(i, i ^ step) for i in range(count)])  6.71 us
    ppermute x4, starting transfers between devices, doubling_gather(): got = lax.ppermute(values, axis, [(i, i ^ step) for i in range(count)])  5.92 us
    ppermute x1, starting transfers between devices, extended(): lax.ppermute(tail, axis, [(i, (i + 1) % count) for i in range(ends)])  4.84 us
    ppermute x1, waiting for transfers between devices, extended(): lax.ppermute(head, axis, [((i + 1) % count, i) for i in range(ends)])  4.17 us
    ppermute x2, waiting for transfers between devices, extended(): lax.ppermute(jnp.where(lower_side, tail, head), axis, [(0, 1), (1, 0)])  3.42 us
    ppermute x2, starting transfers between devices, extended(): lax.ppermute(jnp.where(lower_side, tail, head), axis, [(0, 1), (1, 0)])  2.07 us
    concatenate x2, other arithmetic, extended(): cells = jnp.concatenate(parts, axis=dim)  1.83 us
  transfers between devices with their start and end apart: 8, of which 8 were waited for; matrix products, arithmetic and copies ran while one was open for 3% of the time, Pallas kernels for 0%

profile of v16, /device:TPU:0, one launch (start us, length us, event | category | flops | bytes accessed | tf_op | source)
XLA Modules:
  0.0 50.9 jit_solution(17811296949839735812)
XLA Ops:
  0.6 1.0 %convert_bitcast_fusion = f32[1,16,32,128]{3,2,1,0:T(8,128)S(1)} fusion(s32[16,32,128]{2,1,0:T(8,128)} %param.7), kind=kLoop, calls=%fused_computation.3 | loop fusion | flops 65536 | bytes 524288 | tf_op jit(solution)/shard_map/stack | solution.py:443
  1.7 0.9 %fusion = f32[2,4,32,128]{3,2,1,0:T(8,128)S(1)} fusion(f32[1,16,32,128]{3,2,1,0:T(8,128)S(1)} %convert_bitcast_fusion, f32[1,16,32,128]{3,2,1,0:T(8,128)} %bitcast.50, pred[]{:T(512)S(6)} %eq.27), kind=kLoop, calls=%fused_computation.5 | loop fusion | flops 98304 | bytes 655361 | tf_op jit(solution)/shard_map/jit(_where)/select_n | solution.py:30
  2.6 0.5 %collective-permute-start = (f32[2,4,32,128]{3,2,1,0:T(8,128)S(1)}, f32[2,4,32,128]{3,2,1,0:T(8,128)S(1)}, u32[]{:S(2)}, u32[]{:S(2)}) collective-permute-start(f32[2,4,32,128]{3,2,1,0:T(8,128)S(1)} %fusion), channel_id=1, source_target_pairs={{0,1},{1,0},{2,3},{3,2},{4,5},{5,4},{6,7},{7,6},{8,9},{9,8},{10,11... | collective-permute-start | bytes 393224 | tf_op jit(solution)/shard_map/ppermute | solution.py:30
  3.1 1.0 %collective-permute-done = f32[2,4,32,128]{3,2,1,0:T(8,128)S(1)} collective-permute-done((f32[2,4,32,128]{3,2,1,0:T(8,128)S(1)}, f32[2,4,32,128]{3,2,1,0:T(8,128)S(1)}, u32[]{:S(2)}, u32[]{:S(2)}) %collective-permute-start) | collective-permute-done | bytes 131104 | tf_op jit(solution)/shard_map/ppermute | solution.py:30
  4.1 0.9 %pad_maximum_fusion.6 = (f32[2,24,4,128]{3,2,1,0:T(4,128)S(1)}, f32[2,24,4,128]{3,2,1,0:T(4,128)S(1)}) fusion(f32[2,4,32,128]{3,2,1,0:T(8,128)S(1)} %collective-permute-done, f32[1,16,32,128]{3,2,1,0:T(8,128)S(1)} %convert_bitcast_fusion, f32[1,16,32,128]{3,2,1,0:T(8,128)} %bitcast.51), kind=kLoop, calls=%fused_computation.12 | loop fusion | flops 147456 | bytes 851968 | tf_op jit(solution)/shard_map/slice | solution.py:27
  5.0 4.8 %collective-permute-start.1 = (f32[2,24,4,128]{3,2,1,0:T(4,128)S(1)}, f32[2,24,4,128]{3,2,1,0:T(4,128)S(1)}, u32[]{:S(2)}, u32[]{:S(2)}) collective-permute-start(f32[2,24,4,128]{3,2,1,0:T(4,128)S(1)} %get-tuple-element.14), channel_id=1, source_target_pairs={{0,4},{4,8},{8,12},{1,5},{5,9},{9,13},{2,6},{6,10},{10,14},{3,7},{... | collective-permute-start | bytes 294920 | tf_op jit(solution)/shard_map/ppermute | solution.py:34
  9.8 1.3 %collective-permute-start.2 = (f32[2,24,4,128]{3,2,1,0:T(4,128)S(1)}, f32[2,24,4,128]{3,2,1,0:T(4,128)S(1)}, u32[]{:S(2)}, u32[]{:S(2)}) collective-permute-start(f32[2,24,4,128]{3,2,1,0:T(4,128)S(1)} %get-tuple-element.15), channel_id=1, source_target_pairs={{4,0},{8,4},{12,8},{5,1},{9,5},{13,9},{6,2},{10,6},{14,10},{7,3},{... | collective-permute-start | bytes 294920 | tf_op jit(solution)/shard_map/ppermute | solution.py:35
  11.1 1.0 %collective-permute-done.1 = f32[2,24,4,128]{3,2,1,0:T(4,128)S(1)} collective-permute-done((f32[2,24,4,128]{3,2,1,0:T(4,128)S(1)}, f32[2,24,4,128]{3,2,1,0:T(4,128)S(1)}, u32[]{:S(2)}, u32[]{:S(2)}) %collective-permute-start.1) | collective-permute-done | bytes 98336 | tf_op jit(solution)/shard_map/ppermute | solution.py:34
  12.2 4.2 %collective-permute-done.2 = f32[2,24,4,128]{3,2,1,0:T(4,128)S(1)} collective-permute-done((f32[2,24,4,128]{3,2,1,0:T(4,128)S(1)}, f32[2,24,4,128]{3,2,1,0:T(4,128)S(1)}, u32[]{:S(2)}, u32[]{:S(2)}) %collective-permute-start.2) | collective-permute-done | bytes 98336 | tf_op jit(solution)/shard_map/ppermute | solution.py:35
  16.3 0.1 pad_maximum_fusion.1
  16.5 0.3 slice_select_fusion
  16.8 0.4 copy.18
  17.2 1.6 %collective-permute-start.3 = (f32[2,24,40,4]{2,1,3,0:T(8,128)S(1)}, f32[2,24,40,4]{2,1,3,0:T(8,128)S(1)}, u32[]{:S(2)}, u32[]{:S(2)}) collective-permute-start(f32[2,24,40,4]{2,1,3,0:T(8,128)S(1)} %copy.18), channel_id=1, source_target_pairs={{0,2},{2,0},{1,3},{3,1},{4,6},{6,4},{5,7},{7,5},{8,10},{10,8},{9,1... | collective-permute-start | bytes 92168 | tf_op jit(solution)/shard_map/ppermute | solution.py:30
  18.8 0.6 %stack.48.bounds_ref = s32[6]{0:T(128)} concatenate(s32[1]{0:T(128)} %bitcast, s32[1]{0:T(128)} %bitcast.1, s32[1]{0:T(128)} %bitcast.2, s32[1]{0:T(128)} %bitcast.3, s32[1]{0:T(128)} %bitcast.4, s32[1]{0:T(128)} %bitcast.5), dimensions={0} | concatenate | bytes 48 | tf_op jit(solution)/shard_map/stack | solution.py:449
  19.4 2.4 %collective-permute-done.3 = f32[2,24,40,4]{2,1,3,0:T(8,128)S(1)} collective-permute-done((f32[2,24,40,4]{2,1,3,0:T(8,128)S(1)}, f32[2,24,40,4]{2,1,3,0:T(8,128)S(1)}, u32[]{:S(2)}, u32[]{:S(2)}) %collective-permute-start.3) | collective-permute-done | bytes 30752 | tf_op jit(solution)/shard_map/ppermute | solution.py:30
  21.8 0.4 copy.19
  22.3 1.7 %pad_maximum_fusion.raw_ref = f32[2,24,40,256]{3,2,1,0:T(8,128)} fusion(f32[2,24,40,4]{3,2,1,0:T(8,128)S(1)} %copy.19, f32[2,24,4,128]{3,2,1,0:T(4,128)S(1)} %collective-permute-done.2, f32[2,4,32,128]{3,2,1,0:T(8,128)S(1)} %collective-permute-done, f32[1,16,32,128]{3,2,1,0:T(8,128)S(1)} %convert_bitcast_fusion, f32[1,16,32,128]{3,2,1,0:T(8,128)S(1)} %bitcast.53, ...), kind=kLoop, calls=%fused_computation | loop fusion | flops 3932160 | bytes 2849792 | tf_op jit(solution)/shard_map/concatenate | solution.py:41
  24.0 11.0 %shard_map.77 = f32[3,8,128]{2,1,0:T(8,128)} custom-call(f32[3,4]{1,0:T(4,128)} %table_ref.1, s32[6]{0:T(128)} %stack.48.bounds_ref, f32[2,24,40,256]{3,2,1,0:T(8,128)} %pad_maximum_fusion.raw_ref), custom_call_target="tpu_custom_call" | custom-call | tf_op jit(solution)/shard_map/pallas_call | solution.py:335
  35.0 0.7 %slice.239 = f32[3,3,120]{2,1,0:T(4,128)S(1)} slice(f32[3,8,128]{2,1,0:T(8,128)} %shard_map.77), slice={[0:3], [0:3], [0:120]} | slice | bytes 8640 | tf_op jit(solution)/shard_map/slice | solution.py:346
  35.7 0.1 reshape.68
  35.8 0.1 reduce_sum.9
  36.3 1.6 %collective-permute-start.4 = (f32[6,2,1,4]{3,1,2,0:T(2,128)S(1)}, f32[6,2,1,4]{3,1,2,0:T(2,128)S(1)}, u32[]{:S(2)}, u32[]{:S(2)}) collective-permute-start(f32[6,2,1,4]{3,1,2,0:T(2,128)S(1)} %constant_dynamic-update-slice_fusion), channel_id=1, source_target_pairs={{0,2},{2,0},{1,3},{3,1},{4,6},{6,4},{5,7},{7,5},{8,10},{10,8},{9,1... | collective-permute-start | bytes 584 | tf_op jit(solution)/shard_map/ppermute | solution.py:52
  37.9 2.1 %collective-permute-done.4 = f32[6,2,1,4]{3,1,2,0:T(2,128)S(1)} collective-permute-done((f32[6,2,1,4]{3,1,2,0:T(2,128)S(1)}, f32[6,2,1,4]{3,1,2,0:T(2,128)S(1)}, u32[]{:S(2)}, u32[]{:S(2)}) %collective-permute-start.4) | collective-permute-done | bytes 224 | tf_op jit(solution)/shard_map/ppermute | solution.py:52
  40.1 1.6 %collective-permute-start.5 = (f32[6,2,1,8]{3,1,2,0:T(2,128)S(1)}, f32[6,2,1,8]{3,1,2,0:T(2,128)S(1)}, u32[]{:S(2)}, u32[]{:S(2)}) collective-permute-start(f32[6,2,1,8]{3,1,2,0:T(2,128)S(1)} %maximum_select_fusion.3), channel_id=1, source_target_pairs={{0,4},{4,0},{8,12},{12,8},{1,5},{5,1},{9,13},{13,9},{2,6},{6,2},{1... | collective-permute-start | bytes 1160 | tf_op jit(solution)/shard_map/ppermute | solution.py:52
  41.8 2.1 %collective-permute-done.5 = f32[6,2,1,8]{3,1,2,0:T(2,128)S(1)} collective-permute-done((f32[6,2,1,8]{3,1,2,0:T(2,128)S(1)}, f32[6,2,1,8]{3,1,2,0:T(2,128)S(1)}, u32[]{:S(2)}, u32[]{:S(2)}) %collective-permute-start.5) | collective-permute-done | bytes 416 | tf_op jit(solution)/shard_map/ppermute | solution.py:52
  43.8 2.7 %collective-permute-start.6 = (f32[6,2,2,8]{3,1,2,0:T(2,128)S(1)}, f32[6,2,2,8]{3,1,2,0:T(2,128)S(1)}, u32[]{:S(2)}, u32[]{:S(2)}) collective-permute-start(f32[6,2,2,8]{3,1,2,0:T(2,128)S(1)} %maximum_select_fusion.2), channel_id=1, source_target_pairs={{0,8},{4,12},{8,0},{12,4},{1,9},{5,13},{9,1},{13,5},{2,10},{6,14},... | collective-permute-start | bytes 2312 | tf_op jit(solution)/shard_map/ppermute | solution.py:52
  46.5 2.0 %collective-permute-done.6 = f32[6,2,2,8]{3,1,2,0:T(2,128)S(1)} collective-permute-done((f32[6,2,2,8]{3,1,2,0:T(2,128)S(1)}, f32[6,2,2,8]{3,1,2,0:T(2,128)S(1)}, u32[]{:S(2)}, u32[]{:S(2)}) %collective-permute-start.6) | collective-permute-done | bytes 800 | tf_op jit(solution)/shard_map/ppermute | solution.py:52
  48.6 0.7 %reshape.70 = f32[3,2,1,4]{3,1,0,2:T(2,128)} reshape(f32[3,8]{1,0:T(4,128)S(1)} %bitcast.55) | data formatting | bytes 192 | tf_op jit(solution)/shard_map/reshape | solution.py:348
  49.3 0.5 %collective-permute-done.7 = f32[6,2,4,8]{3,1,2,0:T(2,128)S(1)} collective-permute-done((f32[6,2,4,8]{3,1,2,0:T(2,128)S(1)}, f32[6,2,4,8]{3,1,2,0:T(2,128)S(1)}, u32[]{:S(2)}, u32[]{:S(2)}) %collective-permute-start.7) | collective-permute-done | bytes 1568 | tf_op jit(solution)/shard_map/ppermute | solution.py:52
  49.9 0.1 fusion.11
  50.1 0.1 fusion.18
  50.2 0.7 %dynamic-slice_divide_fusion = f32[2,1,4]{2,0,1:T(2,128)} fusion(f32[4,4,8]{2,0,1:T(4,128)S(1)} %get-tuple-element.17, s32[]{:T(128)S(6)} %select_n.108, s32[]{:T(128)S(6)} %select_n.109, s32[]{:T(128)S(6)} %select_n.110, f32[4,4,8]{2,0,1:T(4,128)S(1)} %get-tuple-element.25, f32[4,4,8]{2,0,1:T(4,128)S(1)} %get-tuple-element.13, ...), kind=kLoop, calls=%fused_computation.83 | loop fusion | flops 80 | bytes 396 | tf_op jit(solution)/shard_map/div | solution.py:369
  (32 shorter events, 0.9 us)
Async XLA Ops:
  0.6 15.7 %copy-start = (f32[16,32,128]{2,1,0:T(8,128)S(1)}, f32[16,32,128]{2,1,0:T(8,128)}, u32[]{:S(2)}) copy-start(f32[16,32,128]{2,1,0:T(8,128)} %param.6) | copy-start | bytes 786436
  2.6 1.5 %collective-permute-start = (f32[2,4,32,128]{3,2,1,0:T(8,128)S(1)}, f32[2,4,32,128]{3,2,1,0:T(8,128)S(1)}, u32[]{:S(2)}, u32[]{:S(2)}) collective-permute-start(f32[2,4,32,128]{3,2,1,0:T(8,128)S(1)} %fusion), channel_id=1, source_target_pairs={{0,1},{1,0},{2,3},{3,2},{4,5},{5,4},{6,7},{7,6},{8,9},{9,8},{10,11... | collective-permute-start | bytes 393224 | tf_op jit(solution)/shard_map/ppermute | solution.py:30
  5.0 7.2 %collective-permute-start.1 = (f32[2,24,4,128]{3,2,1,0:T(4,128)S(1)}, f32[2,24,4,128]{3,2,1,0:T(4,128)S(1)}, u32[]{:S(2)}, u32[]{:S(2)}) collective-permute-start(f32[2,24,4,128]{3,2,1,0:T(4,128)S(1)} %get-tuple-element.14), channel_id=1, source_target_pairs={{0,4},{4,8},{8,12},{1,5},{5,9},{9,13},{2,6},{6,10},{10,14},{3,7},{... | collective-permute-start | bytes 294920 | tf_op jit(solution)/shard_map/ppermute | solution.py:34
  9.8 6.5 %collective-permute-start.2 = (f32[2,24,4,128]{3,2,1,0:T(4,128)S(1)}, f32[2,24,4,128]{3,2,1,0:T(4,128)S(1)}, u32[]{:S(2)}, u32[]{:S(2)}) collective-permute-start(f32[2,24,4,128]{3,2,1,0:T(4,128)S(1)} %get-tuple-element.15), channel_id=1, source_target_pairs={{4,0},{8,4},{12,8},{5,1},{9,5},{13,9},{6,2},{10,6},{14,10},{7,3},{... | collective-permute-start | bytes 294920 | tf_op jit(solution)/shard_map/ppermute | solution.py:35
  17.2 4.7 %collective-permute-start.3 = (f32[2,24,40,4]{2,1,3,0:T(8,128)S(1)}, f32[2,24,40,4]{2,1,3,0:T(8,128)S(1)}, u32[]{:S(2)}, u32[]{:S(2)}) collective-permute-start(f32[2,24,40,4]{2,1,3,0:T(8,128)S(1)} %copy.18), channel_id=1, source_target_pairs={{0,2},{2,0},{1,3},{3,1},{4,6},{6,4},{5,7},{7,5},{8,10},{10,8},{9,1... | collective-permute-start | bytes 92168 | tf_op jit(solution)/shard_map/ppermute | solution.py:30
  24.0 12.3 %copy-start.1 = (f32[2,1,4]{2,1,0:T(1,128)S(1)}, f32[2,1,4]{2,1,0:T(1,128)}, u32[]{:S(2)}) copy-start(f32[2,1,4]{2,1,0:T(1,128)} %param.9) | copy-start | bytes 100
  24.0 12.3 %copy-start.2 = (f32[2,1,4]{2,1,0:T(1,128)S(1)}, f32[2,1,4]{2,1,0:T(1,128)}, u32[]{:S(2)}) copy-start(f32[2,1,4]{2,1,0:T(1,128)} %param.10) | copy-start | bytes 100
  24.0 12.3 %copy-start.3 = (f32[2,1,4]{2,1,0:T(1,128)S(1)}, f32[2,1,4]{2,1,0:T(1,128)}, u32[]{:S(2)}) copy-start(f32[2,1,4]{2,1,0:T(1,128)} %param.11) | copy-start | bytes 100
  36.3 3.7 %collective-permute-start.4 = (f32[6,2,1,4]{3,1,2,0:T(2,128)S(1)}, f32[6,2,1,4]{3,1,2,0:T(2,128)S(1)}, u32[]{:S(2)}, u32[]{:S(2)}) collective-permute-start(f32[6,2,1,4]{3,1,2,0:T(2,128)S(1)} %constant_dynamic-update-slice_fusion), channel_id=1, source_target_pairs={{0,2},{2,0},{1,3},{3,1},{4,6},{6,4},{5,7},{7,5},{8,10},{10,8},{9,1... | collective-permute-start | bytes 584 | tf_op jit(solution)/shard_map/ppermute | solution.py:52
  40.1 3.7 %collective-permute-start.5 = (f32[6,2,1,8]{3,1,2,0:T(2,128)S(1)}, f32[6,2,1,8]{3,1,2,0:T(2,128)S(1)}, u32[]{:S(2)}, u32[]{:S(2)}) collective-permute-start(f32[6,2,1,8]{3,1,2,0:T(2,128)S(1)} %maximum_select_fusion.3), channel_id=1, source_target_pairs={{0,4},{4,0},{8,12},{12,8},{1,5},{5,1},{9,13},{13,9},{2,6},{6,2},{1... | collective-permute-start | bytes 1160 | tf_op jit(solution)/shard_map/ppermute | solution.py:52
  43.8 4.7 %collective-permute-start.6 = (f32[6,2,2,8]{3,1,2,0:T(2,128)S(1)}, f32[6,2,2,8]{3,1,2,0:T(2,128)S(1)}, u32[]{:S(2)}, u32[]{:S(2)}) collective-permute-start(f32[6,2,2,8]{3,1,2,0:T(2,128)S(1)} %maximum_select_fusion.2), channel_id=1, source_target_pairs={{0,8},{4,12},{8,0},{12,4},{1,9},{5,13},{9,1},{13,5},{2,10},{6,14},... | collective-permute-start | bytes 2312 | tf_op jit(solution)/shard_map/ppermute | solution.py:52
  48.5 1.3 %collective-permute-start.7 = (f32[6,2,4,8]{3,1,2,0:T(2,128)S(1)}, f32[6,2,4,8]{3,1,2,0:T(2,128)S(1)}, u32[]{:S(2)}, u32[]{:S(2)}) collective-permute-start(f32[6,2,4,8]{3,1,2,0:T(2,128)S(1)} %maximum_select_fusion.1), channel_id=1, source_target_pairs={{0,1},{1,0},{2,3},{3,2},{4,5},{5,4},{6,7},{7,6},{8,9},{9,8},{10,11... | collective-permute-start | bytes 4616 | tf_op jit(solution)/shard_map/ppermute | solution.py:52

commit v17 on v15

--- a/solution.py
+++ b/solution.py
@@ -30,6 +30,14 @@
             got = lax.ppermute(jnp.where(lower_side, tail, head), axis, [(0, 1), (1, 0)])
             below = got
             above = got
+        elif count % 2 == 0:
+            even = lax.axis_index(axis) % 2 == 0
+            first = [(i, i ^ 1) for i in range(count)]
+            second = [(i, i + 1 if i % 2 else i - 1) for i in range(1, count - 1)]
+            got_first = lax.ppermute(jnp.where(even, tail, head), axis, first)
+            got_second = lax.ppermute(jnp.where(even, head, tail), axis, second)
+            below = jnp.where(even, got_second, got_first)
+            above = jnp.where(even, got_first, got_second)
         else:
             below = lax.ppermute(tail, axis, [(i, (i + 1) % count) for i in range(ends)])
             above = lax.ppermute(head, axis, [((i + 1) % count, i) for i in range(ends)])

time: 51.1 us -> 49 us (0.959)
  waiting for transfers between devices: 15.6 us -> 11 us
  starting transfers between devices: 13.8 us -> 16.1 us
    ppermute x4, starting transfers between devices: 5.92 us -> 10.3 us  [doubling_gather(): got = lax.ppermute(values, axis, [(i, i ^ step) for i in range(count)])]
    ppermute x2, waiting for transfers between devices: 4.85 us -> 1.58 us  [the longest x1 1.58 us: extended(): got_first = lax.ppermute(jnp.where(even, tail, head), axis, first)]
    ppermute x2, starting transfers between devices: 6.22 us -> 3.74 us  [the longest x1 3.09 us: extended(): got_first = lax.ppermute(jnp.where(even, tail, head), axis, first)]
    ppermute x4, waiting for transfers between devices: 6.7 us -> 5.68 us  [doubling_gather(): got = lax.ppermute(values, axis, [(i, i ^ step) for i in range(count)])]
    select_n x0 -> x3, other arithmetic: none -> 0.93 us  [the longest x1 0.91 us: extended(): got_second = lax.ppermute(jnp.where(even, head, tail), axis, second)]
    slice x1 -> x0, other arithmetic: 0.9 us -> none  [extended(): lax.slice_in_dim(cells, cells.shape[dim] - width, cells.shape[dim], axis=...]
  transfers between devices with their start and end apart: 8 -> 8, of which waited for: 8 -> 7; matrix products, arithmetic and copies ran while one was open for 3% -> 3% of each run, Pallas kernels for 0% -> 0%
where the time goes in v17:
time: 49 us; the launch traced here: 48.6 us
  starting transfers between devices  16.1 us (33%)
  waiting for transfers between devices  11 us (22%)
  Pallas kernels  11 us (22%)
  other arithmetic  6.17 us (13%)
  local copies, waits for them, and re-layouts  3.46 us (7%)
  between operations  0.82 us (2%)
    pallas_call x1, Pallas kernels, upscale_windows(): pl.pallas_call(kernel, grid=(packs,), in_specs=[pl.BlockSpec(memory_space...  11 us
    ppermute x4, starting transfers between devices, doubling_gather(): got = lax.ppermute(values, axis, [(i, i ^ step) for i in range(count)])  10.3 us
    ppermute x4, waiting for transfers between devices, doubling_gather(): got = lax.ppermute(values, axis, [(i, i ^ step) for i in range(count)])  5.68 us
    ppermute x2, waiting for transfers between devices, extended(): lax.ppermute(jnp.where(lower_side, tail, head), axis, [(0, 1), (1, 0)])  3.77 us
    ppermute x1, starting transfers between devices, extended(): got_first = lax.ppermute(jnp.where(even, tail, head), axis, first)  3.09 us
    ppermute x2, starting transfers between devices, extended(): lax.ppermute(jnp.where(lower_side, tail, head), axis, [(0, 1), (1, 0)])  2.07 us
    concatenate x2, other arithmetic, extended(): cells = jnp.concatenate(parts, axis=dim)  1.78 us
    ppermute x1, waiting for transfers between devices, extended(): got_first = lax.ppermute(jnp.where(even, tail, head), axis, first)  1.58 us
  transfers between devices with their start and end apart: 8, of which 7 were waited for; matrix products, arithmetic and copies ran while one was open for 3% of the time, Pallas kernels for 0%

profile of v17, /device:TPU:0, one launch (start us, length us, event | category | flops | bytes accessed | tf_op | source)
XLA Modules:
  0.0 48.6 jit_solution(10310050417357405120)
XLA Ops:
  0.7 1.0 %convert_bitcast_fusion = f32[1,16,32,128]{3,2,1,0:T(8,128)S(1)} fusion(s32[16,32,128]{2,1,0:T(8,128)} %param.7), kind=kLoop, calls=%fused_computation.3 | loop fusion | flops 65536 | bytes 524288 | tf_op jit(solution)/shard_map/stack | solution.py:451
  1.7 0.9 %broadcast_select_fusion.3 = (f32[2,16,4,128]{3,2,1,0:T(4,128)S(1)}, f32[2,16,4,128]{3,2,1,0:T(4,128)S(1)}, f32[2,16,4,128]{3,2,1,0:T(4,128)S(1)}) fusion(pred[]{:T(512)S(6)} %eq.27, f32[1,16,32,128]{3,2,1,0:T(8,128)S(1)} %convert_bitcast_fusion, f32[1,16,32,128]{3,2,1,0:T(8,128)} %bitcast.57), kind=kLoop, calls=%fused_computation.35 | loop fusion | flops 49152 | bytes 720897 | tf_op jit(solution)/shard_map/jit(_where)/select_n | solution.py:38
  2.6 3.1 %collective-permute-start.1 = (f32[2,16,4,128]{3,2,1,0:T(4,128)S(1)}, f32[2,16,4,128]{3,2,1,0:T(4,128)S(1)}, u32[]{:S(2)}, u32[]{:S(2)}) collective-permute-start(f32[2,16,4,128]{3,2,1,0:T(4,128)S(1)} %bitcast.69), channel_id=1, source_target_pairs={{0,4},{4,0},{8,12},{12,8},{1,5},{5,1},{9,13},{13,9},{2,6},{6,2},{1... | collective-permute-start | bytes 196616 | tf_op jit(solution)/shard_map/ppermute | solution.py:37
  5.7 0.7 %collective-permute-start = (f32[2,16,4,128]{3,2,1,0:T(4,128)S(1)}, f32[2,16,4,128]{3,2,1,0:T(4,128)S(1)}, u32[]{:S(2)}, u32[]{:S(2)}) collective-permute-start(f32[2,16,4,128]{3,2,1,0:T(4,128)S(1)} %get-tuple-element.14), channel_id=1, source_target_pairs={{4,8},{8,4},{5,9},{9,5},{6,10},{10,6},{7,11},{11,7},{20,24},{24,20... | collective-permute-start | bytes 196616 | tf_op jit(solution)/shard_map/ppermute | solution.py:38
  6.4 1.6 %collective-permute-done.1 = f32[2,16,4,128]{3,2,1,0:T(4,128)S(1)} collective-permute-done((f32[2,16,4,128]{3,2,1,0:T(4,128)S(1)}, f32[2,16,4,128]{3,2,1,0:T(4,128)S(1)}, u32[]{:S(2)}, u32[]{:S(2)}) %collective-permute-start.1) | collective-permute-done | bytes 65568 | tf_op jit(solution)/shard_map/ppermute | solution.py:37
  8.0 0.9 %fusion = f32[2,4,40,128]{3,2,1,0:T(8,128)S(1)} fusion(f32[2,16,4,128]{3,2,1,0:T(4,128)S(1)} %bitcast.64, f32[2,16,4,128]{3,2,1,0:T(4,128)S(1)} %bitcast.61, f32[1,16,32,128]{3,2,1,0:T(8,128)S(1)} %convert_bitcast_fusion, f32[1,16,32,128]{3,2,1,0:T(8,128)} %bitcast.58, pred[]{:T(512)S(6)} %eq.29), kind=kLoop, calls=%fused_computation.5 | loop fusion | flops 286720 | bytes 819201 | tf_op jit(solution)/shard_map/jit(_where)/select_n | solution.py:30
  9.0 1.4 %collective-permute-done.2 = f32[2,4,40,128]{3,2,1,0:T(8,128)S(1)} collective-permute-done((f32[2,4,40,128]{3,2,1,0:T(8,128)S(1)}, f32[2,4,40,128]{3,2,1,0:T(8,128)S(1)}, u32[]{:S(2)}, u32[]{:S(2)}) %collective-permute-start.2) | collective-permute-done | bytes 163872 | tf_op jit(solution)/shard_map/ppermute | solution.py:30
  10.3 0.1 pad_maximum_fusion.1
  10.4 0.3 slice_select_fusion
  10.8 0.4 copy.18
  11.1 2.0 %collective-permute-start.3 = (f32[2,24,40,4]{2,1,3,0:T(8,128)S(1)}, f32[2,24,40,4]{2,1,3,0:T(8,128)S(1)}, u32[]{:S(2)}, u32[]{:S(2)}) collective-permute-start(f32[2,24,40,4]{2,1,3,0:T(8,128)S(1)} %copy.18), channel_id=1, source_target_pairs={{0,2},{2,0},{1,3},{3,1},{4,6},{6,4},{5,7},{7,5},{8,10},{10,8},{9,1... | collective-permute-start | bytes 92168 | tf_op jit(solution)/shard_map/ppermute | solution.py:30
  13.2 0.6 %stack.48.bounds_ref = s32[6]{0:T(128)} concatenate(s32[1]{0:T(128)} %bitcast, s32[1]{0:T(128)} %bitcast.1, s32[1]{0:T(128)} %bitcast.2, s32[1]{0:T(128)} %bitcast.3, s32[1]{0:T(128)} %bitcast.4, s32[1]{0:T(128)} %bitcast.5), dimensions={0} | concatenate | bytes 48 | tf_op jit(solution)/shard_map/stack | solution.py:457
  13.9 2.4 %collective-permute-done.3 = f32[2,24,40,4]{2,1,3,0:T(8,128)S(1)} collective-permute-done((f32[2,24,40,4]{2,1,3,0:T(8,128)S(1)}, f32[2,24,40,4]{2,1,3,0:T(8,128)S(1)}, u32[]{:S(2)}, u32[]{:S(2)}) %collective-permute-start.3) | collective-permute-done | bytes 30752 | tf_op jit(solution)/shard_map/ppermute | solution.py:30
  16.2 0.4 copy.19
  16.7 1.7 %pad_maximum_fusion.raw_ref = f32[2,24,40,256]{3,2,1,0:T(8,128)} fusion(f32[2,24,40,4]{3,2,1,0:T(8,128)S(1)} %copy.19, f32[2,4,40,128]{3,2,1,0:T(8,128)S(1)} %collective-permute-done.2, f32[2,16,4,128]{3,2,1,0:T(4,128)S(1)} %bitcast.66, f32[1,16,32,128]{3,2,1,0:T(8,128)S(1)} %convert_bitcast_fusion, f32[1,16,32,128]{3,2,1,0:T(8,128)S(1)} %bitcast.60, ...), kind=kLoop, calls=%fused_computation | loop fusion | flops 3932160 | bytes 2817024 | tf_op jit(solution)/shard_map/concatenate | solution.py:49
  18.4 11.0 %shard_map.77 = f32[3,8,128]{2,1,0:T(8,128)} custom-call(f32[3,4]{1,0:T(4,128)} %table_ref.1, s32[6]{0:T(128)} %stack.48.bounds_ref, f32[2,24,40,256]{3,2,1,0:T(8,128)} %pad_maximum_fusion.raw_ref), custom_call_target="tpu_custom_call" | custom-call | tf_op jit(solution)/shard_map/pallas_call | solution.py:343
  29.4 0.7 %slice.239 = f32[3,3,120]{2,1,0:T(4,128)S(1)} slice(f32[3,8,128]{2,1,0:T(8,128)} %shard_map.77), slice={[0:3], [0:3], [0:120]} | slice | bytes 8640 | tf_op jit(solution)/shard_map/slice | solution.py:354
  30.1 0.1 reshape.68
  30.2 0.1 reduce_sum.9
  30.4 0.1 slice.197
  30.7 1.8 %collective-permute-start.4 = (f32[6,2,1,4]{3,1,2,0:T(2,128)S(1)}, f32[6,2,1,4]{3,1,2,0:T(2,128)S(1)}, u32[]{:S(2)}, u32[]{:S(2)}) collective-permute-start(f32[6,2,1,4]{3,1,2,0:T(2,128)S(1)} %constant_dynamic-update-slice_fusion), channel_id=1, source_target_pairs={{0,2},{2,0},{1,3},{3,1},{4,6},{6,4},{5,7},{7,5},{8,10},{10,8},{9,1... | collective-permute-start | bytes 584 | tf_op jit(solution)/shard_map/ppermute | solution.py:60
  32.5 1.9 %collective-permute-done.4 = f32[6,2,1,4]{3,1,2,0:T(2,128)S(1)} collective-permute-done((f32[6,2,1,4]{3,1,2,0:T(2,128)S(1)}, f32[6,2,1,4]{3,1,2,0:T(2,128)S(1)}, u32[]{:S(2)}, u32[]{:S(2)}) %collective-permute-start.4) | collective-permute-done | bytes 224 | tf_op jit(solution)/shard_map/ppermute | solution.py:60
  34.5 4.9 %collective-permute-start.5 = (f32[6,2,1,8]{3,1,2,0:T(2,128)S(1)}, f32[6,2,1,8]{3,1,2,0:T(2,128)S(1)}, u32[]{:S(2)}, u32[]{:S(2)}) collective-permute-start(f32[6,2,1,8]{3,1,2,0:T(2,128)S(1)} %maximum_select_fusion.3), channel_id=1, source_target_pairs={{0,4},{4,0},{8,12},{12,8},{1,5},{5,1},{9,13},{13,9},{2,6},{6,2},{1... | collective-permute-start | bytes 1160 | tf_op jit(solution)/shard_map/ppermute | solution.py:60
  39.4 1.6 %collective-permute-done.5 = f32[6,2,1,8]{3,1,2,0:T(2,128)S(1)} collective-permute-done((f32[6,2,1,8]{3,1,2,0:T(2,128)S(1)}, f32[6,2,1,8]{3,1,2,0:T(2,128)S(1)}, u32[]{:S(2)}, u32[]{:S(2)}) %collective-permute-start.5) | collective-permute-done | bytes 416 | tf_op jit(solution)/shard_map/ppermute | solution.py:60
  41.0 3.5 %collective-permute-start.6 = (f32[6,2,2,8]{3,1,2,0:T(2,128)S(1)}, f32[6,2,2,8]{3,1,2,0:T(2,128)S(1)}, u32[]{:S(2)}, u32[]{:S(2)}) collective-permute-start(f32[6,2,2,8]{3,1,2,0:T(2,128)S(1)} %maximum_select_fusion.2), channel_id=1, source_target_pairs={{0,8},{4,12},{8,0},{12,4},{1,9},{5,13},{9,1},{13,5},{2,10},{6,14},... | collective-permute-start | bytes 2312 | tf_op jit(solution)/shard_map/ppermute | solution.py:60
  44.5 1.7 %collective-permute-done.6 = f32[6,2,2,8]{3,1,2,0:T(2,128)S(1)} collective-permute-done((f32[6,2,2,8]{3,1,2,0:T(2,128)S(1)}, f32[6,2,2,8]{3,1,2,0:T(2,128)S(1)}, u32[]{:S(2)}, u32[]{:S(2)}) %collective-permute-start.6) | collective-permute-done | bytes 800 | tf_op jit(solution)/shard_map/ppermute | solution.py:60
  46.3 0.7 %reshape.70 = f32[3,2,1,4]{3,1,0,2:T(2,128)} reshape(f32[3,8]{1,0:T(4,128)S(1)} %bitcast.73) | data formatting | bytes 192 | tf_op jit(solution)/shard_map/reshape | solution.py:356
  47.0 0.5 %collective-permute-done.7 = f32[6,2,4,8]{3,1,2,0:T(2,128)S(1)} collective-permute-done((f32[6,2,4,8]{3,1,2,0:T(2,128)S(1)}, f32[6,2,4,8]{3,1,2,0:T(2,128)S(1)}, u32[]{:S(2)}, u32[]{:S(2)}) %collective-permute-start.7) | collective-permute-done | bytes 1568 | tf_op jit(solution)/shard_map/ppermute | solution.py:60
  47.6 0.1 fusion.3
  47.7 0.1 fusion.11
  47.9 0.1 fusion.18
  48.0 0.7 %dynamic-slice_divide_fusion = f32[2,1,4]{2,0,1:T(2,128)} fusion(f32[4,4,8]{2,0,1:T(4,128)S(1)} %get-tuple-element.20, s32[]{:T(128)S(6)} %select_n.135, s32[]{:T(128)S(6)} %select_n.136, s32[]{:T(128)S(6)} %select_n.137, f32[4,4,8]{2,0,1:T(4,128)S(1)} %get-tuple-element.28, f32[4,4,8]{2,0,1:T(4,128)S(1)} %get-tuple-element.13, ...), kind=kLoop, calls=%fused_computation.87 | loop fusion | flops 80 | bytes 396 | tf_op jit(solution)/shard_map/div | solution.py:377
  (34 shorter events, 0.8 us)
Async XLA Ops:
  0.6 9.7 %copy-start = (f32[16,32,128]{2,1,0:T(8,128)S(1)}, f32[16,32,128]{2,1,0:T(8,128)}, u32[]{:S(2)}) copy-start(f32[16,32,128]{2,1,0:T(8,128)} %param.6) | copy-start | bytes 786436
  2.6 5.3 %collective-permute-start.1 = (f32[2,16,4,128]{3,2,1,0:T(4,128)S(1)}, f32[2,16,4,128]{3,2,1,0:T(4,128)S(1)}, u32[]{:S(2)}, u32[]{:S(2)}) collective-permute-start(f32[2,16,4,128]{3,2,1,0:T(4,128)S(1)} %bitcast.69), channel_id=1, source_target_pairs={{0,4},{4,0},{8,12},{12,8},{1,5},{5,1},{9,13},{13,9},{2,6},{6,2},{1... | collective-permute-start | bytes 196616 | tf_op jit(solution)/shard_map/ppermute | solution.py:37
  5.7 2.2 %collective-permute-start = (f32[2,16,4,128]{3,2,1,0:T(4,128)S(1)}, f32[2,16,4,128]{3,2,1,0:T(4,128)S(1)}, u32[]{:S(2)}, u32[]{:S(2)}) collective-permute-start(f32[2,16,4,128]{3,2,1,0:T(4,128)S(1)} %get-tuple-element.14), channel_id=1, source_target_pairs={{4,8},{8,4},{5,9},{9,5},{6,10},{10,6},{7,11},{11,7},{20,24},{24,20... | collective-permute-start | bytes 196616 | tf_op jit(solution)/shard_map/ppermute | solution.py:38
  8.9 1.5 %collective-permute-start.2 = (f32[2,4,40,128]{3,2,1,0:T(8,128)S(1)}, f32[2,4,40,128]{3,2,1,0:T(8,128)S(1)}, u32[]{:S(2)}, u32[]{:S(2)}) collective-permute-start(f32[2,4,40,128]{3,2,1,0:T(8,128)S(1)} %fusion), channel_id=1, source_target_pairs={{0,1},{1,0},{2,3},{3,2},{4,5},{5,4},{6,7},{7,6},{8,9},{9,8},{10,11... | collective-permute-start | bytes 491528 | tf_op jit(solution)/shard_map/ppermute | solution.py:30
  11.1 5.1 %collective-permute-start.3 = (f32[2,24,40,4]{2,1,3,0:T(8,128)S(1)}, f32[2,24,40,4]{2,1,3,0:T(8,128)S(1)}, u32[]{:S(2)}, u32[]{:S(2)}) collective-permute-start(f32[2,24,40,4]{2,1,3,0:T(8,128)S(1)} %copy.18), channel_id=1, source_target_pairs={{0,2},{2,0},{1,3},{3,1},{4,6},{6,4},{5,7},{7,5},{8,10},{10,8},{9,1... | collective-permute-start | bytes 92168 | tf_op jit(solution)/shard_map/ppermute | solution.py:30
  18.3 12.3 %copy-start.1 = (f32[2,1,4]{2,1,0:T(1,128)S(1)}, f32[2,1,4]{2,1,0:T(1,128)}, u32[]{:S(2)}) copy-start(f32[2,1,4]{2,1,0:T(1,128)} %param.9) | copy-start | bytes 100
  18.3 12.3 %copy-start.2 = (f32[2,1,4]{2,1,0:T(1,128)S(1)}, f32[2,1,4]{2,1,0:T(1,128)}, u32[]{:S(2)}) copy-start(f32[2,1,4]{2,1,0:T(1,128)} %param.10) | copy-start | bytes 100
  18.3 12.3 %copy-start.3 = (f32[2,1,4]{2,1,0:T(1,128)S(1)}, f32[2,1,4]{2,1,0:T(1,128)}, u32[]{:S(2)}) copy-start(f32[2,1,4]{2,1,0:T(1,128)} %param.11) | copy-start | bytes 100
  30.7 3.7 %collective-permute-start.4 = (f32[6,2,1,4]{3,1,2,0:T(2,128)S(1)}, f32[6,2,1,4]{3,1,2,0:T(2,128)S(1)}, u32[]{:S(2)}, u32[]{:S(2)}) collective-permute-start(f32[6,2,1,4]{3,1,2,0:T(2,128)S(1)} %constant_dynamic-update-slice_fusion), channel_id=1, source_target_pairs={{0,2},{2,0},{1,3},{3,1},{4,6},{6,4},{5,7},{7,5},{8,10},{10,8},{9,1... | collective-permute-start | bytes 584 | tf_op jit(solution)/shard_map/ppermute | solution.py:60
  34.5 6.5 %collective-permute-start.5 = (f32[6,2,1,8]{3,1,2,0:T(2,128)S(1)}, f32[6,2,1,8]{3,1,2,0:T(2,128)S(1)}, u32[]{:S(2)}, u32[]{:S(2)}) collective-permute-start(f32[6,2,1,8]{3,1,2,0:T(2,128)S(1)} %maximum_select_fusion.3), channel_id=1, source_target_pairs={{0,4},{4,0},{8,12},{12,8},{1,5},{5,1},{9,13},{13,9},{2,6},{6,2},{1... | collective-permute-start | bytes 1160 | tf_op jit(solution)/shard_map/ppermute | solution.py:60
  41.0 5.2 %collective-permute-start.6 = (f32[6,2,2,8]{3,1,2,0:T(2,128)S(1)}, f32[6,2,2,8]{3,1,2,0:T(2,128)S(1)}, u32[]{:S(2)}, u32[]{:S(2)}) collective-permute-start(f32[6,2,2,8]{3,1,2,0:T(2,128)S(1)} %maximum_select_fusion.2), channel_id=1, source_target_pairs={{0,8},{4,12},{8,0},{12,4},{1,9},{5,13},{9,1},{13,5},{2,10},{6,14},... | collective-permute-start | bytes 2312 | tf_op jit(solution)/shard_map/ppermute | solution.py:60
  46.2 1.3 %collective-permute-start.7 = (f32[6,2,4,8]{3,1,2,0:T(2,128)S(1)}, f32[6,2,4,8]{3,1,2,0:T(2,128)S(1)}, u32[]{:S(2)}, u32[]{:S(2)}) collective-permute-start(f32[6,2,4,8]{3,1,2,0:T(2,128)S(1)} %maximum_select_fusion.1), channel_id=1, source_target_pairs={{0,1},{1,0},{2,3},{3,2},{4,5},{5,4},{6,7},{7,6},{8,9},{9,8},{10,11... | collective-permute-start | bytes 4616 | tf_op jit(solution)/shard_map/ppermute | solution.py:60

commit v18 on v17

--- a/solution.py
+++ b/solution.py
@@ -50,6 +50,49 @@
     return cells
 
 
+def halo_xy_then_z(block, width, lanes):
+    size_x = lax.axis_size("gx")
+    size_y = lax.axis_size("gy")
+    if size_y != 2 or size_x % 2:
+        return extended(block, (("gx", 2), ("gz", 1), ("gy", 3)), width, lanes)
+    even = lax.axis_index("gx") % 2 == 0
+    low_y = lax.axis_index("gy") == 0
+
+    def edge(values, dim, upper):
+        length = values.shape[dim]
+        start = length - width if upper else 0
+        return lax.slice_in_dim(values, start, start + width, axis=dim)
+
+    def y_side(values):
+        return jnp.where(low_y, edge(values, 3, True), edge(values, 3, False))
+
+    def partner(i):
+        return i + 1 if i % 2 else i - 1
+
+    first = [(i, i ^ 1) for i in range(size_x)]
+    second = [(i, partner(i)) for i in range(1, size_x - 1)]
+    send_first = jnp.where(even, edge(block, 2, True), edge(block, 2, False))
+    send_second = jnp.where(even, edge(block, 2, False), edge(block, 2, True))
+    got_first = lax.ppermute(send_first, "gx", first)
+    got_second = lax.ppermute(send_second, "gx", second)
+    got_y = lax.ppermute(y_side(block), "gy", [(0, 1), (1, 0)])
+    names = ("gx", "gy")
+    corner_first = [(i * 2 + j, (i ^ 1) * 2 + 1 - j) for i in range(size_x) for j in range(2)]
+    corner_second = [(i * 2 + j, partner(i) * 2 + 1 - j) for i in range(1, size_x - 1) for j in range(2)]
+    got_corner_first = lax.ppermute(y_side(send_first), names, corner_first)
+    got_corner_second = lax.ppermute(y_side(send_second), names, corner_second)
+    below_x = jnp.where(even, got_second, got_first)
+    above_x = jnp.where(even, got_first, got_second)
+    below_corner = jnp.where(even, got_corner_second, got_corner_first)
+    above_corner = jnp.where(even, got_corner_first, got_corner_second)
+    centre = jnp.concatenate([below_x, block, above_x], axis=2)
+    rim = jnp.concatenate([below_corner, got_y, above_corner], axis=2)
+    extra = lanes - (block.shape[3] + 2 * width)
+    zeros = jnp.zeros(centre.shape[:3] + (extra,), centre.dtype)
+    cells = jnp.concatenate([centre, rim, zeros, rim], axis=3)
+    return extended(cells, (("gz", 1),), width)
+
+
 def doubling_gather(values, axis, dim):
     count = lax.axis_size(axis)
     if count & (count - 1):
@@ -450,7 +493,7 @@
     index_y = lax.axis_index("gy")
     raw = jnp.stack([log_noise, facies.astype(jnp.float32)])
     wide = -(-(cols_len + 2 * RIM) // LANES) * LANES
-    raw = extended(raw, (("gx", 2), ("gz", 1), ("gy", 3)), RIM, wide)
+    raw = halo_xy_then_z(raw, RIM, wide)
     anchor_z = index_z * depth_len
     anchor_y = index_y * cols_len
     anchor_x = index_x * rows_len

time: 49 us -> 58.1 us (1.19)
  waiting for transfers between devices: 11 us -> 20.8 us
  local copies, waits for them, and re-layouts: 3.46 us -> 2.66 us
    ppermute x2 -> x5, waiting for transfers between devices: 1.58 us -> 12.2 us  [the longest x1 11.6 us: halo_xy_then_z(): got_y = lax.ppermute(y_side(block), 'gy', [(0, 1), (1, 0)])]
    ppermute x2 -> x5, starting transfers between devices: 3.74 us -> 10.4 us  [the longest x1 5.39 us: halo_xy_then_z(): got_corner_first = lax.ppermute(y_side(send_first), names, corner_first)]
    ppermute x4, starting transfers between devices: 10.3 us -> 5.98 us  [doubling_gather(): got = lax.ppermute(values, axis, [(i, i ^ step) for i in range(count)])]
    ppermute x2 -> x1, waiting for transfers between devices: 3.77 us -> 0.94 us  [extended(): lax.ppermute(jnp.where(lower_side, tail, head), axis, [(0, 1), (1, 0)])]
    ppermute x2 -> x1, starting transfers between devices: 2.07 us -> 0.07 us  [extended(): lax.ppermute(jnp.where(lower_side, tail, head), axis, [(0, 1), (1, 0)])]
    ppermute x4, waiting for transfers between devices: 5.68 us -> 7.62 us  [doubling_gather(): got = lax.ppermute(values, axis, [(i, i ^ step) for i in range(count)])]
    select_n x2 -> x1, other arithmetic: 1.24 us -> 0.28 us  [extended(): jnp.where(lower_side, tail, head)]
    select_n x3 -> x7, other arithmetic: 0.93 us -> 1.34 us  [the longest x1 0.91 us: halo_xy_then_z(): send_second = jnp.where(even, edge(block, 2, False), edge(block, 2, True))]
  transfers between devices with their start and end apart: 8 -> 10, of which waited for: 7 -> 7; matrix products, arithmetic and copies ran while one was open for 3% -> 3% of each run, Pallas kernels for 0% -> 0%
where the time goes in v18:
time: 58.1 us; the launch traced here: 57.8 us
  waiting for transfers between devices  20.8 us (36%)
  starting transfers between devices  16.4 us (28%)
  Pallas kernels  11 us (19%)
  other arithmetic  5.95 us (10%)
  local copies, waits for them, and re-layouts  2.66 us (5%)
  between operations  0.89 us (2%)
    ppermute x1, waiting for transfers between devices, halo_xy_then_z(): got_y = lax.ppermute(y_side(block), 'gy', [(0, 1), (1, 0)])  11.6 us
    pallas_call x1, Pallas kernels, upscale_windows(): pl.pallas_call(kernel, grid=(packs,), in_specs=[pl.BlockSpec(memory_space...  11 us
    ppermute x4, waiting for transfers between devices, doubling_gather(): got = lax.ppermute(values, axis, [(i, i ^ step) for i in range(count)])  7.62 us
    ppermute x4, starting transfers between devices, doubling_gather(): got = lax.ppermute(values, axis, [(i, i ^ step) for i in range(count)])  5.98 us
    ppermute x1, starting transfers between devices, halo_xy_then_z(): got_corner_first = lax.ppermute(y_side(send_first), names, corner_first)  5.39 us
    ppermute x1, starting transfers between devices, halo_xy_then_z(): got_first = lax.ppermute(send_first, 'gx', first)  3.09 us
    concatenate x1, other arithmetic, extended(): cells = jnp.concatenate(parts, axis=dim)  2.11 us
  transfers between devices with their start and end apart: 10, of which 7 were waited for; matrix products, arithmetic and copies ran while one was open for 3% of the time, Pallas kernels for 0%

profile of v18, /device:TPU:0, one launch (start us, length us, event | category | flops | bytes accessed | tf_op | source)
XLA Modules:
  0.0 57.8 jit_solution(10507420885240654024)
XLA Ops:
  0.7 1.0 %convert_bitcast_fusion = f32[1,16,32,128]{3,2,1,0:T(8,128)S(1)} fusion(s32[16,32,128]{2,1,0:T(8,128)} %param.7), kind=kLoop, calls=%fused_computation.14 | loop fusion | flops 65536 | bytes 524288 | tf_op jit(solution)/shard_map/stack | solution.py:494
  1.7 0.9 %broadcast_select_fusion.5 = (f32[2,16,4,128]{3,2,1,0:T(4,128)S(1)}, f32[2,16,4,128]{3,2,1,0:T(4,128)S(1)}, f32[2,16,4,128]{3,2,1,0:T(4,128)S(1)}) fusion(pred[]{:T(512)S(6)} %eq.27, f32[1,16,32,128]{3,2,1,0:T(8,128)S(1)} %convert_bitcast_fusion, f32[1,16,32,128]{3,2,1,0:T(8,128)} %bitcast.61), kind=kLoop, calls=%fused_computation.46 | loop fusion | flops 49152 | bytes 720897 | tf_op jit(solution)/shard_map/jit(_where)/select_n | solution.py:75
  2.6 3.1 %collective-permute-start.1 = (f32[2,16,4,128]{3,2,1,0:T(4,128)S(1)}, f32[2,16,4,128]{3,2,1,0:T(4,128)S(1)}, u32[]{:S(2)}, u32[]{:S(2)}) collective-permute-start(f32[2,16,4,128]{3,2,1,0:T(4,128)S(1)} %bitcast.73), channel_id=1, source_target_pairs={{0,4},{4,0},{8,12},{12,8},{1,5},{5,1},{9,13},{13,9},{2,6},{6,2},{1... | collective-permute-start | bytes 196616 | tf_op jit(solution)/shard_map/ppermute | solution.py:76
  5.7 0.7 %collective-permute-start = (f32[2,16,4,128]{3,2,1,0:T(4,128)S(1)}, f32[2,16,4,128]{3,2,1,0:T(4,128)S(1)}, u32[]{:S(2)}, u32[]{:S(2)}) collective-permute-start(f32[2,16,4,128]{3,2,1,0:T(4,128)S(1)} %get-tuple-element.16), channel_id=1, source_target_pairs={{4,8},{8,4},{5,9},{9,5},{6,10},{10,6},{7,11},{11,7},{20,24},{24,20... | collective-permute-start | bytes 196616 | tf_op jit(solution)/shard_map/ppermute | solution.py:77
  6.4 0.1 slice_select_fusion
  6.5 5.4 %collective-permute-start.3 = (f32[2,16,4,4]{3,2,1,0:T(4,128)S(1)}, f32[2,16,4,4]{3,2,1,0:T(4,128)S(1)}, u32[]{:S(2)}, u32[]{:S(2)}) collective-permute-start(f32[2,16,4,4]{3,2,1,0:T(4,128)S(1)} %slice_select_fusion), channel_id=1, source_target_pairs={{0,6},{2,4},{4,2},{6,0},{8,14},{10,12},{12,10},{14,8},{1,7},{3,5},... | collective-permute-start | bytes 6152 | tf_op jit(solution)/shard_map/ppermute | solution.py:82
  11.8 0.1 slice_select_fusion.1
  12.0 0.7 %collective-permute-start.2 = (f32[2,16,4,4]{3,2,1,0:T(4,128)S(1)}, f32[2,16,4,4]{3,2,1,0:T(4,128)S(1)}, u32[]{:S(2)}, u32[]{:S(2)}) collective-permute-start(f32[2,16,4,4]{3,2,1,0:T(4,128)S(1)} %slice_select_fusion.1), channel_id=1, source_target_pairs={{4,10},{6,8},{8,6},{10,4},{5,11},{7,9},{9,7},{11,5},{20,26},{22,24... | collective-permute-start | bytes 6152 | tf_op jit(solution)/shard_map/ppermute | solution.py:83
  12.6 0.2 fusion
  12.8 0.6 %collective-permute-start.4 = (f32[2,16,32,4]{3,2,1,0:T(8,128)S(1)}, f32[2,16,32,4]{3,2,1,0:T(8,128)S(1)}, u32[]{:S(2)}, u32[]{:S(2)}) collective-permute-start(f32[2,16,32,4]{3,2,1,0:T(8,128)S(1)} %fusion), channel_id=1, source_target_pairs={{0,2},{2,0},{1,3},{3,1},{4,6},{6,4},{5,7},{7,5},{8,10},{10,8},{9,1... | collective-permute-start | bytes 49160 | tf_op jit(solution)/shard_map/ppermute | solution.py:78
  13.4 0.7 %collective-permute-done.3 = f32[2,16,4,4]{3,2,1,0:T(4,128)S(1)} collective-permute-done((f32[2,16,4,4]{3,2,1,0:T(4,128)S(1)}, f32[2,16,4,4]{3,2,1,0:T(4,128)S(1)}, u32[]{:S(2)}, u32[]{:S(2)}) %collective-permute-start.3) | collective-permute-done | bytes 2080 | tf_op jit(solution)/shard_map/ppermute | solution.py:82
  14.2 11.6 %collective-permute-done.4 = f32[2,16,32,4]{3,2,1,0:T(8,128)S(1)} collective-permute-done((f32[2,16,32,4]{3,2,1,0:T(8,128)S(1)}, f32[2,16,32,4]{3,2,1,0:T(8,128)S(1)}, u32[]{:S(2)}, u32[]{:S(2)}) %collective-permute-start.4) | collective-permute-done | bytes 16416 | tf_op jit(solution)/shard_map/ppermute | solution.py:78
  25.8 0.3 fusion.2
  26.2 0.7 %stack.48.bounds_ref = s32[6]{0:T(128)} concatenate(s32[1]{0:T(128)} %bitcast, s32[1]{0:T(128)} %bitcast.1, s32[1]{0:T(128)} %bitcast.2, s32[1]{0:T(128)} %bitcast.3, s32[1]{0:T(128)} %bitcast.4, s32[1]{0:T(128)} %bitcast.5), dimensions={0} | concatenate | bytes 48 | tf_op jit(solution)/shard_map/stack | solution.py:500
  26.8 0.9 %collective-permute-done.5 = f32[2,4,40,256]{3,2,1,0:T(8,128)S(1)} collective-permute-done((f32[2,4,40,256]{3,2,1,0:T(8,128)S(1)}, f32[2,4,40,256]{3,2,1,0:T(8,128)S(1)}, u32[]{:S(2)}, u32[]{:S(2)}) %collective-permute-start.5) | collective-permute-done | bytes 327712 | tf_op jit(solution)/shard_map/ppermute | solution.py:30
  27.8 2.1 %pad_maximum_fusion.raw_ref = f32[2,24,40,256]{3,2,1,0:T(8,128)} fusion(f32[2,4,40,256]{3,2,1,0:T(8,128)S(1)} %collective-permute-done.5, f32[2,16,4,4]{3,2,1,0:T(4,128)S(1)} %bitcast.68, f32[2,16,32,4]{3,2,1,0:T(8,128)S(1)} %collective-permute-done.4, f32[2,16,4,4]{3,2,1,0:T(4,128)S(1)} %bitcast.66, f32[2,16,40,120]{3,2,1,0:T(8,128)S(1)} %broadcast_in_dim.6, ...), kind=kLoop, calls=%fused_computation | loop fusion | flops 5898240 | bytes 3584000 | tf_op jit(solution)/shard_map/concatenate | solution.py:49
  29.9 11.0 %shard_map.77 = f32[3,8,128]{2,1,0:T(8,128)} custom-call(f32[3,4]{1,0:T(4,128)} %table_ref.1, s32[6]{0:T(128)} %stack.48.bounds_ref, f32[2,24,40,256]{3,2,1,0:T(8,128)} %pad_maximum_fusion.raw_ref), custom_call_target="tpu_custom_call" | custom-call | tf_op jit(solution)/shard_map/pallas_call | solution.py:386
  40.9 0.7 %slice.261 = f32[3,3,120]{2,1,0:T(4,128)S(1)} slice(f32[3,8,128]{2,1,0:T(8,128)} %shard_map.77), slice={[0:3], [0:3], [0:120]} | slice | bytes 8640 | tf_op jit(solution)/shard_map/slice | solution.py:397
  41.6 0.1 reshape.68
  41.7 0.1 reduce_sum.9
  41.9 0.1 slice.215
  42.2 0.6 %collective-permute-start.6 = (f32[6,2,1,4]{3,1,2,0:T(2,128)S(1)}, f32[6,2,1,4]{3,1,2,0:T(2,128)S(1)}, u32[]{:S(2)}, u32[]{:S(2)}) collective-permute-start(f32[6,2,1,4]{3,1,2,0:T(2,128)S(1)} %constant_dynamic-update-slice_fusion), channel_id=1, source_target_pairs={{0,2},{2,0},{1,3},{3,1},{4,6},{6,4},{5,7},{7,5},{8,10},{10,8},{9,1... | collective-permute-start | bytes 584 | tf_op jit(solution)/shard_map/ppermute | solution.py:103
  42.8 3.1 %collective-permute-done.6 = f32[6,2,1,4]{3,1,2,0:T(2,128)S(1)} collective-permute-done((f32[6,2,1,4]{3,1,2,0:T(2,128)S(1)}, f32[6,2,1,4]{3,1,2,0:T(2,128)S(1)}, u32[]{:S(2)}, u32[]{:S(2)}) %collective-permute-start.6) | collective-permute-done | bytes 224 | tf_op jit(solution)/shard_map/ppermute | solution.py:103
  46.0 3.1 %collective-permute-start.7 = (f32[6,2,1,8]{3,1,2,0:T(2,128)S(1)}, f32[6,2,1,8]{3,1,2,0:T(2,128)S(1)}, u32[]{:S(2)}, u32[]{:S(2)}) collective-permute-start(f32[6,2,1,8]{3,1,2,0:T(2,128)S(1)} %maximum_select_fusion.3), channel_id=1, source_target_pairs={{0,4},{4,0},{8,12},{12,8},{1,5},{5,1},{9,13},{13,9},{2,6},{6,2},{1... | collective-permute-start | bytes 1160 | tf_op jit(solution)/shard_map/ppermute | solution.py:103
  49.1 1.6 %collective-permute-done.7 = f32[6,2,1,8]{3,1,2,0:T(2,128)S(1)} collective-permute-done((f32[6,2,1,8]{3,1,2,0:T(2,128)S(1)}, f32[6,2,1,8]{3,1,2,0:T(2,128)S(1)}, u32[]{:S(2)}, u32[]{:S(2)}) %collective-permute-start.7) | collective-permute-done | bytes 416 | tf_op jit(solution)/shard_map/ppermute | solution.py:103
  50.7 2.2 %collective-permute-start.8 = (f32[6,2,2,8]{3,1,2,0:T(2,128)S(1)}, f32[6,2,2,8]{3,1,2,0:T(2,128)S(1)}, u32[]{:S(2)}, u32[]{:S(2)}) collective-permute-start(f32[6,2,2,8]{3,1,2,0:T(2,128)S(1)} %maximum_select_fusion.2), channel_id=1, source_target_pairs={{0,8},{4,12},{8,0},{12,4},{1,9},{5,13},{9,1},{13,5},{2,10},{6,14},... | collective-permute-start | bytes 2312 | tf_op jit(solution)/shard_map/ppermute | solution.py:103
  52.9 2.4 %collective-permute-done.8 = f32[6,2,2,8]{3,1,2,0:T(2,128)S(1)} collective-permute-done((f32[6,2,2,8]{3,1,2,0:T(2,128)S(1)}, f32[6,2,2,8]{3,1,2,0:T(2,128)S(1)}, u32[]{:S(2)}, u32[]{:S(2)}) %collective-permute-start.8) | collective-permute-done | bytes 800 | tf_op jit(solution)/shard_map/ppermute | solution.py:103
  55.5 0.7 %reshape.70 = f32[3,2,1,4]{3,1,0,2:T(2,128)} reshape(f32[3,8]{1,0:T(4,128)S(1)} %bitcast.82) | data formatting | bytes 192 | tf_op jit(solution)/shard_map/reshape | solution.py:399
  56.1 0.5 collective-permute-done.9
  56.8 0.1 fusion.14
  57.0 0.1 fusion.21
  57.1 0.7 %dynamic-slice_divide_fusion = f32[2,1,4]{2,0,1:T(2,128)} fusion(f32[4,4,8]{2,0,1:T(4,128)S(1)} %get-tuple-element.24, s32[]{:T(128)S(6)} %select_n.163, s32[]{:T(128)S(6)} %select_n.164, s32[]{:T(128)S(6)} %select_n.165, f32[4,4,8]{2,0,1:T(4,128)S(1)} %get-tuple-element.32, f32[4,4,8]{2,0,1:T(4,128)S(1)} %get-tuple-element.15, ...), kind=kLoop, calls=%fused_computation.98 | loop fusion | flops 80 | bytes 396 | tf_op jit(solution)/shard_map/div | solution.py:420
  (37 shorter events, 0.9 us)
Async XLA Ops:
  0.6 12.0 %copy-start = (f32[16,32,128]{2,1,0:T(8,128)S(1)}, f32[16,32,128]{2,1,0:T(8,128)}, u32[]{:S(2)}) copy-start(f32[16,32,128]{2,1,0:T(8,128)} %param.6) | copy-start | bytes 786436
  2.6 11.5 %collective-permute-start.1 = (f32[2,16,4,128]{3,2,1,0:T(4,128)S(1)}, f32[2,16,4,128]{3,2,1,0:T(4,128)S(1)}, u32[]{:S(2)}, u32[]{:S(2)}) collective-permute-start(f32[2,16,4,128]{3,2,1,0:T(4,128)S(1)} %bitcast.73), channel_id=1, source_target_pairs={{0,4},{4,0},{8,12},{12,8},{1,5},{5,1},{9,13},{13,9},{2,6},{6,2},{1... | collective-permute-start | bytes 196616 | tf_op jit(solution)/shard_map/ppermute | solution.py:76
  5.7 8.4 %collective-permute-start = (f32[2,16,4,128]{3,2,1,0:T(4,128)S(1)}, f32[2,16,4,128]{3,2,1,0:T(4,128)S(1)}, u32[]{:S(2)}, u32[]{:S(2)}) collective-permute-start(f32[2,16,4,128]{3,2,1,0:T(4,128)S(1)} %get-tuple-element.16), channel_id=1, source_target_pairs={{4,8},{8,4},{5,9},{9,5},{6,10},{10,6},{7,11},{11,7},{20,24},{24,20... | collective-permute-start | bytes 196616 | tf_op jit(solution)/shard_map/ppermute | solution.py:77
  6.5 7.6 %collective-permute-start.3 = (f32[2,16,4,4]{3,2,1,0:T(4,128)S(1)}, f32[2,16,4,4]{3,2,1,0:T(4,128)S(1)}, u32[]{:S(2)}, u32[]{:S(2)}) collective-permute-start(f32[2,16,4,4]{3,2,1,0:T(4,128)S(1)} %slice_select_fusion), channel_id=1, source_target_pairs={{0,6},{2,4},{4,2},{6,0},{8,14},{10,12},{12,10},{14,8},{1,7},{3,5},... | collective-permute-start | bytes 6152 | tf_op jit(solution)/shard_map/ppermute | solution.py:82
  12.0 2.1 %collective-permute-start.2 = (f32[2,16,4,4]{3,2,1,0:T(4,128)S(1)}, f32[2,16,4,4]{3,2,1,0:T(4,128)S(1)}, u32[]{:S(2)}, u32[]{:S(2)}) collective-permute-start(f32[2,16,4,4]{3,2,1,0:T(4,128)S(1)} %slice_select_fusion.1), channel_id=1, source_target_pairs={{4,10},{6,8},{8,6},{10,4},{5,11},{7,9},{9,7},{11,5},{20,26},{22,24... | collective-permute-start | bytes 6152 | tf_op jit(solution)/shard_map/ppermute | solution.py:83
  12.8 12.9 %collective-permute-start.4 = (f32[2,16,32,4]{3,2,1,0:T(8,128)S(1)}, f32[2,16,32,4]{3,2,1,0:T(8,128)S(1)}, u32[]{:S(2)}, u32[]{:S(2)}) collective-permute-start(f32[2,16,32,4]{3,2,1,0:T(8,128)S(1)} %fusion), channel_id=1, source_target_pairs={{0,2},{2,0},{1,3},{3,1},{4,6},{6,4},{5,7},{7,5},{8,10},{10,8},{9,1... | collective-permute-start | bytes 49160 | tf_op jit(solution)/shard_map/ppermute | solution.py:78
  26.1 1.7 %collective-permute-start.5 = (f32[2,4,40,256]{3,2,1,0:T(8,128)S(1)}, f32[2,4,40,256]{3,2,1,0:T(8,128)S(1)}, u32[]{:S(2)}, u32[]{:S(2)}) collective-permute-start(f32[2,4,40,256]{3,2,1,0:T(8,128)S(1)} %fusion.2), channel_id=1, source_target_pairs={{0,1},{1,0},{2,3},{3,2},{4,5},{5,4},{6,7},{7,6},{8,9},{9,8},{10,11... | collective-permute-start | bytes 983048 | tf_op jit(solution)/shard_map/ppermute | solution.py:30
  29.9 12.3 %copy-start.1 = (f32[2,1,4]{2,1,0:T(1,128)S(1)}, f32[2,1,4]{2,1,0:T(1,128)}, u32[]{:S(2)}) copy-start(f32[2,1,4]{2,1,0:T(1,128)} %param.9) | copy-start | bytes 100
  29.9 12.3 %copy-start.2 = (f32[2,1,4]{2,1,0:T(1,128)S(1)}, f32[2,1,4]{2,1,0:T(1,128)}, u32[]{:S(2)}) copy-start(f32[2,1,4]{2,1,0:T(1,128)} %param.10) | copy-start | bytes 100
  29.9 12.3 %copy-start.3 = (f32[2,1,4]{2,1,0:T(1,128)S(1)}, f32[2,1,4]{2,1,0:T(1,128)}, u32[]{:S(2)}) copy-start(f32[2,1,4]{2,1,0:T(1,128)} %param.11) | copy-start | bytes 100
  42.2 3.7 %collective-permute-start.6 = (f32[6,2,1,4]{3,1,2,0:T(2,128)S(1)}, f32[6,2,1,4]{3,1,2,0:T(2,128)S(1)}, u32[]{:S(2)}, u32[]{:S(2)}) collective-permute-start(f32[6,2,1,4]{3,1,2,0:T(2,128)S(1)} %constant_dynamic-update-slice_fusion), channel_id=1, source_target_pairs={{0,2},{2,0},{1,3},{3,1},{4,6},{6,4},{5,7},{7,5},{8,10},{10,8},{9,1... | collective-permute-start | bytes 584 | tf_op jit(solution)/shard_map/ppermute | solution.py:103
  46.0 4.7 %collective-permute-start.7 = (f32[6,2,1,8]{3,1,2,0:T(2,128)S(1)}, f32[6,2,1,8]{3,1,2,0:T(2,128)S(1)}, u32[]{:S(2)}, u32[]{:S(2)}) collective-permute-start(f32[6,2,1,8]{3,1,2,0:T(2,128)S(1)} %maximum_select_fusion.3), channel_id=1, source_target_pairs={{0,4},{4,0},{8,12},{12,8},{1,5},{5,1},{9,13},{13,9},{2,6},{6,2},{1... | collective-permute-start | bytes 1160 | tf_op jit(solution)/shard_map/ppermute | solution.py:103
  50.7 4.7 %collective-permute-start.8 = (f32[6,2,2,8]{3,1,2,0:T(2,128)S(1)}, f32[6,2,2,8]{3,1,2,0:T(2,128)S(1)}, u32[]{:S(2)}, u32[]{:S(2)}) collective-permute-start(f32[6,2,2,8]{3,1,2,0:T(2,128)S(1)} %maximum_select_fusion.2), channel_id=1, source_target_pairs={{0,8},{4,12},{8,0},{12,4},{1,9},{5,13},{9,1},{13,5},{2,10},{6,14},... | collective-permute-start | bytes 2312 | tf_op jit(solution)/shard_map/ppermute | solution.py:103
  55.4 1.3 %collective-permute-start.9 = (f32[6,2,4,8]{3,1,2,0:T(2,128)S(1)}, f32[6,2,4,8]{3,1,2,0:T(2,128)S(1)}, u32[]{:S(2)}, u32[]{:S(2)}) collective-permute-start(f32[6,2,4,8]{3,1,2,0:T(2,128)S(1)} %maximum_select_fusion.1), channel_id=1, source_target_pairs={{0,1},{1,0},{2,3},{3,2},{4,5},{5,4},{6,7},{7,6},{8,9},{9,8},{10,11... | collective-permute-start | bytes 4616 | tf_op jit(solution)/shard_map/ppermute | solution.py:103

commit v19 on v17

--- a/solution.py
+++ b/solution.py
@@ -50,6 +50,56 @@
     return cells
 
 
+def face_slabs(block, axis, dim):
+    count = lax.axis_size(axis)
+    head = lax.slice_in_dim(block, 0, 1, axis=dim)
+    tail = lax.slice_in_dim(block, block.shape[dim] - 1, block.shape[dim], axis=dim)
+    index = lax.axis_index(axis)
+    if count == 1:
+        return jnp.zeros_like(tail), jnp.zeros_like(head)
+    if count == 2:
+        lower_side = index == 0
+        got = lax.ppermute(jnp.where(lower_side, tail, head), axis, [(0, 1), (1, 0)])
+        return jnp.where(lower_side, 0.0, got), jnp.where(lower_side, got, 0.0)
+    if count % 2 == 0:
+        even = index % 2 == 0
+        first = [(i, i ^ 1) for i in range(count)]
+        second = [(i, i + 1 if i % 2 else i - 1) for i in range(1, count - 1)]
+        got_first = lax.ppermute(jnp.where(even, tail, head), axis, first)
+        got_second = lax.ppermute(jnp.where(even, head, tail), axis, second)
+        return jnp.where(even, got_second, got_first), jnp.where(even, got_first, got_second)
+    lower = lax.ppermute(tail, axis, [(i, i + 1) for i in range(count - 1)])
+    upper = lax.ppermute(head, axis, [(i + 1, i) for i in range(count - 1)])
+    return lower, upper
+
+
+def faces(block, sides):
+    return [face_slabs(block, axis, dim) for axis, dim in sides]
+
+
+def neighbour_views(block, got, dim_of):
+    views = []
+    for (lower, upper), dim in zip(got, dim_of):
+        size = block.shape[dim]
+        below = jnp.concatenate([lower, lax.slice_in_dim(block, 0, size - 1, axis=dim)], axis=dim)
+        above = jnp.concatenate([lax.slice_in_dim(block, 1, size, axis=dim), upper], axis=dim)
+        views.append((below, above))
+    return views
+
+
+def coarse_step(upscaled, views, inside_views, pressure, accumulation, fixed):
+    factors = (CCY * CCZ / CCX, CCX * CCZ / CCY, CCX * CCY / CCZ)
+    numer = fixed
+    denom = accumulation
+    for component in range(3):
+        for side in range(2):
+            beside = views[component][side]
+            link = factors[component] * 0.5 * (upscaled[component] + beside[component]) * inside_views[component][side]
+            numer = numer + link * pressure[component][side]
+            denom = denom + jnp.abs(link)
+    return numer / denom
+
+
 def doubling_gather(values, axis, dim):
     count = lax.axis_size(axis)
     if count & (count - 1):
@@ -465,22 +515,19 @@
         ]
     ).astype(jnp.int32)
     upscaled = upscale_windows(raw, facies_table, bounds, cols_len)
-    coarse_z, coarse_x, coarse_y = pressure_old.shape
-    bundle = jnp.stack([upscaled[0], upscaled[1], upscaled[2], pressure_old, accumulation, source])
-    every = doubling_gather(bundle, "gy", 3)
-    every = doubling_gather(every, "gx", 2)
-    every = doubling_gather(every, "gz", 1)
-    perm_pad = jnp.pad(every[:3], ((0, 0), (1, 1), (1, 1), (1, 1)))
-    old_all = every[3]
-    acc_all = every[4]
-    fixed_all = acc_all * old_all + every[5]
-    inside_pad = jnp.pad(jnp.ones(old_all.shape, jnp.float32), 1)
-    pressure = old_all
-    for sweep_index in range(2):
-        pressure = coarse_sweep(perm_pad, jnp.pad(pressure, 1), inside_pad, acc_all, fixed_all)
-    pressure = lax.dynamic_slice(
-        pressure, (index_z * coarse_z, index_x * coarse_x, index_y * coarse_y), (coarse_z, coarse_x, coarse_y)
-    )
+    fixed = accumulation * pressure_old + source
+    ones = jnp.ones_like(pressure_old)
+    bundle = jnp.stack([upscaled[0], upscaled[1], upscaled[2], pressure_old, ones])
+    sides = (("gx", 2), ("gy", 3), ("gz", 1))
+    dim_of = (2, 3, 1)
+    views = neighbour_views(bundle, faces(bundle, sides), dim_of)
+    inside_views = [(below[4], above[4]) for below, above in views]
+    perm_views = [(below[:3], above[:3]) for below, above in views]
+    press_views = [(below[3], above[3]) for below, above in views]
+    pressure = coarse_step(upscaled, perm_views, inside_views, press_views, accumulation, fixed)
+    got = faces(pressure, (("gx", 1), ("gy", 2), ("gz", 0)))
+    press_views = neighbour_views(pressure, got, (1, 2, 0))
+    pressure = coarse_step(upscaled, perm_views, inside_views, press_views, accumulation, fixed)
     return (pressure, upscaled)
 
 

time: 49 us -> 71.8 us (1.47)
  starting transfers between devices: 16.1 us -> 33.1 us
  waiting for transfers between devices: 11 us -> 16.3 us
    ppermute x4 -> x12, starting transfers between devices: 10.3 us -> 27.3 us  [the longest x6 19.5 us: faces(): lower = lax.ppermute(tail, axis, [(i, i + 1) for i in range(ends)])]
    ppermute x4 -> x12, waiting for transfers between devices: 5.68 us -> 11 us  [the longest x6 8.39 us: faces(): upper = lax.ppermute(head, axis, [(i + 1, i) for i in range(ends)])]
  transfers between devices with their start and end apart: 8 -> 16, of which waited for: 7 -> 7; matrix products, arithmetic and copies ran while one was open for 3% -> 2% of each run, Pallas kernels for 0% -> 0%
where the time goes in v19:
time: 71.8 us; the launch traced here: 71 us
  starting transfers between devices  33.1 us (46%)
  waiting for transfers between devices  16.3 us (23%)
  Pallas kernels  11 us (15%)
  other arithmetic  5.79 us (8%)
  local copies, waits for them, and re-layouts  3.94 us (5%)
  between operations  0.89 us (1%)
    ppermute x6, starting transfers between devices, faces(): lower = lax.ppermute(tail, axis, [(i, i + 1) for i in range(ends)])  19.5 us
    pallas_call x1, Pallas kernels, upscale_windows(): pl.pallas_call(kernel, grid=(packs,), in_specs=[pl.BlockSpec(memory_space...  11 us
    ppermute x6, waiting for transfers between devices, faces(): upper = lax.ppermute(head, axis, [(i + 1, i) for i in range(ends)])  8.39 us
    ppermute x6, starting transfers between devices, faces(): upper = lax.ppermute(head, axis, [(i + 1, i) for i in range(ends)])  7.73 us
    ppermute x2, waiting for transfers between devices, extended(): lax.ppermute(jnp.where(lower_side, tail, head), axis, [(0, 1), (1, 0)])  3.73 us
    ppermute x1, starting transfers between devices, extended(): got_first = lax.ppermute(jnp.where(even, tail, head), axis, first)  3.09 us
    ppermute x6, waiting for transfers between devices, faces(): lower = lax.ppermute(tail, axis, [(i, i + 1) for i in range(ends)])  2.61 us
    ppermute x2, starting transfers between devices, extended(): lax.ppermute(jnp.where(lower_side, tail, head), axis, [(0, 1), (1, 0)])  2.07 us
  transfers between devices with their start and end apart: 16, of which 7 were waited for; matrix products, arithmetic and copies ran while one was open for 2% of the time, Pallas kernels for 0%

profile of v19, /device:TPU:0, one launch (start us, length us, event | category | flops | bytes accessed | tf_op | source)
XLA Modules:
  0.0 71.0 jit_solution(3975027187783425889)
XLA Ops:
  0.7 1.0 %convert_bitcast_fusion = f32[1,16,32,128]{3,2,1,0:T(8,128)S(1)} fusion(s32[16,32,128]{2,1,0:T(8,128)} %param.7), kind=kLoop, calls=%fused_computation.3 | loop fusion | flops 65536 | bytes 524288 | tf_op jit(solution)/shard_map/stack | solution.py:501
  1.7 0.9 %broadcast_select_fusion.3 = (f32[2,16,4,128]{3,2,1,0:T(4,128)S(1)}, f32[2,16,4,128]{3,2,1,0:T(4,128)S(1)}, f32[2,16,4,128]{3,2,1,0:T(4,128)S(1)}) fusion(pred[]{:T(512)S(6)} %eq.12, f32[1,16,32,128]{3,2,1,0:T(8,128)S(1)} %convert_bitcast_fusion, f32[1,16,32,128]{3,2,1,0:T(8,128)} %bitcast.232), kind=kLoop, calls=%fused_computation.13 | loop fusion | flops 49152 | bytes 720897 | tf_op jit(solution)/shard_map/jit(_where)/select_n | solution.py:38
  2.6 3.1 %collective-permute-start.1 = (f32[2,16,4,128]{3,2,1,0:T(4,128)S(1)}, f32[2,16,4,128]{3,2,1,0:T(4,128)S(1)}, u32[]{:S(2)}, u32[]{:S(2)}) collective-permute-start(f32[2,16,4,128]{3,2,1,0:T(4,128)S(1)} %bitcast.244), channel_id=1, source_target_pairs={{0,4},{4,0},{8,12},{12,8},{1,5},{5,1},{9,13},{13,9},{2,6},{6,2},{1... | collective-permute-start | bytes 196616 | tf_op jit(solution)/shard_map/ppermute | solution.py:37
  5.7 0.7 collective-permute-start
  6.4 1.6 %collective-permute-done.1 = f32[2,16,4,128]{3,2,1,0:T(4,128)S(1)} collective-permute-done((f32[2,16,4,128]{3,2,1,0:T(4,128)S(1)}, f32[2,16,4,128]{3,2,1,0:T(4,128)S(1)}, u32[]{:S(2)}, u32[]{:S(2)}) %collective-permute-start.1) | collective-permute-done | bytes 65568 | tf_op jit(solution)/shard_map/ppermute | solution.py:37
  8.0 0.9 %fusion = f32[2,4,40,128]{3,2,1,0:T(8,128)S(1)} fusion(f32[2,16,4,128]{3,2,1,0:T(4,128)S(1)} %bitcast.239, f32[2,16,4,128]{3,2,1,0:T(4,128)S(1)} %bitcast.236, f32[1,16,32,128]{3,2,1,0:T(8,128)S(1)} %convert_bitcast_fusion, f32[1,16,32,128]{3,2,1,0:T(8,128)} %bitcast.233, pred[]{:T(512)S(6)} %eq.11), kind=kLoop, calls=%fused_computation.5 | loop fusion | flops 286720 | bytes 819201 | tf_op jit(solution)/shard_map/jit(_where)/select_n | solution.py:30
  9.0 1.4 %collective-permute-done.2 = f32[2,4,40,128]{3,2,1,0:T(8,128)S(1)} collective-permute-done((f32[2,4,40,128]{3,2,1,0:T(8,128)S(1)}, f32[2,4,40,128]{3,2,1,0:T(8,128)S(1)}, u32[]{:S(2)}, u32[]{:S(2)}) %collective-permute-start.2) | collective-permute-done | bytes 163872 | tf_op jit(solution)/shard_map/ppermute | solution.py:30
  11.1 2.0 %collective-permute-start.3 = (f32[2,24,40,4]{2,1,3,0:T(8,128)S(1)}, f32[2,24,40,4]{2,1,3,0:T(8,128)S(1)}, u32[]{:S(2)}, u32[]{:S(2)}) collective-permute-start(f32[2,24,40,4]{2,1,3,0:T(8,128)S(1)} %copy.17), channel_id=1, source_target_pairs={{0,2},{2,0},{1,3},{3,1},{4,6},{6,4},{5,7},{7,5},{8,10},{10,8},{9,1... | collective-permute-start | bytes 92168 | tf_op jit(solution)/shard_map/ppermute | solution.py:30
  13.2 0.7 stack.42.bounds_ref
  13.9 2.4 %collective-permute-done.3 = f32[2,24,40,4]{2,1,3,0:T(8,128)S(1)} collective-permute-done((f32[2,24,40,4]{2,1,3,0:T(8,128)S(1)}, f32[2,24,40,4]{2,1,3,0:T(8,128)S(1)}, u32[]{:S(2)}, u32[]{:S(2)}) %collective-permute-start.3) | collective-permute-done | bytes 30752 | tf_op jit(solution)/shard_map/ppermute | solution.py:30
  16.2 0.4 copy.18
  16.7 1.7 %pad_maximum_fusion.raw_ref = f32[2,24,40,256]{3,2,1,0:T(8,128)} fusion(f32[2,24,40,4]{3,2,1,0:T(8,128)S(1)} %copy.18, f32[2,4,40,128]{3,2,1,0:T(8,128)S(1)} %collective-permute-done.2, f32[2,16,4,128]{3,2,1,0:T(4,128)S(1)} %bitcast.241, f32[1,16,32,128]{3,2,1,0:T(8,128)S(1)} %convert_bitcast_fusion, f32[1,16,32,128]{3,2,1,0:T(8,128)S(1)} %bitcast.235, ...), kind=kLoop, calls=%fused_computation | loop fusion | flops 3932160 | bytes 2817024 | tf_op jit(solution)/shard_map/concatenate | solution.py:49
  18.3 11.0 %shard_map.77 = f32[3,8,128]{2,1,0:T(8,128)} custom-call(f32[3,4]{1,0:T(4,128)} %table_ref.1, s32[6]{0:T(128)} %stack.42.bounds_ref, f32[2,24,40,256]{3,2,1,0:T(8,128)} %pad_maximum_fusion.raw_ref), custom_call_target="tpu_custom_call" | custom-call | tf_op jit(solution)/shard_map/pallas_call | solution.py:393
  29.4 0.7 slice.215
  30.8 1.3 %collective-permute-start.5 = (f32[5,2,1,4]{3,1,2,0:T(2,128)S(1)}, f32[5,2,1,4]{3,1,2,0:T(2,128)S(1)}, u32[]{:S(2)}, u32[]{:S(2)}) collective-permute-start(f32[5,2,1,4]{3,1,2,0:T(2,128)S(1)} %constant_dynamic-update-slice_fusion), channel_id=1, source_target_pairs={{4,0},{8,4},{12,8},{5,1},{9,5},{13,9},{6,2},{10,6},{14,10},{7,3},{... | collective-permute-start | bytes 488 | tf_op jit(solution)/shard_map/ppermute | solution.py:465
  32.1 7.4 %collective-permute-start.4 = (f32[5,2,1,4]{3,1,2,0:T(2,128)S(1)}, f32[5,2,1,4]{3,1,2,0:T(2,128)S(1)}, u32[]{:S(2)}, u32[]{:S(2)}) collective-permute-start(f32[5,2,1,4]{3,1,2,0:T(2,128)S(1)} %constant_dynamic-update-slice_fusion), channel_id=1, source_target_pairs={{0,4},{4,8},{8,12},{1,5},{5,9},{9,13},{2,6},{6,10},{10,14},{3,7},{... | collective-permute-start | bytes 488 | tf_op jit(solution)/shard_map/ppermute | solution.py:464
  39.5 0.7 reshape.589
  40.4 1.3 %collective-permute-start.8 = (f32[5,1,1,4]{3,1,2,0:T(1,128)S(1)}, f32[5,1,1,4]{3,1,2,0:T(1,128)S(1)}, u32[]{:S(2)}, u32[]{:S(2)}) collective-permute-start(f32[5,1,1,4]{3,1,2,0:T(1,128)S(1)} %get-tuple-element.14), channel_id=1, source_target_pairs={{0,1},{2,3},{4,5},{6,7},{8,9},{10,11},{12,13},{14,15},{16,17},{18,... | collective-permute-start | bytes 248 | tf_op jit(solution)/shard_map/ppermute | solution.py:464
  41.7 1.3 %collective-permute-start.9 = (f32[5,1,1,4]{3,1,2,0:T(1,128)S(1)}, f32[5,1,1,4]{3,1,2,0:T(1,128)S(1)}, u32[]{:S(2)}, u32[]{:S(2)}) collective-permute-start(f32[5,1,1,4]{3,1,2,0:T(1,128)S(1)} %get-tuple-element.15), channel_id=1, source_target_pairs={{1,0},{3,2},{5,4},{7,6},{9,8},{11,10},{13,12},{15,14},{17,16},{19,... | collective-permute-start | bytes 248 | tf_op jit(solution)/shard_map/ppermute | solution.py:465
  43.0 3.4 %collective-permute-start.6 = (f32[5,2,1,1]{3,1,2,0:T(2,128)S(1)}, f32[5,2,1,1]{3,1,2,0:T(2,128)S(1)}, u32[]{:S(2)}, u32[]{:S(2)}) collective-permute-start(f32[5,2,1,1]{3,1,2,0:T(2,128)S(1)} %get-tuple-element.16), channel_id=1, source_target_pairs={{0,2},{1,3},{4,6},{5,7},{8,10},{9,11},{12,14},{13,15},{16,18},{17,... | collective-permute-start | bytes 128 | tf_op jit(solution)/shard_map/ppermute | solution.py:464
  46.4 1.3 %collective-permute-done.6 = f32[5,2,1,1]{3,1,2,0:T(2,128)S(1)} collective-permute-done((f32[5,2,1,1]{3,1,2,0:T(2,128)S(1)}, f32[5,2,1,1]{3,1,2,0:T(2,128)S(1)}, u32[]{:S(2)}, u32[]{:S(2)}) %collective-permute-start.6) | collective-permute-done | bytes 72 | tf_op jit(solution)/shard_map/ppermute | solution.py:464
  47.7 1.3 %collective-permute-start.7 = (f32[5,2,1,1]{3,1,2,0:T(2,128)S(1)}, f32[5,2,1,1]{3,1,2,0:T(2,128)S(1)}, u32[]{:S(2)}, u32[]{:S(2)}) collective-permute-start(f32[5,2,1,1]{3,1,2,0:T(2,128)S(1)} %get-tuple-element.17), channel_id=1, source_target_pairs={{2,0},{3,1},{6,4},{7,5},{10,8},{11,9},{14,12},{15,13},{18,16},{19,... | collective-permute-start | bytes 128 | tf_op jit(solution)/shard_map/ppermute | solution.py:465
  49.0 4.2 %collective-permute-done.7 = f32[5,2,1,1]{3,1,2,0:T(2,128)S(1)} collective-permute-done((f32[5,2,1,1]{3,1,2,0:T(2,128)S(1)}, f32[5,2,1,1]{3,1,2,0:T(2,128)S(1)}, u32[]{:S(2)}, u32[]{:S(2)}) %collective-permute-start.7) | collective-permute-done | bytes 72 | tf_op jit(solution)/shard_map/ppermute | solution.py:465
  53.5 1.3 %collective-permute-start.11 = (f32[2,1,4]{2,0,1:T(2,128)S(1)}, f32[2,1,4]{2,0,1:T(2,128)S(1)}, u32[]{:S(2)}, u32[]{:S(2)}) collective-permute-start(f32[2,1,4]{2,0,1:T(2,128)S(1)} %fusion.4), channel_id=1, source_target_pairs={{4,0},{8,4},{12,8},{5,1},{9,5},{13,9},{6,2},{10,6},{14,10},{7,3},{... | collective-permute-start | bytes 104 | tf_op jit(solution)/shard_map/ppermute | solution.py:465
  54.8 4.6 %collective-permute-start.10 = (f32[2,1,4]{2,0,1:T(2,128)S(1)}, f32[2,1,4]{2,0,1:T(2,128)S(1)}, u32[]{:S(2)}, u32[]{:S(2)}) collective-permute-start(f32[2,1,4]{2,0,1:T(2,128)S(1)} %fusion.4), channel_id=1, source_target_pairs={{0,4},{4,8},{8,12},{1,5},{5,9},{9,13},{2,6},{6,10},{10,14},{3,7},{... | collective-permute-start | bytes 104 | tf_op jit(solution)/shard_map/ppermute | solution.py:464
  59.4 1.3 %collective-permute-start.14 = (f32[1,1,4]{2,0,1:T(1,128)S(1)}, f32[1,1,4]{2,0,1:T(1,128)S(1)}, u32[]{:S(2)}, u32[]{:S(2)}) collective-permute-start(f32[1,1,4]{2,0,1:T(1,128)S(1)} %get-tuple-element.23), channel_id=1, source_target_pairs={{0,1},{2,3},{4,5},{6,7},{8,9},{10,11},{12,13},{14,15},{16,17},{18,... | collective-permute-start | bytes 56 | tf_op jit(solution)/shard_map/ppermute | solution.py:464
  60.7 1.3 %collective-permute-start.15 = (f32[1,1,4]{2,0,1:T(1,128)S(1)}, f32[1,1,4]{2,0,1:T(1,128)S(1)}, u32[]{:S(2)}, u32[]{:S(2)}) collective-permute-start(f32[1,1,4]{2,0,1:T(1,128)S(1)} %get-tuple-element.24), channel_id=1, source_target_pairs={{1,0},{3,2},{5,4},{7,6},{9,8},{11,10},{13,12},{15,14},{17,16},{19,... | collective-permute-start | bytes 56 | tf_op jit(solution)/shard_map/ppermute | solution.py:465
  62.0 1.3 %collective-permute-start.13 = (f32[2,1,1]{2,0,1:T(2,128)S(1)}, f32[2,1,1]{2,0,1:T(2,128)S(1)}, u32[]{:S(2)}, u32[]{:S(2)}) collective-permute-start(f32[2,1,1]{2,0,1:T(2,128)S(1)} %get-tuple-element.27), channel_id=1, source_target_pairs={{2,0},{3,1},{6,4},{7,5},{10,8},{11,9},{14,12},{15,13},{18,16},{19,... | collective-permute-start | bytes 32 | tf_op jit(solution)/shard_map/ppermute | solution.py:465
  63.3 4.2 %collective-permute-done.13 = f32[2,1,1]{2,0,1:T(2,128)S(1)} collective-permute-done((f32[2,1,1]{2,0,1:T(2,128)S(1)}, f32[2,1,1]{2,0,1:T(2,128)S(1)}, u32[]{:S(2)}, u32[]{:S(2)}) %collective-permute-start.13) | collective-permute-done | bytes 40 | tf_op jit(solution)/shard_map/ppermute | solution.py:465
  67.4 1.6 %collective-permute-start.12 = (f32[2,1,1]{2,0,1:T(2,128)S(1)}, f32[2,1,1]{2,0,1:T(2,128)S(1)}, u32[]{:S(2)}, u32[]{:S(2)}) collective-permute-start(f32[2,1,1]{2,0,1:T(2,128)S(1)} %get-tuple-element.28), channel_id=1, source_target_pairs={{0,2},{1,3},{4,6},{5,7},{8,10},{9,11},{12,14},{13,15},{16,18},{17,... | collective-permute-start | bytes 32 | tf_op jit(solution)/shard_map/ppermute | solution.py:464
  69.1 1.3 %collective-permute-done.12 = f32[2,1,1]{2,0,1:T(2,128)S(1)} collective-permute-done((f32[2,1,1]{2,0,1:T(2,128)S(1)}, f32[2,1,1]{2,0,1:T(2,128)S(1)}, u32[]{:S(2)}, u32[]{:S(2)}) %collective-permute-start.12) | collective-permute-done | bytes 40 | tf_op jit(solution)/shard_map/ppermute | solution.py:464
  70.4 0.7 fusion.23
  (48 shorter events, 2.2 us)
Async XLA Ops:
  0.6 9.7 %copy-start = (f32[16,32,128]{2,1,0:T(8,128)S(1)}, f32[16,32,128]{2,1,0:T(8,128)}, u32[]{:S(2)}) copy-start(f32[16,32,128]{2,1,0:T(8,128)} %param.6) | copy-start | bytes 786436
  2.6 5.3 %collective-permute-start.1 = (f32[2,16,4,128]{3,2,1,0:T(4,128)S(1)}, f32[2,16,4,128]{3,2,1,0:T(4,128)S(1)}, u32[]{:S(2)}, u32[]{:S(2)}) collective-permute-start(f32[2,16,4,128]{3,2,1,0:T(4,128)S(1)} %bitcast.244), channel_id=1, source_target_pairs={{0,4},{4,0},{8,12},{12,8},{1,5},{5,1},{9,13},{13,9},{2,6},{6,2},{1... | collective-permute-start | bytes 196616 | tf_op jit(solution)/shard_map/ppermute | solution.py:37
  5.7 2.2 %collective-permute-start = (f32[2,16,4,128]{3,2,1,0:T(4,128)S(1)}, f32[2,16,4,128]{3,2,1,0:T(4,128)S(1)}, u32[]{:S(2)}, u32[]{:S(2)}) collective-permute-start(f32[2,16,4,128]{3,2,1,0:T(4,128)S(1)} %get-tuple-element.9), channel_id=1, source_target_pairs={{4,8},{8,4},{5,9},{9,5},{6,10},{10,6},{7,11},{11,7},{20,24},{24,20... | collective-permute-start | bytes 196616 | tf_op jit(solution)/shard_map/ppermute | solution.py:38
  8.9 1.5 %collective-permute-start.2 = (f32[2,4,40,128]{3,2,1,0:T(8,128)S(1)}, f32[2,4,40,128]{3,2,1,0:T(8,128)S(1)}, u32[]{:S(2)}, u32[]{:S(2)}) collective-permute-start(f32[2,4,40,128]{3,2,1,0:T(8,128)S(1)} %fusion), channel_id=1, source_target_pairs={{0,1},{1,0},{2,3},{3,2},{4,5},{5,4},{6,7},{7,6},{8,9},{9,8},{10,11... | collective-permute-start | bytes 491528 | tf_op jit(solution)/shard_map/ppermute | solution.py:30
  11.1 5.1 %collective-permute-start.3 = (f32[2,24,40,4]{2,1,3,0:T(8,128)S(1)}, f32[2,24,40,4]{2,1,3,0:T(8,128)S(1)}, u32[]{:S(2)}, u32[]{:S(2)}) collective-permute-start(f32[2,24,40,4]{2,1,3,0:T(8,128)S(1)} %copy.17), channel_id=1, source_target_pairs={{0,2},{2,0},{1,3},{3,1},{4,6},{6,4},{5,7},{7,5},{8,10},{10,8},{9,1... | collective-permute-start | bytes 92168 | tf_op jit(solution)/shard_map/ppermute | solution.py:30
  18.3 12.3 %copy-start.1 = (f32[2,1,4]{2,1,0:T(1,128)S(1)}, f32[2,1,4]{2,1,0:T(1,128)}, u32[]{:S(2)}) copy-start(f32[2,1,4]{2,1,0:T(1,128)} %param.9) | copy-start | bytes 100
  18.3 34.9 %copy-start.2 = (f32[2,1,4]{2,1,0:T(1,128)S(1)}, f32[2,1,4]{2,1,0:T(1,128)}, u32[]{:S(2)}) copy-start(f32[2,1,4]{2,1,0:T(1,128)} %param.10) | copy-start | bytes 100
  18.3 34.9 %copy-start.3 = (f32[2,1,4]{2,1,0:T(1,128)S(1)}, f32[2,1,4]{2,1,0:T(1,128)}, u32[]{:S(2)}) copy-start(f32[2,1,4]{2,1,0:T(1,128)} %param.11) | copy-start | bytes 100
  30.8 22.4 %collective-permute-start.5 = (f32[5,2,1,4]{3,1,2,0:T(2,128)S(1)}, f32[5,2,1,4]{3,1,2,0:T(2,128)S(1)}, u32[]{:S(2)}, u32[]{:S(2)}) collective-permute-start(f32[5,2,1,4]{3,1,2,0:T(2,128)S(1)} %constant_dynamic-update-slice_fusion), channel_id=1, source_target_pairs={{4,0},{8,4},{12,8},{5,1},{9,5},{13,9},{6,2},{10,6},{14,10},{7,3},{... | collective-permute-start | bytes 488 | tf_op jit(solution)/shard_map/ppermute | solution.py:465
  32.1 21.1 %collective-permute-start.4 = (f32[5,2,1,4]{3,1,2,0:T(2,128)S(1)}, f32[5,2,1,4]{3,1,2,0:T(2,128)S(1)}, u32[]{:S(2)}, u32[]{:S(2)}) collective-permute-start(f32[5,2,1,4]{3,1,2,0:T(2,128)S(1)} %constant_dynamic-update-slice_fusion), channel_id=1, source_target_pairs={{0,4},{4,8},{8,12},{1,5},{5,9},{9,13},{2,6},{6,10},{10,14},{3,7},{... | collective-permute-start | bytes 488 | tf_op jit(solution)/shard_map/ppermute | solution.py:464
  40.4 12.8 %collective-permute-start.8 = (f32[5,1,1,4]{3,1,2,0:T(1,128)S(1)}, f32[5,1,1,4]{3,1,2,0:T(1,128)S(1)}, u32[]{:S(2)}, u32[]{:S(2)}) collective-permute-start(f32[5,1,1,4]{3,1,2,0:T(1,128)S(1)} %get-tuple-element.14), channel_id=1, source_target_pairs={{0,1},{2,3},{4,5},{6,7},{8,9},{10,11},{12,13},{14,15},{16,17},{18,... | collective-permute-start | bytes 248 | tf_op jit(solution)/shard_map/ppermute | solution.py:464
  41.7 11.5 %collective-permute-start.9 = (f32[5,1,1,4]{3,1,2,0:T(1,128)S(1)}, f32[5,1,1,4]{3,1,2,0:T(1,128)S(1)}, u32[]{:S(2)}, u32[]{:S(2)}) collective-permute-start(f32[5,1,1,4]{3,1,2,0:T(1,128)S(1)} %get-tuple-element.15), channel_id=1, source_target_pairs={{1,0},{3,2},{5,4},{7,6},{9,8},{11,10},{13,12},{15,14},{17,16},{19,... | collective-permute-start | bytes 248 | tf_op jit(solution)/shard_map/ppermute | solution.py:465
  43.0 4.7 %collective-permute-start.6 = (f32[5,2,1,1]{3,1,2,0:T(2,128)S(1)}, f32[5,2,1,1]{3,1,2,0:T(2,128)S(1)}, u32[]{:S(2)}, u32[]{:S(2)}) collective-permute-start(f32[5,2,1,1]{3,1,2,0:T(2,128)S(1)} %get-tuple-element.16), channel_id=1, source_target_pairs={{0,2},{1,3},{4,6},{5,7},{8,10},{9,11},{12,14},{13,15},{16,18},{17,... | collective-permute-start | bytes 128 | tf_op jit(solution)/shard_map/ppermute | solution.py:464
  47.7 5.5 %collective-permute-start.7 = (f32[5,2,1,1]{3,1,2,0:T(2,128)S(1)}, f32[5,2,1,1]{3,1,2,0:T(2,128)S(1)}, u32[]{:S(2)}, u32[]{:S(2)}) collective-permute-start(f32[5,2,1,1]{3,1,2,0:T(2,128)S(1)} %get-tuple-element.17), channel_id=1, source_target_pairs={{2,0},{3,1},{6,4},{7,5},{10,8},{11,9},{14,12},{15,13},{18,16},{19,... | collective-permute-start | bytes 128 | tf_op jit(solution)/shard_map/ppermute | solution.py:465
  53.5 16.9 %collective-permute-start.11 = (f32[2,1,4]{2,0,1:T(2,128)S(1)}, f32[2,1,4]{2,0,1:T(2,128)S(1)}, u32[]{:S(2)}, u32[]{:S(2)}) collective-permute-start(f32[2,1,4]{2,0,1:T(2,128)S(1)} %fusion.4), channel_id=1, source_target_pairs={{4,0},{8,4},{12,8},{5,1},{9,5},{13,9},{6,2},{10,6},{14,10},{7,3},{... | collective-permute-start | bytes 104 | tf_op jit(solution)/shard_map/ppermute | solution.py:465
  54.8 15.6 %collective-permute-start.10 = (f32[2,1,4]{2,0,1:T(2,128)S(1)}, f32[2,1,4]{2,0,1:T(2,128)S(1)}, u32[]{:S(2)}, u32[]{:S(2)}) collective-permute-start(f32[2,1,4]{2,0,1:T(2,128)S(1)} %fusion.4), channel_id=1, source_target_pairs={{0,4},{4,8},{8,12},{1,5},{5,9},{9,13},{2,6},{6,10},{10,14},{3,7},{... | collective-permute-start | bytes 104 | tf_op jit(solution)/shard_map/ppermute | solution.py:464
  59.4 11.0 %collective-permute-start.14 = (f32[1,1,4]{2,0,1:T(1,128)S(1)}, f32[1,1,4]{2,0,1:T(1,128)S(1)}, u32[]{:S(2)}, u32[]{:S(2)}) collective-permute-start(f32[1,1,4]{2,0,1:T(1,128)S(1)} %get-tuple-element.23), channel_id=1, source_target_pairs={{0,1},{2,3},{4,5},{6,7},{8,9},{10,11},{12,13},{14,15},{16,17},{18,... | collective-permute-start | bytes 56 | tf_op jit(solution)/shard_map/ppermute | solution.py:464
  60.7 9.7 %collective-permute-start.15 = (f32[1,1,4]{2,0,1:T(1,128)S(1)}, f32[1,1,4]{2,0,1:T(1,128)S(1)}, u32[]{:S(2)}, u32[]{:S(2)}) collective-permute-start(f32[1,1,4]{2,0,1:T(1,128)S(1)} %get-tuple-element.24), channel_id=1, source_target_pairs={{1,0},{3,2},{5,4},{7,6},{9,8},{11,10},{13,12},{15,14},{17,16},{19,... | collective-permute-start | bytes 56 | tf_op jit(solution)/shard_map/ppermute | solution.py:465
  62.0 5.5 %collective-permute-start.13 = (f32[2,1,1]{2,0,1:T(2,128)S(1)}, f32[2,1,1]{2,0,1:T(2,128)S(1)}, u32[]{:S(2)}, u32[]{:S(2)}) collective-permute-start(f32[2,1,1]{2,0,1:T(2,128)S(1)} %get-tuple-element.27), channel_id=1, source_target_pairs={{2,0},{3,1},{6,4},{7,5},{10,8},{11,9},{14,12},{15,13},{18,16},{19,... | collective-permute-start | bytes 32 | tf_op jit(solution)/shard_map/ppermute | solution.py:465
  67.4 2.9 %collective-permute-start.12 = (f32[2,1,1]{2,0,1:T(2,128)S(1)}, f32[2,1,1]{2,0,1:T(2,128)S(1)}, u32[]{:S(2)}, u32[]{:S(2)}) collective-permute-start(f32[2,1,1]{2,0,1:T(2,128)S(1)} %get-tuple-element.28), channel_id=1, source_target_pairs={{0,2},{1,3},{4,6},{5,7},{8,10},{9,11},{12,14},{13,15},{16,18},{17,... | collective-permute-start | bytes 32 | tf_op jit(solution)/shard_map/ppermute | solution.py:464

commit v20 on v17

--- a/solution.py
+++ b/solution.py
@@ -25,19 +25,26 @@
         ends = count - 1
         head = lax.slice_in_dim(cells, 0, width, axis=dim)
         tail = lax.slice_in_dim(cells, cells.shape[dim] - width, cells.shape[dim], axis=dim)
+        both = jnp.concatenate([tail, head], axis=dim)
+
+        def lower_half(values):
+            return lax.slice_in_dim(values, 0, width, axis=dim)
+
+        def upper_half(values):
+            return lax.slice_in_dim(values, width, 2 * width, axis=dim)
+
         if count == 2:
-            lower_side = lax.axis_index(axis) == 0
-            got = lax.ppermute(jnp.where(lower_side, tail, head), axis, [(0, 1), (1, 0)])
-            below = got
-            above = got
+            got = lax.ppermute(both, axis, [(0, 1), (1, 0)])
+            below = lower_half(got)
+            above = upper_half(got)
         elif count % 2 == 0:
             even = lax.axis_index(axis) % 2 == 0
             first = [(i, i ^ 1) for i in range(count)]
             second = [(i, i + 1 if i % 2 else i - 1) for i in range(1, count - 1)]
-            got_first = lax.ppermute(jnp.where(even, tail, head), axis, first)
-            got_second = lax.ppermute(jnp.where(even, head, tail), axis, second)
-            below = jnp.where(even, got_second, got_first)
-            above = jnp.where(even, got_first, got_second)
+            got_first = lax.ppermute(both, axis, first)
+            got_second = lax.ppermute(both, axis, second)
+            below = jnp.where(even, lower_half(got_second), lower_half(got_first))
+            above = jnp.where(even, upper_half(got_first), upper_half(got_second))
         else:
             below = lax.ppermute(tail, axis, [(i, (i + 1) % count) for i in range(ends)])
             above = lax.ppermute(head, axis, [((i + 1) % count, i) for i in range(ends)])

time: 49 us -> 53.1 us (1.084)
  waiting for transfers between devices: 11 us -> 17.1 us
  starting transfers between devices: 16.1 us -> 13.3 us
  local copies, waits for them, and re-layouts: 3.46 us -> 4.59 us
    ppermute x4, starting transfers between devices: 10.3 us -> 5.14 us  [doubling_gather(): got = lax.ppermute(values, axis, [(i, i ^ step) for i in range(count)])]
    ppermute x4, waiting for transfers between devices: 5.35 us -> 9.63 us  [the longest x2 6.42 us: extended(): got = lax.ppermute(both, axis, [(0, 1), (1, 0)])]
    ppermute x4, starting transfers between devices: 5.81 us -> 8.2 us  [the longest x1 5.9 us: extended(): got_first = lax.ppermute(both, axis, first)]
    select_n x5 -> x1, other arithmetic: 2.17 us -> 0.03 us  [extended(): below = jnp.where(even, lower_half(got_second), lower_half(got_first))]
    concatenate x0 -> x3, other arithmetic: none -> 1.89 us  [extended(): both = jnp.concatenate([tail, head], axis=dim)]
    ppermute x4, waiting for transfers between devices: 5.68 us -> 7.48 us  [doubling_gather(): got = lax.ppermute(values, axis, [(i, i ^ step) for i in range(count)])]
    slice x0 -> x5, local copies, waits for them, and re-layouts: none -> 1.15 us  [the longest x2 0.7 us: extended(): lax.slice_in_dim(cells, cells.shape[dim] - width, cells.shape[dim], axis=...]
    unnamed x13 -> x15, local copies, waits for them, and re-layouts: 0.05 us -> 0.88 us
  transfers between devices with their start and end apart: 8 -> 8, of which waited for: 7 -> 7; matrix products, arithmetic and copies ran while one was open for 3% -> 2% of each run, Pallas kernels for 0% -> 0%
where the time goes in v20:
time: 53.1 us; the launch traced here: 52.8 us
  waiting for transfers between devices  17.1 us (32%)
  starting transfers between devices  13.3 us (25%)
  Pallas kernels  11 us (21%)
  other arithmetic  5.93 us (11%)
  local copies, waits for them, and re-layouts  4.59 us (9%)
  between operations  0.81 us (2%)
    pallas_call x1, Pallas kernels, upscale_windows(): pl.pallas_call(kernel, grid=(packs,), in_specs=[pl.BlockSpec(memory_space...  11 us
    ppermute x4, waiting for transfers between devices, doubling_gather(): got = lax.ppermute(values, axis, [(i, i ^ step) for i in range(count)])  7.48 us
    ppermute x2, waiting for transfers between devices, extended(): got = lax.ppermute(both, axis, [(0, 1), (1, 0)])  6.42 us
    ppermute x1, starting transfers between devices, extended(): got_first = lax.ppermute(both, axis, first)  5.9 us
    ppermute x4, starting transfers between devices, doubling_gather(): got = lax.ppermute(values, axis, [(i, i ^ step) for i in range(count)])  5.14 us
    ppermute x1, waiting for transfers between devices, extended(): got_first = lax.ppermute(both, axis, first)  3.21 us
    concatenate x3, other arithmetic, extended(): both = jnp.concatenate([tail, head], axis=dim)  1.89 us
    concatenate x2, other arithmetic, extended(): cells = jnp.concatenate(parts, axis=dim)  1.78 us
  transfers between devices with their start and end apart: 8, of which 7 were waited for; matrix products, arithmetic and copies ran while one was open for 2% of the time, Pallas kernels for 0%

profile of v20, /device:TPU:0, one launch (start us, length us, event | category | flops | bytes accessed | tf_op | source)
XLA Modules:
  0.0 52.8 jit_solution(11060423445074142189)
XLA Ops:
  0.6 1.0 %convert_bitcast_fusion = f32[1,16,32,128]{3,2,1,0:T(8,128)S(1)} fusion(s32[16,32,128]{2,1,0:T(8,128)} %param.7), kind=kLoop, calls=%fused_computation.9 | loop fusion | flops 65536 | bytes 524288 | tf_op jit(solution)/shard_map/stack | solution.py:458
  1.7 0.9 %fusion.1 = f32[2,16,8,128]{3,2,1,0:T(8,128)S(1)} fusion(f32[1,16,32,128]{3,2,1,0:T(8,128)S(1)} %convert_bitcast_fusion, f32[1,16,32,128]{3,2,1,0:T(8,128)} %bitcast.50), kind=kLoop, calls=%fused_computation.12 | loop fusion | flops 98304 | bytes 655360 | tf_op jit(solution)/shard_map/concatenate | solution.py:28
  2.6 0.7 %collective-permute-start = (f32[2,16,8,128]{3,2,1,0:T(8,128)S(1)}, f32[2,16,8,128]{3,2,1,0:T(8,128)S(1)}, u32[]{:S(2)}, u32[]{:S(2)}) collective-permute-start(f32[2,16,8,128]{3,2,1,0:T(8,128)S(1)} %fusion.1), channel_id=1, source_target_pairs={{4,8},{8,4},{5,9},{9,5},{6,10},{10,6},{7,11},{11,7},{20,24},{24,20... | collective-permute-start | bytes 393224 | tf_op jit(solution)/shard_map/ppermute | solution.py:45
  3.2 5.9 %collective-permute-start.1 = (f32[2,16,8,128]{3,2,1,0:T(8,128)S(1)}, f32[2,16,8,128]{3,2,1,0:T(8,128)S(1)}, u32[]{:S(2)}, u32[]{:S(2)}) collective-permute-start(f32[2,16,8,128]{3,2,1,0:T(8,128)S(1)} %fusion.1), channel_id=1, source_target_pairs={{0,4},{4,0},{8,12},{12,8},{1,5},{5,1},{9,13},{13,9},{2,6},{6,2},{1... | collective-permute-start | bytes 393224 | tf_op jit(solution)/shard_map/ppermute | solution.py:44
  9.1 3.2 %collective-permute-done.1 = f32[2,16,8,128]{3,2,1,0:T(8,128)S(1)} collective-permute-done((f32[2,16,8,128]{3,2,1,0:T(8,128)S(1)}, f32[2,16,8,128]{3,2,1,0:T(8,128)S(1)}, u32[]{:S(2)}, u32[]{:S(2)}) %collective-permute-start.1) | collective-permute-done | bytes 131104 | tf_op jit(solution)/shard_map/ppermute | solution.py:44
  12.4 0.9 %fusion = f32[2,8,40,128]{3,2,1,0:T(8,128)S(1)} fusion(f32[2,16,4,128]{3,2,1,0:T(4,128)S(1)} %get-tuple-element.19, f32[2,16,4,128]{3,2,1,0:T(4,128)S(1)} %get-tuple-element.18, f32[1,16,32,128]{3,2,1,0:T(8,128)S(1)} %convert_bitcast_fusion, f32[1,16,32,128]{3,2,1,0:T(8,128)} %bitcast.51), kind=kLoop, calls=%fused_computation.3 | loop fusion | flops 573440 | bytes 983040 | tf_op jit(solution)/shard_map/concatenate | solution.py:28
  13.4 1.6 %collective-permute-done.2 = f32[2,8,40,128]{3,2,1,0:T(8,128)S(1)} collective-permute-done((f32[2,8,40,128]{3,2,1,0:T(8,128)S(1)}, f32[2,8,40,128]{3,2,1,0:T(8,128)S(1)}, u32[]{:S(2)}, u32[]{:S(2)}) %collective-permute-start.2) | collective-permute-done | bytes 327712 | tf_op jit(solution)/shard_map/ppermute | solution.py:37
  15.1 0.1 pad_maximum_fusion.1
  15.2 0.3 fusion.42
  15.5 0.4 copy.18
  15.9 0.4 copy.19
  16.3 1.6 %collective-permute-start.3 = (f32[2,24,40,8]{2,3,1,0:T(8,128)S(1)}, f32[2,24,40,8]{2,3,1,0:T(8,128)S(1)}, u32[]{:S(2)}, u32[]{:S(2)}) collective-permute-start(f32[2,24,40,8]{2,3,1,0:T(8,128)S(1)} %pad_maximum_fusion.8), channel_id=1, source_target_pairs={{0,2},{2,0},{1,3},{3,1},{4,6},{6,4},{5,7},{7,5},{8,10},{10,8},{9,1... | collective-permute-start | bytes 184328 | tf_op jit(solution)/shard_map/ppermute | solution.py:37
  18.0 0.6 %stack.48.bounds_ref = s32[6]{0:T(128)} concatenate(s32[1]{0:T(128)} %bitcast, s32[1]{0:T(128)} %bitcast.1, s32[1]{0:T(128)} %bitcast.2, s32[1]{0:T(128)} %bitcast.3, s32[1]{0:T(128)} %bitcast.4, s32[1]{0:T(128)} %bitcast.5), dimensions={0} | concatenate | bytes 48 | tf_op jit(solution)/shard_map/stack | solution.py:464
  18.5 4.8 %collective-permute-done.3 = f32[2,24,40,8]{2,3,1,0:T(8,128)S(1)} collective-permute-done((f32[2,24,40,8]{2,3,1,0:T(8,128)S(1)}, f32[2,24,40,8]{2,3,1,0:T(8,128)S(1)}, u32[]{:S(2)}, u32[]{:S(2)}) %collective-permute-start.3) | collective-permute-done | bytes 61472 | tf_op jit(solution)/shard_map/ppermute | solution.py:37
  23.4 0.4 copy.36
  23.8 0.4 copy.37
  24.2 1.7 %pad_maximum_fusion.raw_ref = f32[2,24,40,256]{3,2,1,0:T(8,128)} fusion(f32[2,24,40,4]{3,2,1,0:T(8,128)S(1)} %copy.37, f32[2,24,40,4]{3,2,1,0:T(8,128)S(1)} %copy.36, f32[2,4,40,128]{3,2,1,0:T(8,128)S(1)} %get-tuple-element.17, f32[2,16,4,128]{3,2,1,0:T(4,128)S(1)} %get-tuple-element.19, f32[1,16,32,128]{3,2,1,0:T(8,128)S(1)} %convert_bitcast_fusion, ...), kind=kLoop, calls=%fused_computation | loop fusion | flops 3932160 | bytes 3011584 | tf_op jit(solution)/shard_map/concatenate | solution.py:56
  25.9 11.0 %shard_map.77 = f32[3,8,128]{2,1,0:T(8,128)} custom-call(f32[3,4]{1,0:T(4,128)} %table_ref.1, s32[6]{0:T(128)} %stack.48.bounds_ref, f32[2,24,40,256]{3,2,1,0:T(8,128)} %pad_maximum_fusion.raw_ref), custom_call_target="tpu_custom_call" | custom-call | tf_op jit(solution)/shard_map/pallas_call | solution.py:350
  36.9 0.7 %slice.279 = f32[3,3,120]{2,1,0:T(4,128)S(1)} slice(f32[3,8,128]{2,1,0:T(8,128)} %shard_map.77), slice={[0:3], [0:3], [0:120]} | slice | bytes 8640 | tf_op jit(solution)/shard_map/slice | solution.py:361
  37.6 0.1 reshape.68
  37.7 0.1 reduce_sum.9
  38.3 1.6 %collective-permute-start.4 = (f32[6,2,1,4]{3,1,2,0:T(2,128)S(1)}, f32[6,2,1,4]{3,1,2,0:T(2,128)S(1)}, u32[]{:S(2)}, u32[]{:S(2)}) collective-permute-start(f32[6,2,1,4]{3,1,2,0:T(2,128)S(1)} %constant_dynamic-update-slice_fusion), channel_id=1, source_target_pairs={{0,2},{2,0},{1,3},{3,1},{4,6},{6,4},{5,7},{7,5},{8,10},{10,8},{9,1... | collective-permute-start | bytes 584 | tf_op jit(solution)/shard_map/ppermute | solution.py:67
  39.8 2.1 %collective-permute-done.4 = f32[6,2,1,4]{3,1,2,0:T(2,128)S(1)} collective-permute-done((f32[6,2,1,4]{3,1,2,0:T(2,128)S(1)}, f32[6,2,1,4]{3,1,2,0:T(2,128)S(1)}, u32[]{:S(2)}, u32[]{:S(2)}) %collective-permute-start.4) | collective-permute-done | bytes 224 | tf_op jit(solution)/shard_map/ppermute | solution.py:67
  42.0 1.8 %collective-permute-start.5 = (f32[6,2,1,8]{3,1,2,0:T(2,128)S(1)}, f32[6,2,1,8]{3,1,2,0:T(2,128)S(1)}, u32[]{:S(2)}, u32[]{:S(2)}) collective-permute-start(f32[6,2,1,8]{3,1,2,0:T(2,128)S(1)} %maximum_select_fusion.3), channel_id=1, source_target_pairs={{0,4},{4,0},{8,12},{12,8},{1,5},{5,1},{9,13},{13,9},{2,6},{6,2},{1... | collective-permute-start | bytes 1160 | tf_op jit(solution)/shard_map/ppermute | solution.py:67
  43.9 1.9 %collective-permute-done.5 = f32[6,2,1,8]{3,1,2,0:T(2,128)S(1)} collective-permute-done((f32[6,2,1,8]{3,1,2,0:T(2,128)S(1)}, f32[6,2,1,8]{3,1,2,0:T(2,128)S(1)}, u32[]{:S(2)}, u32[]{:S(2)}) %collective-permute-start.5) | collective-permute-done | bytes 416 | tf_op jit(solution)/shard_map/ppermute | solution.py:67
  45.7 1.7 %collective-permute-start.6 = (f32[6,2,2,8]{3,1,2,0:T(2,128)S(1)}, f32[6,2,2,8]{3,1,2,0:T(2,128)S(1)}, u32[]{:S(2)}, u32[]{:S(2)}) collective-permute-start(f32[6,2,2,8]{3,1,2,0:T(2,128)S(1)} %maximum_select_fusion.2), channel_id=1, source_target_pairs={{0,8},{4,12},{8,0},{12,4},{1,9},{5,13},{9,1},{13,5},{2,10},{6,14},... | collective-permute-start | bytes 2312 | tf_op jit(solution)/shard_map/ppermute | solution.py:67
  47.4 3.0 %collective-permute-done.6 = f32[6,2,2,8]{3,1,2,0:T(2,128)S(1)} collective-permute-done((f32[6,2,2,8]{3,1,2,0:T(2,128)S(1)}, f32[6,2,2,8]{3,1,2,0:T(2,128)S(1)}, u32[]{:S(2)}, u32[]{:S(2)}) %collective-permute-start.6) | collective-permute-done | bytes 800 | tf_op jit(solution)/shard_map/ppermute | solution.py:67
  50.5 0.7 %reshape.70 = f32[3,2,1,4]{3,1,0,2:T(2,128)} reshape(f32[3,8]{1,0:T(4,128)S(1)} %bitcast.55) | data formatting | bytes 192 | tf_op jit(solution)/shard_map/reshape | solution.py:363
  51.2 0.5 collective-permute-done.7
  51.8 0.1 fusion.12
  52.1 0.1 fusion.19
  52.2 0.7 %dynamic-slice_divide_fusion = f32[2,1,4]{2,0,1:T(2,128)} fusion(f32[4,4,8]{2,0,1:T(4,128)S(1)} %get-tuple-element.23, s32[]{:T(128)S(6)} %select_n.105, s32[]{:T(128)S(6)} %select_n.106, s32[]{:T(128)S(6)} %select_n.107, f32[4,4,8]{2,0,1:T(4,128)S(1)} %get-tuple-element.31, f32[4,4,8]{2,0,1:T(4,128)S(1)} %get-tuple-element.13, ...), kind=kLoop, calls=%fused_computation.89 | loop fusion | flops 80 | bytes 396 | tf_op jit(solution)/shard_map/div | solution.py:384
  (38 shorter events, 1.1 us)
Async XLA Ops:
  0.6 14.4 %copy-start = (f32[16,32,128]{2,1,0:T(8,128)S(1)}, f32[16,32,128]{2,1,0:T(8,128)}, u32[]{:S(2)}) copy-start(f32[16,32,128]{2,1,0:T(8,128)} %param.6) | copy-start | bytes 786436
  2.6 6.6 %collective-permute-start = (f32[2,16,8,128]{3,2,1,0:T(8,128)S(1)}, f32[2,16,8,128]{3,2,1,0:T(8,128)S(1)}, u32[]{:S(2)}, u32[]{:S(2)}) collective-permute-start(f32[2,16,8,128]{3,2,1,0:T(8,128)S(1)} %fusion.1), channel_id=1, source_target_pairs={{4,8},{8,4},{5,9},{9,5},{6,10},{10,6},{7,11},{11,7},{20,24},{24,20... | collective-permute-start | bytes 393224 | tf_op jit(solution)/shard_map/ppermute | solution.py:45
  3.2 9.1 %collective-permute-start.1 = (f32[2,16,8,128]{3,2,1,0:T(8,128)S(1)}, f32[2,16,8,128]{3,2,1,0:T(8,128)S(1)}, u32[]{:S(2)}, u32[]{:S(2)}) collective-permute-start(f32[2,16,8,128]{3,2,1,0:T(8,128)S(1)} %fusion.1), channel_id=1, source_target_pairs={{0,4},{4,0},{8,12},{12,8},{1,5},{5,1},{9,13},{13,9},{2,6},{6,2},{1... | collective-permute-start | bytes 393224 | tf_op jit(solution)/shard_map/ppermute | solution.py:44
  13.3 1.7 %collective-permute-start.2 = (f32[2,8,40,128]{3,2,1,0:T(8,128)S(1)}, f32[2,8,40,128]{3,2,1,0:T(8,128)S(1)}, u32[]{:S(2)}, u32[]{:S(2)}) collective-permute-start(f32[2,8,40,128]{3,2,1,0:T(8,128)S(1)} %fusion), channel_id=1, source_target_pairs={{0,1},{1,0},{2,3},{3,2},{4,5},{5,4},{6,7},{7,6},{8,9},{9,8},{10,11... | collective-permute-start | bytes 983048 | tf_op jit(solution)/shard_map/ppermute | solution.py:37
  16.3 7.0 %collective-permute-start.3 = (f32[2,24,40,8]{2,3,1,0:T(8,128)S(1)}, f32[2,24,40,8]{2,3,1,0:T(8,128)S(1)}, u32[]{:S(2)}, u32[]{:S(2)}) collective-permute-start(f32[2,24,40,8]{2,3,1,0:T(8,128)S(1)} %pad_maximum_fusion.8), channel_id=1, source_target_pairs={{0,2},{2,0},{1,3},{3,1},{4,6},{6,4},{5,7},{7,5},{8,10},{10,8},{9,1... | collective-permute-start | bytes 184328 | tf_op jit(solution)/shard_map/ppermute | solution.py:37
  25.9 12.3 %copy-start.1 = (f32[2,1,4]{2,1,0:T(1,128)S(1)}, f32[2,1,4]{2,1,0:T(1,128)}, u32[]{:S(2)}) copy-start(f32[2,1,4]{2,1,0:T(1,128)} %param.9) | copy-start | bytes 100
  25.9 12.3 %copy-start.2 = (f32[2,1,4]{2,1,0:T(1,128)S(1)}, f32[2,1,4]{2,1,0:T(1,128)}, u32[]{:S(2)}) copy-start(f32[2,1,4]{2,1,0:T(1,128)} %param.10) | copy-start | bytes 100
  25.9 12.4 %copy-start.3 = (f32[2,1,4]{2,1,0:T(1,128)S(1)}, f32[2,1,4]{2,1,0:T(1,128)}, u32[]{:S(2)}) copy-start(f32[2,1,4]{2,1,0:T(1,128)} %param.11) | copy-start | bytes 100
  38.3 3.7 %collective-permute-start.4 = (f32[6,2,1,4]{3,1,2,0:T(2,128)S(1)}, f32[6,2,1,4]{3,1,2,0:T(2,128)S(1)}, u32[]{:S(2)}, u32[]{:S(2)}) collective-permute-start(f32[6,2,1,4]{3,1,2,0:T(2,128)S(1)} %constant_dynamic-update-slice_fusion), channel_id=1, source_target_pairs={{0,2},{2,0},{1,3},{3,1},{4,6},{6,4},{5,7},{7,5},{8,10},{10,8},{9,1... | collective-permute-start | bytes 584 | tf_op jit(solution)/shard_map/ppermute | solution.py:67
  42.0 3.7 %collective-permute-start.5 = (f32[6,2,1,8]{3,1,2,0:T(2,128)S(1)}, f32[6,2,1,8]{3,1,2,0:T(2,128)S(1)}, u32[]{:S(2)}, u32[]{:S(2)}) collective-permute-start(f32[6,2,1,8]{3,1,2,0:T(2,128)S(1)} %maximum_select_fusion.3), channel_id=1, source_target_pairs={{0,4},{4,0},{8,12},{12,8},{1,5},{5,1},{9,13},{13,9},{2,6},{6,2},{1... | collective-permute-start | bytes 1160 | tf_op jit(solution)/shard_map/ppermute | solution.py:67
  45.7 4.7 %collective-permute-start.6 = (f32[6,2,2,8]{3,1,2,0:T(2,128)S(1)}, f32[6,2,2,8]{3,1,2,0:T(2,128)S(1)}, u32[]{:S(2)}, u32[]{:S(2)}) collective-permute-start(f32[6,2,2,8]{3,1,2,0:T(2,128)S(1)} %maximum_select_fusion.2), channel_id=1, source_target_pairs={{0,8},{4,12},{8,0},{12,4},{1,9},{5,13},{9,1},{13,5},{2,10},{6,14},... | collective-permute-start | bytes 2312 | tf_op jit(solution)/shard_map/ppermute | solution.py:67
  50.4 1.3 %collective-permute-start.7 = (f32[6,2,4,8]{3,1,2,0:T(2,128)S(1)}, f32[6,2,4,8]{3,1,2,0:T(2,128)S(1)}, u32[]{:S(2)}, u32[]{:S(2)}) collective-permute-start(f32[6,2,4,8]{3,1,2,0:T(2,128)S(1)} %maximum_select_fusion.1), channel_id=1, source_target_pairs={{0,1},{1,0},{2,3},{3,2},{4,5},{5,4},{6,7},{7,6},{8,9},{9,8},{10,11... | collective-permute-start | bytes 4616 | tf_op jit(solution)/shard_map/ppermute | solution.py:67

commit v21 on v17

--- a/solution.py
+++ b/solution.py
@@ -467,8 +467,8 @@
     upscaled = upscale_windows(raw, facies_table, bounds, cols_len)
     coarse_z, coarse_x, coarse_y = pressure_old.shape
     bundle = jnp.stack([upscaled[0], upscaled[1], upscaled[2], pressure_old, accumulation, source])
-    every = doubling_gather(bundle, "gy", 3)
-    every = doubling_gather(every, "gx", 2)
+    every = doubling_gather(bundle, "gx", 2)
+    every = doubling_gather(every, "gy", 3)
     every = doubling_gather(every, "gz", 1)
     perm_pad = jnp.pad(every[:3], ((0, 0), (1, 1), (1, 1), (1, 1)))
     old_all = every[3]

time: 49 us -> 49.2 us (level)
  waiting for transfers between devices: 11 us -> 11.5 us
where the time goes in v21:
time: 49.2 us; the launch traced here: 48.9 us
  starting transfers between devices  15.9 us (32%)
  waiting for transfers between devices  11.5 us (23%)
  Pallas kernels  11 us (22%)
  other arithmetic  6.21 us (13%)
  local copies, waits for them, and re-layouts  3.46 us (7%)
  between operations  0.83 us (2%)
    pallas_call x1, Pallas kernels, upscale_windows(): pl.pallas_call(kernel, grid=(packs,), in_specs=[pl.BlockSpec(memory_space...  11 us
    ppermute x4, starting transfers between devices, doubling_gather(): got = lax.ppermute(values, axis, [(i, i ^ step) for i in range(count)])  10.1 us
    ppermute x4, waiting for transfers between devices, doubling_gather(): got = lax.ppermute(values, axis, [(i, i ^ step) for i in range(count)])  6.13 us
    ppermute x2, waiting for transfers between devices, extended(): lax.ppermute(jnp.where(lower_side, tail, head), axis, [(0, 1), (1, 0)])  3.77 us
    ppermute x1, starting transfers between devices, extended(): got_first = lax.ppermute(jnp.where(even, tail, head), axis, first)  3.09 us
    ppermute x2, starting transfers between devices, extended(): lax.ppermute(jnp.where(lower_side, tail, head), axis, [(0, 1), (1, 0)])  2.07 us
    concatenate x2, other arithmetic, extended(): cells = jnp.concatenate(parts, axis=dim)  1.78 us
    ppermute x1, waiting for transfers between devices, extended(): got_first = lax.ppermute(jnp.where(even, tail, head), axis, first)  1.58 us
  transfers between devices with their start and end apart: 8, of which 7 were waited for; matrix products, arithmetic and copies ran while one was open for 3% of the time, Pallas kernels for 0%

profile of v21, /device:TPU:0, one launch (start us, length us, event | category | flops | bytes accessed | tf_op | source)
XLA Modules:
  0.0 48.9 jit_solution(4585022751183051479)
XLA Ops:
  0.7 1.0 %convert_bitcast_fusion = f32[1,16,32,128]{3,2,1,0:T(8,128)S(1)} fusion(s32[16,32,128]{2,1,0:T(8,128)} %param.7), kind=kLoop, calls=%fused_computation.3 | loop fusion | flops 65536 | bytes 524288 | tf_op jit(solution)/shard_map/stack | solution.py:451
  1.7 0.9 %broadcast_select_fusion.3 = (f32[2,16,4,128]{3,2,1,0:T(4,128)S(1)}, f32[2,16,4,128]{3,2,1,0:T(4,128)S(1)}, f32[2,16,4,128]{3,2,1,0:T(4,128)S(1)}) fusion(pred[]{:T(512)S(6)} %eq.28, f32[1,16,32,128]{3,2,1,0:T(8,128)S(1)} %convert_bitcast_fusion, f32[1,16,32,128]{3,2,1,0:T(8,128)} %bitcast.57), kind=kLoop, calls=%fused_computation.35 | loop fusion | flops 49152 | bytes 720897 | tf_op jit(solution)/shard_map/jit(_where)/select_n | solution.py:38
  2.6 3.1 %collective-permute-start.1 = (f32[2,16,4,128]{3,2,1,0:T(4,128)S(1)}, f32[2,16,4,128]{3,2,1,0:T(4,128)S(1)}, u32[]{:S(2)}, u32[]{:S(2)}) collective-permute-start(f32[2,16,4,128]{3,2,1,0:T(4,128)S(1)} %bitcast.69), channel_id=1, source_target_pairs={{0,4},{4,0},{8,12},{12,8},{1,5},{5,1},{9,13},{13,9},{2,6},{6,2},{1... | collective-permute-start | bytes 196616 | tf_op jit(solution)/shard_map/ppermute | solution.py:37
  5.7 0.7 %collective-permute-start = (f32[2,16,4,128]{3,2,1,0:T(4,128)S(1)}, f32[2,16,4,128]{3,2,1,0:T(4,128)S(1)}, u32[]{:S(2)}, u32[]{:S(2)}) collective-permute-start(f32[2,16,4,128]{3,2,1,0:T(4,128)S(1)} %get-tuple-element.14), channel_id=1, source_target_pairs={{4,8},{8,4},{5,9},{9,5},{6,10},{10,6},{7,11},{11,7},{20,24},{24,20... | collective-permute-start | bytes 196616 | tf_op jit(solution)/shard_map/ppermute | solution.py:38
  6.4 1.6 %collective-permute-done.1 = f32[2,16,4,128]{3,2,1,0:T(4,128)S(1)} collective-permute-done((f32[2,16,4,128]{3,2,1,0:T(4,128)S(1)}, f32[2,16,4,128]{3,2,1,0:T(4,128)S(1)}, u32[]{:S(2)}, u32[]{:S(2)}) %collective-permute-start.1) | collective-permute-done | bytes 65568 | tf_op jit(solution)/shard_map/ppermute | solution.py:37
  8.0 0.9 %fusion = f32[2,4,40,128]{3,2,1,0:T(8,128)S(1)} fusion(f32[2,16,4,128]{3,2,1,0:T(4,128)S(1)} %bitcast.64, f32[2,16,4,128]{3,2,1,0:T(4,128)S(1)} %bitcast.61, f32[1,16,32,128]{3,2,1,0:T(8,128)S(1)} %convert_bitcast_fusion, f32[1,16,32,128]{3,2,1,0:T(8,128)} %bitcast.58, pred[]{:T(512)S(6)} %eq.29), kind=kLoop, calls=%fused_computation.5 | loop fusion | flops 286720 | bytes 819201 | tf_op jit(solution)/shard_map/jit(_where)/select_n | solution.py:30
  9.0 1.4 %collective-permute-done.2 = f32[2,4,40,128]{3,2,1,0:T(8,128)S(1)} collective-permute-done((f32[2,4,40,128]{3,2,1,0:T(8,128)S(1)}, f32[2,4,40,128]{3,2,1,0:T(8,128)S(1)}, u32[]{:S(2)}, u32[]{:S(2)}) %collective-permute-start.2) | collective-permute-done | bytes 163872 | tf_op jit(solution)/shard_map/ppermute | solution.py:30
  10.3 0.1 pad_maximum_fusion.1
  10.4 0.3 slice_select_fusion
  10.8 0.4 copy.18
  11.1 2.0 %collective-permute-start.3 = (f32[2,24,40,4]{2,1,3,0:T(8,128)S(1)}, f32[2,24,40,4]{2,1,3,0:T(8,128)S(1)}, u32[]{:S(2)}, u32[]{:S(2)}) collective-permute-start(f32[2,24,40,4]{2,1,3,0:T(8,128)S(1)} %copy.18), channel_id=1, source_target_pairs={{0,2},{2,0},{1,3},{3,1},{4,6},{6,4},{5,7},{7,5},{8,10},{10,8},{9,1... | collective-permute-start | bytes 92168 | tf_op jit(solution)/shard_map/ppermute | solution.py:30
  13.2 0.6 %stack.48.bounds_ref = s32[6]{0:T(128)} concatenate(s32[1]{0:T(128)} %bitcast, s32[1]{0:T(128)} %bitcast.1, s32[1]{0:T(128)} %bitcast.2, s32[1]{0:T(128)} %bitcast.3, s32[1]{0:T(128)} %bitcast.4, s32[1]{0:T(128)} %bitcast.5), dimensions={0} | concatenate | bytes 48 | tf_op jit(solution)/shard_map/stack | solution.py:457
  13.9 2.4 %collective-permute-done.3 = f32[2,24,40,4]{2,1,3,0:T(8,128)S(1)} collective-permute-done((f32[2,24,40,4]{2,1,3,0:T(8,128)S(1)}, f32[2,24,40,4]{2,1,3,0:T(8,128)S(1)}, u32[]{:S(2)}, u32[]{:S(2)}) %collective-permute-start.3) | collective-permute-done | bytes 30752 | tf_op jit(solution)/shard_map/ppermute | solution.py:30
  16.2 0.4 copy.19
  16.7 1.7 %pad_maximum_fusion.raw_ref = f32[2,24,40,256]{3,2,1,0:T(8,128)} fusion(f32[2,24,40,4]{3,2,1,0:T(8,128)S(1)} %copy.19, f32[2,4,40,128]{3,2,1,0:T(8,128)S(1)} %collective-permute-done.2, f32[2,16,4,128]{3,2,1,0:T(4,128)S(1)} %bitcast.66, f32[1,16,32,128]{3,2,1,0:T(8,128)S(1)} %convert_bitcast_fusion, f32[1,16,32,128]{3,2,1,0:T(8,128)S(1)} %bitcast.60, ...), kind=kLoop, calls=%fused_computation | loop fusion | flops 3932160 | bytes 2817024 | tf_op jit(solution)/shard_map/concatenate | solution.py:49
  18.4 11.0 %shard_map.77 = f32[3,8,128]{2,1,0:T(8,128)} custom-call(f32[3,4]{1,0:T(4,128)} %table_ref.1, s32[6]{0:T(128)} %stack.48.bounds_ref, f32[2,24,40,256]{3,2,1,0:T(8,128)} %pad_maximum_fusion.raw_ref), custom_call_target="tpu_custom_call" | custom-call | tf_op jit(solution)/shard_map/pallas_call | solution.py:343
  29.4 0.7 %slice.239 = f32[3,3,120]{2,1,0:T(4,128)S(1)} slice(f32[3,8,128]{2,1,0:T(8,128)} %shard_map.77), slice={[0:3], [0:3], [0:120]} | slice | bytes 8640 | tf_op jit(solution)/shard_map/slice | solution.py:354
  30.1 0.1 reshape.16
  30.2 0.1 reduce_sum.9
  30.4 0.1 slice.197
  30.7 4.9 %collective-permute-start.4 = (f32[6,2,1,4]{3,1,2,0:T(2,128)S(1)}, f32[6,2,1,4]{3,1,2,0:T(2,128)S(1)}, u32[]{:S(2)}, u32[]{:S(2)}) collective-permute-start(f32[6,2,1,4]{3,1,2,0:T(2,128)S(1)} %constant_dynamic-update-slice_fusion), channel_id=1, source_target_pairs={{0,4},{4,0},{8,12},{12,8},{1,5},{5,1},{9,13},{13,9},{2,6},{6,2},{1... | collective-permute-start | bytes 584 | tf_op jit(solution)/shard_map/ppermute | solution.py:60
  35.6 1.6 %collective-permute-done.4 = f32[6,2,1,4]{3,1,2,0:T(2,128)S(1)} collective-permute-done((f32[6,2,1,4]{3,1,2,0:T(2,128)S(1)}, f32[6,2,1,4]{3,1,2,0:T(2,128)S(1)}, u32[]{:S(2)}, u32[]{:S(2)}) %collective-permute-start.4) | collective-permute-done | bytes 224 | tf_op jit(solution)/shard_map/ppermute | solution.py:60
  37.2 3.5 %collective-permute-start.5 = (f32[6,2,2,4]{3,1,2,0:T(2,128)S(1)}, f32[6,2,2,4]{3,1,2,0:T(2,128)S(1)}, u32[]{:S(2)}, u32[]{:S(2)}) collective-permute-start(f32[6,2,2,4]{3,1,2,0:T(2,128)S(1)} %maximum_select_fusion.3), channel_id=1, source_target_pairs={{0,8},{4,12},{8,0},{12,4},{1,9},{5,13},{9,1},{13,5},{2,10},{6,14},... | collective-permute-start | bytes 1160 | tf_op jit(solution)/shard_map/ppermute | solution.py:60
  40.8 1.7 %collective-permute-done.5 = f32[6,2,2,4]{3,1,2,0:T(2,128)S(1)} collective-permute-done((f32[6,2,2,4]{3,1,2,0:T(2,128)S(1)}, f32[6,2,2,4]{3,1,2,0:T(2,128)S(1)}, u32[]{:S(2)}, u32[]{:S(2)}) %collective-permute-start.5) | collective-permute-done | bytes 416 | tf_op jit(solution)/shard_map/ppermute | solution.py:60
  42.5 1.6 %collective-permute-start.6 = (f32[6,2,4,4]{3,1,2,0:T(2,128)S(1)}, f32[6,2,4,4]{3,1,2,0:T(2,128)S(1)}, u32[]{:S(2)}, u32[]{:S(2)}) collective-permute-start(f32[6,2,4,4]{3,1,2,0:T(2,128)S(1)} %maximum_select_fusion.1), channel_id=1, source_target_pairs={{0,2},{2,0},{1,3},{3,1},{4,6},{6,4},{5,7},{7,5},{8,10},{10,8},{9,1... | collective-permute-start | bytes 2312 | tf_op jit(solution)/shard_map/ppermute | solution.py:60
  44.0 2.3 %collective-permute-done.6 = f32[6,2,4,4]{3,1,2,0:T(2,128)S(1)} collective-permute-done((f32[6,2,4,4]{3,1,2,0:T(2,128)S(1)}, f32[6,2,4,4]{3,1,2,0:T(2,128)S(1)}, u32[]{:S(2)}, u32[]{:S(2)}) %collective-permute-start.6) | collective-permute-done | bytes 800 | tf_op jit(solution)/shard_map/ppermute | solution.py:60
  46.4 0.1 maximum_select_fusion.2
  46.6 0.7 %reshape.18 = f32[3,2,1,4]{3,1,0,2:T(2,128)} reshape(f32[3,8]{1,0:T(4,128)S(1)} %bitcast.73) | data formatting | bytes 192 | tf_op jit(solution)/shard_map/reshape | solution.py:356
  47.2 0.5 %collective-permute-done.7 = f32[6,2,4,8]{3,1,2,0:T(2,128)S(1)} collective-permute-done((f32[6,2,4,8]{3,1,2,0:T(2,128)S(1)}, f32[6,2,4,8]{3,1,2,0:T(2,128)S(1)}, u32[]{:S(2)}, u32[]{:S(2)}) %collective-permute-start.7) | collective-permute-done | bytes 1568 | tf_op jit(solution)/shard_map/ppermute | solution.py:60
  47.9 0.1 fusion.11
  48.1 0.1 fusion.18
  48.2 0.7 %dynamic-slice_divide_fusion = f32[2,1,4]{2,0,1:T(2,128)} fusion(f32[4,4,8]{2,0,1:T(4,128)S(1)} %get-tuple-element.20, s32[]{:T(128)S(6)} %select_n.127, s32[]{:T(128)S(6)} %select_n.128, s32[]{:T(128)S(6)} %select_n.129, f32[4,4,8]{2,0,1:T(4,128)S(1)} %get-tuple-element.28, f32[4,4,8]{2,0,1:T(4,128)S(1)} %get-tuple-element.13, ...), kind=kLoop, calls=%fused_computation.87 | loop fusion | flops 80 | bytes 396 | tf_op jit(solution)/shard_map/div | solution.py:377
  (34 shorter events, 0.8 us)
Async XLA Ops:
  0.6 9.7 %copy-start = (f32[16,32,128]{2,1,0:T(8,128)S(1)}, f32[16,32,128]{2,1,0:T(8,128)}, u32[]{:S(2)}) copy-start(f32[16,32,128]{2,1,0:T(8,128)} %param.6) | copy-start | bytes 786436
  2.6 5.3 %collective-permute-start.1 = (f32[2,16,4,128]{3,2,1,0:T(4,128)S(1)}, f32[2,16,4,128]{3,2,1,0:T(4,128)S(1)}, u32[]{:S(2)}, u32[]{:S(2)}) collective-permute-start(f32[2,16,4,128]{3,2,1,0:T(4,128)S(1)} %bitcast.69), channel_id=1, source_target_pairs={{0,4},{4,0},{8,12},{12,8},{1,5},{5,1},{9,13},{13,9},{2,6},{6,2},{1... | collective-permute-start | bytes 196616 | tf_op jit(solution)/shard_map/ppermute | solution.py:37
  5.7 2.2 %collective-permute-start = (f32[2,16,4,128]{3,2,1,0:T(4,128)S(1)}, f32[2,16,4,128]{3,2,1,0:T(4,128)S(1)}, u32[]{:S(2)}, u32[]{:S(2)}) collective-permute-start(f32[2,16,4,128]{3,2,1,0:T(4,128)S(1)} %get-tuple-element.14), channel_id=1, source_target_pairs={{4,8},{8,4},{5,9},{9,5},{6,10},{10,6},{7,11},{11,7},{20,24},{24,20... | collective-permute-start | bytes 196616 | tf_op jit(solution)/shard_map/ppermute | solution.py:38
  8.9 1.5 %collective-permute-start.2 = (f32[2,4,40,128]{3,2,1,0:T(8,128)S(1)}, f32[2,4,40,128]{3,2,1,0:T(8,128)S(1)}, u32[]{:S(2)}, u32[]{:S(2)}) collective-permute-start(f32[2,4,40,128]{3,2,1,0:T(8,128)S(1)} %fusion), channel_id=1, source_target_pairs={{0,1},{1,0},{2,3},{3,2},{4,5},{5,4},{6,7},{7,6},{8,9},{9,8},{10,11... | collective-permute-start | bytes 491528 | tf_op jit(solution)/shard_map/ppermute | solution.py:30
  11.1 5.1 %collective-permute-start.3 = (f32[2,24,40,4]{2,1,3,0:T(8,128)S(1)}, f32[2,24,40,4]{2,1,3,0:T(8,128)S(1)}, u32[]{:S(2)}, u32[]{:S(2)}) collective-permute-start(f32[2,24,40,4]{2,1,3,0:T(8,128)S(1)} %copy.18), channel_id=1, source_target_pairs={{0,2},{2,0},{1,3},{3,1},{4,6},{6,4},{5,7},{7,5},{8,10},{10,8},{9,1... | collective-permute-start | bytes 92168 | tf_op jit(solution)/shard_map/ppermute | solution.py:30
  18.3 12.3 %copy-start.1 = (f32[2,1,4]{2,1,0:T(1,128)S(1)}, f32[2,1,4]{2,1,0:T(1,128)}, u32[]{:S(2)}) copy-start(f32[2,1,4]{2,1,0:T(1,128)} %param.9) | copy-start | bytes 100
  18.3 12.3 %copy-start.2 = (f32[2,1,4]{2,1,0:T(1,128)S(1)}, f32[2,1,4]{2,1,0:T(1,128)}, u32[]{:S(2)}) copy-start(f32[2,1,4]{2,1,0:T(1,128)} %param.10) | copy-start | bytes 100
  18.3 12.3 %copy-start.3 = (f32[2,1,4]{2,1,0:T(1,128)S(1)}, f32[2,1,4]{2,1,0:T(1,128)}, u32[]{:S(2)}) copy-start(f32[2,1,4]{2,1,0:T(1,128)} %param.11) | copy-start | bytes 100
  30.7 6.5 %collective-permute-start.4 = (f32[6,2,1,4]{3,1,2,0:T(2,128)S(1)}, f32[6,2,1,4]{3,1,2,0:T(2,128)S(1)}, u32[]{:S(2)}, u32[]{:S(2)}) collective-permute-start(f32[6,2,1,4]{3,1,2,0:T(2,128)S(1)} %constant_dynamic-update-slice_fusion), channel_id=1, source_target_pairs={{0,4},{4,0},{8,12},{12,8},{1,5},{5,1},{9,13},{13,9},{2,6},{6,2},{1... | collective-permute-start | bytes 584 | tf_op jit(solution)/shard_map/ppermute | solution.py:60
  37.2 5.2 %collective-permute-start.5 = (f32[6,2,2,4]{3,1,2,0:T(2,128)S(1)}, f32[6,2,2,4]{3,1,2,0:T(2,128)S(1)}, u32[]{:S(2)}, u32[]{:S(2)}) collective-permute-start(f32[6,2,2,4]{3,1,2,0:T(2,128)S(1)} %maximum_select_fusion.3), channel_id=1, source_target_pairs={{0,8},{4,12},{8,0},{12,4},{1,9},{5,13},{9,1},{13,5},{2,10},{6,14},... | collective-permute-start | bytes 1160 | tf_op jit(solution)/shard_map/ppermute | solution.py:60
  42.5 3.9 %collective-permute-start.6 = (f32[6,2,4,4]{3,1,2,0:T(2,128)S(1)}, f32[6,2,4,4]{3,1,2,0:T(2,128)S(1)}, u32[]{:S(2)}, u32[]{:S(2)}) collective-permute-start(f32[6,2,4,4]{3,1,2,0:T(2,128)S(1)} %maximum_select_fusion.1), channel_id=1, source_target_pairs={{0,2},{2,0},{1,3},{3,1},{4,6},{6,4},{5,7},{7,5},{8,10},{10,8},{9,1... | collective-permute-start | bytes 2312 | tf_op jit(solution)/shard_map/ppermute | solution.py:60
  46.5 1.3 %collective-permute-start.7 = (f32[6,2,4,8]{3,1,2,0:T(2,128)S(1)}, f32[6,2,4,8]{3,1,2,0:T(2,128)S(1)}, u32[]{:S(2)}, u32[]{:S(2)}) collective-permute-start(f32[6,2,4,8]{3,1,2,0:T(2,128)S(1)} %maximum_select_fusion.2), channel_id=1, source_target_pairs={{0,1},{1,0},{2,3},{3,2},{4,5},{5,4},{6,7},{7,6},{8,9},{9,8},{10,11... | collective-permute-start | bytes 4616 | tf_op jit(solution)/shard_map/ppermute | solution.py:60

commit v22 on v18

--- a/solution.py
+++ b/solution.py
@@ -50,21 +50,21 @@
     return cells
 
 
-def halo_xy_then_z(block, width, lanes):
+def halo_xz_then_y(block, width, lanes):
     size_x = lax.axis_size("gx")
-    size_y = lax.axis_size("gy")
-    if size_y != 2 or size_x % 2:
+    size_z = lax.axis_size("gz")
+    if size_z != 2 or size_x % 2:
         return extended(block, (("gx", 2), ("gz", 1), ("gy", 3)), width, lanes)
     even = lax.axis_index("gx") % 2 == 0
-    low_y = lax.axis_index("gy") == 0
+    low_z = lax.axis_index("gz") == 0
 
     def edge(values, dim, upper):
         length = values.shape[dim]
         start = length - width if upper else 0
         return lax.slice_in_dim(values, start, start + width, axis=dim)
 
-    def y_side(values):
-        return jnp.where(low_y, edge(values, 3, True), edge(values, 3, False))
+    def z_side(values):
+        return jnp.where(low_z, edge(values, 1, True), edge(values, 1, False))
 
     def partner(i):
         return i + 1 if i % 2 else i - 1
@@ -75,22 +75,20 @@
     send_second = jnp.where(even, edge(block, 2, False), edge(block, 2, True))
     got_first = lax.ppermute(send_first, "gx", first)
     got_second = lax.ppermute(send_second, "gx", second)
-    got_y = lax.ppermute(y_side(block), "gy", [(0, 1), (1, 0)])
-    names = ("gx", "gy")
+    got_z = lax.ppermute(z_side(block), "gz", [(0, 1), (1, 0)])
+    names = ("gx", "gz")
     corner_first = [(i * 2 + j, (i ^ 1) * 2 + 1 - j) for i in range(size_x) for j in range(2)]
     corner_second = [(i * 2 + j, partner(i) * 2 + 1 - j) for i in range(1, size_x - 1) for j in range(2)]
-    got_corner_first = lax.ppermute(y_side(send_first), names, corner_first)
-    got_corner_second = lax.ppermute(y_side(send_second), names, corner_second)
+    got_corner_first = lax.ppermute(z_side(send_first), names, corner_first)
+    got_corner_second = lax.ppermute(z_side(send_second), names, corner_second)
     below_x = jnp.where(even, got_second, got_first)
     above_x = jnp.where(even, got_first, got_second)
     below_corner = jnp.where(even, got_corner_second, got_corner_first)
     above_corner = jnp.where(even, got_corner_first, got_corner_second)
     centre = jnp.concatenate([below_x, block, above_x], axis=2)
-    rim = jnp.concatenate([below_corner, got_y, above_corner], axis=2)
-    extra = lanes - (block.shape[3] + 2 * width)
-    zeros = jnp.zeros(centre.shape[:3] + (extra,), centre.dtype)
-    cells = jnp.concatenate([centre, rim, zeros, rim], axis=3)
-    return extended(cells, (("gz", 1),), width)
+    rim = jnp.concatenate([below_corner, got_z, above_corner], axis=2)
+    cells = jnp.concatenate([rim, centre, rim], axis=1)
+    return extended(cells, (("gy", 3),), width, lanes)
 
 
 def doubling_gather(values, axis, dim):
@@ -493,7 +491,7 @@
     index_y = lax.axis_index("gy")
     raw = jnp.stack([log_noise, facies.astype(jnp.float32)])
     wide = -(-(cols_len + 2 * RIM) // LANES) * LANES
-    raw = halo_xy_then_z(raw, RIM, wide)
+    raw = halo_xz_then_y(raw, RIM, wide)
     anchor_z = index_z * depth_len
     anchor_y = index_y * cols_len
     anchor_x = index_x * rows_len

time: 58.1 us -> 49.4 us (0.85)
  waiting for transfers between devices: 20.8 us -> 9.91 us
  local copies, waits for them, and re-layouts: 2.66 us -> 3.49 us
  other arithmetic: 5.95 us -> 6.72 us
  starting transfers between devices: 16.4 us -> 17.1 us
    ppermute x5, waiting for transfers between devices: 12.2 us -> 0.94 us  [the longest x1 0.93 us: halo_xz_then_y(): got_z = lax.ppermute(z_side(block), 'gz', [(0, 1), (1, 0)])]
    ppermute x1, waiting for transfers between devices: 0.94 us -> 2.82 us  [extended(): lax.ppermute(jnp.where(lower_side, tail, head), axis, [(0, 1), (1, 0)])]
    ppermute x1, starting transfers between devices: 0.07 us -> 1.57 us  [extended(): lax.ppermute(jnp.where(lower_side, tail, head), axis, [(0, 1), (1, 0)])]
    ppermute x4, waiting for transfers between devices: 7.62 us -> 6.15 us  [doubling_gather(): got = lax.ppermute(values, axis, [(i, i ^ step) for i in range(count)])]
    ppermute x5, starting transfers between devices: 10.4 us -> 9.03 us  [the longest x1 3.34 us: halo_xz_then_y(): got_corner_first = lax.ppermute(z_side(send_first), names, corner_first)]
  transfers between devices with their start and end apart: 10 -> 10, of which waited for: 7 -> 6; matrix products, arithmetic and copies ran while one was open for 3% -> 5% of each run, Pallas kernels for 0% -> 0%
where the time goes in v22:
time: 49.4 us; the launch traced here: 49.1 us
  starting transfers between devices  17.1 us (35%)
  Pallas kernels  11 us (22%)
  waiting for transfers between devices  9.91 us (20%)
  other arithmetic  6.72 us (14%)
  local copies, waits for them, and re-layouts  3.49 us (7%)
  between operations  0.85 us (2%)
    pallas_call x1, Pallas kernels, upscale_windows(): pl.pallas_call(kernel, grid=(packs,), in_specs=[pl.BlockSpec(memory_space...  11 us
    ppermute x4, starting transfers between devices, doubling_gather(): got = lax.ppermute(values, axis, [(i, i ^ step) for i in range(count)])  6.48 us
    ppermute x4, waiting for transfers between devices, doubling_gather(): got = lax.ppermute(values, axis, [(i, i ^ step) for i in range(count)])  6.15 us
    ppermute x1, starting transfers between devices, halo_xz_then_y(): got_corner_first = lax.ppermute(z_side(send_first), names, corner_first)  3.34 us
    ppermute x1, starting transfers between devices, halo_xz_then_y(): got_first = lax.ppermute(send_first, 'gx', first)  3.09 us
    ppermute x1, waiting for transfers between devices, extended(): lax.ppermute(jnp.where(lower_side, tail, head), axis, [(0, 1), (1, 0)])  2.82 us
    concatenate x1, other arithmetic, extended(): cells = jnp.concatenate(parts, axis=dim)  2.23 us
    ppermute x1, starting transfers between devices, extended(): lax.ppermute(jnp.where(lower_side, tail, head), axis, [(0, 1), (1, 0)])  1.57 us
  transfers between devices with their start and end apart: 10, of which 6 were waited for; matrix products, arithmetic and copies ran while one was open for 5% of the time, Pallas kernels for 0%

profile of v22, /device:TPU:0, one launch (start us, length us, event | category | flops | bytes accessed | tf_op | source)
XLA Modules:
  0.0 49.1 jit_solution(11713567800040608349)
XLA Ops:
  0.7 1.0 %convert_bitcast_fusion = f32[1,16,32,128]{3,2,1,0:T(8,128)S(1)} fusion(s32[16,32,128]{2,1,0:T(8,128)} %param.7), kind=kLoop, calls=%fused_computation.3 | loop fusion | flops 65536 | bytes 524288 | tf_op jit(solution)/shard_map/stack | solution.py:492
  1.7 0.9 %broadcast_select_fusion.3 = (f32[2,16,4,128]{3,2,1,0:T(4,128)S(1)}, f32[2,16,4,128]{3,2,1,0:T(4,128)S(1)}, f32[2,16,4,128]{3,2,1,0:T(4,128)S(1)}) fusion(pred[]{:T(512)S(6)} %eq.27, f32[1,16,32,128]{3,2,1,0:T(8,128)S(1)} %convert_bitcast_fusion, f32[1,16,32,128]{3,2,1,0:T(8,128)} %bitcast.61), kind=kLoop, calls=%fused_computation.33 | loop fusion | flops 49152 | bytes 720897 | tf_op jit(solution)/shard_map/jit(_where)/select_n | solution.py:75
  2.6 3.1 %collective-permute-start.4 = (f32[2,16,4,128]{3,2,1,0:T(4,128)S(1)}, f32[2,16,4,128]{3,2,1,0:T(4,128)S(1)}, u32[]{:S(2)}, u32[]{:S(2)}) collective-permute-start(f32[2,16,4,128]{3,2,1,0:T(4,128)S(1)} %bitcast.75), channel_id=1, source_target_pairs={{0,4},{4,0},{8,12},{12,8},{1,5},{5,1},{9,13},{13,9},{2,6},{6,2},{1... | collective-permute-start | bytes 196616 | tf_op jit(solution)/shard_map/ppermute | solution.py:76
  5.7 0.7 %collective-permute-start.3 = (f32[2,16,4,128]{3,2,1,0:T(4,128)S(1)}, f32[2,16,4,128]{3,2,1,0:T(4,128)S(1)}, u32[]{:S(2)}, u32[]{:S(2)}) collective-permute-start(f32[2,16,4,128]{3,2,1,0:T(4,128)S(1)} %get-tuple-element.14), channel_id=1, source_target_pairs={{4,8},{8,4},{5,9},{9,5},{6,10},{10,6},{7,11},{11,7},{20,24},{24,20... | collective-permute-start | bytes 196616 | tf_op jit(solution)/shard_map/ppermute | solution.py:77
  6.4 3.3 %collective-permute-start.1 = (f32[2,4,4,128]{3,2,1,0:T(4,128)S(1)}, f32[2,4,4,128]{3,2,1,0:T(4,128)S(1)}, u32[]{:S(2)}, u32[]{:S(2)}) collective-permute-start(f32[2,4,4,128]{3,2,1,0:T(4,128)S(1)} %slice_select_fusion.1), channel_id=1, source_target_pairs={{0,5},{1,4},{4,1},{5,0},{8,13},{9,12},{12,9},{13,8},{2,7},{3,6},{6... | collective-permute-start | bytes 49160 | tf_op jit(solution)/shard_map/ppermute | solution.py:82
  9.7 0.7 %collective-permute-start = (f32[2,4,4,128]{3,2,1,0:T(4,128)S(1)}, f32[2,4,4,128]{3,2,1,0:T(4,128)S(1)}, u32[]{:S(2)}, u32[]{:S(2)}) collective-permute-start(f32[2,4,4,128]{3,2,1,0:T(4,128)S(1)} %slice_select_fusion.2), channel_id=1, source_target_pairs={{4,9},{5,8},{8,5},{9,4},{6,11},{7,10},{10,7},{11,6},{20,25},{21,24... | collective-permute-start | bytes 49160 | tf_op jit(solution)/shard_map/ppermute | solution.py:83
  10.4 0.9 %fusion = f32[2,4,32,128]{3,2,1,0:T(8,128)S(1)} fusion(f32[1,16,32,128]{3,2,1,0:T(8,128)S(1)} %convert_bitcast_fusion, f32[1,16,32,128]{3,2,1,0:T(8,128)} %bitcast.62, pred[]{:T(512)S(6)} %eq.29), kind=kLoop, calls=%fused_computation.5 | loop fusion | flops 98304 | bytes 655361 | tf_op jit(solution)/shard_map/jit(_where)/select_n | solution.py:67
  11.3 1.3 %collective-permute-start.2 = (f32[2,4,32,128]{3,2,1,0:T(8,128)S(1)}, f32[2,4,32,128]{3,2,1,0:T(8,128)S(1)}, u32[]{:S(2)}, u32[]{:S(2)}) collective-permute-start(f32[2,4,32,128]{3,2,1,0:T(8,128)S(1)} %fusion), channel_id=1, source_target_pairs={{0,1},{1,0},{2,3},{3,2},{4,5},{5,4},{6,7},{7,6},{8,9},{9,8},{10,11... | collective-permute-start | bytes 393224 | tf_op jit(solution)/shard_map/ppermute | solution.py:78
  12.6 0.9 %collective-permute-done.2 = f32[2,4,32,128]{3,2,1,0:T(8,128)S(1)} collective-permute-done((f32[2,4,32,128]{3,2,1,0:T(8,128)S(1)}, f32[2,4,32,128]{3,2,1,0:T(8,128)S(1)}, u32[]{:S(2)}, u32[]{:S(2)}) %collective-permute-start.2) | collective-permute-done | bytes 131104 | tf_op jit(solution)/shard_map/ppermute | solution.py:78
  13.6 0.1 maximum_maximum_fusion
  13.7 0.3 slice_select_fusion
  14.0 0.4 copy.18
  14.4 1.6 %collective-permute-start.5 = (f32[2,24,40,4]{2,1,3,0:T(8,128)S(1)}, f32[2,24,40,4]{2,1,3,0:T(8,128)S(1)}, u32[]{:S(2)}, u32[]{:S(2)}) collective-permute-start(f32[2,24,40,4]{2,1,3,0:T(8,128)S(1)} %copy.18), channel_id=1, source_target_pairs={{0,2},{2,0},{1,3},{3,1},{4,6},{6,4},{5,7},{7,5},{8,10},{10,8},{9,1... | collective-permute-start | bytes 92168 | tf_op jit(solution)/shard_map/ppermute | solution.py:30
  16.0 0.7 %stack.48.bounds_ref = s32[6]{0:T(128)} concatenate(s32[1]{0:T(128)} %bitcast, s32[1]{0:T(128)} %bitcast.1, s32[1]{0:T(128)} %bitcast.2, s32[1]{0:T(128)} %bitcast.3, s32[1]{0:T(128)} %bitcast.4, s32[1]{0:T(128)} %bitcast.5), dimensions={0} | concatenate | bytes 48 | tf_op jit(solution)/shard_map/stack | solution.py:498
  16.7 2.8 %collective-permute-done.5 = f32[2,24,40,4]{2,1,3,0:T(8,128)S(1)} collective-permute-done((f32[2,24,40,4]{2,1,3,0:T(8,128)S(1)}, f32[2,24,40,4]{2,1,3,0:T(8,128)S(1)}, u32[]{:S(2)}, u32[]{:S(2)}) %collective-permute-start.5) | collective-permute-done | bytes 30752 | tf_op jit(solution)/shard_map/ppermute | solution.py:30
  19.5 0.4 copy.19
  19.9 2.2 %pad_maximum_fusion.raw_ref = f32[2,24,40,256]{3,2,1,0:T(8,128)} fusion(f32[2,24,40,4]{3,2,1,0:T(8,128)S(1)} %copy.19, f32[2,4,4,128]{3,2,1,0:T(4,128)S(1)} %bitcast.74, f32[2,4,32,128]{3,2,1,0:T(8,128)S(1)} %collective-permute-done.2, f32[2,4,4,128]{3,2,1,0:T(4,128)S(1)} %bitcast.72, f32[2,16,4,128]{3,2,1,0:T(4,128)S(1)} %bitcast.68, ...), kind=kLoop, calls=%fused_computation | loop fusion | flops 5898240 | bytes 2817024 | tf_op jit(solution)/shard_map/concatenate | solution.py:49
  22.2 11.0 %shard_map.77 = f32[3,8,128]{2,1,0:T(8,128)} custom-call(f32[3,4]{1,0:T(4,128)} %table_ref.1, s32[6]{0:T(128)} %stack.48.bounds_ref, f32[2,24,40,256]{3,2,1,0:T(8,128)} %pad_maximum_fusion.raw_ref), custom_call_target="tpu_custom_call" | custom-call | tf_op jit(solution)/shard_map/pallas_call | solution.py:384
  33.2 0.7 %slice.261 = f32[3,3,120]{2,1,0:T(4,128)S(1)} slice(f32[3,8,128]{2,1,0:T(8,128)} %shard_map.77), slice={[0:3], [0:3], [0:120]} | slice | bytes 8640 | tf_op jit(solution)/shard_map/slice | solution.py:395
  33.9 0.1 reshape.68
  34.0 0.1 reduce_sum.9
  34.5 1.6 %collective-permute-start.6 = (f32[6,2,1,4]{3,1,2,0:T(2,128)S(1)}, f32[6,2,1,4]{3,1,2,0:T(2,128)S(1)}, u32[]{:S(2)}, u32[]{:S(2)}) collective-permute-start(f32[6,2,1,4]{3,1,2,0:T(2,128)S(1)} %constant_dynamic-update-slice_fusion), channel_id=1, source_target_pairs={{0,2},{2,0},{1,3},{3,1},{4,6},{6,4},{5,7},{7,5},{8,10},{10,8},{9,1... | collective-permute-start | bytes 584 | tf_op jit(solution)/shard_map/ppermute | solution.py:101
  36.1 2.1 %collective-permute-done.6 = f32[6,2,1,4]{3,1,2,0:T(2,128)S(1)} collective-permute-done((f32[6,2,1,4]{3,1,2,0:T(2,128)S(1)}, f32[6,2,1,4]{3,1,2,0:T(2,128)S(1)}, u32[]{:S(2)}, u32[]{:S(2)}) %collective-permute-start.6) | collective-permute-done | bytes 224 | tf_op jit(solution)/shard_map/ppermute | solution.py:101
  38.3 2.0 %collective-permute-start.7 = (f32[6,2,1,8]{3,1,2,0:T(2,128)S(1)}, f32[6,2,1,8]{3,1,2,0:T(2,128)S(1)}, u32[]{:S(2)}, u32[]{:S(2)}) collective-permute-start(f32[6,2,1,8]{3,1,2,0:T(2,128)S(1)} %maximum_select_fusion.3), channel_id=1, source_target_pairs={{0,4},{4,0},{8,12},{12,8},{1,5},{5,1},{9,13},{13,9},{2,6},{6,2},{1... | collective-permute-start | bytes 1160 | tf_op jit(solution)/shard_map/ppermute | solution.py:101
  40.3 1.6 %collective-permute-done.7 = f32[6,2,1,8]{3,1,2,0:T(2,128)S(1)} collective-permute-done((f32[6,2,1,8]{3,1,2,0:T(2,128)S(1)}, f32[6,2,1,8]{3,1,2,0:T(2,128)S(1)}, u32[]{:S(2)}, u32[]{:S(2)}) %collective-permute-start.7) | collective-permute-done | bytes 416 | tf_op jit(solution)/shard_map/ppermute | solution.py:101
  42.0 2.8 %collective-permute-start.8 = (f32[6,2,2,8]{3,1,2,0:T(2,128)S(1)}, f32[6,2,2,8]{3,1,2,0:T(2,128)S(1)}, u32[]{:S(2)}, u32[]{:S(2)}) collective-permute-start(f32[6,2,2,8]{3,1,2,0:T(2,128)S(1)} %maximum_select_fusion.2), channel_id=1, source_target_pairs={{0,8},{4,12},{8,0},{12,4},{1,9},{5,13},{9,1},{13,5},{2,10},{6,14},... | collective-permute-start | bytes 2312 | tf_op jit(solution)/shard_map/ppermute | solution.py:101
  44.8 1.9 %collective-permute-done.8 = f32[6,2,2,8]{3,1,2,0:T(2,128)S(1)} collective-permute-done((f32[6,2,2,8]{3,1,2,0:T(2,128)S(1)}, f32[6,2,2,8]{3,1,2,0:T(2,128)S(1)}, u32[]{:S(2)}, u32[]{:S(2)}) %collective-permute-start.8) | collective-permute-done | bytes 800 | tf_op jit(solution)/shard_map/ppermute | solution.py:101
  46.8 0.7 %reshape.70 = f32[3,2,1,4]{3,1,0,2:T(2,128)} reshape(f32[3,8]{1,0:T(4,128)S(1)} %bitcast.82) | data formatting | bytes 192 | tf_op jit(solution)/shard_map/reshape | solution.py:397
  47.4 0.5 %collective-permute-done.9 = f32[6,2,4,8]{3,1,2,0:T(2,128)S(1)} collective-permute-done((f32[6,2,4,8]{3,1,2,0:T(2,128)S(1)}, f32[6,2,4,8]{3,1,2,0:T(2,128)S(1)}, u32[]{:S(2)}, u32[]{:S(2)}) %collective-permute-start.9) | collective-permute-done | bytes 1568 | tf_op jit(solution)/shard_map/ppermute | solution.py:101
  48.1 0.1 fusion.11
  48.3 0.1 fusion.18
  48.4 0.7 %dynamic-slice_divide_fusion = f32[2,1,4]{2,0,1:T(2,128)} fusion(f32[4,4,8]{2,0,1:T(4,128)S(1)} %get-tuple-element.20, s32[]{:T(128)S(6)} %select_n.163, s32[]{:T(128)S(6)} %select_n.164, s32[]{:T(128)S(6)} %select_n.165, f32[4,4,8]{2,0,1:T(4,128)S(1)} %get-tuple-element.30, f32[4,4,8]{2,0,1:T(4,128)S(1)} %get-tuple-element.13, ...), kind=kLoop, calls=%fused_computation.89 | loop fusion | flops 80 | bytes 396 | tf_op jit(solution)/shard_map/div | solution.py:418
  (41 shorter events, 1.0 us)
Async XLA Ops:
  0.6 12.9 %copy-start = (f32[16,32,128]{2,1,0:T(8,128)S(1)}, f32[16,32,128]{2,1,0:T(8,128)}, u32[]{:S(2)}) copy-start(f32[16,32,128]{2,1,0:T(8,128)} %param.6) | copy-start | bytes 786436
  2.6 10.0 %collective-permute-start.4 = (f32[2,16,4,128]{3,2,1,0:T(4,128)S(1)}, f32[2,16,4,128]{3,2,1,0:T(4,128)S(1)}, u32[]{:S(2)}, u32[]{:S(2)}) collective-permute-start(f32[2,16,4,128]{3,2,1,0:T(4,128)S(1)} %bitcast.75), channel_id=1, source_target_pairs={{0,4},{4,0},{8,12},{12,8},{1,5},{5,1},{9,13},{13,9},{2,6},{6,2},{1... | collective-permute-start | bytes 196616 | tf_op jit(solution)/shard_map/ppermute | solution.py:76
  5.7 6.9 %collective-permute-start.3 = (f32[2,16,4,128]{3,2,1,0:T(4,128)S(1)}, f32[2,16,4,128]{3,2,1,0:T(4,128)S(1)}, u32[]{:S(2)}, u32[]{:S(2)}) collective-permute-start(f32[2,16,4,128]{3,2,1,0:T(4,128)S(1)} %get-tuple-element.14), channel_id=1, source_target_pairs={{4,8},{8,4},{5,9},{9,5},{6,10},{10,6},{7,11},{11,7},{20,24},{24,20... | collective-permute-start | bytes 196616 | tf_op jit(solution)/shard_map/ppermute | solution.py:77
  6.4 6.2 %collective-permute-start.1 = (f32[2,4,4,128]{3,2,1,0:T(4,128)S(1)}, f32[2,4,4,128]{3,2,1,0:T(4,128)S(1)}, u32[]{:S(2)}, u32[]{:S(2)}) collective-permute-start(f32[2,4,4,128]{3,2,1,0:T(4,128)S(1)} %slice_select_fusion.1), channel_id=1, source_target_pairs={{0,5},{1,4},{4,1},{5,0},{8,13},{9,12},{12,9},{13,8},{2,7},{3,6},{6... | collective-permute-start | bytes 49160 | tf_op jit(solution)/shard_map/ppermute | solution.py:82
  9.7 2.9 %collective-permute-start = (f32[2,4,4,128]{3,2,1,0:T(4,128)S(1)}, f32[2,4,4,128]{3,2,1,0:T(4,128)S(1)}, u32[]{:S(2)}, u32[]{:S(2)}) collective-permute-start(f32[2,4,4,128]{3,2,1,0:T(4,128)S(1)} %slice_select_fusion.2), channel_id=1, source_target_pairs={{4,9},{5,8},{8,5},{9,4},{6,11},{7,10},{10,7},{11,6},{20,25},{21,24... | collective-permute-start | bytes 49160 | tf_op jit(solution)/shard_map/ppermute | solution.py:83
  11.3 2.3 %collective-permute-start.2 = (f32[2,4,32,128]{3,2,1,0:T(8,128)S(1)}, f32[2,4,32,128]{3,2,1,0:T(8,128)S(1)}, u32[]{:S(2)}, u32[]{:S(2)}) collective-permute-start(f32[2,4,32,128]{3,2,1,0:T(8,128)S(1)} %fusion), channel_id=1, source_target_pairs={{0,1},{1,0},{2,3},{3,2},{4,5},{5,4},{6,7},{7,6},{8,9},{9,8},{10,11... | collective-permute-start | bytes 393224 | tf_op jit(solution)/shard_map/ppermute | solution.py:78
  14.4 5.1 %collective-permute-start.5 = (f32[2,24,40,4]{2,1,3,0:T(8,128)S(1)}, f32[2,24,40,4]{2,1,3,0:T(8,128)S(1)}, u32[]{:S(2)}, u32[]{:S(2)}) collective-permute-start(f32[2,24,40,4]{2,1,3,0:T(8,128)S(1)} %copy.18), channel_id=1, source_target_pairs={{0,2},{2,0},{1,3},{3,1},{4,6},{6,4},{5,7},{7,5},{8,10},{10,8},{9,1... | collective-permute-start | bytes 92168 | tf_op jit(solution)/shard_map/ppermute | solution.py:30
  22.2 12.3 %copy-start.1 = (f32[2,1,4]{2,1,0:T(1,128)S(1)}, f32[2,1,4]{2,1,0:T(1,128)}, u32[]{:S(2)}) copy-start(f32[2,1,4]{2,1,0:T(1,128)} %param.9) | copy-start | bytes 100
  22.2 12.3 %copy-start.2 = (f32[2,1,4]{2,1,0:T(1,128)S(1)}, f32[2,1,4]{2,1,0:T(1,128)}, u32[]{:S(2)}) copy-start(f32[2,1,4]{2,1,0:T(1,128)} %param.10) | copy-start | bytes 100
  22.2 12.3 %copy-start.3 = (f32[2,1,4]{2,1,0:T(1,128)S(1)}, f32[2,1,4]{2,1,0:T(1,128)}, u32[]{:S(2)}) copy-start(f32[2,1,4]{2,1,0:T(1,128)} %param.11) | copy-start | bytes 100
  34.5 3.7 %collective-permute-start.6 = (f32[6,2,1,4]{3,1,2,0:T(2,128)S(1)}, f32[6,2,1,4]{3,1,2,0:T(2,128)S(1)}, u32[]{:S(2)}, u32[]{:S(2)}) collective-permute-start(f32[6,2,1,4]{3,1,2,0:T(2,128)S(1)} %constant_dynamic-update-slice_fusion), channel_id=1, source_target_pairs={{0,2},{2,0},{1,3},{3,1},{4,6},{6,4},{5,7},{7,5},{8,10},{10,8},{9,1... | collective-permute-start | bytes 584 | tf_op jit(solution)/shard_map/ppermute | solution.py:101
  38.3 3.7 %collective-permute-start.7 = (f32[6,2,1,8]{3,1,2,0:T(2,128)S(1)}, f32[6,2,1,8]{3,1,2,0:T(2,128)S(1)}, u32[]{:S(2)}, u32[]{:S(2)}) collective-permute-start(f32[6,2,1,8]{3,1,2,0:T(2,128)S(1)} %maximum_select_fusion.3), channel_id=1, source_target_pairs={{0,4},{4,0},{8,12},{12,8},{1,5},{5,1},{9,13},{13,9},{2,6},{6,2},{1... | collective-permute-start | bytes 1160 | tf_op jit(solution)/shard_map/ppermute | solution.py:101
  42.0 4.7 %collective-permute-start.8 = (f32[6,2,2,8]{3,1,2,0:T(2,128)S(1)}, f32[6,2,2,8]{3,1,2,0:T(2,128)S(1)}, u32[]{:S(2)}, u32[]{:S(2)}) collective-permute-start(f32[6,2,2,8]{3,1,2,0:T(2,128)S(1)} %maximum_select_fusion.2), channel_id=1, source_target_pairs={{0,8},{4,12},{8,0},{12,4},{1,9},{5,13},{9,1},{13,5},{2,10},{6,14},... | collective-permute-start | bytes 2312 | tf_op jit(solution)/shard_map/ppermute | solution.py:101
  46.7 1.3 %collective-permute-start.9 = (f32[6,2,4,8]{3,1,2,0:T(2,128)S(1)}, f32[6,2,4,8]{3,1,2,0:T(2,128)S(1)}, u32[]{:S(2)}, u32[]{:S(2)}) collective-permute-start(f32[6,2,4,8]{3,1,2,0:T(2,128)S(1)} %maximum_select_fusion.1), channel_id=1, source_target_pairs={{0,1},{1,0},{2,3},{3,2},{4,5},{5,4},{6,7},{7,6},{8,9},{9,8},{10,11... | collective-permute-start | bytes 4616 | tf_op jit(solution)/shard_map/ppermute | solution.py:101

commit v23 on v17

--- a/solution.py
+++ b/solution.py
@@ -25,7 +25,11 @@
         ends = count - 1
         head = lax.slice_in_dim(cells, 0, width, axis=dim)
         tail = lax.slice_in_dim(cells, cells.shape[dim] - width, cells.shape[dim], axis=dim)
-        if count == 2:
+        if count == 2 and dim == cells.ndim - 1:
+            got = lax.ppermute(jnp.concatenate([tail, head], axis=dim), axis, [(0, 1), (1, 0)])
+            below = lax.slice_in_dim(got, 0, width, axis=dim)
+            above = lax.slice_in_dim(got, width, 2 * width, axis=dim)
+        elif count == 2:
             lower_side = lax.axis_index(axis) == 0
             got = lax.ppermute(jnp.where(lower_side, tail, head), axis, [(0, 1), (1, 0)])
             below = got

time: 49 us -> 52 us (1.061)
  waiting for transfers between devices: 11 us -> 13.2 us
  local copies, waits for them, and re-layouts: 3.46 us -> 4.56 us
    ppermute x0 -> x1, waiting for transfers between devices: none -> 4.56 us  [extended(): lax.ppermute(jnp.concatenate([tail, head], axis=dim), axis, [(0, 1), (1,...]
    ppermute x2 -> x1, waiting for transfers between devices: 3.77 us -> 1.38 us  [extended(): lax.ppermute(jnp.where(lower_side, tail, head), axis, [(0, 1), (1, 0)])]
    ppermute x0 -> x1, starting transfers between devices: none -> 2 us  [extended(): lax.ppermute(jnp.concatenate([tail, head], axis=dim), axis, [(0, 1), (1,...]
    ppermute x2 -> x1, starting transfers between devices: 2.07 us -> 0.07 us  [extended(): lax.ppermute(jnp.where(lower_side, tail, head), axis, [(0, 1), (1, 0)])]
    slice x0 -> x4, local copies, waits for them, and re-layouts: none -> 1.13 us  [the longest x2 0.7 us: extended(): lax.slice_in_dim(cells, cells.shape[dim] - width, cells.shape[dim], axis=...]
    unnamed x13 -> x15, local copies, waits for them, and re-layouts: 0.05 us -> 0.88 us
    select_n x2 -> x1, other arithmetic: 1.24 us -> 0.93 us  [extended(): jnp.where(lower_side, tail, head)]
where the time goes in v23:
time: 52 us; the launch traced here: 51.7 us
  starting transfers between devices  16.1 us (31%)
  waiting for transfers between devices  13.2 us (25%)
  Pallas kernels  11 us (21%)
  other arithmetic  5.92 us (11%)
  local copies, waits for them, and re-layouts  4.56 us (9%)
  between operations  0.83 us (2%)
    pallas_call x1, Pallas kernels, upscale_windows(): pl.pallas_call(kernel, grid=(packs,), in_specs=[pl.BlockSpec(memory_space...  11 us
    ppermute x4, starting transfers between devices, doubling_gather(): got = lax.ppermute(values, axis, [(i, i ^ step) for i in range(count)])  10.3 us
    ppermute x4, waiting for transfers between devices, doubling_gather(): got = lax.ppermute(values, axis, [(i, i ^ step) for i in range(count)])  5.68 us
    ppermute x1, waiting for transfers between devices, extended(): lax.ppermute(jnp.concatenate([tail, head], axis=dim), axis, [(0, 1), (1,...  4.56 us
    ppermute x1, starting transfers between devices, extended(): got_first = lax.ppermute(jnp.where(even, tail, head), axis, first)  3.09 us
    ppermute x1, starting transfers between devices, extended(): lax.ppermute(jnp.concatenate([tail, head], axis=dim), axis, [(0, 1), (1,...  2 us
    concatenate x2, other arithmetic, extended(): cells = jnp.concatenate(parts, axis=dim)  1.78 us
    ppermute x1, waiting for transfers between devices, extended(): got_first = lax.ppermute(jnp.where(even, tail, head), axis, first)  1.58 us
  transfers between devices with their start and end apart: 8, of which 7 were waited for; matrix products, arithmetic and copies ran while one was open for 3% of the time, Pallas kernels for 0%

profile of v23, /device:TPU:0, one launch (start us, length us, event | category | flops | bytes accessed | tf_op | source)
XLA Modules:
  0.0 51.7 jit_solution(3347069897799572224)
XLA Ops:
  0.7 1.0 %convert_bitcast_fusion = f32[1,16,32,128]{3,2,1,0:T(8,128)S(1)} fusion(s32[16,32,128]{2,1,0:T(8,128)} %param.7), kind=kLoop, calls=%fused_computation.2 | loop fusion | flops 65536 | bytes 524288 | tf_op jit(solution)/shard_map/stack | solution.py:455
  1.7 0.9 %broadcast_select_fusion.3 = (f32[2,16,4,128]{3,2,1,0:T(4,128)S(1)}, f32[2,16,4,128]{3,2,1,0:T(4,128)S(1)}, f32[2,16,4,128]{3,2,1,0:T(4,128)S(1)}) fusion(pred[]{:T(512)S(6)} %eq.24, f32[1,16,32,128]{3,2,1,0:T(8,128)S(1)} %convert_bitcast_fusion, f32[1,16,32,128]{3,2,1,0:T(8,128)} %bitcast.57), kind=kLoop, calls=%fused_computation.35 | loop fusion | flops 49152 | bytes 720897 | tf_op jit(solution)/shard_map/jit(_where)/select_n | solution.py:42
  2.6 3.1 %collective-permute-start.1 = (f32[2,16,4,128]{3,2,1,0:T(4,128)S(1)}, f32[2,16,4,128]{3,2,1,0:T(4,128)S(1)}, u32[]{:S(2)}, u32[]{:S(2)}) collective-permute-start(f32[2,16,4,128]{3,2,1,0:T(4,128)S(1)} %bitcast.69), channel_id=1, source_target_pairs={{0,4},{4,0},{8,12},{12,8},{1,5},{5,1},{9,13},{13,9},{2,6},{6,2},{1... | collective-permute-start | bytes 196616 | tf_op jit(solution)/shard_map/ppermute | solution.py:41
  5.7 0.7 %collective-permute-start = (f32[2,16,4,128]{3,2,1,0:T(4,128)S(1)}, f32[2,16,4,128]{3,2,1,0:T(4,128)S(1)}, u32[]{:S(2)}, u32[]{:S(2)}) collective-permute-start(f32[2,16,4,128]{3,2,1,0:T(4,128)S(1)} %get-tuple-element.14), channel_id=1, source_target_pairs={{4,8},{8,4},{5,9},{9,5},{6,10},{10,6},{7,11},{11,7},{20,24},{24,20... | collective-permute-start | bytes 196616 | tf_op jit(solution)/shard_map/ppermute | solution.py:42
  6.4 1.6 %collective-permute-done.1 = f32[2,16,4,128]{3,2,1,0:T(4,128)S(1)} collective-permute-done((f32[2,16,4,128]{3,2,1,0:T(4,128)S(1)}, f32[2,16,4,128]{3,2,1,0:T(4,128)S(1)}, u32[]{:S(2)}, u32[]{:S(2)}) %collective-permute-start.1) | collective-permute-done | bytes 65568 | tf_op jit(solution)/shard_map/ppermute | solution.py:41
  8.0 0.9 %fusion = f32[2,4,40,128]{3,2,1,0:T(8,128)S(1)} fusion(f32[2,16,4,128]{3,2,1,0:T(4,128)S(1)} %bitcast.64, f32[2,16,4,128]{3,2,1,0:T(4,128)S(1)} %bitcast.61, f32[1,16,32,128]{3,2,1,0:T(8,128)S(1)} %convert_bitcast_fusion, f32[1,16,32,128]{3,2,1,0:T(8,128)} %bitcast.58, pred[]{:T(512)S(6)} %eq.26), kind=kLoop, calls=%fused_computation.5 | loop fusion | flops 286720 | bytes 819201 | tf_op jit(solution)/shard_map/jit(_where)/select_n | solution.py:34
  9.0 1.4 %collective-permute-done.2 = f32[2,4,40,128]{3,2,1,0:T(8,128)S(1)} collective-permute-done((f32[2,4,40,128]{3,2,1,0:T(8,128)S(1)}, f32[2,4,40,128]{3,2,1,0:T(8,128)S(1)}, u32[]{:S(2)}, u32[]{:S(2)}) %collective-permute-start.2) | collective-permute-done | bytes 163872 | tf_op jit(solution)/shard_map/ppermute | solution.py:34
  10.3 0.1 pad_maximum_fusion.1
  10.4 0.3 fusion.41
  10.8 0.4 copy.18
  11.1 0.4 copy.19
  11.6 2.0 %collective-permute-start.3 = (f32[2,24,40,8]{2,3,1,0:T(8,128)S(1)}, f32[2,24,40,8]{2,3,1,0:T(8,128)S(1)}, u32[]{:S(2)}, u32[]{:S(2)}) collective-permute-start(f32[2,24,40,8]{2,3,1,0:T(8,128)S(1)} %pad_maximum_fusion.2), channel_id=1, source_target_pairs={{0,2},{2,0},{1,3},{3,1},{4,6},{6,4},{5,7},{7,5},{8,10},{10,8},{9,1... | collective-permute-start | bytes 184328 | tf_op jit(solution)/shard_map/ppermute | solution.py:29
  13.7 0.6 %stack.48.bounds_ref = s32[6]{0:T(128)} concatenate(s32[1]{0:T(128)} %bitcast, s32[1]{0:T(128)} %bitcast.1, s32[1]{0:T(128)} %bitcast.2, s32[1]{0:T(128)} %bitcast.3, s32[1]{0:T(128)} %bitcast.4, s32[1]{0:T(128)} %bitcast.5), dimensions={0} | concatenate | bytes 48 | tf_op jit(solution)/shard_map/stack | solution.py:461
  14.3 4.6 %collective-permute-done.3 = f32[2,24,40,8]{2,3,1,0:T(8,128)S(1)} collective-permute-done((f32[2,24,40,8]{2,3,1,0:T(8,128)S(1)}, f32[2,24,40,8]{2,3,1,0:T(8,128)S(1)}, u32[]{:S(2)}, u32[]{:S(2)}) %collective-permute-start.3) | collective-permute-done | bytes 61472 | tf_op jit(solution)/shard_map/ppermute | solution.py:29
  18.9 0.4 copy.36
  19.3 0.4 copy.37
  19.7 1.7 %pad_maximum_fusion.raw_ref = f32[2,24,40,256]{3,2,1,0:T(8,128)} fusion(f32[2,24,40,4]{3,2,1,0:T(8,128)S(1)} %copy.37, f32[2,24,40,4]{3,2,1,0:T(8,128)S(1)} %copy.36, f32[2,4,40,128]{3,2,1,0:T(8,128)S(1)} %collective-permute-done.2, f32[2,16,4,128]{3,2,1,0:T(4,128)S(1)} %bitcast.66, f32[1,16,32,128]{3,2,1,0:T(8,128)S(1)} %convert_bitcast_fusion, ...), kind=kLoop, calls=%fused_computation | loop fusion | flops 3932160 | bytes 2847744 | tf_op jit(solution)/shard_map/concatenate | solution.py:53
  21.4 11.0 %shard_map.77 = f32[3,8,128]{2,1,0:T(8,128)} custom-call(f32[3,4]{1,0:T(4,128)} %table_ref.1, s32[6]{0:T(128)} %stack.48.bounds_ref, f32[2,24,40,256]{3,2,1,0:T(8,128)} %pad_maximum_fusion.raw_ref), custom_call_target="tpu_custom_call" | custom-call | tf_op jit(solution)/shard_map/pallas_call | solution.py:347
  32.4 0.7 %slice.249 = f32[3,3,120]{2,1,0:T(4,128)S(1)} slice(f32[3,8,128]{2,1,0:T(8,128)} %shard_map.77), slice={[0:3], [0:3], [0:120]} | slice | bytes 8640 | tf_op jit(solution)/shard_map/slice | solution.py:358
  33.1 0.1 reshape.68
  33.2 0.1 reduce_sum.9
  33.7 1.8 %collective-permute-start.4 = (f32[6,2,1,4]{3,1,2,0:T(2,128)S(1)}, f32[6,2,1,4]{3,1,2,0:T(2,128)S(1)}, u32[]{:S(2)}, u32[]{:S(2)}) collective-permute-start(f32[6,2,1,4]{3,1,2,0:T(2,128)S(1)} %constant_dynamic-update-slice_fusion), channel_id=1, source_target_pairs={{0,2},{2,0},{1,3},{3,1},{4,6},{6,4},{5,7},{7,5},{8,10},{10,8},{9,1... | collective-permute-start | bytes 584 | tf_op jit(solution)/shard_map/ppermute | solution.py:64
  35.5 1.9 %collective-permute-done.4 = f32[6,2,1,4]{3,1,2,0:T(2,128)S(1)} collective-permute-done((f32[6,2,1,4]{3,1,2,0:T(2,128)S(1)}, f32[6,2,1,4]{3,1,2,0:T(2,128)S(1)}, u32[]{:S(2)}, u32[]{:S(2)}) %collective-permute-start.4) | collective-permute-done | bytes 224 | tf_op jit(solution)/shard_map/ppermute | solution.py:64
  37.5 4.9 %collective-permute-start.5 = (f32[6,2,1,8]{3,1,2,0:T(2,128)S(1)}, f32[6,2,1,8]{3,1,2,0:T(2,128)S(1)}, u32[]{:S(2)}, u32[]{:S(2)}) collective-permute-start(f32[6,2,1,8]{3,1,2,0:T(2,128)S(1)} %maximum_select_fusion.3), channel_id=1, source_target_pairs={{0,4},{4,0},{8,12},{12,8},{1,5},{5,1},{9,13},{13,9},{2,6},{6,2},{1... | collective-permute-start | bytes 1160 | tf_op jit(solution)/shard_map/ppermute | solution.py:64
  42.4 1.6 %collective-permute-done.5 = f32[6,2,1,8]{3,1,2,0:T(2,128)S(1)} collective-permute-done((f32[6,2,1,8]{3,1,2,0:T(2,128)S(1)}, f32[6,2,1,8]{3,1,2,0:T(2,128)S(1)}, u32[]{:S(2)}, u32[]{:S(2)}) %collective-permute-start.5) | collective-permute-done | bytes 416 | tf_op jit(solution)/shard_map/ppermute | solution.py:64
  44.0 3.5 %collective-permute-start.6 = (f32[6,2,2,8]{3,1,2,0:T(2,128)S(1)}, f32[6,2,2,8]{3,1,2,0:T(2,128)S(1)}, u32[]{:S(2)}, u32[]{:S(2)}) collective-permute-start(f32[6,2,2,8]{3,1,2,0:T(2,128)S(1)} %maximum_select_fusion.2), channel_id=1, source_target_pairs={{0,8},{4,12},{8,0},{12,4},{1,9},{5,13},{9,1},{13,5},{2,10},{6,14},... | collective-permute-start | bytes 2312 | tf_op jit(solution)/shard_map/ppermute | solution.py:64
  47.6 1.7 %collective-permute-done.6 = f32[6,2,2,8]{3,1,2,0:T(2,128)S(1)} collective-permute-done((f32[6,2,2,8]{3,1,2,0:T(2,128)S(1)}, f32[6,2,2,8]{3,1,2,0:T(2,128)S(1)}, u32[]{:S(2)}, u32[]{:S(2)}) %collective-permute-start.6) | collective-permute-done | bytes 800 | tf_op jit(solution)/shard_map/ppermute | solution.py:64
  49.4 0.7 %reshape.70 = f32[3,2,1,4]{3,1,0,2:T(2,128)} reshape(f32[3,8]{1,0:T(4,128)S(1)} %bitcast.73) | data formatting | bytes 192 | tf_op jit(solution)/shard_map/reshape | solution.py:360
  50.0 0.5 collective-permute-done.7
  50.7 0.1 fusion.11
  50.9 0.1 fusion.18
  51.0 0.7 %dynamic-slice_divide_fusion = f32[2,1,4]{2,0,1:T(2,128)} fusion(f32[4,4,8]{2,0,1:T(4,128)S(1)} %get-tuple-element.24, s32[]{:T(128)S(6)} %select_n.125, s32[]{:T(128)S(6)} %select_n.126, s32[]{:T(128)S(6)} %select_n.127, f32[4,4,8]{2,0,1:T(4,128)S(1)} %get-tuple-element.32, f32[4,4,8]{2,0,1:T(4,128)S(1)} %get-tuple-element.13, ...), kind=kLoop, calls=%fused_computation.87 | loop fusion | flops 80 | bytes 396 | tf_op jit(solution)/shard_map/div | solution.py:381
  (38 shorter events, 1.1 us)
Async XLA Ops:
  0.6 9.7 %copy-start = (f32[16,32,128]{2,1,0:T(8,128)S(1)}, f32[16,32,128]{2,1,0:T(8,128)}, u32[]{:S(2)}) copy-start(f32[16,32,128]{2,1,0:T(8,128)} %param.6) | copy-start | bytes 786436
  2.6 5.3 %collective-permute-start.1 = (f32[2,16,4,128]{3,2,1,0:T(4,128)S(1)}, f32[2,16,4,128]{3,2,1,0:T(4,128)S(1)}, u32[]{:S(2)}, u32[]{:S(2)}) collective-permute-start(f32[2,16,4,128]{3,2,1,0:T(4,128)S(1)} %bitcast.69), channel_id=1, source_target_pairs={{0,4},{4,0},{8,12},{12,8},{1,5},{5,1},{9,13},{13,9},{2,6},{6,2},{1... | collective-permute-start | bytes 196616 | tf_op jit(solution)/shard_map/ppermute | solution.py:41
  5.7 2.2 %collective-permute-start = (f32[2,16,4,128]{3,2,1,0:T(4,128)S(1)}, f32[2,16,4,128]{3,2,1,0:T(4,128)S(1)}, u32[]{:S(2)}, u32[]{:S(2)}) collective-permute-start(f32[2,16,4,128]{3,2,1,0:T(4,128)S(1)} %get-tuple-element.14), channel_id=1, source_target_pairs={{4,8},{8,4},{5,9},{9,5},{6,10},{10,6},{7,11},{11,7},{20,24},{24,20... | collective-permute-start | bytes 196616 | tf_op jit(solution)/shard_map/ppermute | solution.py:42
  8.9 1.5 %collective-permute-start.2 = (f32[2,4,40,128]{3,2,1,0:T(8,128)S(1)}, f32[2,4,40,128]{3,2,1,0:T(8,128)S(1)}, u32[]{:S(2)}, u32[]{:S(2)}) collective-permute-start(f32[2,4,40,128]{3,2,1,0:T(8,128)S(1)} %fusion), channel_id=1, source_target_pairs={{0,1},{1,0},{2,3},{3,2},{4,5},{5,4},{6,7},{7,6},{8,9},{9,8},{10,11... | collective-permute-start | bytes 491528 | tf_op jit(solution)/shard_map/ppermute | solution.py:34
  11.6 7.2 %collective-permute-start.3 = (f32[2,24,40,8]{2,3,1,0:T(8,128)S(1)}, f32[2,24,40,8]{2,3,1,0:T(8,128)S(1)}, u32[]{:S(2)}, u32[]{:S(2)}) collective-permute-start(f32[2,24,40,8]{2,3,1,0:T(8,128)S(1)} %pad_maximum_fusion.2), channel_id=1, source_target_pairs={{0,2},{2,0},{1,3},{3,1},{4,6},{6,4},{5,7},{7,5},{8,10},{10,8},{9,1... | collective-permute-start | bytes 184328 | tf_op jit(solution)/shard_map/ppermute | solution.py:29
  21.4 12.3 %copy-start.1 = (f32[2,1,4]{2,1,0:T(1,128)S(1)}, f32[2,1,4]{2,1,0:T(1,128)}, u32[]{:S(2)}) copy-start(f32[2,1,4]{2,1,0:T(1,128)} %param.9) | copy-start | bytes 100
  21.4 12.3 %copy-start.2 = (f32[2,1,4]{2,1,0:T(1,128)S(1)}, f32[2,1,4]{2,1,0:T(1,128)}, u32[]{:S(2)}) copy-start(f32[2,1,4]{2,1,0:T(1,128)} %param.10) | copy-start | bytes 100
  21.4 12.4 %copy-start.3 = (f32[2,1,4]{2,1,0:T(1,128)S(1)}, f32[2,1,4]{2,1,0:T(1,128)}, u32[]{:S(2)}) copy-start(f32[2,1,4]{2,1,0:T(1,128)} %param.11) | copy-start | bytes 100
  33.7 3.7 %collective-permute-start.4 = (f32[6,2,1,4]{3,1,2,0:T(2,128)S(1)}, f32[6,2,1,4]{3,1,2,0:T(2,128)S(1)}, u32[]{:S(2)}, u32[]{:S(2)}) collective-permute-start(f32[6,2,1,4]{3,1,2,0:T(2,128)S(1)} %constant_dynamic-update-slice_fusion), channel_id=1, source_target_pairs={{0,2},{2,0},{1,3},{3,1},{4,6},{6,4},{5,7},{7,5},{8,10},{10,8},{9,1... | collective-permute-start | bytes 584 | tf_op jit(solution)/shard_map/ppermute | solution.py:64
  37.5 6.5 %collective-permute-start.5 = (f32[6,2,1,8]{3,1,2,0:T(2,128)S(1)}, f32[6,2,1,8]{3,1,2,0:T(2,128)S(1)}, u32[]{:S(2)}, u32[]{:S(2)}) collective-permute-start(f32[6,2,1,8]{3,1,2,0:T(2,128)S(1)} %maximum_select_fusion.3), channel_id=1, source_target_pairs={{0,4},{4,0},{8,12},{12,8},{1,5},{5,1},{9,13},{13,9},{2,6},{6,2},{1... | collective-permute-start | bytes 1160 | tf_op jit(solution)/shard_map/ppermute | solution.py:64
  44.0 5.2 %collective-permute-start.6 = (f32[6,2,2,8]{3,1,2,0:T(2,128)S(1)}, f32[6,2,2,8]{3,1,2,0:T(2,128)S(1)}, u32[]{:S(2)}, u32[]{:S(2)}) collective-permute-start(f32[6,2,2,8]{3,1,2,0:T(2,128)S(1)} %maximum_select_fusion.2), channel_id=1, source_target_pairs={{0,8},{4,12},{8,0},{12,4},{1,9},{5,13},{9,1},{13,5},{2,10},{6,14},... | collective-permute-start | bytes 2312 | tf_op jit(solution)/shard_map/ppermute | solution.py:64
  49.3 1.3 %collective-permute-start.7 = (f32[6,2,4,8]{3,1,2,0:T(2,128)S(1)}, f32[6,2,4,8]{3,1,2,0:T(2,128)S(1)}, u32[]{:S(2)}, u32[]{:S(2)}) collective-permute-start(f32[6,2,4,8]{3,1,2,0:T(2,128)S(1)} %maximum_select_fusion.1), channel_id=1, source_target_pairs={{0,1},{1,0},{2,3},{3,2},{4,5},{5,4},{6,7},{7,6},{8,9},{9,8},{10,11... | collective-permute-start | bytes 4616 | tf_op jit(solution)/shard_map/ppermute | solution.py:64

commit v24 on v17

--- a/solution.py
+++ b/solution.py
@@ -224,16 +224,16 @@
             slab = raw_ref[field, pl.ds(block_z * CCZ, span_z), pl.ds(block_x * CCX, span_x), :]
             return pltpu.roll(slab, shift, 2)[:, :, :LANES]
 
-        depth_at = depth_pos + block_z * CCZ
-        column_at = column_pos + block_x * CCX
-        row_at = row_pos + block_y * CCY
+        depth_at = block_z * CCZ
+        column_at = block_x * CCX
+        row_at = block_y * CCY
         held = (
-            (depth_at >= bounds_ref[0])
-            & (depth_at < bounds_ref[1])
-            & (column_at >= bounds_ref[2])
-            & (column_at < bounds_ref[3])
-            & (row_at >= bounds_ref[4])
-            & (row_at < bounds_ref[5])
+            (depth_pos >= bounds_ref[0] - depth_at)
+            & (depth_pos < bounds_ref[1] - depth_at)
+            & (column_pos >= bounds_ref[2] - column_at)
+            & (column_pos < bounds_ref[3] - column_at)
+            & (row_pos >= bounds_ref[4] - row_at)
+            & (row_pos < bounds_ref[5] - row_at)
         )
         noise = jnp.where(here, cut(0), noise)
         codes = jnp.where(here, cut(1), codes)

time: 49 us -> 49 us (level)
  no operation moved by 1% of the time
where the time goes in v24:
time: 49 us; the launch traced here: 48.7 us
  starting transfers between devices  16.1 us (33%)
  waiting for transfers between devices  11 us (22%)
  Pallas kernels  11 us (22%)
  other arithmetic  6.17 us (13%)
  local copies, waits for them, and re-layouts  3.46 us (7%)
  between operations  0.82 us (2%)
    pallas_call x1, Pallas kernels, upscale_windows(): pl.pallas_call(kernel, grid=(packs,), in_specs=[pl.BlockSpec(memory_space...  11 us
    ppermute x4, starting transfers between devices, doubling_gather(): got = lax.ppermute(values, axis, [(i, i ^ step) for i in range(count)])  10.3 us
    ppermute x4, waiting for transfers between devices, doubling_gather(): got = lax.ppermute(values, axis, [(i, i ^ step) for i in range(count)])  5.68 us
    ppermute x2, waiting for transfers between devices, extended(): lax.ppermute(jnp.where(lower_side, tail, head), axis, [(0, 1), (1, 0)])  3.77 us
    ppermute x1, starting transfers between devices, extended(): got_first = lax.ppermute(jnp.where(even, tail, head), axis, first)  3.09 us
    ppermute x2, starting transfers between devices, extended(): lax.ppermute(jnp.where(lower_side, tail, head), axis, [(0, 1), (1, 0)])  2.07 us
    concatenate x2, other arithmetic, extended(): cells = jnp.concatenate(parts, axis=dim)  1.78 us
    ppermute x1, waiting for transfers between devices, extended(): got_first = lax.ppermute(jnp.where(even, tail, head), axis, first)  1.58 us
  transfers between devices with their start and end apart: 8, of which 7 were waited for; matrix products, arithmetic and copies ran while one was open for 3% of the time, Pallas kernels for 0%

profile of v24, /device:TPU:0, one launch (start us, length us, event | category | flops | bytes accessed | tf_op | source)
XLA Modules:
  0.0 48.7 jit_solution(730604195508985111)
XLA Ops:
  0.7 1.0 %convert_bitcast_fusion = f32[1,16,32,128]{3,2,1,0:T(8,128)S(1)} fusion(s32[16,32,128]{2,1,0:T(8,128)} %param.7), kind=kLoop, calls=%fused_computation.3 | loop fusion | flops 65536 | bytes 524288 | tf_op jit(solution)/shard_map/stack | solution.py:451
  1.7 0.9 %broadcast_select_fusion.3 = (f32[2,16,4,128]{3,2,1,0:T(4,128)S(1)}, f32[2,16,4,128]{3,2,1,0:T(4,128)S(1)}, f32[2,16,4,128]{3,2,1,0:T(4,128)S(1)}) fusion(pred[]{:T(512)S(6)} %eq.27, f32[1,16,32,128]{3,2,1,0:T(8,128)S(1)} %convert_bitcast_fusion, f32[1,16,32,128]{3,2,1,0:T(8,128)} %bitcast.57), kind=kLoop, calls=%fused_computation.35 | loop fusion | flops 49152 | bytes 720897 | tf_op jit(solution)/shard_map/jit(_where)/select_n | solution.py:38
  2.6 3.1 %collective-permute-start.1 = (f32[2,16,4,128]{3,2,1,0:T(4,128)S(1)}, f32[2,16,4,128]{3,2,1,0:T(4,128)S(1)}, u32[]{:S(2)}, u32[]{:S(2)}) collective-permute-start(f32[2,16,4,128]{3,2,1,0:T(4,128)S(1)} %bitcast.69), channel_id=1, source_target_pairs={{0,4},{4,0},{8,12},{12,8},{1,5},{5,1},{9,13},{13,9},{2,6},{6,2},{1... | collective-permute-start | bytes 196616 | tf_op jit(solution)/shard_map/ppermute | solution.py:37
  5.7 0.7 %collective-permute-start = (f32[2,16,4,128]{3,2,1,0:T(4,128)S(1)}, f32[2,16,4,128]{3,2,1,0:T(4,128)S(1)}, u32[]{:S(2)}, u32[]{:S(2)}) collective-permute-start(f32[2,16,4,128]{3,2,1,0:T(4,128)S(1)} %get-tuple-element.14), channel_id=1, source_target_pairs={{4,8},{8,4},{5,9},{9,5},{6,10},{10,6},{7,11},{11,7},{20,24},{24,20... | collective-permute-start | bytes 196616 | tf_op jit(solution)/shard_map/ppermute | solution.py:38
  6.4 1.6 %collective-permute-done.1 = f32[2,16,4,128]{3,2,1,0:T(4,128)S(1)} collective-permute-done((f32[2,16,4,128]{3,2,1,0:T(4,128)S(1)}, f32[2,16,4,128]{3,2,1,0:T(4,128)S(1)}, u32[]{:S(2)}, u32[]{:S(2)}) %collective-permute-start.1) | collective-permute-done | bytes 65568 | tf_op jit(solution)/shard_map/ppermute | solution.py:37
  8.0 0.9 %fusion = f32[2,4,40,128]{3,2,1,0:T(8,128)S(1)} fusion(f32[2,16,4,128]{3,2,1,0:T(4,128)S(1)} %bitcast.64, f32[2,16,4,128]{3,2,1,0:T(4,128)S(1)} %bitcast.61, f32[1,16,32,128]{3,2,1,0:T(8,128)S(1)} %convert_bitcast_fusion, f32[1,16,32,128]{3,2,1,0:T(8,128)} %bitcast.58, pred[]{:T(512)S(6)} %eq.29), kind=kLoop, calls=%fused_computation.5 | loop fusion | flops 286720 | bytes 819201 | tf_op jit(solution)/shard_map/jit(_where)/select_n | solution.py:30
  9.0 1.4 %collective-permute-done.2 = f32[2,4,40,128]{3,2,1,0:T(8,128)S(1)} collective-permute-done((f32[2,4,40,128]{3,2,1,0:T(8,128)S(1)}, f32[2,4,40,128]{3,2,1,0:T(8,128)S(1)}, u32[]{:S(2)}, u32[]{:S(2)}) %collective-permute-start.2) | collective-permute-done | bytes 163872 | tf_op jit(solution)/shard_map/ppermute | solution.py:30
  10.3 0.1 pad_maximum_fusion.1
  10.4 0.3 slice_select_fusion
  10.8 0.4 copy.18
  11.1 2.0 %collective-permute-start.3 = (f32[2,24,40,4]{2,1,3,0:T(8,128)S(1)}, f32[2,24,40,4]{2,1,3,0:T(8,128)S(1)}, u32[]{:S(2)}, u32[]{:S(2)}) collective-permute-start(f32[2,24,40,4]{2,1,3,0:T(8,128)S(1)} %copy.18), channel_id=1, source_target_pairs={{0,2},{2,0},{1,3},{3,1},{4,6},{6,4},{5,7},{7,5},{8,10},{10,8},{9,1... | collective-permute-start | bytes 92168 | tf_op jit(solution)/shard_map/ppermute | solution.py:30
  13.2 0.6 %stack.48.bounds_ref = s32[6]{0:T(128)} concatenate(s32[1]{0:T(128)} %bitcast, s32[1]{0:T(128)} %bitcast.1, s32[1]{0:T(128)} %bitcast.2, s32[1]{0:T(128)} %bitcast.3, s32[1]{0:T(128)} %bitcast.4, s32[1]{0:T(128)} %bitcast.5), dimensions={0} | concatenate | bytes 48 | tf_op jit(solution)/shard_map/stack | solution.py:457
  13.9 2.4 %collective-permute-done.3 = f32[2,24,40,4]{2,1,3,0:T(8,128)S(1)} collective-permute-done((f32[2,24,40,4]{2,1,3,0:T(8,128)S(1)}, f32[2,24,40,4]{2,1,3,0:T(8,128)S(1)}, u32[]{:S(2)}, u32[]{:S(2)}) %collective-permute-start.3) | collective-permute-done | bytes 30752 | tf_op jit(solution)/shard_map/ppermute | solution.py:30
  16.2 0.4 copy.19
  16.7 1.7 %pad_maximum_fusion.raw_ref = f32[2,24,40,256]{3,2,1,0:T(8,128)} fusion(f32[2,24,40,4]{3,2,1,0:T(8,128)S(1)} %copy.19, f32[2,4,40,128]{3,2,1,0:T(8,128)S(1)} %collective-permute-done.2, f32[2,16,4,128]{3,2,1,0:T(4,128)S(1)} %bitcast.66, f32[1,16,32,128]{3,2,1,0:T(8,128)S(1)} %convert_bitcast_fusion, f32[1,16,32,128]{3,2,1,0:T(8,128)S(1)} %bitcast.60, ...), kind=kLoop, calls=%fused_computation | loop fusion | flops 3932160 | bytes 2817024 | tf_op jit(solution)/shard_map/concatenate | solution.py:49
  18.4 11.0 %shard_map.77 = f32[3,8,128]{2,1,0:T(8,128)} custom-call(f32[3,4]{1,0:T(4,128)} %table_ref.1, s32[6]{0:T(128)} %stack.48.bounds_ref, f32[2,24,40,256]{3,2,1,0:T(8,128)} %pad_maximum_fusion.raw_ref), custom_call_target="tpu_custom_call" | custom-call | tf_op jit(solution)/shard_map/pallas_call | solution.py:343
  29.4 0.7 %slice.239 = f32[3,3,120]{2,1,0:T(4,128)S(1)} slice(f32[3,8,128]{2,1,0:T(8,128)} %shard_map.77), slice={[0:3], [0:3], [0:120]} | slice | bytes 8640 | tf_op jit(solution)/shard_map/slice | solution.py:354
  30.1 0.1 reshape.68
  30.2 0.1 reduce_sum.9
  30.4 0.1 slice.197
  30.7 1.8 %collective-permute-start.4 = (f32[6,2,1,4]{3,1,2,0:T(2,128)S(1)}, f32[6,2,1,4]{3,1,2,0:T(2,128)S(1)}, u32[]{:S(2)}, u32[]{:S(2)}) collective-permute-start(f32[6,2,1,4]{3,1,2,0:T(2,128)S(1)} %constant_dynamic-update-slice_fusion), channel_id=1, source_target_pairs={{0,2},{2,0},{1,3},{3,1},{4,6},{6,4},{5,7},{7,5},{8,10},{10,8},{9,1... | collective-permute-start | bytes 584 | tf_op jit(solution)/shard_map/ppermute | solution.py:60
  32.5 1.9 %collective-permute-done.4 = f32[6,2,1,4]{3,1,2,0:T(2,128)S(1)} collective-permute-done((f32[6,2,1,4]{3,1,2,0:T(2,128)S(1)}, f32[6,2,1,4]{3,1,2,0:T(2,128)S(1)}, u32[]{:S(2)}, u32[]{:S(2)}) %collective-permute-start.4) | collective-permute-done | bytes 224 | tf_op jit(solution)/shard_map/ppermute | solution.py:60
  34.5 4.9 %collective-permute-start.5 = (f32[6,2,1,8]{3,1,2,0:T(2,128)S(1)}, f32[6,2,1,8]{3,1,2,0:T(2,128)S(1)}, u32[]{:S(2)}, u32[]{:S(2)}) collective-permute-start(f32[6,2,1,8]{3,1,2,0:T(2,128)S(1)} %maximum_select_fusion.3), channel_id=1, source_target_pairs={{0,4},{4,0},{8,12},{12,8},{1,5},{5,1},{9,13},{13,9},{2,6},{6,2},{1... | collective-permute-start | bytes 1160 | tf_op jit(solution)/shard_map/ppermute | solution.py:60
  39.4 1.6 %collective-permute-done.5 = f32[6,2,1,8]{3,1,2,0:T(2,128)S(1)} collective-permute-done((f32[6,2,1,8]{3,1,2,0:T(2,128)S(1)}, f32[6,2,1,8]{3,1,2,0:T(2,128)S(1)}, u32[]{:S(2)}, u32[]{:S(2)}) %collective-permute-start.5) | collective-permute-done | bytes 416 | tf_op jit(solution)/shard_map/ppermute | solution.py:60
  41.0 3.5 %collective-permute-start.6 = (f32[6,2,2,8]{3,1,2,0:T(2,128)S(1)}, f32[6,2,2,8]{3,1,2,0:T(2,128)S(1)}, u32[]{:S(2)}, u32[]{:S(2)}) collective-permute-start(f32[6,2,2,8]{3,1,2,0:T(2,128)S(1)} %maximum_select_fusion.2), channel_id=1, source_target_pairs={{0,8},{4,12},{8,0},{12,4},{1,9},{5,13},{9,1},{13,5},{2,10},{6,14},... | collective-permute-start | bytes 2312 | tf_op jit(solution)/shard_map/ppermute | solution.py:60
  44.6 1.7 %collective-permute-done.6 = f32[6,2,2,8]{3,1,2,0:T(2,128)S(1)} collective-permute-done((f32[6,2,2,8]{3,1,2,0:T(2,128)S(1)}, f32[6,2,2,8]{3,1,2,0:T(2,128)S(1)}, u32[]{:S(2)}, u32[]{:S(2)}) %collective-permute-start.6) | collective-permute-done | bytes 800 | tf_op jit(solution)/shard_map/ppermute | solution.py:60
  46.3 0.7 %reshape.70 = f32[3,2,1,4]{3,1,0,2:T(2,128)} reshape(f32[3,8]{1,0:T(4,128)S(1)} %bitcast.73) | data formatting | bytes 192 | tf_op jit(solution)/shard_map/reshape | solution.py:356
  47.0 0.5 %collective-permute-done.7 = f32[6,2,4,8]{3,1,2,0:T(2,128)S(1)} collective-permute-done((f32[6,2,4,8]{3,1,2,0:T(2,128)S(1)}, f32[6,2,4,8]{3,1,2,0:T(2,128)S(1)}, u32[]{:S(2)}, u32[]{:S(2)}) %collective-permute-start.7) | collective-permute-done | bytes 1568 | tf_op jit(solution)/shard_map/ppermute | solution.py:60
  47.6 0.1 fusion.3
  47.7 0.1 fusion.11
  47.9 0.1 fusion.18
  48.0 0.7 %dynamic-slice_divide_fusion = f32[2,1,4]{2,0,1:T(2,128)} fusion(f32[4,4,8]{2,0,1:T(4,128)S(1)} %get-tuple-element.20, s32[]{:T(128)S(6)} %select_n.135, s32[]{:T(128)S(6)} %select_n.136, s32[]{:T(128)S(6)} %select_n.137, f32[4,4,8]{2,0,1:T(4,128)S(1)} %get-tuple-element.28, f32[4,4,8]{2,0,1:T(4,128)S(1)} %get-tuple-element.13, ...), kind=kLoop, calls=%fused_computation.87 | loop fusion | flops 80 | bytes 396 | tf_op jit(solution)/shard_map/div | solution.py:377
  (34 shorter events, 0.8 us)
Async XLA Ops:
  0.6 9.7 %copy-start = (f32[16,32,128]{2,1,0:T(8,128)S(1)}, f32[16,32,128]{2,1,0:T(8,128)}, u32[]{:S(2)}) copy-start(f32[16,32,128]{2,1,0:T(8,128)} %param.6) | copy-start | bytes 786436
  2.6 5.3 %collective-permute-start.1 = (f32[2,16,4,128]{3,2,1,0:T(4,128)S(1)}, f32[2,16,4,128]{3,2,1,0:T(4,128)S(1)}, u32[]{:S(2)}, u32[]{:S(2)}) collective-permute-start(f32[2,16,4,128]{3,2,1,0:T(4,128)S(1)} %bitcast.69), channel_id=1, source_target_pairs={{0,4},{4,0},{8,12},{12,8},{1,5},{5,1},{9,13},{13,9},{2,6},{6,2},{1... | collective-permute-start | bytes 196616 | tf_op jit(solution)/shard_map/ppermute | solution.py:37
  5.7 2.2 %collective-permute-start = (f32[2,16,4,128]{3,2,1,0:T(4,128)S(1)}, f32[2,16,4,128]{3,2,1,0:T(4,128)S(1)}, u32[]{:S(2)}, u32[]{:S(2)}) collective-permute-start(f32[2,16,4,128]{3,2,1,0:T(4,128)S(1)} %get-tuple-element.14), channel_id=1, source_target_pairs={{4,8},{8,4},{5,9},{9,5},{6,10},{10,6},{7,11},{11,7},{20,24},{24,20... | collective-permute-start | bytes 196616 | tf_op jit(solution)/shard_map/ppermute | solution.py:38
  8.9 1.5 %collective-permute-start.2 = (f32[2,4,40,128]{3,2,1,0:T(8,128)S(1)}, f32[2,4,40,128]{3,2,1,0:T(8,128)S(1)}, u32[]{:S(2)}, u32[]{:S(2)}) collective-permute-start(f32[2,4,40,128]{3,2,1,0:T(8,128)S(1)} %fusion), channel_id=1, source_target_pairs={{0,1},{1,0},{2,3},{3,2},{4,5},{5,4},{6,7},{7,6},{8,9},{9,8},{10,11... | collective-permute-start | bytes 491528 | tf_op jit(solution)/shard_map/ppermute | solution.py:30
  11.1 5.1 %collective-permute-start.3 = (f32[2,24,40,4]{2,1,3,0:T(8,128)S(1)}, f32[2,24,40,4]{2,1,3,0:T(8,128)S(1)}, u32[]{:S(2)}, u32[]{:S(2)}) collective-permute-start(f32[2,24,40,4]{2,1,3,0:T(8,128)S(1)} %copy.18), channel_id=1, source_target_pairs={{0,2},{2,0},{1,3},{3,1},{4,6},{6,4},{5,7},{7,5},{8,10},{10,8},{9,1... | collective-permute-start | bytes 92168 | tf_op jit(solution)/shard_map/ppermute | solution.py:30
  18.3 12.3 %copy-start.1 = (f32[2,1,4]{2,1,0:T(1,128)S(1)}, f32[2,1,4]{2,1,0:T(1,128)}, u32[]{:S(2)}) copy-start(f32[2,1,4]{2,1,0:T(1,128)} %param.9) | copy-start | bytes 100
  18.3 12.3 %copy-start.2 = (f32[2,1,4]{2,1,0:T(1,128)S(1)}, f32[2,1,4]{2,1,0:T(1,128)}, u32[]{:S(2)}) copy-start(f32[2,1,4]{2,1,0:T(1,128)} %param.10) | copy-start | bytes 100
  18.3 12.4 %copy-start.3 = (f32[2,1,4]{2,1,0:T(1,128)S(1)}, f32[2,1,4]{2,1,0:T(1,128)}, u32[]{:S(2)}) copy-start(f32[2,1,4]{2,1,0:T(1,128)} %param.11) | copy-start | bytes 100
  30.7 3.7 %collective-permute-start.4 = (f32[6,2,1,4]{3,1,2,0:T(2,128)S(1)}, f32[6,2,1,4]{3,1,2,0:T(2,128)S(1)}, u32[]{:S(2)}, u32[]{:S(2)}) collective-permute-start(f32[6,2,1,4]{3,1,2,0:T(2,128)S(1)} %constant_dynamic-update-slice_fusion), channel_id=1, source_target_pairs={{0,2},{2,0},{1,3},{3,1},{4,6},{6,4},{5,7},{7,5},{8,10},{10,8},{9,1... | collective-permute-start | bytes 584 | tf_op jit(solution)/shard_map/ppermute | solution.py:60
  34.5 6.5 %collective-permute-start.5 = (f32[6,2,1,8]{3,1,2,0:T(2,128)S(1)}, f32[6,2,1,8]{3,1,2,0:T(2,128)S(1)}, u32[]{:S(2)}, u32[]{:S(2)}) collective-permute-start(f32[6,2,1,8]{3,1,2,0:T(2,128)S(1)} %maximum_select_fusion.3), channel_id=1, source_target_pairs={{0,4},{4,0},{8,12},{12,8},{1,5},{5,1},{9,13},{13,9},{2,6},{6,2},{1... | collective-permute-start | bytes 1160 | tf_op jit(solution)/shard_map/ppermute | solution.py:60
  41.0 5.2 %collective-permute-start.6 = (f32[6,2,2,8]{3,1,2,0:T(2,128)S(1)}, f32[6,2,2,8]{3,1,2,0:T(2,128)S(1)}, u32[]{:S(2)}, u32[]{:S(2)}) collective-permute-start(f32[6,2,2,8]{3,1,2,0:T(2,128)S(1)} %maximum_select_fusion.2), channel_id=1, source_target_pairs={{0,8},{4,12},{8,0},{12,4},{1,9},{5,13},{9,1},{13,5},{2,10},{6,14},... | collective-permute-start | bytes 2312 | tf_op jit(solution)/shard_map/ppermute | solution.py:60
  46.3 1.3 %collective-permute-start.7 = (f32[6,2,4,8]{3,1,2,0:T(2,128)S(1)}, f32[6,2,4,8]{3,1,2,0:T(2,128)S(1)}, u32[]{:S(2)}, u32[]{:S(2)}) collective-permute-start(f32[6,2,4,8]{3,1,2,0:T(2,128)S(1)} %maximum_select_fusion.1), channel_id=1, source_target_pairs={{0,1},{1,0},{2,3},{3,2},{4,5},{5,4},{6,7},{7,6},{8,9},{9,8},{10,11... | collective-permute-start | bytes 4616 | tf_op jit(solution)/shard_map/ppermute | solution.py:60

commit v25 on v17

--- a/solution.py
+++ b/solution.py
@@ -450,7 +450,7 @@
     index_y = lax.axis_index("gy")
     raw = jnp.stack([log_noise, facies.astype(jnp.float32)])
     wide = -(-(cols_len + 2 * RIM) // LANES) * LANES
-    raw = extended(raw, (("gx", 2), ("gz", 1), ("gy", 3)), RIM, wide)
+    raw = extended(raw, (("gx", 2), ("gy", 3), ("gz", 1)), RIM, wide)
     anchor_z = index_z * depth_len
     anchor_y = index_y * cols_len
     anchor_x = index_x * rows_len

time: 49 us -> 48.7 us (level)
  waiting for transfers between devices: 11 us -> 10.4 us
  starting transfers between devices: 16.1 us -> 16.6 us
    concatenate x2, other arithmetic: 1.78 us -> 2.82 us  [extended(): cells = jnp.concatenate(parts, axis=dim)]
    select_n x2, other arithmetic: 1.24 us -> 0.47 us  [extended(): jnp.where(lower_side, tail, head)]
where the time goes in v25:
time: 48.7 us; the launch traced here: 48.4 us
  starting transfers between devices  16.6 us (34%)
  Pallas kernels  11 us (23%)
  waiting for transfers between devices  10.4 us (21%)
  other arithmetic  6.4 us (13%)
  local copies, waits for them, and re-layouts  3.22 us (7%)
  between operations  0.85 us (2%)
    pallas_call x1, Pallas kernels, upscale_windows(): pl.pallas_call(kernel, grid=(packs,), in_specs=[pl.BlockSpec(memory_space...  11 us
    ppermute x4, starting transfers between devices, doubling_gather(): got = lax.ppermute(values, axis, [(i, i ^ step) for i in range(count)])  10.7 us
    ppermute x4, waiting for transfers between devices, doubling_gather(): got = lax.ppermute(values, axis, [(i, i ^ step) for i in range(count)])  5.49 us
    ppermute x2, waiting for transfers between devices, extended(): lax.ppermute(jnp.where(lower_side, tail, head), axis, [(0, 1), (1, 0)])  3.29 us
    ppermute x1, starting transfers between devices, extended(): got_first = lax.ppermute(jnp.where(even, tail, head), axis, first)  3.09 us
    concatenate x2, other arithmetic, extended(): cells = jnp.concatenate(parts, axis=dim)  2.82 us
    ppermute x2, starting transfers between devices, extended(): lax.ppermute(jnp.where(lower_side, tail, head), axis, [(0, 1), (1, 0)])  2.07 us
    ppermute x1, waiting for transfers between devices, extended(): got_first = lax.ppermute(jnp.where(even, tail, head), axis, first)  1.58 us
  transfers between devices with their start and end apart: 8, of which 7 were waited for; matrix products, arithmetic and copies ran while one was open for 3% of the time, Pallas kernels for 0%

profile of v25, /device:TPU:0, one launch (start us, length us, event | category | flops | bytes accessed | tf_op | source)
XLA Modules:
  0.0 48.4 jit_solution(9796407972089572441)
XLA Ops:
  0.6 1.0 %convert_bitcast_fusion = f32[1,16,32,128]{3,2,1,0:T(8,128)S(1)} fusion(s32[16,32,128]{2,1,0:T(8,128)} %param.7), kind=kLoop, calls=%fused_computation.10 | loop fusion | flops 65536 | bytes 524288 | tf_op jit(solution)/shard_map/stack | solution.py:451
  1.6 0.9 %broadcast_select_fusion.3 = (f32[2,16,4,128]{3,2,1,0:T(4,128)S(1)}, f32[2,16,4,128]{3,2,1,0:T(4,128)S(1)}, f32[2,16,4,128]{3,2,1,0:T(4,128)S(1)}) fusion(pred[]{:T(512)S(6)} %eq.27, f32[1,16,32,128]{3,2,1,0:T(8,128)S(1)} %convert_bitcast_fusion, f32[1,16,32,128]{3,2,1,0:T(8,128)} %bitcast.57), kind=kLoop, calls=%fused_computation.38 | loop fusion | flops 49152 | bytes 720897 | tf_op jit(solution)/shard_map/jit(_where)/select_n | solution.py:38
  2.5 3.1 %collective-permute-start.1 = (f32[2,16,4,128]{3,2,1,0:T(4,128)S(1)}, f32[2,16,4,128]{3,2,1,0:T(4,128)S(1)}, u32[]{:S(2)}, u32[]{:S(2)}) collective-permute-start(f32[2,16,4,128]{3,2,1,0:T(4,128)S(1)} %bitcast.69), channel_id=1, source_target_pairs={{0,4},{4,0},{8,12},{12,8},{1,5},{5,1},{9,13},{13,9},{2,6},{6,2},{1... | collective-permute-start | bytes 196616 | tf_op jit(solution)/shard_map/ppermute | solution.py:37
  5.6 0.7 %collective-permute-start = (f32[2,16,4,128]{3,2,1,0:T(4,128)S(1)}, f32[2,16,4,128]{3,2,1,0:T(4,128)S(1)}, u32[]{:S(2)}, u32[]{:S(2)}) collective-permute-start(f32[2,16,4,128]{3,2,1,0:T(4,128)S(1)} %get-tuple-element.14), channel_id=1, source_target_pairs={{4,8},{8,4},{5,9},{9,5},{6,10},{10,6},{7,11},{11,7},{20,24},{24,20... | collective-permute-start | bytes 196616 | tf_op jit(solution)/shard_map/ppermute | solution.py:38
  6.3 1.6 %collective-permute-done.1 = f32[2,16,4,128]{3,2,1,0:T(4,128)S(1)} collective-permute-done((f32[2,16,4,128]{3,2,1,0:T(4,128)S(1)}, f32[2,16,4,128]{3,2,1,0:T(4,128)S(1)}, u32[]{:S(2)}, u32[]{:S(2)}) %collective-permute-start.1) | collective-permute-done | bytes 65568 | tf_op jit(solution)/shard_map/ppermute | solution.py:37
  7.9 1.0 %pad_maximum_fusion.1 = f32[2,16,40,128]{3,2,1,0:T(8,128)S(1)} fusion(f32[2,16,4,128]{3,2,1,0:T(4,128)S(1)} %bitcast.64, f32[1,16,32,128]{3,2,1,0:T(8,128)S(1)} %convert_bitcast_fusion, f32[1,16,32,128]{3,2,1,0:T(8,128)} %bitcast.58, f32[2,16,4,128]{3,2,1,0:T(4,128)S(1)} %bitcast.61), kind=kLoop, calls=%fused_computation.2 | loop fusion | flops 491520 | bytes 1310720 | tf_op jit(solution)/shard_map/concatenate | solution.py:49
  8.9 0.2 slice_select_fusion
  9.2 0.3 copy.18
  9.5 2.0 %collective-permute-start.2 = (f32[2,16,40,4]{2,1,3,0:T(8,128)S(1)}, f32[2,16,40,4]{2,1,3,0:T(8,128)S(1)}, u32[]{:S(2)}, u32[]{:S(2)}) collective-permute-start(f32[2,16,40,4]{2,1,3,0:T(8,128)S(1)} %copy.18), channel_id=1, source_target_pairs={{0,2},{2,0},{1,3},{3,1},{4,6},{6,4},{5,7},{7,5},{8,10},{10,8},{9,1... | collective-permute-start | bytes 61448 | tf_op jit(solution)/shard_map/ppermute | solution.py:30
  11.5 2.3 %collective-permute-done.2 = f32[2,16,40,4]{2,1,3,0:T(8,128)S(1)} collective-permute-done((f32[2,16,40,4]{2,1,3,0:T(8,128)S(1)}, f32[2,16,40,4]{2,1,3,0:T(8,128)S(1)}, u32[]{:S(2)}, u32[]{:S(2)}) %collective-permute-start.2) | collective-permute-done | bytes 20512 | tf_op jit(solution)/shard_map/ppermute | solution.py:30
  13.8 0.3 copy.19
  14.2 0.2 fusion
  14.5 0.6 %stack.48.bounds_ref = s32[6]{0:T(128)} concatenate(s32[1]{0:T(128)} %bitcast, s32[1]{0:T(128)} %bitcast.1, s32[1]{0:T(128)} %bitcast.2, s32[1]{0:T(128)} %bitcast.3, s32[1]{0:T(128)} %bitcast.4, s32[1]{0:T(128)} %bitcast.5), dimensions={0} | concatenate | bytes 48 | tf_op jit(solution)/shard_map/stack | solution.py:457
  15.1 1.0 %collective-permute-done.3 = f32[2,4,40,256]{3,2,1,0:T(8,128)S(1)} collective-permute-done((f32[2,4,40,256]{3,2,1,0:T(8,128)S(1)}, f32[2,4,40,256]{3,2,1,0:T(8,128)S(1)}, u32[]{:S(2)}, u32[]{:S(2)}) %collective-permute-start.3) | collective-permute-done | bytes 327712 | tf_op jit(solution)/shard_map/ppermute | solution.py:30
  16.1 1.8 %pad_maximum_fusion.raw_ref = f32[2,24,40,256]{3,2,1,0:T(8,128)} fusion(f32[2,4,40,256]{3,2,1,0:T(8,128)S(1)} %collective-permute-done.3, f32[2,16,40,4]{3,2,1,0:T(8,128)S(1)} %copy.19, f32[2,16,40,120]{3,2,1,0:T(8,128)S(1)} %broadcast_in_dim.6, f32[2,16,4,128]{3,2,1,0:T(4,128)S(1)} %bitcast.66, f32[1,16,32,128]{3,2,1,0:T(8,128)S(1)} %convert_bitcast_fusion, ...), kind=kLoop, calls=%fused_computation | loop fusion | flops 3932160 | bytes 3584000 | tf_op jit(solution)/shard_map/concatenate | solution.py:49
  17.9 11.0 %shard_map.77 = f32[3,8,128]{2,1,0:T(8,128)} custom-call(f32[3,4]{1,0:T(4,128)} %table_ref.1, s32[6]{0:T(128)} %stack.48.bounds_ref, f32[2,24,40,256]{3,2,1,0:T(8,128)} %pad_maximum_fusion.raw_ref), custom_call_target="tpu_custom_call" | custom-call | tf_op jit(solution)/shard_map/pallas_call | solution.py:343
  28.9 0.7 %slice.239 = f32[3,3,120]{2,1,0:T(4,128)S(1)} slice(f32[3,8,128]{2,1,0:T(8,128)} %shard_map.77), slice={[0:3], [0:3], [0:120]} | slice | bytes 8640 | tf_op jit(solution)/shard_map/slice | solution.py:354
  29.6 0.1 reshape.68
  29.7 0.1 reduce_sum.9
  29.9 0.1 slice.197
  30.2 2.0 %collective-permute-start.4 = (f32[6,2,1,4]{3,1,2,0:T(2,128)S(1)}, f32[6,2,1,4]{3,1,2,0:T(2,128)S(1)}, u32[]{:S(2)}, u32[]{:S(2)}) collective-permute-start(f32[6,2,1,4]{3,1,2,0:T(2,128)S(1)} %constant_dynamic-update-slice_fusion), channel_id=1, source_target_pairs={{0,2},{2,0},{1,3},{3,1},{4,6},{6,4},{5,7},{7,5},{8,10},{10,8},{9,1... | collective-permute-start | bytes 584 | tf_op jit(solution)/shard_map/ppermute | solution.py:60
  32.2 1.7 %collective-permute-done.4 = f32[6,2,1,4]{3,1,2,0:T(2,128)S(1)} collective-permute-done((f32[6,2,1,4]{3,1,2,0:T(2,128)S(1)}, f32[6,2,1,4]{3,1,2,0:T(2,128)S(1)}, u32[]{:S(2)}, u32[]{:S(2)}) %collective-permute-start.4) | collective-permute-done | bytes 224 | tf_op jit(solution)/shard_map/ppermute | solution.py:60
  34.0 5.1 %collective-permute-start.5 = (f32[6,2,1,8]{3,1,2,0:T(2,128)S(1)}, f32[6,2,1,8]{3,1,2,0:T(2,128)S(1)}, u32[]{:S(2)}, u32[]{:S(2)}) collective-permute-start(f32[6,2,1,8]{3,1,2,0:T(2,128)S(1)} %maximum_select_fusion.3), channel_id=1, source_target_pairs={{0,4},{4,0},{8,12},{12,8},{1,5},{5,1},{9,13},{13,9},{2,6},{6,2},{1... | collective-permute-start | bytes 1160 | tf_op jit(solution)/shard_map/ppermute | solution.py:60
  39.1 1.6 %collective-permute-done.5 = f32[6,2,1,8]{3,1,2,0:T(2,128)S(1)} collective-permute-done((f32[6,2,1,8]{3,1,2,0:T(2,128)S(1)}, f32[6,2,1,8]{3,1,2,0:T(2,128)S(1)}, u32[]{:S(2)}, u32[]{:S(2)}) %collective-permute-start.5) | collective-permute-done | bytes 416 | tf_op jit(solution)/shard_map/ppermute | solution.py:60
  40.7 3.6 %collective-permute-start.6 = (f32[6,2,2,8]{3,1,2,0:T(2,128)S(1)}, f32[6,2,2,8]{3,1,2,0:T(2,128)S(1)}, u32[]{:S(2)}, u32[]{:S(2)}) collective-permute-start(f32[6,2,2,8]{3,1,2,0:T(2,128)S(1)} %maximum_select_fusion.2), channel_id=1, source_target_pairs={{0,8},{4,12},{8,0},{12,4},{1,9},{5,13},{9,1},{13,5},{2,10},{6,14},... | collective-permute-start | bytes 2312 | tf_op jit(solution)/shard_map/ppermute | solution.py:60
  44.3 1.7 %collective-permute-done.6 = f32[6,2,2,8]{3,1,2,0:T(2,128)S(1)} collective-permute-done((f32[6,2,2,8]{3,1,2,0:T(2,128)S(1)}, f32[6,2,2,8]{3,1,2,0:T(2,128)S(1)}, u32[]{:S(2)}, u32[]{:S(2)}) %collective-permute-start.6) | collective-permute-done | bytes 800 | tf_op jit(solution)/shard_map/ppermute | solution.py:60
  46.1 0.7 %reshape.70 = f32[3,2,1,4]{3,1,0,2:T(2,128)} reshape(f32[3,8]{1,0:T(4,128)S(1)} %bitcast.73) | data formatting | bytes 192 | tf_op jit(solution)/shard_map/reshape | solution.py:356
  46.8 0.5 %collective-permute-done.7 = f32[6,2,4,8]{3,1,2,0:T(2,128)S(1)} collective-permute-done((f32[6,2,4,8]{3,1,2,0:T(2,128)S(1)}, f32[6,2,4,8]{3,1,2,0:T(2,128)S(1)}, u32[]{:S(2)}, u32[]{:S(2)}) %collective-permute-start.7) | collective-permute-done | bytes 1568 | tf_op jit(solution)/shard_map/ppermute | solution.py:60
  47.4 0.1 fusion.3
  47.4 0.1 fusion.11
  47.7 0.1 fusion.18
  47.7 0.7 %dynamic-slice_divide_fusion = f32[2,1,4]{2,0,1:T(2,128)} fusion(f32[4,4,8]{2,0,1:T(4,128)S(1)} %get-tuple-element.20, s32[]{:T(128)S(6)} %select_n.135, s32[]{:T(128)S(6)} %select_n.136, s32[]{:T(128)S(6)} %select_n.137, f32[4,4,8]{2,0,1:T(4,128)S(1)} %get-tuple-element.28, f32[4,4,8]{2,0,1:T(4,128)S(1)} %get-tuple-element.13, ...), kind=kLoop, calls=%fused_computation.90 | loop fusion | flops 80 | bytes 396 | tf_op jit(solution)/shard_map/div | solution.py:377
  (33 shorter events, 0.8 us)
Async XLA Ops:
  2.5 5.3 %collective-permute-start.1 = (f32[2,16,4,128]{3,2,1,0:T(4,128)S(1)}, f32[2,16,4,128]{3,2,1,0:T(4,128)S(1)}, u32[]{:S(2)}, u32[]{:S(2)}) collective-permute-start(f32[2,16,4,128]{3,2,1,0:T(4,128)S(1)} %bitcast.69), channel_id=1, source_target_pairs={{0,4},{4,0},{8,12},{12,8},{1,5},{5,1},{9,13},{13,9},{2,6},{6,2},{1... | collective-permute-start | bytes 196616 | tf_op jit(solution)/shard_map/ppermute | solution.py:37
  5.6 2.2 %collective-permute-start = (f32[2,16,4,128]{3,2,1,0:T(4,128)S(1)}, f32[2,16,4,128]{3,2,1,0:T(4,128)S(1)}, u32[]{:S(2)}, u32[]{:S(2)}) collective-permute-start(f32[2,16,4,128]{3,2,1,0:T(4,128)S(1)} %get-tuple-element.14), channel_id=1, source_target_pairs={{4,8},{8,4},{5,9},{9,5},{6,10},{10,6},{7,11},{11,7},{20,24},{24,20... | collective-permute-start | bytes 196616 | tf_op jit(solution)/shard_map/ppermute | solution.py:38
  8.9 5.2 %copy-start = (f32[16,32,128]{2,1,0:T(8,128)S(1)}, f32[16,32,128]{2,1,0:T(8,128)}, u32[]{:S(2)}) copy-start(f32[16,32,128]{2,1,0:T(8,128)} %param.6) | copy-start | bytes 786436
  9.5 4.3 %collective-permute-start.2 = (f32[2,16,40,4]{2,1,3,0:T(8,128)S(1)}, f32[2,16,40,4]{2,1,3,0:T(8,128)S(1)}, u32[]{:S(2)}, u32[]{:S(2)}) collective-permute-start(f32[2,16,40,4]{2,1,3,0:T(8,128)S(1)} %copy.18), channel_id=1, source_target_pairs={{0,2},{2,0},{1,3},{3,1},{4,6},{6,4},{5,7},{7,5},{8,10},{10,8},{9,1... | collective-permute-start | bytes 61448 | tf_op jit(solution)/shard_map/ppermute | solution.py:30
  14.4 1.7 %collective-permute-start.3 = (f32[2,4,40,256]{3,2,1,0:T(8,128)S(1)}, f32[2,4,40,256]{3,2,1,0:T(8,128)S(1)}, u32[]{:S(2)}, u32[]{:S(2)}) collective-permute-start(f32[2,4,40,256]{3,2,1,0:T(8,128)S(1)} %fusion), channel_id=1, source_target_pairs={{0,1},{1,0},{2,3},{3,2},{4,5},{5,4},{6,7},{7,6},{8,9},{9,8},{10,11... | collective-permute-start | bytes 983048 | tf_op jit(solution)/shard_map/ppermute | solution.py:30
  17.9 12.3 %copy-start.1 = (f32[2,1,4]{2,1,0:T(1,128)S(1)}, f32[2,1,4]{2,1,0:T(1,128)}, u32[]{:S(2)}) copy-start(f32[2,1,4]{2,1,0:T(1,128)} %param.9) | copy-start | bytes 100
  17.9 12.3 %copy-start.2 = (f32[2,1,4]{2,1,0:T(1,128)S(1)}, f32[2,1,4]{2,1,0:T(1,128)}, u32[]{:S(2)}) copy-start(f32[2,1,4]{2,1,0:T(1,128)} %param.10) | copy-start | bytes 100
  17.9 12.3 %copy-start.3 = (f32[2,1,4]{2,1,0:T(1,128)S(1)}, f32[2,1,4]{2,1,0:T(1,128)}, u32[]{:S(2)}) copy-start(f32[2,1,4]{2,1,0:T(1,128)} %param.11) | copy-start | bytes 100
  30.2 3.7 %collective-permute-start.4 = (f32[6,2,1,4]{3,1,2,0:T(2,128)S(1)}, f32[6,2,1,4]{3,1,2,0:T(2,128)S(1)}, u32[]{:S(2)}, u32[]{:S(2)}) collective-permute-start(f32[6,2,1,4]{3,1,2,0:T(2,128)S(1)} %constant_dynamic-update-slice_fusion), channel_id=1, source_target_pairs={{0,2},{2,0},{1,3},{3,1},{4,6},{6,4},{5,7},{7,5},{8,10},{10,8},{9,1... | collective-permute-start | bytes 584 | tf_op jit(solution)/shard_map/ppermute | solution.py:60
  34.0 6.7 %collective-permute-start.5 = (f32[6,2,1,8]{3,1,2,0:T(2,128)S(1)}, f32[6,2,1,8]{3,1,2,0:T(2,128)S(1)}, u32[]{:S(2)}, u32[]{:S(2)}) collective-permute-start(f32[6,2,1,8]{3,1,2,0:T(2,128)S(1)} %maximum_select_fusion.3), channel_id=1, source_target_pairs={{0,4},{4,0},{8,12},{12,8},{1,5},{5,1},{9,13},{13,9},{2,6},{6,2},{1... | collective-permute-start | bytes 1160 | tf_op jit(solution)/shard_map/ppermute | solution.py:60
  40.7 5.2 %collective-permute-start.6 = (f32[6,2,2,8]{3,1,2,0:T(2,128)S(1)}, f32[6,2,2,8]{3,1,2,0:T(2,128)S(1)}, u32[]{:S(2)}, u32[]{:S(2)}) collective-permute-start(f32[6,2,2,8]{3,1,2,0:T(2,128)S(1)} %maximum_select_fusion.2), channel_id=1, source_target_pairs={{0,8},{4,12},{8,0},{12,4},{1,9},{5,13},{9,1},{13,5},{2,10},{6,14},... | collective-permute-start | bytes 2312 | tf_op jit(solution)/shard_map/ppermute | solution.py:60
  46.0 1.3 %collective-permute-start.7 = (f32[6,2,4,8]{3,1,2,0:T(2,128)S(1)}, f32[6,2,4,8]{3,1,2,0:T(2,128)S(1)}, u32[]{:S(2)}, u32[]{:S(2)}) collective-permute-start(f32[6,2,4,8]{3,1,2,0:T(2,128)S(1)} %maximum_select_fusion.1), channel_id=1, source_target_pairs={{0,1},{1,0},{2,3},{3,2},{4,5},{5,4},{6,7},{7,6},{8,9},{9,8},{10,11... | collective-permute-start | bytes 4616 | tf_op jit(solution)/shard_map/ppermute | solution.py:60

commit v26 on v17

--- a/solution.py
+++ b/solution.py
@@ -327,7 +327,6 @@
         total = jnp.sum(flux, axis=0)
         total = jnp.sum(total, axis=0, keepdims=True)
         rows.append(total * (0.5 / area))
-    rows.append(jnp.zeros((8 - len(rows), LANES), jnp.float32))
     o_ref[0] = jnp.concatenate(rows, axis=0)
 
 
@@ -348,10 +347,10 @@
             pl.BlockSpec(memory_space=pltpu.SMEM),
             pl.BlockSpec(raw.shape, lambda p: (0, 0, 0, 0)),
         ],
-        out_specs=pl.BlockSpec((1, 8, LANES), lambda p: (p, 0, 0)),
-        out_shape=jax.ShapeDtypeStruct((packs, 8, LANES), jnp.float32),
+        out_specs=pl.BlockSpec((1, 3, LANES), lambda p: (p, 0, 0)),
+        out_shape=jax.ShapeDtypeStruct((packs, 3, LANES), jnp.float32),
     )(facies_table, bounds, raw)
-    sums = sums[:, :3, : segments * span_y].reshape(packs, 3, segments, span_y).sum(axis=3)
+    sums = sums[:, :, : segments * span_y].reshape(packs, 3, segments, span_y).sum(axis=3)
     sums = sums.transpose(1, 0, 2).reshape(3, packs * segments)[:, :count]
     return sums.reshape((3, count_z, count_x, count_y))
 

time: 49 us -> 48.9 us (level)
    slice x1 -> x0, local copies, waits for them, and re-layouts: 0.71 us -> none  [upscale_windows(): sums[:, :3, :segments * span_y].reshape(packs, 3, segments, span_y)]
    reshape x1, local copies, waits for them, and re-layouts: 0.09 us -> 0.77 us  [upscale_windows(): sums[:, :, :segments * span_y].reshape(packs, 3, segments, span_y)]
where the time goes in v26:
time: 48.9 us; the launch traced here: 48.6 us
  starting transfers between devices  16.1 us (33%)
  waiting for transfers between devices  11 us (22%)
  Pallas kernels  11 us (22%)
  other arithmetic  6.17 us (13%)
  local copies, waits for them, and re-layouts  3.44 us (7%)
  between operations  0.83 us (2%)
    pallas_call x1, Pallas kernels, upscale_windows(): pl.pallas_call(kernel, grid=(packs,), in_specs=[pl.BlockSpec(memory_space...  11 us
    ppermute x4, starting transfers between devices, doubling_gather(): got = lax.ppermute(values, axis, [(i, i ^ step) for i in range(count)])  10.3 us
    ppermute x4, waiting for transfers between devices, doubling_gather(): got = lax.ppermute(values, axis, [(i, i ^ step) for i in range(count)])  5.68 us
    ppermute x2, waiting for transfers between devices, extended(): lax.ppermute(jnp.where(lower_side, tail, head), axis, [(0, 1), (1, 0)])  3.77 us
    ppermute x1, starting transfers between devices, extended(): got_first = lax.ppermute(jnp.where(even, tail, head), axis, first)  3.09 us
    ppermute x2, starting transfers between devices, extended(): lax.ppermute(jnp.where(lower_side, tail, head), axis, [(0, 1), (1, 0)])  2.07 us
    concatenate x2, other arithmetic, extended(): cells = jnp.concatenate(parts, axis=dim)  1.78 us
    ppermute x1, waiting for transfers between devices, extended(): got_first = lax.ppermute(jnp.where(even, tail, head), axis, first)  1.58 us
  transfers between devices with their start and end apart: 8, of which 7 were waited for; matrix products, arithmetic and copies ran while one was open for 3% of the time, Pallas kernels for 0%

profile of v26, /device:TPU:0, one launch (start us, length us, event | category | flops | bytes accessed | tf_op | source)
XLA Modules:
  0.0 48.6 jit_solution(8212438584112099277)
XLA Ops:
  0.7 1.0 %convert_bitcast_fusion = f32[1,16,32,128]{3,2,1,0:T(8,128)S(1)} fusion(s32[16,32,128]{2,1,0:T(8,128)} %param.7), kind=kLoop, calls=%fused_computation.3 | loop fusion | flops 65536 | bytes 524288 | tf_op jit(solution)/shard_map/stack | solution.py:450
  1.7 0.9 %broadcast_select_fusion.3 = (f32[2,16,4,128]{3,2,1,0:T(4,128)S(1)}, f32[2,16,4,128]{3,2,1,0:T(4,128)S(1)}, f32[2,16,4,128]{3,2,1,0:T(4,128)S(1)}) fusion(pred[]{:T(512)S(6)} %eq.27, f32[1,16,32,128]{3,2,1,0:T(8,128)S(1)} %convert_bitcast_fusion, f32[1,16,32,128]{3,2,1,0:T(8,128)} %bitcast.58), kind=kLoop, calls=%fused_computation.35 | loop fusion | flops 49152 | bytes 720897 | tf_op jit(solution)/shard_map/jit(_where)/select_n | solution.py:38
  2.6 3.1 %collective-permute-start.1 = (f32[2,16,4,128]{3,2,1,0:T(4,128)S(1)}, f32[2,16,4,128]{3,2,1,0:T(4,128)S(1)}, u32[]{:S(2)}, u32[]{:S(2)}) collective-permute-start(f32[2,16,4,128]{3,2,1,0:T(4,128)S(1)} %bitcast.70), channel_id=1, source_target_pairs={{0,4},{4,0},{8,12},{12,8},{1,5},{5,1},{9,13},{13,9},{2,6},{6,2},{1... | collective-permute-start | bytes 196616 | tf_op jit(solution)/shard_map/ppermute | solution.py:37
  5.7 0.7 %collective-permute-start = (f32[2,16,4,128]{3,2,1,0:T(4,128)S(1)}, f32[2,16,4,128]{3,2,1,0:T(4,128)S(1)}, u32[]{:S(2)}, u32[]{:S(2)}) collective-permute-start(f32[2,16,4,128]{3,2,1,0:T(4,128)S(1)} %get-tuple-element.14), channel_id=1, source_target_pairs={{4,8},{8,4},{5,9},{9,5},{6,10},{10,6},{7,11},{11,7},{20,24},{24,20... | collective-permute-start | bytes 196616 | tf_op jit(solution)/shard_map/ppermute | solution.py:38
  6.4 1.6 %collective-permute-done.1 = f32[2,16,4,128]{3,2,1,0:T(4,128)S(1)} collective-permute-done((f32[2,16,4,128]{3,2,1,0:T(4,128)S(1)}, f32[2,16,4,128]{3,2,1,0:T(4,128)S(1)}, u32[]{:S(2)}, u32[]{:S(2)}) %collective-permute-start.1) | collective-permute-done | bytes 65568 | tf_op jit(solution)/shard_map/ppermute | solution.py:37
  8.0 0.9 %fusion = f32[2,4,40,128]{3,2,1,0:T(8,128)S(1)} fusion(f32[2,16,4,128]{3,2,1,0:T(4,128)S(1)} %bitcast.65, f32[2,16,4,128]{3,2,1,0:T(4,128)S(1)} %bitcast.62, f32[1,16,32,128]{3,2,1,0:T(8,128)S(1)} %convert_bitcast_fusion, f32[1,16,32,128]{3,2,1,0:T(8,128)} %bitcast.59, pred[]{:T(512)S(6)} %eq.29), kind=kLoop, calls=%fused_computation.5 | loop fusion | flops 286720 | bytes 819201 | tf_op jit(solution)/shard_map/jit(_where)/select_n | solution.py:30
  9.0 1.4 %collective-permute-done.2 = f32[2,4,40,128]{3,2,1,0:T(8,128)S(1)} collective-permute-done((f32[2,4,40,128]{3,2,1,0:T(8,128)S(1)}, f32[2,4,40,128]{3,2,1,0:T(8,128)S(1)}, u32[]{:S(2)}, u32[]{:S(2)}) %collective-permute-start.2) | collective-permute-done | bytes 163872 | tf_op jit(solution)/shard_map/ppermute | solution.py:30
  10.3 0.1 pad_maximum_fusion.1
  10.4 0.3 slice_select_fusion
  10.8 0.4 copy.18
  11.1 2.0 %collective-permute-start.3 = (f32[2,24,40,4]{2,1,3,0:T(8,128)S(1)}, f32[2,24,40,4]{2,1,3,0:T(8,128)S(1)}, u32[]{:S(2)}, u32[]{:S(2)}) collective-permute-start(f32[2,24,40,4]{2,1,3,0:T(8,128)S(1)} %copy.18), channel_id=1, source_target_pairs={{0,2},{2,0},{1,3},{3,1},{4,6},{6,4},{5,7},{7,5},{8,10},{10,8},{9,1... | collective-permute-start | bytes 92168 | tf_op jit(solution)/shard_map/ppermute | solution.py:30
  13.2 0.6 %stack.48.bounds_ref = s32[6]{0:T(128)} concatenate(s32[1]{0:T(128)} %bitcast, s32[1]{0:T(128)} %bitcast.1, s32[1]{0:T(128)} %bitcast.2, s32[1]{0:T(128)} %bitcast.3, s32[1]{0:T(128)} %bitcast.4, s32[1]{0:T(128)} %bitcast.5), dimensions={0} | concatenate | bytes 48 | tf_op jit(solution)/shard_map/stack | solution.py:456
  13.9 2.4 %collective-permute-done.3 = f32[2,24,40,4]{2,1,3,0:T(8,128)S(1)} collective-permute-done((f32[2,24,40,4]{2,1,3,0:T(8,128)S(1)}, f32[2,24,40,4]{2,1,3,0:T(8,128)S(1)}, u32[]{:S(2)}, u32[]{:S(2)}) %collective-permute-start.3) | collective-permute-done | bytes 30752 | tf_op jit(solution)/shard_map/ppermute | solution.py:30
  16.2 0.4 copy.19
  16.7 1.7 %pad_maximum_fusion.raw_ref = f32[2,24,40,256]{3,2,1,0:T(8,128)} fusion(f32[2,24,40,4]{3,2,1,0:T(8,128)S(1)} %copy.19, f32[2,4,40,128]{3,2,1,0:T(8,128)S(1)} %collective-permute-done.2, f32[2,16,4,128]{3,2,1,0:T(4,128)S(1)} %bitcast.67, f32[1,16,32,128]{3,2,1,0:T(8,128)S(1)} %convert_bitcast_fusion, f32[1,16,32,128]{3,2,1,0:T(8,128)S(1)} %bitcast.61, ...), kind=kLoop, calls=%fused_computation | loop fusion | flops 3932160 | bytes 2817024 | tf_op jit(solution)/shard_map/concatenate | solution.py:49
  18.4 11.0 %shard_map.77 = f32[3,3,128]{2,1,0:T(4,128)} custom-call(f32[3,4]{1,0:T(4,128)} %table_ref.1, s32[6]{0:T(128)} %stack.48.bounds_ref, f32[2,24,40,256]{3,2,1,0:T(8,128)} %pad_maximum_fusion.raw_ref), custom_call_target="tpu_custom_call" | custom-call | tf_op jit(solution)/shard_map/pallas_call | solution.py:342
  29.4 0.8 %reshape.68 = f32[3,3,3,40]{3,2,1,0:T(4,128)S(1)} reshape(f32[3,3,120]{2,1,0:T(4,128)} %bitcast.74) | data formatting | bytes 8640 | tf_op jit(solution)/shard_map/reshape | solution.py:353
  30.2 0.1 reduce_sum.9
  30.3 0.1 reshape.69
  30.4 0.1 slice.197
  30.7 1.8 %collective-permute-start.4 = (f32[6,2,1,4]{3,1,2,0:T(2,128)S(1)}, f32[6,2,1,4]{3,1,2,0:T(2,128)S(1)}, u32[]{:S(2)}, u32[]{:S(2)}) collective-permute-start(f32[6,2,1,4]{3,1,2,0:T(2,128)S(1)} %constant_dynamic-update-slice_fusion), channel_id=1, source_target_pairs={{0,2},{2,0},{1,3},{3,1},{4,6},{6,4},{5,7},{7,5},{8,10},{10,8},{9,1... | collective-permute-start | bytes 584 | tf_op jit(solution)/shard_map/ppermute | solution.py:60
  32.5 1.9 %collective-permute-done.4 = f32[6,2,1,4]{3,1,2,0:T(2,128)S(1)} collective-permute-done((f32[6,2,1,4]{3,1,2,0:T(2,128)S(1)}, f32[6,2,1,4]{3,1,2,0:T(2,128)S(1)}, u32[]{:S(2)}, u32[]{:S(2)}) %collective-permute-start.4) | collective-permute-done | bytes 224 | tf_op jit(solution)/shard_map/ppermute | solution.py:60
  34.5 4.9 %collective-permute-start.5 = (f32[6,2,1,8]{3,1,2,0:T(2,128)S(1)}, f32[6,2,1,8]{3,1,2,0:T(2,128)S(1)}, u32[]{:S(2)}, u32[]{:S(2)}) collective-permute-start(f32[6,2,1,8]{3,1,2,0:T(2,128)S(1)} %maximum_select_fusion.3), channel_id=1, source_target_pairs={{0,4},{4,0},{8,12},{12,8},{1,5},{5,1},{9,13},{13,9},{2,6},{6,2},{1... | collective-permute-start | bytes 1160 | tf_op jit(solution)/shard_map/ppermute | solution.py:60
  39.4 1.6 %collective-permute-done.5 = f32[6,2,1,8]{3,1,2,0:T(2,128)S(1)} collective-permute-done((f32[6,2,1,8]{3,1,2,0:T(2,128)S(1)}, f32[6,2,1,8]{3,1,2,0:T(2,128)S(1)}, u32[]{:S(2)}, u32[]{:S(2)}) %collective-permute-start.5) | collective-permute-done | bytes 416 | tf_op jit(solution)/shard_map/ppermute | solution.py:60
  41.0 3.5 %collective-permute-start.6 = (f32[6,2,2,8]{3,1,2,0:T(2,128)S(1)}, f32[6,2,2,8]{3,1,2,0:T(2,128)S(1)}, u32[]{:S(2)}, u32[]{:S(2)}) collective-permute-start(f32[6,2,2,8]{3,1,2,0:T(2,128)S(1)} %maximum_select_fusion.2), channel_id=1, source_target_pairs={{0,8},{4,12},{8,0},{12,4},{1,9},{5,13},{9,1},{13,5},{2,10},{6,14},... | collective-permute-start | bytes 2312 | tf_op jit(solution)/shard_map/ppermute | solution.py:60
  44.5 1.7 %collective-permute-done.6 = f32[6,2,2,8]{3,1,2,0:T(2,128)S(1)} collective-permute-done((f32[6,2,2,8]{3,1,2,0:T(2,128)S(1)}, f32[6,2,2,8]{3,1,2,0:T(2,128)S(1)}, u32[]{:S(2)}, u32[]{:S(2)}) %collective-permute-start.6) | collective-permute-done | bytes 800 | tf_op jit(solution)/shard_map/ppermute | solution.py:60
  46.3 0.7 %reshape.70 = f32[3,2,1,4]{3,1,0,2:T(2,128)} reshape(f32[3,8]{1,0:T(4,128)S(1)} %bitcast.75) | data formatting | bytes 192 | tf_op jit(solution)/shard_map/reshape | solution.py:355
  47.0 0.5 %collective-permute-done.7 = f32[6,2,4,8]{3,1,2,0:T(2,128)S(1)} collective-permute-done((f32[6,2,4,8]{3,1,2,0:T(2,128)S(1)}, f32[6,2,4,8]{3,1,2,0:T(2,128)S(1)}, u32[]{:S(2)}, u32[]{:S(2)}) %collective-permute-start.7) | collective-permute-done | bytes 1568 | tf_op jit(solution)/shard_map/ppermute | solution.py:60
  47.6 0.1 fusion.3
  47.7 0.1 fusion.11
  47.9 0.1 fusion.18
  48.0 0.7 %dynamic-slice_divide_fusion = f32[2,1,4]{2,0,1:T(2,128)} fusion(f32[4,4,8]{2,0,1:T(4,128)S(1)} %get-tuple-element.20, s32[]{:T(128)S(6)} %select_n.135, s32[]{:T(128)S(6)} %select_n.136, s32[]{:T(128)S(6)} %select_n.137, f32[4,4,8]{2,0,1:T(4,128)S(1)} %get-tuple-element.28, f32[4,4,8]{2,0,1:T(4,128)S(1)} %get-tuple-element.13, ...), kind=kLoop, calls=%fused_computation.87 | loop fusion | flops 80 | bytes 396 | tf_op jit(solution)/shard_map/div | solution.py:376
  (33 shorter events, 0.7 us)
Async XLA Ops:
  0.6 9.7 %copy-start = (f32[16,32,128]{2,1,0:T(8,128)S(1)}, f32[16,32,128]{2,1,0:T(8,128)}, u32[]{:S(2)}) copy-start(f32[16,32,128]{2,1,0:T(8,128)} %param.6) | copy-start | bytes 786436
  2.6 5.3 %collective-permute-start.1 = (f32[2,16,4,128]{3,2,1,0:T(4,128)S(1)}, f32[2,16,4,128]{3,2,1,0:T(4,128)S(1)}, u32[]{:S(2)}, u32[]{:S(2)}) collective-permute-start(f32[2,16,4,128]{3,2,1,0:T(4,128)S(1)} %bitcast.70), channel_id=1, source_target_pairs={{0,4},{4,0},{8,12},{12,8},{1,5},{5,1},{9,13},{13,9},{2,6},{6,2},{1... | collective-permute-start | bytes 196616 | tf_op jit(solution)/shard_map/ppermute | solution.py:37
  5.7 2.2 %collective-permute-start = (f32[2,16,4,128]{3,2,1,0:T(4,128)S(1)}, f32[2,16,4,128]{3,2,1,0:T(4,128)S(1)}, u32[]{:S(2)}, u32[]{:S(2)}) collective-permute-start(f32[2,16,4,128]{3,2,1,0:T(4,128)S(1)} %get-tuple-element.14), channel_id=1, source_target_pairs={{4,8},{8,4},{5,9},{9,5},{6,10},{10,6},{7,11},{11,7},{20,24},{24,20... | collective-permute-start | bytes 196616 | tf_op jit(solution)/shard_map/ppermute | solution.py:38
  8.9 1.5 %collective-permute-start.2 = (f32[2,4,40,128]{3,2,1,0:T(8,128)S(1)}, f32[2,4,40,128]{3,2,1,0:T(8,128)S(1)}, u32[]{:S(2)}, u32[]{:S(2)}) collective-permute-start(f32[2,4,40,128]{3,2,1,0:T(8,128)S(1)} %fusion), channel_id=1, source_target_pairs={{0,1},{1,0},{2,3},{3,2},{4,5},{5,4},{6,7},{7,6},{8,9},{9,8},{10,11... | collective-permute-start | bytes 491528 | tf_op jit(solution)/shard_map/ppermute | solution.py:30
  11.1 5.1 %collective-permute-start.3 = (f32[2,24,40,4]{2,1,3,0:T(8,128)S(1)}, f32[2,24,40,4]{2,1,3,0:T(8,128)S(1)}, u32[]{:S(2)}, u32[]{:S(2)}) collective-permute-start(f32[2,24,40,4]{2,1,3,0:T(8,128)S(1)} %copy.18), channel_id=1, source_target_pairs={{0,2},{2,0},{1,3},{3,1},{4,6},{6,4},{5,7},{7,5},{8,10},{10,8},{9,1... | collective-permute-start | bytes 92168 | tf_op jit(solution)/shard_map/ppermute | solution.py:30
  18.3 12.3 %copy-start.1 = (f32[2,1,4]{2,1,0:T(1,128)S(1)}, f32[2,1,4]{2,1,0:T(1,128)}, u32[]{:S(2)}) copy-start(f32[2,1,4]{2,1,0:T(1,128)} %param.9) | copy-start | bytes 100
  18.3 12.3 %copy-start.2 = (f32[2,1,4]{2,1,0:T(1,128)S(1)}, f32[2,1,4]{2,1,0:T(1,128)}, u32[]{:S(2)}) copy-start(f32[2,1,4]{2,1,0:T(1,128)} %param.10) | copy-start | bytes 100
  18.3 12.3 %copy-start.3 = (f32[2,1,4]{2,1,0:T(1,128)S(1)}, f32[2,1,4]{2,1,0:T(1,128)}, u32[]{:S(2)}) copy-start(f32[2,1,4]{2,1,0:T(1,128)} %param.11) | copy-start | bytes 100
  30.7 3.7 %collective-permute-start.4 = (f32[6,2,1,4]{3,1,2,0:T(2,128)S(1)}, f32[6,2,1,4]{3,1,2,0:T(2,128)S(1)}, u32[]{:S(2)}, u32[]{:S(2)}) collective-permute-start(f32[6,2,1,4]{3,1,2,0:T(2,128)S(1)} %constant_dynamic-update-slice_fusion), channel_id=1, source_target_pairs={{0,2},{2,0},{1,3},{3,1},{4,6},{6,4},{5,7},{7,5},{8,10},{10,8},{9,1... | collective-permute-start | bytes 584 | tf_op jit(solution)/shard_map/ppermute | solution.py:60
  34.5 6.5 %collective-permute-start.5 = (f32[6,2,1,8]{3,1,2,0:T(2,128)S(1)}, f32[6,2,1,8]{3,1,2,0:T(2,128)S(1)}, u32[]{:S(2)}, u32[]{:S(2)}) collective-permute-start(f32[6,2,1,8]{3,1,2,0:T(2,128)S(1)} %maximum_select_fusion.3), channel_id=1, source_target_pairs={{0,4},{4,0},{8,12},{12,8},{1,5},{5,1},{9,13},{13,9},{2,6},{6,2},{1... | collective-permute-start | bytes 1160 | tf_op jit(solution)/shard_map/ppermute | solution.py:60
  41.0 5.2 %collective-permute-start.6 = (f32[6,2,2,8]{3,1,2,0:T(2,128)S(1)}, f32[6,2,2,8]{3,1,2,0:T(2,128)S(1)}, u32[]{:S(2)}, u32[]{:S(2)}) collective-permute-start(f32[6,2,2,8]{3,1,2,0:T(2,128)S(1)} %maximum_select_fusion.2), channel_id=1, source_target_pairs={{0,8},{4,12},{8,0},{12,4},{1,9},{5,13},{9,1},{13,5},{2,10},{6,14},... | collective-permute-start | bytes 2312 | tf_op jit(solution)/shard_map/ppermute | solution.py:60
  46.2 1.3 %collective-permute-start.7 = (f32[6,2,4,8]{3,1,2,0:T(2,128)S(1)}, f32[6,2,4,8]{3,1,2,0:T(2,128)S(1)}, u32[]{:S(2)}, u32[]{:S(2)}) collective-permute-start(f32[6,2,4,8]{3,1,2,0:T(2,128)S(1)} %maximum_select_fusion.1), channel_id=1, source_target_pairs={{0,1},{1,0},{2,3},{3,2},{4,5},{5,4},{6,7},{7,6},{8,9},{9,8},{10,11... | collective-permute-start | bytes 4616 | tf_op jit(solution)/shard_map/ppermute | solution.py:60
